TPU v7x, 512 devices: a whole 4x4x16 slice. The times are simulated.
512 devices in a mesh: seq: 128 (over y_hi, z, x), head: 4 (over y_lo, core).
Axes of the slice: x: 4, y: 4 (y_hi: 2, y_lo: 2; y = y_hi * 2 + y_lo), z: 16, core: 2. Of those that a mesh axis runs over, the one named last changes fastest.
Arguments:
- single: bfloat16 [16384, 384], P('seq'), may hold values from -6 to 6
- atoms: bfloat16 [131072, 128], P('seq'), may hold values from -6 to 6
- gain_single: float32 [384], replicated, may hold values from 0.25 to 1.75
- gain_atom: float32 [128], replicated, may hold values from 0.25 to 1.75
- w_token: bfloat16 [4, 384, 384], P(None, None, 'head'), may hold values from -0.3125 to 0.3125
- w_token_out: bfloat16 [384, 384], P('head'), may hold values from -0.3125 to 0.3125
- w_cond: bfloat16 [384, 128], replicated, may hold values from -0.3125 to 0.3125
- w_atom: bfloat16 [4, 128, 128], P(None, None, 'head'), may hold values from -0.5 to 0.5
- w_atom_out: bfloat16 [128, 128], P('head'), may hold values from -0.5 to 0.5
- pair_bias: bfloat16 [16, 16384, 512], P('head', 'seq'), may hold values from -6 to 300
- atom_bias: bfloat16 [4, 131072, 128], P('head', 'seq'), may hold values from -6 to 300
- used_blocks: int32 [128, 4], P('seq'), may hold values from 0 to 127, as said below
- used_count: int32 [128], P('seq'), may hold values from 1 to 4, as said below
- atom_counts: int32 [128, 128], P('seq'), may hold values from 1 to 24, 1024 in all within a row
- key_offset: int32 [4096], P('seq'), may hold values from -64 to -32
- grad_token: bfloat16 [16384, 384], P('seq'), may hold values from -6 to 6
- grad_atom: bfloat16 [131072, 128], P('seq'), may hold values from -6 to 6
Outputs:
- token_out: bfloat16 [16384, 384], P('seq')
- atom_out: bfloat16 [131072, 128], P('seq')
- grad_single: bfloat16 [16384, 384], P('seq')
- grad_atoms: bfloat16 [131072, 128], P('seq')
- grad_pair_bias: bfloat16 [16, 16384, 512], P('head', 'seq')
- grad_atom_bias: bfloat16 [4, 131072, 128], P('head', 'seq')
Inputs may be any that keep to these rules, and one draw needn't show every extreme that they name: `used_blocks`: for query block b the first used_count[b] entries are distinct key blocks whose shard (block) lies at most 2 shards from b's shard around the loop of 128 shards; the other entries equal b. `used_count`: some query block lists 4 key blocks. `atom_counts`: each row sums to 1024.
All inputs are finite; a program needn't handle non-finite values.
Results may differ from a plain program's by a relative error of at most 0.025.
Values may be sent and summed in bfloat16 or wider, within the bound.
No kernel may reach another device: no remote copies, remote signals or barrier semaphores. Data moves between devices by JAX's collectives and lax.ppermute only.
A program may use at most 64 MiB of HBM per device.

v0:
```python
import jax
import jax.numpy as jnp
from jax import lax
from jax.sharding import PartitionSpec as P

DH = 24
DA = 32
BLK = 128
S = 4
WIN = 2
AQ = 32
AK = 128


EPSILON = 1e-05
HIGHEST = lax.Precision.HIGHEST


def shifted(block, axis, distance):
    devices = range(lax.axis_size(axis))
    route = [((i - distance) % len(devices), i) for i in devices]
    return lax.ppermute(block, axis, route)


def extended_2(block, sides, width):
    for axis, dim in sides:
        count = lax.axis_size(axis)
        forward = [(i, i + 1) for i in range(count - 1)]
        forward.append((count - 1, 0))
        backward = [(target, source) for source, target in forward]
        low = lax.ppermute(
            lax.slice_in_dim(block, block.shape[dim] - width, None, axis=dim), axis, forward
        )
        high = lax.ppermute(lax.slice_in_dim(block, 0, width, axis=dim), axis, backward)
        block = jnp.concatenate([low, block, high], axis=dim)
    return block


def norm_rows(inputs, gains):
    row_mean = jnp.mean(inputs, axis=-1, keepdims=True)
    centred = inputs - row_mean
    variance = jnp.mean(centred * centred, axis=-1, keepdims=True)
    return centred * lax.rsqrt(variance + EPSILON) * gains


def norm_back(inputs, gains, cotangent):
    row_mean = jnp.mean(inputs, axis=-1, keepdims=True)
    centred = inputs - row_mean
    variance = jnp.mean(centred * centred, axis=-1, keepdims=True)
    inverse = lax.rsqrt(variance + EPSILON)
    standard = centred * inverse
    scaled = cotangent * gains
    return inverse * (
        scaled
        - jnp.mean(scaled, axis=-1, keepdims=True)
        - standard * jnp.mean(scaled * standard, axis=-1, keepdims=True)
    )


def attend_local(queries, key_block, value_block, bias_block, valid_keys, scaling):
    scores = (
        jnp.einsum("bqhd,bkhd->bhqk", queries, key_block, preferred_element_type=jnp.float32)
        * scaling
        + bias_block
    )
    scores = jnp.where(valid_keys[:, None, None, :], scores, -jnp.inf)
    row_max = jnp.max(scores, axis=-1, keepdims=True)
    exponent = jnp.exp(scores - row_max)
    weights = exponent / jnp.sum(exponent, axis=-1, keepdims=True)
    weights_low = weights.astype(jnp.bfloat16)
    attended = jnp.einsum(
        "bhqk,bkhd->bqhd", weights_low, value_block, preferred_element_type=jnp.float32
    )
    return (weights, weights_low, attended)


def attend_grads(
    weights, weights_low, queries, key_block, value_block, grad_out, row_delta, scaling
):
    weight_grad = jnp.einsum(
        "bqhd,bkhd->bhqk", grad_out, value_block, preferred_element_type=jnp.float32
    )
    dscore = weights * (weight_grad - row_delta[..., None])
    dscore_low = dscore.astype(jnp.bfloat16)
    dquery = (
        jnp.einsum("bhqk,bkhd->bqhd", dscore_low, key_block, preferred_element_type=jnp.float32)
        * scaling
    )
    key_grad = (
        jnp.einsum("bhqk,bqhd->bkhd", dscore_low, queries, preferred_element_type=jnp.float32)
        * scaling
    )
    dvalue = jnp.einsum(
        "bhqk,bqhd->bkhd", weights_low, grad_out, preferred_element_type=jnp.float32
    )
    return (dscore_low, dquery, key_grad, dvalue)


def body(
    single,
    atoms,
    gain_single,
    gain_atom,
    w_token,
    w_token_out,
    w_cond,
    w_atom,
    w_atom_out,
    pair_bias,
    atom_bias,
    used_blocks,
    used_count,
    atom_counts,
    key_offset,
    grad_token,
    grad_atom,
):
    device = lax.axis_index("seq")
    shards = lax.axis_size("seq")
    tok_rows = single.shape[0]
    blocks_here = tok_rows // BLK
    local_heads = w_token.shape[2] // DH
    features = local_heads * DH
    scaling = DH ** (-0.5)
    normed_low = norm_rows(single.astype(jnp.float32), gain_single).astype(jnp.bfloat16)
    projected = [
        jnp.dot(normed_low, w_token[which], preferred_element_type=jnp.float32)
        for which in range(4)
    ]
    queries = projected[0].astype(jnp.bfloat16)
    gate_act = jax.nn.sigmoid(projected[3])
    key_value = jnp.concatenate(
        [projected[1].astype(jnp.bfloat16), projected[2].astype(jnp.bfloat16)], axis=1
    )
    owner_dev = used_blocks // blocks_here
    relative = jnp.mod(owner_dev - device, shards)
    relative = jnp.where(relative > shards // 2, relative - shards, relative)
    pieces = [key_value for distance in range(-WIN, WIN + 1)]
    for distance in range(-WIN, WIN + 1):
        if distance != 0:
            pieces[distance + WIN] = shifted(key_value, "seq", -distance)
    window = jnp.stack(pieces)
    candidates = (2 * WIN + 1) * blocks_here
    window_flat = window.reshape(candidates, BLK * 2 * features)
    picked = (relative + WIN) * blocks_here + used_blocks % blocks_here
    selector_mask = picked[:, :, None] == jnp.arange(candidates, dtype=jnp.int32)[None, None, :]
    selector = selector_mask.astype(jnp.bfloat16)
    stashed = jnp.einsum(
        "bsc,cx->bsx", selector, window_flat, preferred_element_type=jnp.float32
    ).astype(jnp.bfloat16)
    stashed = stashed.reshape(blocks_here, S, BLK, 2 * features)
    key_blocks = stashed[..., :features].reshape(blocks_here, S * BLK, local_heads, DH)
    value_blocks = stashed[..., features:].reshape(blocks_here, S * BLK, local_heads, DH)
    query_blocks = queries.reshape(blocks_here, BLK, local_heads, DH)
    bias_blocks = (
        pair_bias.reshape(local_heads, blocks_here, BLK, S * BLK)
        .transpose(1, 0, 2, 3)
        .astype(jnp.float32)
    )
    valid_keys = jnp.repeat(
        jnp.arange(S, dtype=jnp.int32)[None, :] < used_count[:, None], BLK, axis=1
    )
    weights, weights_low, attended = attend_local(
        query_blocks, key_blocks, value_blocks, bias_blocks, valid_keys, scaling
    )
    attended = attended.reshape(tok_rows, features)
    token_part = jnp.dot(
        (attended * gate_act).astype(jnp.bfloat16), w_token_out, preferred_element_type=jnp.float32
    )
    grad_gated = jnp.dot(grad_token, w_token_out.T, preferred_element_type=jnp.float32)
    grad_attended = (grad_gated * gate_act).astype(jnp.bfloat16)
    grad_gate = (grad_gated * attended * gate_act * (1.0 - gate_act)).astype(jnp.bfloat16)
    row_delta = jnp.sum(
        (grad_attended.astype(jnp.float32) * attended).reshape(blocks_here, BLK, local_heads, DH),
        axis=-1,
    ).transpose(0, 2, 1)
    score_low, dquery, key_grad, dvalue = attend_grads(
        weights,
        weights_low,
        query_blocks,
        key_blocks,
        value_blocks,
        grad_attended.reshape(blocks_here, BLK, local_heads, DH),
        row_delta,
        scaling,
    )
    grad_pair = score_low.transpose(1, 0, 2, 3).reshape(local_heads, tok_rows, S * BLK)
    returned = jnp.concatenate(
        [
            key_grad.reshape(blocks_here, S, BLK, features),
            dvalue.reshape(blocks_here, S, BLK, features),
        ],
        axis=-1,
    )
    returned_flat = returned.reshape(blocks_here, S, BLK * 2 * features)
    outgoing = jnp.einsum(
        "bsc,bsx->cx", selector_mask.astype(jnp.float32), returned_flat, precision=HIGHEST
    )
    outgoing = outgoing.reshape(2 * WIN + 1, tok_rows, 2 * features)
    collected = outgoing[WIN]
    for distance in range(-WIN, WIN + 1):
        if distance != 0:
            collected = collected + shifted(
                outgoing[distance + WIN].astype(jnp.bfloat16), "seq", distance
            ).astype(jnp.float32)
    token_grads = [
        dquery.reshape(tok_rows, features).astype(jnp.bfloat16),
        collected[:, :features].astype(jnp.bfloat16),
        collected[:, features:].astype(jnp.bfloat16),
        grad_gate,
    ]
    w_atom_all, w_atom_out_all, atom_bias_all = (w_atom, w_atom_out, atom_bias)
    atom_rows = atoms.shape[0]
    heads_atom = w_atom_all.shape[2] // DA
    atom_feat = heads_atom * DA
    halo_rows = AK // 2
    windows_here = atom_rows // AQ
    group_span = AK // AQ + 1
    slab_rows = group_span * AQ
    atom_scaling = DA ** (-0.5)
    normed_atoms = norm_rows(atoms.astype(jnp.float32), gain_atom)
    counts = atom_counts[0]
    ends = jnp.cumsum(counts)
    atom_place = jnp.arange(atom_rows, dtype=jnp.int32)
    token_local = jnp.sum((ends[None, :] <= atom_place[:, None]).astype(jnp.int32), axis=1)
    token_pick = (token_local[:, None] == jnp.arange(tok_rows, dtype=jnp.int32)[None, :]).astype(
        jnp.float32
    )
    condition = jnp.dot(normed_low, w_cond, preferred_element_type=jnp.float32)
    atom_input = (normed_atoms + jnp.dot(token_pick, condition, precision=HIGHEST)).astype(
        jnp.bfloat16
    )
    atom_proj = [
        jnp.dot(atom_input, w_atom_all[which], preferred_element_type=jnp.float32)
        for which in range(4)
    ]
    atom_gate = jax.nn.sigmoid(atom_proj[3])
    atom_kv = jnp.concatenate(
        [atom_proj[1].astype(jnp.bfloat16), atom_proj[2].astype(jnp.bfloat16)], axis=1
    )
    extended = extended_2(atom_kv, (("seq", 0),), halo_rows)
    ext_groups = extended.reshape(windows_here + AK // AQ, AQ, 2 * atom_feat)
    slabs = jnp.concatenate(
        [ext_groups[step : step + windows_here] for step in range(group_span)], axis=1
    )
    shift_here = key_offset + halo_rows
    placer_mask = (
        jnp.arange(slab_rows, dtype=jnp.int32)[None, None, :]
        == jnp.arange(AK, dtype=jnp.int32)[None, :, None] + shift_here[:, None, None]
    )
    window_kv = jnp.einsum(
        "wrs,wsf->wrf", placer_mask.astype(jnp.bfloat16), slabs, preferred_element_type=jnp.float32
    ).astype(jnp.bfloat16)
    atom_keys = window_kv[..., :atom_feat].reshape(windows_here, AK, heads_atom, DA)
    atom_values = window_kv[..., atom_feat:].reshape(windows_here, AK, heads_atom, DA)
    atom_queries = atom_proj[0].astype(jnp.bfloat16).reshape(windows_here, AQ, heads_atom, DA)
    atom_bias_blocks = (
        atom_bias_all.reshape(heads_atom, windows_here, AQ, AK)
        .transpose(1, 0, 2, 3)
        .astype(jnp.float32)
    )
    all_valid = jnp.ones((windows_here, AK), dtype=bool)
    aweights, aweights_low, atom_attended = attend_local(
        atom_queries, atom_keys, atom_values, atom_bias_blocks, all_valid, atom_scaling
    )
    atom_attended = atom_attended.reshape(atom_rows, atom_feat)
    atom_part = jnp.dot(
        (atom_attended * atom_gate).astype(jnp.bfloat16),
        w_atom_out_all,
        preferred_element_type=jnp.float32,
    )
    agrad_gated = jnp.dot(grad_atom, w_atom_out_all.T, preferred_element_type=jnp.float32)
    agrad_attended = (agrad_gated * atom_gate).astype(jnp.bfloat16)
    agrad_gate = (agrad_gated * atom_attended * atom_gate * (1.0 - atom_gate)).astype(jnp.bfloat16)
    atom_delta = jnp.sum(
        (agrad_attended.astype(jnp.float32) * atom_attended).reshape(
            windows_here, AQ, heads_atom, DA
        ),
        axis=-1,
    ).transpose(0, 2, 1)
    ascore_low, aquery_grad, akey_grad, avalue_grad = attend_grads(
        aweights,
        aweights_low,
        atom_queries,
        atom_keys,
        atom_values,
        agrad_attended.reshape(windows_here, AQ, heads_atom, DA),
        atom_delta,
        atom_scaling,
    )
    grad_abias = ascore_low.transpose(1, 0, 2, 3).reshape(heads_atom, atom_rows, AK)
    spread_grads = jnp.concatenate(
        [
            akey_grad.reshape(windows_here, AK, atom_feat),
            avalue_grad.reshape(windows_here, AK, atom_feat),
        ],
        axis=-1,
    )
    slab_grads = jnp.einsum(
        "wrs,wrf->wsf", placer_mask.astype(jnp.float32), spread_grads, precision=HIGHEST
    )
    slab_grads = slab_grads.reshape(windows_here, group_span, AQ, 2 * atom_feat)
    ext_grad = jnp.pad(slab_grads[:, 0], ((0, group_span - 1), (0, 0), (0, 0)))
    for step in range(1, group_span):
        ext_grad = ext_grad + jnp.pad(
            slab_grads[:, step], ((step, group_span - 1 - step), (0, 0), (0, 0))
        )
    ext_grad = ext_grad.reshape(atom_rows + 2 * halo_rows, 2 * atom_feat)
    rims = jnp.concatenate([ext_grad[:halo_rows], ext_grad[atom_rows + halo_rows :]], axis=0)
    edges = extended_2(rims.astype(jnp.bfloat16), (("seq", 0),), halo_rows).astype(rims.dtype)
    own_grad = ext_grad[halo_rows : halo_rows + atom_rows]
    own_grad = jnp.concatenate(
        [
            own_grad[:halo_rows] + edges[:halo_rows],
            own_grad[halo_rows : atom_rows - halo_rows],
            own_grad[atom_rows - halo_rows :] + edges[3 * halo_rows :],
        ],
        axis=0,
    )
    atom_grads = [
        aquery_grad.reshape(atom_rows, atom_feat).astype(jnp.bfloat16),
        own_grad[:, :atom_feat].astype(jnp.bfloat16),
        own_grad[:, atom_feat:].astype(jnp.bfloat16),
        agrad_gate,
    ]
    agrad_input = jnp.dot(atom_grads[0], w_atom_all[0].T, preferred_element_type=jnp.float32)
    for which in range(1, 4):
        agrad_input = agrad_input + jnp.dot(
            atom_grads[which], w_atom_all[which].T, preferred_element_type=jnp.float32
        )
    atoms_part = norm_back(atoms.astype(jnp.float32), gain_atom, agrad_input)
    cond_grad = jnp.dot(token_pick.T, agrad_input, precision=HIGHEST)
    cond_term = jnp.dot(cond_grad, w_cond.astype(jnp.float32).T, precision=HIGHEST)
    grad_normed = cond_term
    for which in range(4):
        grad_normed = grad_normed + jnp.dot(
            token_grads[which], w_token[which].T, preferred_element_type=jnp.float32
        )
    single_part = norm_back(single.astype(jnp.float32), gain_single, grad_normed)
    token_total, atom_total, single_total, atoms_total = (
        lax.psum(token_part.astype(jnp.bfloat16), "head").astype(jnp.float32),
        lax.psum(atom_part.astype(jnp.bfloat16), "head").astype(jnp.float32),
        lax.psum(single_part.astype(jnp.bfloat16), "head").astype(jnp.float32),
        lax.psum(atoms_part.astype(jnp.bfloat16), "head").astype(jnp.float32),
    )
    return (
        token_total.astype(jnp.bfloat16),
        atom_total.astype(jnp.bfloat16),
        single_total.astype(jnp.bfloat16),
        atoms_total.astype(jnp.bfloat16),
        grad_pair,
        grad_abias,
    )


def solution(mesh):
    return jax.shard_map(
        body,
        mesh=mesh,
        in_specs=(
            P("seq", None),
            P("seq", None),
            P(),
            P(),
            P(None, None, "head"),
            P("head", None),
            P(),
            P(None, None, "head"),
            P("head", None),
            P("head", "seq", None),
            P("head", "seq", None),
            P("seq", None),
            P("seq"),
            P("seq", None),
            P("seq"),
            P("seq", None),
            P("seq", None),
        ),
        out_specs=(
            P("seq", None),
            P("seq", None),
            P("seq", None),
            P("seq", None),
            P("head", "seq", None),
            P("head", "seq", None),
        ),
        check_vma=False,
    )
```

profile of v0, /device:TPU:1, one launch (start us, length us, event | category | flops | bytes accessed | tf_op | source)
XLA Modules:
  0.0 196.9 jit_solution(16144267644967217117)
XLA Ops:
  13.7 5.5 %collective-permute-start = (bf16[128,192]{0,1:T(8,128)(2,1)}, bf16[128,192]{0,1:T(8,128)(2,1)}, u32[]{:S(2)}, u32[]{:S(2)}) collective-permute-start(bf16[128,192]{0,1:T(8,128)(2,1)} %pad_maximum_fusion.3), channel_id=1, source_target_pairs={{504,0},{508,4},{0,8},{4,12},{8,16},{12,20},{16,24},{20,28},{24,32... | collective-permute-start | bytes 147464 | tf_op jit(solution)/shard_map/ppermute | solution.py:22
  19.2 2.2 %collective-permute-start.1 = (bf16[128,192]{0,1:T(8,128)(2,1)}, bf16[128,192]{0,1:T(8,128)(2,1)}, u32[]{:S(2)}, u32[]{:S(2)}) collective-permute-start(bf16[128,192]{0,1:T(8,128)(2,1)} %pad_maximum_fusion.3), channel_id=1, source_target_pairs={{508,0},{0,4},{4,8},{8,12},{12,16},{16,20},{20,24},{24,28},{28,32}... | collective-permute-start | bytes 147464 | tf_op jit(solution)/shard_map/ppermute | solution.py:22
  21.4 12.9 %collective-permute-start.2 = (bf16[128,192]{0,1:T(8,128)(2,1)}, bf16[128,192]{0,1:T(8,128)(2,1)}, u32[]{:S(2)}, u32[]{:S(2)}) collective-permute-start(bf16[128,192]{0,1:T(8,128)(2,1)} %pad_maximum_fusion.3), channel_id=1, source_target_pairs={{4,0},{8,4},{12,8},{16,12},{20,16},{24,20},{28,24},{32,28},{36,32}... | collective-permute-start | bytes 147464 | tf_op jit(solution)/shard_map/ppermute | solution.py:22
  39.1 1.4 fusion.19
  41.1 1.9 collective-permute-start.4
  43.0 9.1 %collective-permute-start.5 = (bf16[64,64]{0,1:T(8,128)(2,1)S(1)}, bf16[64,64]{0,1:T(8,128)(2,1)S(1)}, u32[]{:S(2)}, u32[]{:S(2)}) collective-permute-start(bf16[64,64]{0,1:T(8,128)(2,1)S(1)} %get-tuple-element.42), channel_id=1, source_target_pairs={{4,0},{8,4},{12,8},{16,12},{20,16},{24,20},{28,24},{32,28},{36,32}... | collective-permute-start | bytes 24584 | tf_op jit(solution)/shard_map/ppermute | solution.py:34
  62.7 2.3 %concatenate.38 = bf16[32,160,64]{1,2,0:T(8,128)(2,1)} concatenate(bf16[32,32,64]{1,2,0:T(8,128)(2,1)S(1)} %copy.91, bf16[32,32,64]{1,2,0:T(8,128)(2,1)S(1)} %copy.92, bf16[32,32,64]{1,2,0:T(8,128)(2,1)S(1)} %copy.93, bf16[32,32,64]{1,2,0:T(8,128)(2,1)S(1)} %copy.94, bf16[32,32,64]{1,2,0:T(8,128)(2,1)S(1)} %copy.95), dimensions={1} | concatenate | bytes 1310720 | tf_op jit(solution)/shard_map/concatenate | solution.py:243
  65.0 1.9 fusion.11
  68.1 5.4 %fusion.136 = (f32[32,32]{1,0:T(8,128)S(1)}, f32[32,32,128]{2,1,0:T(8,128)S(1)}) fusion(f32[32,32,128]{2,1,0:T(8,128)S(1)} %fusion.17), kind=kOutput, calls=%fused_computation.227 | output fusion | flops 262271 | bytes 1052672 | tf_op jit(solution)/shard_map/sub | solution.py:68
  73.5 1.8 convolution_bitcast_fusion.1
  76.4 1.8 convolution_bitcast_fusion
  80.2 1.5 fusion.2
  82.4 1.9 collective-permute-start.6
  84.3 9.4 %collective-permute-start.7 = (bf16[64,64]{1,0:T(8,128)(2,1)S(1)}, bf16[64,64]{1,0:T(8,128)(2,1)S(1)}, u32[]{:S(2)}, u32[]{:S(2)}) collective-permute-start(bf16[64,64]{1,0:T(8,128)(2,1)S(1)} %bitcast.234), channel_id=1, source_target_pairs={{4,0},{8,4},{12,8},{16,12},{20,16},{24,20},{28,24},{32,28},{36,32}... | collective-permute-start | bytes 24584 | tf_op jit(solution)/shard_map/ppermute | solution.py:34
  94.4 1.9 collective-permute-start.3
  110.4 2.5 %collective-permute-start.10 = (bf16[128,192]{1,0:T(8,128)(2,1)S(1)}, bf16[128,192]{1,0:T(8,128)(2,1)S(1)}, u32[]{:S(2)}, u32[]{:S(2)}) collective-permute-start(bf16[128,192]{1,0:T(8,128)(2,1)S(1)} %convert_element_type.231), channel_id=1, source_target_pairs={{508,0},{0,4},{4,8},{8,12},{12,16},{16,20},{20,24},{24,28},{28,32}... | collective-permute-start | bytes 147464 | tf_op jit(solution)/shard_map/ppermute | solution.py:22
  113.0 4.3 %collective-permute-start.11 = (bf16[128,192]{1,0:T(8,128)(2,1)S(1)}, bf16[128,192]{1,0:T(8,128)(2,1)S(1)}, u32[]{:S(2)}, u32[]{:S(2)}) collective-permute-start(bf16[128,192]{1,0:T(8,128)(2,1)S(1)} %convert_element_type.233), channel_id=1, source_target_pairs={{504,0},{508,4},{0,8},{4,12},{8,16},{12,20},{16,24},{20,28},{24,32... | collective-permute-start | bytes 147464 | tf_op jit(solution)/shard_map/ppermute | solution.py:22
  117.4 7.0 %collective-permute-start.8 = (bf16[128,192]{1,0:T(8,128)(2,1)S(1)}, bf16[128,192]{1,0:T(8,128)(2,1)S(1)}, u32[]{:S(2)}, u32[]{:S(2)}) collective-permute-start(bf16[128,192]{1,0:T(8,128)(2,1)S(1)} %convert_element_type.227), channel_id=1, source_target_pairs={{8,0},{12,4},{16,8},{20,12},{24,16},{28,20},{32,24},{36,28},{40,32... | collective-permute-start | bytes 147464 | tf_op jit(solution)/shard_map/ppermute | solution.py:22
  124.5 4.0 %collective-permute-start.9 = (bf16[128,192]{1,0:T(8,128)(2,1)S(1)}, bf16[128,192]{1,0:T(8,128)(2,1)S(1)}, u32[]{:S(2)}, u32[]{:S(2)}) collective-permute-start(bf16[128,192]{1,0:T(8,128)(2,1)S(1)} %convert_element_type.229), channel_id=1, source_target_pairs={{4,0},{8,4},{12,8},{16,12},{20,16},{24,20},{28,24},{32,28},{36,32}... | collective-permute-start | bytes 147464 | tf_op jit(solution)/shard_map/ppermute | solution.py:22
  131.9 51.7 %all-reduce.8.cloned.1.call-done = (bf16[128,384]{1,0:T(8,128)(2,1)}, bf16[1024,128]{1,0:T(8,128)(2,1)}, bf16[128,384]{1,0:T(8,128)(2,1)}, bf16[1024,128]{1,0:T(8,128)(2,1)}) async-done(((bf16[128,384]{1,0:T(8,128)(2,1)}, bf16[1024,128]{1,0:T(8,128)(2,1)}, bf16[128,384]{1,0:T(8,128)(2,1)}, bf16[1024,128]{1,0:T(8,128)(2,1)}), (bf16[128,384]{1,0:T(8,128)(2,1)}, bf16[1024,128]{1,0:T(8,128)(2,1)}, ...) | async-done | bytes 720912 | tf_op jit(solution)/shard_map/psum | solution.py:341
  183.6 1.5 copy.135
  185.1 1.7 copy.136
  186.8 1.5 copy.137
  188.3 1.7 copy.138
  (187 shorter events, 44.2 us)
Async XLA Ops:
  7.2 68.8 %copy-start = (bf16[1024,128]{1,0:T(8,128)(2,1)S(1)}, bf16[1024,128]{1,0:T(8,128)(2,1)}, u32[]{:S(2)}) copy-start(bf16[1024,128]{1,0:T(8,128)(2,1)} %param.33) | copy-start | bytes 786436
  7.2 45.3 %copy-start.5 = (bf16[4,384,96]{1,2,0:T(8,128)(2,1)S(1)}, bf16[4,384,96]{1,2,0:T(8,128)(2,1)}, u32[]{:S(2)}) copy-start(bf16[4,384,96]{1,2,0:T(8,128)(2,1)} %param.21) | copy-start | bytes 884740
  7.2 33.4 %copy-start.10 = (bf16[4,128,32]{1,2,0:T(8,128)(2,1)S(1)}, bf16[4,128,32]{1,2,0:T(8,128)(2,1)}, u32[]{:S(2)}) copy-start(bf16[4,128,32]{1,2,0:T(8,128)(2,1)} %param.24) | copy-start | bytes 98308
  7.2 46.9 %copy-start.23 = (s32[32]{0:T(128)S(1)}, s32[32]{0:T(128)}, u32[]{:S(2)}) copy-start(s32[32]{0:T(128)} %param.31) | copy-start | bytes 388
  7.2 176.4 %all-reduce.8.cloned.1.call-start = ((), (), s32[]{:S(2)}) async-start(), calls=%async_computation | async-start | bytes 1441792 | tf_op jit(solution)/shard_map/psum | solution.py:341
  8.3 47.7 %copy-start.24 = (s32[1,4]{1,0:T(1,128)S(1)}, s32[1,4]{1,0:T(1,128)}, u32[]{:S(2)}) copy-start(s32[1,4]{1,0:T(1,128)} %param.28) | copy-start | bytes 52
  13.7 86.2 %collective-permute-start = (bf16[128,192]{0,1:T(8,128)(2,1)}, bf16[128,192]{0,1:T(8,128)(2,1)}, u32[]{:S(2)}, u32[]{:S(2)}) collective-permute-start(bf16[128,192]{0,1:T(8,128)(2,1)} %pad_maximum_fusion.3), channel_id=1, source_target_pairs={{504,0},{508,4},{0,8},{4,12},{8,16},{12,20},{16,24},{20,28},{24,32... | collective-permute-start | bytes 147464 | tf_op jit(solution)/shard_map/ppermute | solution.py:22
  19.2 81.8 %collective-permute-start.1 = (bf16[128,192]{0,1:T(8,128)(2,1)}, bf16[128,192]{0,1:T(8,128)(2,1)}, u32[]{:S(2)}, u32[]{:S(2)}) collective-permute-start(bf16[128,192]{0,1:T(8,128)(2,1)} %pad_maximum_fusion.3), channel_id=1, source_target_pairs={{508,0},{0,4},{4,8},{8,12},{12,16},{16,20},{20,24},{24,28},{28,32}... | collective-permute-start | bytes 147464 | tf_op jit(solution)/shard_map/ppermute | solution.py:22
  21.4 80.6 %collective-permute-start.2 = (bf16[128,192]{0,1:T(8,128)(2,1)}, bf16[128,192]{0,1:T(8,128)(2,1)}, u32[]{:S(2)}, u32[]{:S(2)}) collective-permute-start(bf16[128,192]{0,1:T(8,128)(2,1)} %pad_maximum_fusion.3), channel_id=1, source_target_pairs={{4,0},{8,4},{12,8},{16,12},{20,16},{24,20},{28,24},{32,28},{36,32}... | collective-permute-start | bytes 147464 | tf_op jit(solution)/shard_map/ppermute | solution.py:22
  41.1 17.9 %collective-permute-start.4 = (bf16[64,64]{0,1:T(8,128)(2,1)S(1)}, bf16[64,64]{0,1:T(8,128)(2,1)S(1)}, u32[]{:S(2)}, u32[]{:S(2)}) collective-permute-start(bf16[64,64]{0,1:T(8,128)(2,1)S(1)} %get-tuple-element.43), channel_id=1, source_target_pairs={{0,4},{4,8},{8,12},{12,16},{16,20},{20,24},{24,28},{28,32},{32,36}... | collective-permute-start | bytes 24584 | tf_op jit(solution)/shard_map/ppermute | solution.py:31
  43.0 16.0 %collective-permute-start.5 = (bf16[64,64]{0,1:T(8,128)(2,1)S(1)}, bf16[64,64]{0,1:T(8,128)(2,1)S(1)}, u32[]{:S(2)}, u32[]{:S(2)}) collective-permute-start(bf16[64,64]{0,1:T(8,128)(2,1)S(1)} %get-tuple-element.42), channel_id=1, source_target_pairs={{4,0},{8,4},{12,8},{16,12},{20,16},{24,20},{28,24},{32,28},{36,32}... | collective-permute-start | bytes 24584 | tf_op jit(solution)/shard_map/ppermute | solution.py:34
  82.4 12.1 %collective-permute-start.6 = (bf16[64,64]{1,0:T(8,128)(2,1)S(1)}, bf16[64,64]{1,0:T(8,128)(2,1)S(1)}, u32[]{:S(2)}, u32[]{:S(2)}) collective-permute-start(bf16[64,64]{1,0:T(8,128)(2,1)S(1)} %bitcast.232), channel_id=1, source_target_pairs={{0,4},{4,8},{8,12},{12,16},{16,20},{20,24},{24,28},{28,32},{32,36}... | collective-permute-start | bytes 24584 | tf_op jit(solution)/shard_map/ppermute | solution.py:31
  84.3 12.7 %copy-start.1 = (bf16[1024,128]{1,0:T(8,128)(2,1)S(1)}, bf16[1024,128]{1,0:T(8,128)(2,1)}, u32[]{:S(2)}) copy-start(bf16[1024,128]{1,0:T(8,128)(2,1)} %param.18) | copy-start | bytes 786436
  84.3 12.1 %collective-permute-start.7 = (bf16[64,64]{1,0:T(8,128)(2,1)S(1)}, bf16[64,64]{1,0:T(8,128)(2,1)S(1)}, u32[]{:S(2)}, u32[]{:S(2)}) collective-permute-start(bf16[64,64]{1,0:T(8,128)(2,1)S(1)} %bitcast.234), channel_id=1, source_target_pairs={{4,0},{8,4},{12,8},{16,12},{20,16},{24,20},{28,24},{32,28},{36,32}... | collective-permute-start | bytes 24584 | tf_op jit(solution)/shard_map/ppermute | solution.py:34
  94.4 8.6 %collective-permute-start.3 = (bf16[128,192]{0,1:T(8,128)(2,1)}, bf16[128,192]{0,1:T(8,128)(2,1)S(1)}, u32[]{:S(2)}, u32[]{:S(2)}) collective-permute-start(bf16[128,192]{0,1:T(8,128)(2,1)} %pad_maximum_fusion.3), channel_id=1, source_target_pairs={{8,0},{12,4},{16,8},{20,12},{24,16},{28,20},{32,24},{36,28},{40,32... | collective-permute-start | bytes 147464 | tf_op jit(solution)/shard_map/ppermute | solution.py:22
  107.9 20.7 %copy-start.6 = (bf16[4,384,96]{1,2,0:T(8,128)(2,1)S(1)}, bf16[4,384,96]{1,2,0:T(8,128)(2,1)}, u32[]{:S(2)}) copy-start(bf16[4,384,96]{1,2,0:T(8,128)(2,1)} %param.21) | copy-start | bytes 884740
  108.0 21.6 %copy-start.8 = (bf16[384,128]{1,0:T(8,128)(2,1)S(1)}, bf16[384,128]{1,0:T(8,128)(2,1)}, u32[]{:S(2)}) copy-start(bf16[384,128]{1,0:T(8,128)(2,1)} %param.23) | copy-start | bytes 294916
  108.6 22.2 %copy-start.2 = (bf16[128,384]{1,0:T(8,128)(2,1)S(1)}, bf16[128,384]{1,0:T(8,128)(2,1)}, u32[]{:S(2)}) copy-start(bf16[128,384]{1,0:T(8,128)(2,1)} %param.17) | copy-start | bytes 294916
  108.6 22.2 %copy-start.17 = (f32[384]{0:T(512)S(1)}, f32[384]{0:T(512)}, u32[]{:S(2)}) copy-start(f32[384]{0:T(512)} %param.19) | copy-start | bytes 4612
  108.6 22.2 %copy-start.19 = (f32[128]{0:T(128)S(1)}, f32[128]{0:T(128)}, u32[]{:S(2)}) copy-start(f32[128]{0:T(128)} %copy-done.18) | copy-start | bytes 1540
  110.4 19.9 %collective-permute-start.10 = (bf16[128,192]{1,0:T(8,128)(2,1)S(1)}, bf16[128,192]{1,0:T(8,128)(2,1)S(1)}, u32[]{:S(2)}, u32[]{:S(2)}) collective-permute-start(bf16[128,192]{1,0:T(8,128)(2,1)S(1)} %convert_element_type.231), channel_id=1, source_target_pairs={{508,0},{0,4},{4,8},{8,12},{12,16},{16,20},{20,24},{24,28},{28,32}... | collective-permute-start | bytes 147464 | tf_op jit(solution)/shard_map/ppermute | solution.py:22
  113.0 17.3 %collective-permute-start.11 = (bf16[128,192]{1,0:T(8,128)(2,1)S(1)}, bf16[128,192]{1,0:T(8,128)(2,1)S(1)}, u32[]{:S(2)}, u32[]{:S(2)}) collective-permute-start(bf16[128,192]{1,0:T(8,128)(2,1)S(1)} %convert_element_type.233), channel_id=1, source_target_pairs={{504,0},{508,4},{0,8},{4,12},{8,16},{12,20},{16,24},{20,28},{24,32... | collective-permute-start | bytes 147464 | tf_op jit(solution)/shard_map/ppermute | solution.py:22
  117.4 12.9 %collective-permute-start.8 = (bf16[128,192]{1,0:T(8,128)(2,1)S(1)}, bf16[128,192]{1,0:T(8,128)(2,1)S(1)}, u32[]{:S(2)}, u32[]{:S(2)}) collective-permute-start(bf16[128,192]{1,0:T(8,128)(2,1)S(1)} %convert_element_type.227), channel_id=1, source_target_pairs={{8,0},{12,4},{16,8},{20,12},{24,16},{28,20},{32,24},{36,28},{40,32... | collective-permute-start | bytes 147464 | tf_op jit(solution)/shard_map/ppermute | solution.py:22
  124.5 5.8 %collective-permute-start.9 = (bf16[128,192]{1,0:T(8,128)(2,1)S(1)}, bf16[128,192]{1,0:T(8,128)(2,1)S(1)}, u32[]{:S(2)}, u32[]{:S(2)}) collective-permute-start(bf16[128,192]{1,0:T(8,128)(2,1)S(1)} %convert_element_type.229), channel_id=1, source_target_pairs={{4,0},{8,4},{12,8},{16,12},{20,16},{24,20},{28,24},{32,28},{36,32}... | collective-permute-start | bytes 147464 | tf_op jit(solution)/shard_map/ppermute | solution.py:22
  (15 other events, 76.8 us)
Sparse Core Ops, SparseCore 0:
  132.0 51.4 all-reduce.7
where the time goes:
time: 198 us; the launch traced here: 197 us
  starting transfers between devices  62.7 us (32%)
  waiting for transfers between devices  51.7 us (26%)
  local copies, waits for them, and re-layouts  25.5 us (13%)
  matrix products  24.7 us (12%)
  other arithmetic  16.5 us (8%)
  between operations  15.8 us (8%)
    psum x1, waiting for transfers between devices, body(): lax.psum(token_part.astype(jnp.bfloat16), 'head').astype(jnp.float32)  51.7 us
    ppermute x8, starting transfers between devices, shifted(): return lax.ppermute(block, axis, route)  40.3 us
    ppermute x2, starting transfers between devices, extended_2(): lax.ppermute(lax.slice_in_dim(block, 0, width, axis=dim), axis, backward)  18.5 us
    unnamed x56, local copies, waits for them, and re-layouts  7.1 us
    sub x1, other arithmetic, attend_local(): exponent = jnp.exp(scores - row_max)  5.4 us
  transfers between devices with their start and end apart: 13, of which 1 were waited for; matrix products, arithmetic and copies ran while one was open for 23% of the time, Pallas kernels for 0%

commit v1 on v0

--- a/solution.py
+++ b/solution.py
@@ -34,6 +34,49 @@
         high = lax.ppermute(lax.slice_in_dim(block, 0, width, axis=dim), axis, backward)
         block = jnp.concatenate([low, block, high], axis=dim)
     return block
+
+
+def head_sum(parts, axis):
+    count = lax.axis_size(axis)
+    if count != 4:
+        return [lax.psum(p.astype(jnp.bfloat16), axis) for p in parts]
+    pieces = []
+    for part in parts:
+        for col in range(part.shape[1] // 128):
+            pieces.append(part[:, col * 128 : (col + 1) * 128])
+    buf = jnp.concatenate(pieces, axis=0)
+    rows = buf.shape[0]
+    place = lax.axis_index(axis)
+    low_bit = place % 2
+    high_bit = (place // 2) % 2
+    pair_near = [(i, i ^ 1) for i in range(count)]
+    pair_far = [(i, i ^ 2) for i in range(count)]
+    halves = buf.reshape(2, rows // 2, 128)
+    keep = jnp.where(low_bit == 0, halves[0], halves[1])
+    give = jnp.where(low_bit == 0, halves[1], halves[0])
+    got = lax.ppermute(give.astype(jnp.bfloat16), axis, pair_near)
+    summed = (keep + got.astype(jnp.float32)).reshape(2, rows // 4, 128)
+    keep = jnp.where(high_bit == 0, summed[0], summed[1])
+    give = jnp.where(high_bit == 0, summed[1], summed[0])
+    got = lax.ppermute(give.astype(jnp.bfloat16), axis, pair_far)
+    own = (keep + got.astype(jnp.float32)).astype(jnp.bfloat16)
+    got = lax.ppermute(own, axis, pair_far)
+    half = jnp.where(
+        high_bit == 0, jnp.concatenate([own, got], axis=0), jnp.concatenate([got, own], axis=0)
+    )
+    got = lax.ppermute(half, axis, pair_near)
+    full = jnp.where(
+        low_bit == 0, jnp.concatenate([half, got], axis=0), jnp.concatenate([got, half], axis=0)
+    )
+    outs = []
+    start = 0
+    for part in parts:
+        width = part.shape[1] // 128
+        rows_here = part.shape[0]
+        cols = [full[start + k * rows_here : start + (k + 1) * rows_here] for k in range(width)]
+        start += width * rows_here
+        outs.append(jnp.concatenate(cols, axis=1) if width > 1 else cols[0])
+    return outs
 
 
 def norm_rows(inputs, gains):
@@ -337,11 +380,8 @@
             token_grads[which], w_token[which].T, preferred_element_type=jnp.float32
         )
     single_part = norm_back(single.astype(jnp.float32), gain_single, grad_normed)
-    token_total, atom_total, single_total, atoms_total = (
-        lax.psum(token_part.astype(jnp.bfloat16), "head").astype(jnp.float32),
-        lax.psum(atom_part.astype(jnp.bfloat16), "head").astype(jnp.float32),
-        lax.psum(single_part.astype(jnp.bfloat16), "head").astype(jnp.float32),
-        lax.psum(atoms_part.astype(jnp.bfloat16), "head").astype(jnp.float32),
+    token_total, atom_total, single_total, atoms_total = head_sum(
+        [token_part, atom_part, single_part, atoms_part], "head"
     )
     return (
         token_total.astype(jnp.bfloat16),

time: 198 us -> 154 us (0.78)
  waiting for transfers between devices: 51.7 us -> 18.6 us
  between operations: 15.8 us -> 2.57 us
  starting transfers between devices: 62.7 us -> 70.9 us
  local copies, waits for them, and re-layouts: 25.5 us -> 19.6 us
  matrix products: 24.7 us -> 28.7 us
  other arithmetic: 16.5 us -> 12.5 us
    psum x1 -> x0, waiting for transfers between devices: 51.7 us -> none  [body(): lax.psum(token_part.astype(jnp.bfloat16), 'head').astype(jnp.float32)]
    ppermute x0 -> x4, starting transfers between devices: none -> 14.6 us  [the longest x1 5.96 us: head_sum(): got = lax.ppermute(give.astype(jnp.bfloat16), axis, pair_near)]
    ppermute x0 -> x4, waiting for transfers between devices: none -> 12.3 us  [the longest x1 5.35 us: head_sum(): got = lax.ppermute(give.astype(jnp.bfloat16), axis, pair_far)]
    ppermute x2, starting transfers between devices: 18.5 us -> 11.2 us  [extended_2(): lax.ppermute(lax.slice_in_dim(block, 0, width, axis=dim), axis, backward)]
    unnamed x56, local copies, waits for them, and re-layouts: 7.1 us -> 0.69 us
    ppermute x2, waiting for transfers between devices: 0.01 us -> 6.3 us  [extended_2(): lax.ppermute(lax.slice_in_dim(block, block.shape[dim] - width, None, axis...]
    sub x1, other arithmetic: 5.4 us -> 1.01 us  [attend_local(): exponent = jnp.exp(scores - row_max)]
  transfers between devices with their start and end apart: 13 -> 16, of which waited for: 1 -> 6; matrix products, arithmetic and copies ran while one was open for 23% -> 26% of each run, Pallas kernels for 0% -> 0%
where the time goes in v1:
time: 154 us; the launch traced here: 153 us
  starting transfers between devices  70.9 us (46%)
  matrix products  28.7 us (19%)
  local copies, waits for them, and re-layouts  19.6 us (13%)
  waiting for transfers between devices  18.6 us (12%)
  other arithmetic  12.5 us (8%)
  between operations  2.57 us (2%)
    ppermute x8, starting transfers between devices, shifted(): return lax.ppermute(block, axis, route)  41.3 us
    ppermute x2, starting transfers between devices, extended_2(): lax.ppermute(lax.slice_in_dim(block, 0, width, axis=dim), axis, backward)  11.2 us
    ppermute x2, waiting for transfers between devices, extended_2(): lax.ppermute(lax.slice_in_dim(block, block.shape[dim] - width, None, axis...  6.3 us
    ppermute x1, starting transfers between devices, head_sum(): got = lax.ppermute(give.astype(jnp.bfloat16), axis, pair_near)  5.96 us
    ppermute x1, waiting for transfers between devices, head_sum(): got = lax.ppermute(give.astype(jnp.bfloat16), axis, pair_far)  5.35 us
    ppermute x1, waiting for transfers between devices, head_sum(): got = lax.ppermute(own, axis, pair_far)  4.42 us
    ppermute x1, starting transfers between devices, head_sum(): got = lax.ppermute(half, axis, pair_near)  4.03 us
    ppermute x2, starting transfers between devices, extended_2(): lax.ppermute(lax.slice_in_dim(block, block.shape[dim] - width, None, axis...  3.84 us
  transfers between devices with their start and end apart: 16, of which 6 were waited for; matrix products, arithmetic and copies ran while one was open for 26% of the time, Pallas kernels for 0%

profile of v1, /device:TPU:1, one launch (start us, length us, event | category | flops | bytes accessed | tf_op | source)
XLA Modules:
  0.0 152.9 jit_solution(15866869999478821065)
XLA Ops:
  7.1 5.5 %collective-permute-start = (bf16[128,192]{0,1:T(8,128)(2,1)}, bf16[128,192]{0,1:T(8,128)(2,1)}, u32[]{:S(2)}, u32[]{:S(2)}) collective-permute-start(bf16[128,192]{0,1:T(8,128)(2,1)} %pad_maximum_fusion.7), channel_id=1, source_target_pairs={{504,0},{508,4},{0,8},{4,12},{8,16},{12,20},{16,24},{20,28},{24,32... | collective-permute-start | bytes 147464 | tf_op jit(solution)/shard_map/ppermute | solution.py:22
  12.6 2.2 %collective-permute-start.1 = (bf16[128,192]{0,1:T(8,128)(2,1)}, bf16[128,192]{0,1:T(8,128)(2,1)}, u32[]{:S(2)}, u32[]{:S(2)}) collective-permute-start(bf16[128,192]{0,1:T(8,128)(2,1)} %pad_maximum_fusion.7), channel_id=1, source_target_pairs={{508,0},{0,4},{4,8},{8,12},{12,16},{16,20},{20,24},{24,28},{28,32}... | collective-permute-start | bytes 147464 | tf_op jit(solution)/shard_map/ppermute | solution.py:22
  14.9 12.9 %collective-permute-start.2 = (bf16[128,192]{0,1:T(8,128)(2,1)}, bf16[128,192]{0,1:T(8,128)(2,1)}, u32[]{:S(2)}, u32[]{:S(2)}) collective-permute-start(bf16[128,192]{0,1:T(8,128)(2,1)} %pad_maximum_fusion.7), channel_id=1, source_target_pairs={{4,0},{8,4},{12,8},{16,12},{20,16},{24,20},{28,24},{32,28},{36,32}... | collective-permute-start | bytes 147464 | tf_op jit(solution)/shard_map/ppermute | solution.py:22
  34.5 3.4 %collective-permute-start.5 = (bf16[64,64]{0,1:T(8,128)(2,1)S(1)}, bf16[64,64]{0,1:T(8,128)(2,1)S(1)}, u32[]{:S(2)}, u32[]{:S(2)}) collective-permute-start(bf16[64,64]{0,1:T(8,128)(2,1)S(1)} %get-tuple-element.52), channel_id=1, source_target_pairs={{4,0},{8,4},{12,8},{16,12},{20,16},{24,20},{28,24},{32,28},{36,32}... | collective-permute-start | bytes 24584 | tf_op jit(solution)/shard_map/ppermute | solution.py:34
  37.9 1.9 %collective-permute-start.4 = (bf16[64,64]{0,1:T(8,128)(2,1)S(1)}, bf16[64,64]{0,1:T(8,128)(2,1)S(1)}, u32[]{:S(2)}, u32[]{:S(2)}) collective-permute-start(bf16[64,64]{0,1:T(8,128)(2,1)S(1)} %get-tuple-element.53), channel_id=1, source_target_pairs={{0,4},{4,8},{8,12},{12,16},{16,20},{20,24},{24,28},{28,32},{32,36}... | collective-permute-start | bytes 24584 | tf_op jit(solution)/shard_map/ppermute | solution.py:31
  50.2 2.3 %concatenate.63 = bf16[32,160,64]{1,2,0:T(8,128)(2,1)} concatenate(bf16[32,32,64]{1,2,0:T(8,128)(2,1)S(1)} %copy.91, bf16[32,32,64]{1,2,0:T(8,128)(2,1)S(1)} %copy.92, bf16[32,32,64]{1,2,0:T(8,128)(2,1)S(1)} %copy.93, bf16[32,32,64]{1,2,0:T(8,128)(2,1)S(1)} %copy.94, bf16[32,32,64]{1,2,0:T(8,128)(2,1)S(1)} %copy.95), dimensions={1} | concatenate | bytes 1310720 | tf_op jit(solution)/shard_map/concatenate | solution.py:286
  52.5 1.9 %fusion.11 = bf16[32,128,64]{1,2,0:T(8,128)(2,1)S(1)} fusion(bf16[32,160,64]{1,2,0:T(8,128)(2,1)} %concatenate.63, s32[32,128]{1,0:T(8,128)} %iota_add_fusion), kind=kOutput, calls=%fused_computation.15 | convolution fusion | flops 84803584 | bytes 1196032 | tf_op jit(solution)/shard_map/wrs,wsf->wrf/dot_general | solution.py:294
  55.7 1.8 %convolution_bitcast_fusion.1 = f32[32,32,1,32]{1,3,0,2:T(8,128)S(1)} fusion(bf16[32,128,64]{1,2,0:T(8,128)(2,1)S(1)} %fusion.11, f32[32,32]{1,0:T(8,128)S(1)} %get-tuple-element.57, f32[32,32,128]{2,1,0:T(8,128)S(1)} %fusion.17), kind=kOutput, calls=%fused_computation.23 | convolution fusion | flops 8782975 | bytes 1458176 | tf_op jit(solution)/shard_map/bhqk,bkhd->bqhd/dot_general | solution.py:114
  58.6 1.8 %convolution_bitcast_fusion = f32[32,128,32]{1,2,0:T(8,128)S(1)} fusion(bf16[32,32,32]{1,0,2:T(8,128)(2,1)S(1)} %reshape.430, f32[32,32]{1,0:T(8,128)S(1)} %get-tuple-element.57, f32[32,32,128]{2,1,0:T(8,128)S(1)} %fusion.17), kind=kOutput, calls=%fused_computation.22 | convolution fusion | flops 8782975 | bytes 1118208 | tf_op jit(solution)/shard_map/bhqk,bqhd->bkhd/dot_general | solution.py:136
  65.5 7.8 %collective-permute-start.7 = (bf16[64,64]{1,0:T(8,128)(2,1)S(1)}, bf16[64,64]{1,0:T(8,128)(2,1)S(1)}, u32[]{:S(2)}, u32[]{:S(2)}) collective-permute-start(bf16[64,64]{1,0:T(8,128)(2,1)S(1)} %bitcast.234), channel_id=1, source_target_pairs={{4,0},{8,4},{12,8},{16,12},{20,16},{24,20},{28,24},{32,28},{36,32}... | collective-permute-start | bytes 24584 | tf_op jit(solution)/shard_map/ppermute | solution.py:34
  73.4 1.9 %collective-permute-start.6 = (bf16[64,64]{1,0:T(8,128)(2,1)S(1)}, bf16[64,64]{1,0:T(8,128)(2,1)S(1)}, u32[]{:S(2)}, u32[]{:S(2)}) collective-permute-start(bf16[64,64]{1,0:T(8,128)(2,1)S(1)} %bitcast.232), channel_id=1, source_target_pairs={{0,4},{4,8},{8,12},{12,16},{16,20},{20,24},{24,28},{28,32},{32,36}... | collective-permute-start | bytes 24584 | tf_op jit(solution)/shard_map/ppermute | solution.py:31
  75.4 3.3 %collective-permute-start.3 = (bf16[128,192]{0,1:T(8,128)(2,1)}, bf16[128,192]{0,1:T(8,128)(2,1)S(1)}, u32[]{:S(2)}, u32[]{:S(2)}) collective-permute-start(bf16[128,192]{0,1:T(8,128)(2,1)} %pad_maximum_fusion.7), channel_id=1, source_target_pairs={{8,0},{12,4},{16,8},{20,12},{24,16},{28,20},{32,24},{36,28},{40,32... | collective-permute-start | bytes 147464 | tf_op jit(solution)/shard_map/ppermute | solution.py:22
  78.7 4.9 %collective-permute-done.6 = bf16[64,64]{1,0:T(8,128)(2,1)S(1)} collective-permute-done((bf16[64,64]{1,0:T(8,128)(2,1)S(1)}, bf16[64,64]{1,0:T(8,128)(2,1)S(1)}, u32[]{:S(2)}, u32[]{:S(2)}) %collective-permute-start.6) | collective-permute-done | bytes 8224 | tf_op jit(solution)/shard_map/ppermute | solution.py:31
  97.5 2.2 %fusion.140 = (bf16[5,24576]{1,0:T(8,128)(2,1)S(1)}, f32[5,24576]{1,0:T(8,128)}) fusion(f32[4,24576]{1,0:T(4,128)S(1)} %reshape.438, s32[4]{0:T(128)} %fusion.119), kind=kOutput, calls=%fused_computation.239 | convolution fusion | flops 6021140 | bytes 1130512 | tf_op jit(solution)/shard_map/bsc,bsx->cx/dot_general | solution.py:239
  100.8 1.9 %collective-permute-start.11 = (bf16[128,192]{1,0:T(8,128)(2,1)S(1)}, bf16[128,192]{1,0:T(8,128)(2,1)S(1)}, u32[]{:S(2)}, u32[]{:S(2)}) collective-permute-start(bf16[128,192]{1,0:T(8,128)(2,1)S(1)} %convert_element_type.226), channel_id=1, source_target_pairs={{504,0},{508,4},{0,8},{4,12},{8,16},{12,20},{16,24},{20,28},{24,32... | collective-permute-start | bytes 147464 | tf_op jit(solution)/shard_map/ppermute | solution.py:22
  102.8 3.6 %collective-permute-start.10 = (bf16[128,192]{1,0:T(8,128)(2,1)S(1)}, bf16[128,192]{1,0:T(8,128)(2,1)S(1)}, u32[]{:S(2)}, u32[]{:S(2)}) collective-permute-start(bf16[128,192]{1,0:T(8,128)(2,1)S(1)} %convert_element_type.224), channel_id=1, source_target_pairs={{508,0},{0,4},{4,8},{8,12},{12,16},{16,20},{20,24},{24,28},{28,32}... | collective-permute-start | bytes 147464 | tf_op jit(solution)/shard_map/ppermute | solution.py:22
  106.5 8.8 %collective-permute-start.9 = (bf16[128,192]{1,0:T(8,128)(2,1)S(1)}, bf16[128,192]{1,0:T(8,128)(2,1)S(1)}, u32[]{:S(2)}, u32[]{:S(2)}) collective-permute-start(bf16[128,192]{1,0:T(8,128)(2,1)S(1)} %convert_element_type.222), channel_id=1, source_target_pairs={{4,0},{8,4},{12,8},{16,12},{20,16},{24,20},{28,24},{32,28},{36,32}... | collective-permute-start | bytes 147464 | tf_op jit(solution)/shard_map/ppermute | solution.py:22
  115.4 3.1 %collective-permute-start.8 = (bf16[128,192]{1,0:T(8,128)(2,1)S(1)}, bf16[128,192]{1,0:T(8,128)(2,1)S(1)}, u32[]{:S(2)}, u32[]{:S(2)}) collective-permute-start(bf16[128,192]{1,0:T(8,128)(2,1)S(1)} %convert_element_type.220), channel_id=1, source_target_pairs={{8,0},{12,4},{16,8},{20,12},{24,16},{28,20},{32,24},{36,28},{40,32... | collective-permute-start | bytes 147464 | tf_op jit(solution)/shard_map/ppermute | solution.py:22
  123.3 6.0 %collective-permute-start.12 = (bf16[1408,128]{1,0:T(8,128)(2,1)S(1)}, bf16[1408,128]{1,0:T(8,128)(2,1)S(1)}, u32[]{:S(2)}, u32[]{:S(2)}) collective-permute-start(bf16[1408,128]{1,0:T(8,128)(2,1)S(1)} %select_convert_fusion), channel_id=1, source_target_pairs={{0,1},{1,0},{2,3},{3,2},{4,5},{5,4},{6,7},{7,6},{8,9},{9,8},{10,11... | collective-permute-start | bytes 1081352 | tf_op jit(solution)/shard_map/ppermute | solution.py:57
  130.7 2.3 %collective-permute-start.13 = (bf16[704,128]{1,0:T(8,128)(2,1)S(1)}, bf16[704,128]{1,0:T(8,128)(2,1)S(1)}, u32[]{:S(2)}, u32[]{:S(2)}) collective-permute-start(bf16[704,128]{1,0:T(8,128)(2,1)S(1)} %select_convert_fusion.1), channel_id=1, source_target_pairs={{0,2},{1,3},{2,0},{3,1},{4,6},{5,7},{6,4},{7,5},{8,10},{9,11},{10,... | collective-permute-start | bytes 540680 | tf_op jit(solution)/shard_map/ppermute | solution.py:61
  133.0 5.3 %collective-permute-done.13 = bf16[704,128]{1,0:T(8,128)(2,1)S(1)} collective-permute-done((bf16[704,128]{1,0:T(8,128)(2,1)S(1)}, bf16[704,128]{1,0:T(8,128)(2,1)S(1)}, u32[]{:S(2)}, u32[]{:S(2)}) %collective-permute-start.13) | collective-permute-done | bytes 180256 | tf_op jit(solution)/shard_map/ppermute | solution.py:61
  138.4 2.3 %collective-permute-start.14 = (bf16[704,128]{1,0:T(8,128)(2,1)S(1)}, bf16[704,128]{1,0:T(8,128)(2,1)S(1)}, u32[]{:S(2)}, u32[]{:S(2)}) collective-permute-start(bf16[704,128]{1,0:T(8,128)(2,1)S(1)} %add_convert_fusion), channel_id=1, source_target_pairs={{0,2},{1,3},{2,0},{3,1},{4,6},{5,7},{6,4},{7,5},{8,10},{9,11},{10,... | collective-permute-start | bytes 540680 | tf_op jit(solution)/shard_map/ppermute | solution.py:63
  140.7 4.4 %collective-permute-done.14 = bf16[704,128]{1,0:T(8,128)(2,1)S(1)} collective-permute-done((bf16[704,128]{1,0:T(8,128)(2,1)S(1)}, bf16[704,128]{1,0:T(8,128)(2,1)S(1)}, u32[]{:S(2)}, u32[]{:S(2)}) %collective-permute-start.14) | collective-permute-done | bytes 180256 | tf_op jit(solution)/shard_map/ppermute | solution.py:63
  145.2 4.0 %collective-permute-start.15 = (bf16[1408,128]{1,0:T(8,128)(2,1)S(1)}, bf16[1408,128]{1,0:T(8,128)(2,1)S(1)}, u32[]{:S(2)}, u32[]{:S(2)}) collective-permute-start(bf16[1408,128]{1,0:T(8,128)(2,1)S(1)} %maximum_select_fusion.1), channel_id=1, source_target_pairs={{0,1},{1,0},{2,3},{3,2},{4,5},{5,4},{6,7},{7,6},{8,9},{9,8},{10,11... | collective-permute-start | bytes 1081352 | tf_op jit(solution)/shard_map/ppermute | solution.py:67
  (204 shorter events, 54.8 us)
Async XLA Ops:
  0.6 57.5 %copy-start = (bf16[1024,128]{1,0:T(8,128)(2,1)S(1)}, bf16[1024,128]{1,0:T(8,128)(2,1)}, u32[]{:S(2)}) copy-start(bf16[1024,128]{1,0:T(8,128)(2,1)} %param.33) | copy-start | bytes 786436
  0.6 39.6 %copy-start.5 = (bf16[4,384,96]{1,2,0:T(8,128)(2,1)S(1)}, bf16[4,384,96]{1,2,0:T(8,128)(2,1)}, u32[]{:S(2)}) copy-start(bf16[4,384,96]{1,2,0:T(8,128)(2,1)} %param.21) | copy-start | bytes 884740
  0.7 33.3 %copy-start.11 = (bf16[4,128,32]{1,2,0:T(8,128)(2,1)S(1)}, bf16[4,128,32]{1,2,0:T(8,128)(2,1)}, u32[]{:S(2)}) copy-start(bf16[4,128,32]{1,2,0:T(8,128)(2,1)} %param.24) | copy-start | bytes 98308
  0.7 41.1 %copy-start.25 = (s32[32]{0:T(128)S(1)}, s32[32]{0:T(128)}, u32[]{:S(2)}) copy-start(s32[32]{0:T(128)} %param.31) | copy-start | bytes 388
  1.7 42.1 %copy-start.26 = (s32[1,4]{1,0:T(1,128)S(1)}, s32[1,4]{1,0:T(1,128)}, u32[]{:S(2)}) copy-start(s32[1,4]{1,0:T(1,128)} %param.28) | copy-start | bytes 52
  7.1 80.0 %collective-permute-start = (bf16[128,192]{0,1:T(8,128)(2,1)}, bf16[128,192]{0,1:T(8,128)(2,1)}, u32[]{:S(2)}, u32[]{:S(2)}) collective-permute-start(bf16[128,192]{0,1:T(8,128)(2,1)} %pad_maximum_fusion.7), channel_id=1, source_target_pairs={{504,0},{508,4},{0,8},{4,12},{8,16},{12,20},{16,24},{20,28},{24,32... | collective-permute-start | bytes 147464 | tf_op jit(solution)/shard_map/ppermute | solution.py:22
  12.6 75.5 %collective-permute-start.1 = (bf16[128,192]{0,1:T(8,128)(2,1)}, bf16[128,192]{0,1:T(8,128)(2,1)}, u32[]{:S(2)}, u32[]{:S(2)}) collective-permute-start(bf16[128,192]{0,1:T(8,128)(2,1)} %pad_maximum_fusion.7), channel_id=1, source_target_pairs={{508,0},{0,4},{4,8},{8,12},{12,16},{16,20},{20,24},{24,28},{28,32}... | collective-permute-start | bytes 147464 | tf_op jit(solution)/shard_map/ppermute | solution.py:22
  14.9 74.3 %collective-permute-start.2 = (bf16[128,192]{0,1:T(8,128)(2,1)}, bf16[128,192]{0,1:T(8,128)(2,1)}, u32[]{:S(2)}, u32[]{:S(2)}) collective-permute-start(bf16[128,192]{0,1:T(8,128)(2,1)} %pad_maximum_fusion.7), channel_id=1, source_target_pairs={{4,0},{8,4},{12,8},{16,12},{20,16},{24,20},{28,24},{32,28},{36,32}... | collective-permute-start | bytes 147464 | tf_op jit(solution)/shard_map/ppermute | solution.py:22
  34.5 12.2 %collective-permute-start.5 = (bf16[64,64]{0,1:T(8,128)(2,1)S(1)}, bf16[64,64]{0,1:T(8,128)(2,1)S(1)}, u32[]{:S(2)}, u32[]{:S(2)}) collective-permute-start(bf16[64,64]{0,1:T(8,128)(2,1)S(1)} %get-tuple-element.52), channel_id=1, source_target_pairs={{4,0},{8,4},{12,8},{16,12},{20,16},{24,20},{28,24},{32,28},{36,32}... | collective-permute-start | bytes 24584 | tf_op jit(solution)/shard_map/ppermute | solution.py:34
  37.9 10.2 %collective-permute-start.4 = (bf16[64,64]{0,1:T(8,128)(2,1)S(1)}, bf16[64,64]{0,1:T(8,128)(2,1)S(1)}, u32[]{:S(2)}, u32[]{:S(2)}) collective-permute-start(bf16[64,64]{0,1:T(8,128)(2,1)S(1)} %get-tuple-element.53), channel_id=1, source_target_pairs={{0,4},{4,8},{8,12},{12,16},{16,20},{20,24},{24,28},{28,32},{32,36}... | collective-permute-start | bytes 24584 | tf_op jit(solution)/shard_map/ppermute | solution.py:31
  65.5 9.8 %collective-permute-start.7 = (bf16[64,64]{1,0:T(8,128)(2,1)S(1)}, bf16[64,64]{1,0:T(8,128)(2,1)S(1)}, u32[]{:S(2)}, u32[]{:S(2)}) collective-permute-start(bf16[64,64]{1,0:T(8,128)(2,1)S(1)} %bitcast.234), channel_id=1, source_target_pairs={{4,0},{8,4},{12,8},{16,12},{20,16},{24,20},{28,24},{32,28},{36,32}... | collective-permute-start | bytes 24584 | tf_op jit(solution)/shard_map/ppermute | solution.py:34
  73.4 10.2 %collective-permute-start.6 = (bf16[64,64]{1,0:T(8,128)(2,1)S(1)}, bf16[64,64]{1,0:T(8,128)(2,1)S(1)}, u32[]{:S(2)}, u32[]{:S(2)}) collective-permute-start(bf16[64,64]{1,0:T(8,128)(2,1)S(1)} %bitcast.232), channel_id=1, source_target_pairs={{0,4},{4,8},{8,12},{12,16},{16,20},{20,24},{24,28},{28,32},{32,36}... | collective-permute-start | bytes 24584 | tf_op jit(solution)/shard_map/ppermute | solution.py:31
  75.4 14.9 %collective-permute-start.3 = (bf16[128,192]{0,1:T(8,128)(2,1)}, bf16[128,192]{0,1:T(8,128)(2,1)S(1)}, u32[]{:S(2)}, u32[]{:S(2)}) collective-permute-start(bf16[128,192]{0,1:T(8,128)(2,1)} %pad_maximum_fusion.7), channel_id=1, source_target_pairs={{8,0},{12,4},{16,8},{20,12},{24,16},{28,20},{32,24},{36,28},{40,32... | collective-permute-start | bytes 147464 | tf_op jit(solution)/shard_map/ppermute | solution.py:22
  97.4 24.8 %copy-start.6 = (bf16[4,384,96]{1,2,0:T(8,128)(2,1)S(1)}, bf16[4,384,96]{1,2,0:T(8,128)(2,1)}, u32[]{:S(2)}) copy-start(bf16[4,384,96]{1,2,0:T(8,128)(2,1)} %param.21) | copy-start | bytes 884740
  97.4 25.2 %copy-start.2 = (bf16[128,384]{1,0:T(8,128)(2,1)S(1)}, bf16[128,384]{1,0:T(8,128)(2,1)}, u32[]{:S(2)}) copy-start(bf16[128,384]{1,0:T(8,128)(2,1)} %param.17) | copy-start | bytes 294916
  97.4 25.2 %copy-start.19 = (f32[384]{0:T(512)S(1)}, f32[384]{0:T(512)}, u32[]{:S(2)}) copy-start(f32[384]{0:T(512)} %param.19) | copy-start | bytes 4612
  100.8 21.4 %collective-permute-start.11 = (bf16[128,192]{1,0:T(8,128)(2,1)S(1)}, bf16[128,192]{1,0:T(8,128)(2,1)S(1)}, u32[]{:S(2)}, u32[]{:S(2)}) collective-permute-start(bf16[128,192]{1,0:T(8,128)(2,1)S(1)} %convert_element_type.226), channel_id=1, source_target_pairs={{504,0},{508,4},{0,8},{4,12},{8,16},{12,20},{16,24},{20,28},{24,32... | collective-permute-start | bytes 147464 | tf_op jit(solution)/shard_map/ppermute | solution.py:22
  102.8 19.4 %collective-permute-start.10 = (bf16[128,192]{1,0:T(8,128)(2,1)S(1)}, bf16[128,192]{1,0:T(8,128)(2,1)S(1)}, u32[]{:S(2)}, u32[]{:S(2)}) collective-permute-start(bf16[128,192]{1,0:T(8,128)(2,1)S(1)} %convert_element_type.224), channel_id=1, source_target_pairs={{508,0},{0,4},{4,8},{8,12},{12,16},{16,20},{20,24},{24,28},{28,32}... | collective-permute-start | bytes 147464 | tf_op jit(solution)/shard_map/ppermute | solution.py:22
  106.5 15.7 %collective-permute-start.9 = (bf16[128,192]{1,0:T(8,128)(2,1)S(1)}, bf16[128,192]{1,0:T(8,128)(2,1)S(1)}, u32[]{:S(2)}, u32[]{:S(2)}) collective-permute-start(bf16[128,192]{1,0:T(8,128)(2,1)S(1)} %convert_element_type.222), channel_id=1, source_target_pairs={{4,0},{8,4},{12,8},{16,12},{20,16},{24,20},{28,24},{32,28},{36,32}... | collective-permute-start | bytes 147464 | tf_op jit(solution)/shard_map/ppermute | solution.py:22
  115.4 6.8 %collective-permute-start.8 = (bf16[128,192]{1,0:T(8,128)(2,1)S(1)}, bf16[128,192]{1,0:T(8,128)(2,1)S(1)}, u32[]{:S(2)}, u32[]{:S(2)}) collective-permute-start(bf16[128,192]{1,0:T(8,128)(2,1)S(1)} %convert_element_type.220), channel_id=1, source_target_pairs={{8,0},{12,4},{16,8},{20,12},{24,16},{28,20},{32,24},{36,28},{40,32... | collective-permute-start | bytes 147464 | tf_op jit(solution)/shard_map/ppermute | solution.py:22
  123.3 7.2 %collective-permute-start.12 = (bf16[1408,128]{1,0:T(8,128)(2,1)S(1)}, bf16[1408,128]{1,0:T(8,128)(2,1)S(1)}, u32[]{:S(2)}, u32[]{:S(2)}) collective-permute-start(bf16[1408,128]{1,0:T(8,128)(2,1)S(1)} %select_convert_fusion), channel_id=1, source_target_pairs={{0,1},{1,0},{2,3},{3,2},{4,5},{5,4},{6,7},{7,6},{8,9},{9,8},{10,11... | collective-permute-start | bytes 1081352 | tf_op jit(solution)/shard_map/ppermute | solution.py:57
  130.7 7.7 %collective-permute-start.13 = (bf16[704,128]{1,0:T(8,128)(2,1)S(1)}, bf16[704,128]{1,0:T(8,128)(2,1)S(1)}, u32[]{:S(2)}, u32[]{:S(2)}) collective-permute-start(bf16[704,128]{1,0:T(8,128)(2,1)S(1)} %select_convert_fusion.1), channel_id=1, source_target_pairs={{0,2},{1,3},{2,0},{3,1},{4,6},{5,7},{6,4},{7,5},{8,10},{9,11},{10,... | collective-permute-start | bytes 540680 | tf_op jit(solution)/shard_map/ppermute | solution.py:61
  138.4 6.7 %collective-permute-start.14 = (bf16[704,128]{1,0:T(8,128)(2,1)S(1)}, bf16[704,128]{1,0:T(8,128)(2,1)S(1)}, u32[]{:S(2)}, u32[]{:S(2)}) collective-permute-start(bf16[704,128]{1,0:T(8,128)(2,1)S(1)} %add_convert_fusion), channel_id=1, source_target_pairs={{0,2},{1,3},{2,0},{3,1},{4,6},{5,7},{6,4},{7,5},{8,10},{9,11},{10,... | collective-permute-start | bytes 540680 | tf_op jit(solution)/shard_map/ppermute | solution.py:63
  145.2 5.3 %collective-permute-start.15 = (bf16[1408,128]{1,0:T(8,128)(2,1)S(1)}, bf16[1408,128]{1,0:T(8,128)(2,1)S(1)}, u32[]{:S(2)}, u32[]{:S(2)}) collective-permute-start(bf16[1408,128]{1,0:T(8,128)(2,1)S(1)} %maximum_select_fusion.1), channel_id=1, source_target_pairs={{0,1},{1,0},{2,3},{3,2},{4,5},{5,4},{6,7},{7,6},{8,9},{9,8},{10,11... | collective-permute-start | bytes 1081352 | tf_op jit(solution)/shard_map/ppermute | solution.py:67
  (20 other events, 161.7 us)

commit v2 on v1

--- a/solution.py
+++ b/solution.py
@@ -20,6 +20,13 @@
     devices = range(lax.axis_size(axis))
     route = [((i - distance) % len(devices), i) for i in devices]
     return lax.ppermute(block, axis, route)
+
+
+def shifted_pair(block, extra, axis, distance):
+    width = block.shape[1]
+    padded = jnp.pad(extra, ((0, block.shape[0] - extra.shape[0]), (0, 0)))
+    both = shifted(jnp.concatenate([block, padded], axis=1), axis, distance)
+    return both[:, :width], both[: extra.shape[0], width:]
 
 
 def extended_2(block, sides, width):
@@ -175,13 +182,46 @@
     key_value = jnp.concatenate(
         [projected[1].astype(jnp.bfloat16), projected[2].astype(jnp.bfloat16)], axis=1
     )
+    w_atom_all, w_atom_out_all, atom_bias_all = (w_atom, w_atom_out, atom_bias)
+    atom_rows = atoms.shape[0]
+    heads_atom = w_atom_all.shape[2] // DA
+    atom_feat = heads_atom * DA
+    halo_rows = AK // 2
+    windows_here = atom_rows // AQ
+    group_span = AK // AQ + 1
+    slab_rows = group_span * AQ
+    atom_scaling = DA ** (-0.5)
+    normed_atoms = norm_rows(atoms.astype(jnp.float32), gain_atom)
+    counts = atom_counts[0]
+    ends = jnp.cumsum(counts)
+    atom_place = jnp.arange(atom_rows, dtype=jnp.int32)
+    token_local = jnp.sum((ends[None, :] <= atom_place[:, None]).astype(jnp.int32), axis=1)
+    token_pick = (token_local[:, None] == jnp.arange(tok_rows, dtype=jnp.int32)[None, :]).astype(
+        jnp.float32
+    )
+    condition = jnp.dot(normed_low, w_cond, preferred_element_type=jnp.float32)
+    atom_input = (normed_atoms + jnp.dot(token_pick, condition, precision=HIGHEST)).astype(
+        jnp.bfloat16
+    )
+    atom_proj = [
+        jnp.dot(atom_input, w_atom_all[which], preferred_element_type=jnp.float32)
+        for which in range(4)
+    ]
+    atom_gate = jax.nn.sigmoid(atom_proj[3])
+    atom_kv = jnp.concatenate(
+        [atom_proj[1].astype(jnp.bfloat16), atom_proj[2].astype(jnp.bfloat16)], axis=1
+    )
     owner_dev = used_blocks // blocks_here
     relative = jnp.mod(owner_dev - device, shards)
     relative = jnp.where(relative > shards // 2, relative - shards, relative)
     pieces = [key_value for distance in range(-WIN, WIN + 1)]
     for distance in range(-WIN, WIN + 1):
-        if distance != 0:
+        if abs(distance) > 1:
             pieces[distance + WIN] = shifted(key_value, "seq", -distance)
+    pieces[WIN - 1], halo_low = shifted_pair(
+        key_value, atom_kv[atom_kv.shape[0] - AK // 2 :], "seq", 1
+    )
+    pieces[WIN + 1], halo_high = shifted_pair(key_value, atom_kv[: AK // 2], "seq", -1)
     window = jnp.stack(pieces)
     candidates = (2 * WIN + 1) * blocks_here
     window_flat = window.reshape(candidates, BLK * 2 * features)
@@ -240,48 +280,7 @@
         "bsc,bsx->cx", selector_mask.astype(jnp.float32), returned_flat, precision=HIGHEST
     )
     outgoing = outgoing.reshape(2 * WIN + 1, tok_rows, 2 * features)
-    collected = outgoing[WIN]
-    for distance in range(-WIN, WIN + 1):
-        if distance != 0:
-            collected = collected + shifted(
-                outgoing[distance + WIN].astype(jnp.bfloat16), "seq", distance
-            ).astype(jnp.float32)
-    token_grads = [
-        dquery.reshape(tok_rows, features).astype(jnp.bfloat16),
-        collected[:, :features].astype(jnp.bfloat16),
-        collected[:, features:].astype(jnp.bfloat16),
-        grad_gate,
-    ]
-    w_atom_all, w_atom_out_all, atom_bias_all = (w_atom, w_atom_out, atom_bias)
-    atom_rows = atoms.shape[0]
-    heads_atom = w_atom_all.shape[2] // DA
-    atom_feat = heads_atom * DA
-    halo_rows = AK // 2
-    windows_here = atom_rows // AQ
-    group_span = AK // AQ + 1
-    slab_rows = group_span * AQ
-    atom_scaling = DA ** (-0.5)
-    normed_atoms = norm_rows(atoms.astype(jnp.float32), gain_atom)
-    counts = atom_counts[0]
-    ends = jnp.cumsum(counts)
-    atom_place = jnp.arange(atom_rows, dtype=jnp.int32)
-    token_local = jnp.sum((ends[None, :] <= atom_place[:, None]).astype(jnp.int32), axis=1)
-    token_pick = (token_local[:, None] == jnp.arange(tok_rows, dtype=jnp.int32)[None, :]).astype(
-        jnp.float32
-    )
-    condition = jnp.dot(normed_low, w_cond, preferred_element_type=jnp.float32)
-    atom_input = (normed_atoms + jnp.dot(token_pick, condition, precision=HIGHEST)).astype(
-        jnp.bfloat16
-    )
-    atom_proj = [
-        jnp.dot(atom_input, w_atom_all[which], preferred_element_type=jnp.float32)
-        for which in range(4)
-    ]
-    atom_gate = jax.nn.sigmoid(atom_proj[3])
-    atom_kv = jnp.concatenate(
-        [atom_proj[1].astype(jnp.bfloat16), atom_proj[2].astype(jnp.bfloat16)], axis=1
-    )
-    extended = extended_2(atom_kv, (("seq", 0),), halo_rows)
+    extended = jnp.concatenate([halo_low, atom_kv, halo_high], axis=0)
     ext_groups = extended.reshape(windows_here + AK // AQ, AQ, 2 * atom_feat)
     slabs = jnp.concatenate(
         [ext_groups[step : step + windows_here] for step in range(group_span)], axis=1
@@ -350,7 +349,28 @@
         )
     ext_grad = ext_grad.reshape(atom_rows + 2 * halo_rows, 2 * atom_feat)
     rims = jnp.concatenate([ext_grad[:halo_rows], ext_grad[atom_rows + halo_rows :]], axis=0)
-    edges = extended_2(rims.astype(jnp.bfloat16), (("seq", 0),), halo_rows).astype(rims.dtype)
+    collected = outgoing[WIN]
+    for distance in range(-WIN, WIN + 1):
+        if abs(distance) > 1:
+            collected = collected + shifted(
+                outgoing[distance + WIN].astype(jnp.bfloat16), "seq", distance
+            ).astype(jnp.float32)
+    came_low, edge_low = shifted_pair(
+        outgoing[WIN + 1].astype(jnp.bfloat16), rims[halo_rows:].astype(jnp.bfloat16), "seq", 1
+    )
+    came_high, edge_high = shifted_pair(
+        outgoing[WIN - 1].astype(jnp.bfloat16), rims[:halo_rows].astype(jnp.bfloat16), "seq", -1
+    )
+    collected = collected + came_low.astype(jnp.float32) + came_high.astype(jnp.float32)
+    edges = jnp.concatenate(
+        [edge_low, rims.astype(jnp.bfloat16), edge_high], axis=0
+    ).astype(rims.dtype)
+    token_grads = [
+        dquery.reshape(tok_rows, features).astype(jnp.bfloat16),
+        collected[:, :features].astype(jnp.bfloat16),
+        collected[:, features:].astype(jnp.bfloat16),
+        grad_gate,
+    ]
     own_grad = ext_grad[halo_rows : halo_rows + atom_rows]
     own_grad = jnp.concatenate(
         [

time: 154 us -> 198 us (1.29)
  local copies, waits for them, and re-layouts: 19.6 us -> 46.3 us
  matrix products: 28.7 us -> 46.3 us
  other arithmetic: 12.5 us -> 26.3 us
  starting transfers between devices: 70.9 us -> 61.1 us
  waiting for transfers between devices: 18.6 us -> 12.3 us
    ppermute x4 -> x0, starting transfers between devices: 15 us -> none  [the longest x2 11.2 us: extended_2(): lax.ppermute(lax.slice_in_dim(block, 0, width, axis=dim), axis, backward)]
    ppermute x8, starting transfers between devices: 41.3 us -> 47.9 us  [shifted(): return lax.ppermute(block, axis, route)]
    ppermute x4 -> x0, waiting for transfers between devices: 6.31 us -> none  [the longest x2 6.3 us: extended_2(): lax.ppermute(lax.slice_in_dim(block, block.shape[dim] - width, None, axis...]
    sub x1, other arithmetic: 1.01 us -> 5.4 us  [attend_local(): exponent = jnp.exp(scores - row_max)]
    dot_general x4, matrix products: 1.79 us -> 5.74 us  [body(): jnp.dot(token_grads[which], w_token[which].T, preferred_element_type=jnp....]
    convert_element_type x2, local copies, waits for them, and re-layouts: 0.38 us -> 3.62 us  [body(): aquery_grad.reshape(atom_rows, atom_feat).astype(jnp.bfloat16)]
    reshape x2, local copies, waits for them, and re-layouts: 0.2 us -> 3.43 us  [body(): key_grad.reshape(blocks_here, S, BLK, features)]
    another operation x6, local copies, waits for them, and re-layouts: 2.08 us -> 5.31 us  [body(): window = jnp.stack(pieces)]
  transfers between devices with their start and end apart: 16 -> 12, of which waited for: 6 -> 4; matrix products, arithmetic and copies ran while one was open for 26% -> 18% of each run, Pallas kernels for 0% -> 0%
where the time goes in v2:
time: 198 us; the launch traced here: 195 us
  starting transfers between devices  61.1 us (31%)
  local copies, waits for them, and re-layouts  46.3 us (23%)
  matrix products  46.3 us (23%)
  other arithmetic  26.3 us (13%)
  waiting for transfers between devices  12.3 us (6%)
  between operations  2.54 us (1%)
    ppermute x8, starting transfers between devices, shifted(): return lax.ppermute(block, axis, route)  47.9 us
    dot_general x4, matrix products, body(): jnp.dot(token_grads[which], w_token[which].T, preferred_element_type=jnp....  5.74 us
    sub x1, other arithmetic, attend_local(): exponent = jnp.exp(scores - row_max)  5.4 us
    ppermute x1, waiting for transfers between devices, head_sum(): got = lax.ppermute(give.astype(jnp.bfloat16), axis, pair_far)  5.35 us
    another operation x6, local copies, waits for them, and re-layouts, body(): window = jnp.stack(pieces)  5.31 us
    ppermute x1, starting transfers between devices, head_sum(): got = lax.ppermute(give.astype(jnp.bfloat16), axis, pair_near)  4.55 us
    ppermute x1, waiting for transfers between devices, head_sum(): got = lax.ppermute(own, axis, pair_far)  4.42 us
    ppermute x1, starting transfers between devices, head_sum(): got = lax.ppermute(half, axis, pair_near)  4.03 us
  transfers between devices with their start and end apart: 12, of which 4 were waited for; matrix products, arithmetic and copies ran while one was open for 18% of the time, Pallas kernels for 0%

profile of v2, /device:TPU:1, one launch (start us, length us, event | category | flops | bytes accessed | tf_op | source)
XLA Modules:
  0.0 195.0 jit_solution(105164249755580854)
XLA Ops:
  6.0 5.5 %collective-permute-start = (bf16[128,192]{0,1:T(8,128)(2,1)S(1)}, bf16[128,192]{0,1:T(8,128)(2,1)S(1)}, u32[]{:S(2)}, u32[]{:S(2)}) collective-permute-start(bf16[128,192]{0,1:T(8,128)(2,1)S(1)} %pad_maximum_fusion.9), channel_id=1, source_target_pairs={{504,0},{508,4},{0,8},{4,12},{8,16},{12,20},{16,24},{20,28},{24,32... | collective-permute-start | bytes 147464 | tf_op jit(solution)/shard_map/ppermute | solution.py:22
  11.5 13.5 %collective-permute-start.3 = (bf16[128,192]{0,1:T(8,128)(2,1)S(1)}, bf16[128,192]{0,1:T(8,128)(2,1)S(1)}, u32[]{:S(2)}, u32[]{:S(2)}) collective-permute-start(bf16[128,192]{0,1:T(8,128)(2,1)S(1)} %pad_maximum_fusion.9), channel_id=1, source_target_pairs={{8,0},{12,4},{16,8},{20,12},{24,16},{28,20},{32,24},{36,28},{40,32... | collective-permute-start | bytes 147464 | tf_op jit(solution)/shard_map/ppermute | solution.py:22
  31.8 2.2 %collective-permute-start.1 = (bf16[128,256]{0,1:T(8,128)(2,1)S(1)}, bf16[128,256]{0,1:T(8,128)(2,1)S(1)}, u32[]{:S(2)}, u32[]{:S(2)}) collective-permute-start(bf16[128,256]{0,1:T(8,128)(2,1)S(1)} %get-tuple-element.53), channel_id=1, source_target_pairs={{508,0},{0,4},{4,8},{8,12},{12,16},{16,20},{20,24},{24,28},{28,32}... | collective-permute-start | bytes 196616 | tf_op jit(solution)/shard_map/ppermute | solution.py:22
  34.0 8.8 %collective-permute-start.2 = (bf16[128,256]{0,1:T(8,128)(2,1)S(1)}, bf16[128,256]{0,1:T(8,128)(2,1)S(1)}, u32[]{:S(2)}, u32[]{:S(2)}) collective-permute-start(bf16[128,256]{0,1:T(8,128)(2,1)S(1)} %get-tuple-element.52), channel_id=1, source_target_pairs={{4,0},{8,4},{12,8},{16,12},{20,16},{24,20},{28,24},{32,28},{36,32}... | collective-permute-start | bytes 196616 | tf_op jit(solution)/shard_map/ppermute | solution.py:22
  54.0 2.4 %concatenate.79 = bf16[32,160,64]{1,2,0:T(8,128)(2,1)} concatenate(bf16[32,32,64]{1,2,0:T(8,128)(2,1)S(1)} %copy.91, bf16[32,32,64]{1,2,0:T(8,128)(2,1)S(1)} %copy.92, bf16[32,32,64]{1,2,0:T(8,128)(2,1)S(1)} %copy.93, bf16[32,32,64]{1,2,0:T(8,128)(2,1)S(1)} %copy.94, bf16[32,32,64]{1,2,0:T(8,128)(2,1)S(1)} %copy.95), dimensions={1} | concatenate | bytes 1310720 | tf_op jit(solution)/shard_map/concatenate | solution.py:285
  59.8 5.4 %fusion.148 = (f32[32,32]{1,0:T(8,128)S(1)}, f32[32,32,128]{2,1,0:T(8,128)S(1)}) fusion(f32[32,32,128]{2,1,0:T(8,128)S(1)} %fusion.17), kind=kOutput, calls=%fused_computation.252 | output fusion | flops 262271 | bytes 1052672 | tf_op jit(solution)/shard_map/sub | solution.py:118
  77.1 2.1 %stack.23 = bf16[5,24576]{1,0:T(8,128)(2,1)S(1)} concatenate(bf16[1,24576]{1,0:T(2,128)(2,1)} %stack.18, bf16[1,24576]{1,0:T(2,128)(2,1)S(1)} %stack.19, bf16[1,24576]{1,0:T(2,128)(2,1)} %stack.20, bf16[1,24576]{1,0:T(2,128)(2,1)} %stack.21, bf16[1,24576]{1,0:T(2,128)(2,1)} %stack.22), dimensions={0} | concatenate | bytes 491520 | tf_op jit(solution)/shard_map/stack | solution.py:225
  83.1 3.1 %fusion.149 = (f32[4,128]{1,0:T(4,128)}, f32[4,128,512]{2,1,0:T(8,128)}) fusion(bf16[128,4,24]{0,2,1:T(8,128)(2,1)} %bitcast.229, bf16[512,4,24]{0,2,1:T(8,128)(2,1)S(1)} %reshape.424, bf16[4,128,512]{2,1,0:T(8,128)(2,1)} %param.26, pred[512]{0:T(512)(128)(4,1)} %broadcast_bitcast_fusion), kind=kOutput, calls=%fused_computation.253 | convolution fusion | flops 14156287 | bytes 1698304 | tf_op jit(solution)/shard_map/sub | solution.py:118
  105.0 2.0 %pad_maximum_fusion.2 = f32[1,4,128,192]{3,2,1,0:T(8,128)} fusion(f32[1,4,128,96]{3,2,1,0:T(8,128)} %copy.108, f32[1,4,128,96]{3,2,1,0:T(8,128)} %copy.107), kind=kLoop, calls=%fused_computation.85 | loop fusion | flops 98304 | bytes 786432 | tf_op jit(solution)/shard_map/concatenate | solution.py:271
  107.0 2.1 %reshape.436 = f32[4,24576]{1,0:T(4,128)} reshape(f32[1,4,128,192]{3,2,1,0:T(8,128)} %pad_maximum_fusion.2) | data formatting | bytes 786432 | tf_op jit(solution)/shard_map/reshape.94
  109.1 2.5 %fusion.150 = (bf16[5,24576]{1,0:T(8,128)(2,1)S(1)}, f32[5,24576]{1,0:T(8,128)}) fusion(f32[4,24576]{1,0:T(4,128)} %reshape.436, s32[4]{0:T(128)} %fusion.132), kind=kOutput, calls=%fused_computation.254 | convolution fusion | flops 6021140 | bytes 1130512 | tf_op jit(solution)/shard_map/bsc,bsx->cx/dot_general | solution.py:279
  116.4 2.1 %collective-permute-start.4 = (bf16[128,256]{1,0:T(8,128)(2,1)}, bf16[128,256]{1,0:T(8,128)(2,1)}, u32[]{:S(2)}, u32[]{:S(2)}) collective-permute-start(bf16[128,256]{1,0:T(8,128)(2,1)} %fusion.88), channel_id=1, source_target_pairs={{508,0},{0,4},{4,8},{8,12},{12,16},{16,20},{20,24},{24,28},{28,32}... | collective-permute-start | bytes 196616 | tf_op jit(solution)/shard_map/ppermute | solution.py:22
  121.6 9.1 %collective-permute-start.5 = (bf16[128,256]{1,0:T(8,128)(2,1)}, bf16[128,256]{1,0:T(8,128)(2,1)}, u32[]{:S(2)}, u32[]{:S(2)}) collective-permute-start(bf16[128,256]{1,0:T(8,128)(2,1)} %fusion.89), channel_id=1, source_target_pairs={{4,0},{8,4},{12,8},{16,12},{20,16},{24,20},{28,24},{32,28},{36,32}... | collective-permute-start | bytes 196616 | tf_op jit(solution)/shard_map/ppermute | solution.py:22
  132.3 1.9 collective-permute-start.6
  135.7 4.9 %collective-permute-start.7 = (bf16[128,192]{1,0:T(8,128)(2,1)}, bf16[128,192]{1,0:T(8,128)(2,1)}, u32[]{:S(2)}, u32[]{:S(2)}) collective-permute-start(bf16[128,192]{1,0:T(8,128)(2,1)} %convert_element_type.234), channel_id=1, source_target_pairs={{504,0},{508,4},{0,8},{4,12},{8,16},{12,20},{16,24},{20,28},{24,32... | collective-permute-start | bytes 147464 | tf_op jit(solution)/shard_map/ppermute | solution.py:22
  140.6 2.1 %slice_reduce_fusion.2 = f32[24576]{0:T(1024)} fusion(f32[5,24576]{1,0:T(8,128)} %get-tuple-element.60), kind=kLoop, calls=%fused_computation.142 | loop fusion | bytes 196608 | tf_op jit(solution)/shard_map/slice | solution.py:352
  144.4 1.9 convert_element_type.219
  146.3 1.9 fusion.110
  166.8 4.6 %collective-permute-start.8 = (bf16[1408,128]{1,0:T(8,128)(2,1)S(1)}, bf16[1408,128]{1,0:T(8,128)(2,1)S(1)}, u32[]{:S(2)}, u32[]{:S(2)}) collective-permute-start(bf16[1408,128]{1,0:T(8,128)(2,1)S(1)} %select_convert_fusion), channel_id=1, source_target_pairs={{0,1},{1,0},{2,3},{3,2},{4,5},{5,4},{6,7},{7,6},{8,9},{9,8},{10,11... | collective-permute-start | bytes 1081352 | tf_op jit(solution)/shard_map/ppermute | solution.py:64
  172.7 2.3 %collective-permute-start.9 = (bf16[704,128]{1,0:T(8,128)(2,1)S(1)}, bf16[704,128]{1,0:T(8,128)(2,1)S(1)}, u32[]{:S(2)}, u32[]{:S(2)}) collective-permute-start(bf16[704,128]{1,0:T(8,128)(2,1)S(1)} %select_convert_fusion.1), channel_id=1, source_target_pairs={{0,2},{1,3},{2,0},{3,1},{4,6},{5,7},{6,4},{7,5},{8,10},{9,11},{10,... | collective-permute-start | bytes 540680 | tf_op jit(solution)/shard_map/ppermute | solution.py:68
  175.1 5.3 %collective-permute-done.9 = bf16[704,128]{1,0:T(8,128)(2,1)S(1)} collective-permute-done((bf16[704,128]{1,0:T(8,128)(2,1)S(1)}, bf16[704,128]{1,0:T(8,128)(2,1)S(1)}, u32[]{:S(2)}, u32[]{:S(2)}) %collective-permute-start.9) | collective-permute-done | bytes 180256 | tf_op jit(solution)/shard_map/ppermute | solution.py:68
  180.5 2.3 %collective-permute-start.10 = (bf16[704,128]{1,0:T(8,128)(2,1)S(1)}, bf16[704,128]{1,0:T(8,128)(2,1)S(1)}, u32[]{:S(2)}, u32[]{:S(2)}) collective-permute-start(bf16[704,128]{1,0:T(8,128)(2,1)S(1)} %add_convert_fusion), channel_id=1, source_target_pairs={{0,2},{1,3},{2,0},{3,1},{4,6},{5,7},{6,4},{7,5},{8,10},{9,11},{10,... | collective-permute-start | bytes 540680 | tf_op jit(solution)/shard_map/ppermute | solution.py:70
  182.8 4.4 %collective-permute-done.10 = bf16[704,128]{1,0:T(8,128)(2,1)S(1)} collective-permute-done((bf16[704,128]{1,0:T(8,128)(2,1)S(1)}, bf16[704,128]{1,0:T(8,128)(2,1)S(1)}, u32[]{:S(2)}, u32[]{:S(2)}) %collective-permute-start.10) | collective-permute-done | bytes 180256 | tf_op jit(solution)/shard_map/ppermute | solution.py:70
  187.3 4.0 %collective-permute-start.11 = (bf16[1408,128]{1,0:T(8,128)(2,1)S(1)}, bf16[1408,128]{1,0:T(8,128)(2,1)S(1)}, u32[]{:S(2)}, u32[]{:S(2)}) collective-permute-start(bf16[1408,128]{1,0:T(8,128)(2,1)S(1)} %maximum_select_fusion.1), channel_id=1, source_target_pairs={{0,1},{1,0},{2,3},{3,2},{4,5},{5,4},{6,7},{7,6},{8,9},{9,8},{10,11... | collective-permute-start | bytes 1081352 | tf_op jit(solution)/shard_map/ppermute | solution.py:74
  (236 shorter events, 96.1 us)
Async XLA Ops:
  0.6 67.0 %copy-start = (bf16[1024,128]{1,0:T(8,128)(2,1)S(1)}, bf16[1024,128]{1,0:T(8,128)(2,1)}, u32[]{:S(2)}) copy-start(bf16[1024,128]{1,0:T(8,128)(2,1)} %param.33) | copy-start | bytes 786436
  0.6 31.1 %copy-start.40 = (pred[128]{0:T(512)(128)(4,1)S(1)}, pred[128]{0:T(512)(128)(4,1)}, u32[]{:S(2)}) copy-start(pred[128]{0:T(512)(128)(4,1)} %constant.112.clone.1) | copy-start | bytes 388
  0.7 42.6 %copy-start.9 = (bf16[4,384,96]{1,2,0:T(8,128)(2,1)S(1)}, bf16[4,384,96]{1,2,0:T(8,128)(2,1)}, u32[]{:S(2)}) copy-start(bf16[4,384,96]{1,2,0:T(8,128)(2,1)} %param.21) | copy-start | bytes 884740
  0.7 30.6 %copy-start.20 = (bf16[4,128,32]{1,2,0:T(8,128)(2,1)S(1)}, bf16[4,128,32]{1,2,0:T(8,128)(2,1)}, u32[]{:S(2)}) copy-start(bf16[4,128,32]{1,2,0:T(8,128)(2,1)} %param.24) | copy-start | bytes 98308
  1.8 25.4 %copy-start.34 = (f32[128]{0:T(128)}, f32[128]{0:T(128)S(1)}, u32[]{:S(2)}) copy-start(f32[128]{0:T(128)S(1)} %broadcast_multiply_fusion.5) | copy-start | bytes 1540
  2.8 24.3 %copy-start.37 = (f32[128]{0:T(128)}, f32[128]{0:T(128)S(1)}, u32[]{:S(2)}) copy-start(f32[128]{0:T(128)S(1)} %add_rsqrt_fusion.1) | copy-start | bytes 1540
  3.9 41.0 %copy-start.41 = (s32[32]{0:T(128)S(1)}, s32[32]{0:T(128)}, u32[]{:S(2)}) copy-start(s32[32]{0:T(128)} %param.31) | copy-start | bytes 388
  3.9 42.4 %copy-start.42 = (s32[1,4]{1,0:T(1,128)S(1)}, s32[1,4]{1,0:T(1,128)}, u32[]{:S(2)}) copy-start(s32[1,4]{1,0:T(1,128)} %param.28) | copy-start | bytes 52
  6.0 42.3 %collective-permute-start = (bf16[128,192]{0,1:T(8,128)(2,1)S(1)}, bf16[128,192]{0,1:T(8,128)(2,1)S(1)}, u32[]{:S(2)}, u32[]{:S(2)}) collective-permute-start(bf16[128,192]{0,1:T(8,128)(2,1)S(1)} %pad_maximum_fusion.9), channel_id=1, source_target_pairs={{504,0},{508,4},{0,8},{4,12},{8,16},{12,20},{16,24},{20,28},{24,32... | collective-permute-start | bytes 147464 | tf_op jit(solution)/shard_map/ppermute | solution.py:22
  11.5 37.7 %collective-permute-start.3 = (bf16[128,192]{0,1:T(8,128)(2,1)S(1)}, bf16[128,192]{0,1:T(8,128)(2,1)S(1)}, u32[]{:S(2)}, u32[]{:S(2)}) collective-permute-start(bf16[128,192]{0,1:T(8,128)(2,1)S(1)} %pad_maximum_fusion.9), channel_id=1, source_target_pairs={{8,0},{12,4},{16,8},{20,12},{24,16},{28,20},{32,24},{36,28},{40,32... | collective-permute-start | bytes 147464 | tf_op jit(solution)/shard_map/ppermute | solution.py:22
  27.2 15.6 %copy-start.23 = (f32[1024]{0:T(1024)}, f32[1024]{0:T(1024)S(1)}, u32[]{:S(2)}) copy-start(f32[1024]{0:T(1024)S(1)} %broadcast_multiply_fusion.2) | copy-start | bytes 12292
  28.5 14.3 %copy-start.28 = (f32[1024]{0:T(1024)}, f32[1024]{0:T(1024)S(1)}, u32[]{:S(2)}) copy-start(f32[1024]{0:T(1024)S(1)} %add_rsqrt_fusion) | copy-start | bytes 12292
  29.8 13.0 %copy-start.32 = (s32[1024]{0:T(1024)}, s32[1024]{0:T(1024)S(1)}, u32[]{:S(2)}) copy-start(s32[1024]{0:T(1024)S(1)} %convert_reduce_fusion.1) | copy-start | bytes 12292
  31.8 18.3 %collective-permute-start.1 = (bf16[128,256]{0,1:T(8,128)(2,1)S(1)}, bf16[128,256]{0,1:T(8,128)(2,1)S(1)}, u32[]{:S(2)}, u32[]{:S(2)}) collective-permute-start(bf16[128,256]{0,1:T(8,128)(2,1)S(1)} %get-tuple-element.53), channel_id=1, source_target_pairs={{508,0},{0,4},{4,8},{8,12},{12,16},{16,20},{20,24},{24,28},{28,32}... | collective-permute-start | bytes 196616 | tf_op jit(solution)/shard_map/ppermute | solution.py:22
  34.0 16.1 %collective-permute-start.2 = (bf16[128,256]{0,1:T(8,128)(2,1)S(1)}, bf16[128,256]{0,1:T(8,128)(2,1)S(1)}, u32[]{:S(2)}, u32[]{:S(2)}) collective-permute-start(bf16[128,256]{0,1:T(8,128)(2,1)S(1)} %get-tuple-element.52), channel_id=1, source_target_pairs={{4,0},{8,4},{12,8},{16,12},{20,16},{24,20},{28,24},{32,28},{36,32}... | collective-permute-start | bytes 196616 | tf_op jit(solution)/shard_map/ppermute | solution.py:22
  43.3 24.3 %copy-start.5 = (f32[1024,32]{0,1:T(8,128)}, f32[1024,32]{0,1:T(8,128)S(1)}, u32[]{:S(2)}) copy-start(f32[1024,32]{0,1:T(8,128)S(1)} %fusion.29) | copy-start | bytes 393220
  116.4 40.2 %collective-permute-start.4 = (bf16[128,256]{1,0:T(8,128)(2,1)}, bf16[128,256]{1,0:T(8,128)(2,1)}, u32[]{:S(2)}, u32[]{:S(2)}) collective-permute-start(bf16[128,256]{1,0:T(8,128)(2,1)} %fusion.88), channel_id=1, source_target_pairs={{508,0},{0,4},{4,8},{8,12},{12,16},{16,20},{20,24},{24,28},{28,32}... | collective-permute-start | bytes 196616 | tf_op jit(solution)/shard_map/ppermute | solution.py:22
  121.6 35.0 %collective-permute-start.5 = (bf16[128,256]{1,0:T(8,128)(2,1)}, bf16[128,256]{1,0:T(8,128)(2,1)}, u32[]{:S(2)}, u32[]{:S(2)}) collective-permute-start(bf16[128,256]{1,0:T(8,128)(2,1)} %fusion.89), channel_id=1, source_target_pairs={{4,0},{8,4},{12,8},{16,12},{20,16},{24,20},{28,24},{32,28},{36,32}... | collective-permute-start | bytes 196616 | tf_op jit(solution)/shard_map/ppermute | solution.py:22
  132.3 24.3 %collective-permute-start.6 = (bf16[128,192]{1,0:T(8,128)(2,1)}, bf16[128,192]{1,0:T(8,128)(2,1)}, u32[]{:S(2)}, u32[]{:S(2)}) collective-permute-start(bf16[128,192]{1,0:T(8,128)(2,1)} %convert_element_type.232), channel_id=1, source_target_pairs={{8,0},{12,4},{16,8},{20,12},{24,16},{28,20},{32,24},{36,28},{40,32... | collective-permute-start | bytes 147464 | tf_op jit(solution)/shard_map/ppermute | solution.py:22
  135.7 20.9 %collective-permute-start.7 = (bf16[128,192]{1,0:T(8,128)(2,1)}, bf16[128,192]{1,0:T(8,128)(2,1)}, u32[]{:S(2)}, u32[]{:S(2)}) collective-permute-start(bf16[128,192]{1,0:T(8,128)(2,1)} %convert_element_type.234), channel_id=1, source_target_pairs={{504,0},{508,4},{0,8},{4,12},{8,16},{12,20},{16,24},{20,28},{24,32... | collective-permute-start | bytes 147464 | tf_op jit(solution)/shard_map/ppermute | solution.py:22
  166.8 5.8 %collective-permute-start.8 = (bf16[1408,128]{1,0:T(8,128)(2,1)S(1)}, bf16[1408,128]{1,0:T(8,128)(2,1)S(1)}, u32[]{:S(2)}, u32[]{:S(2)}) collective-permute-start(bf16[1408,128]{1,0:T(8,128)(2,1)S(1)} %select_convert_fusion), channel_id=1, source_target_pairs={{0,1},{1,0},{2,3},{3,2},{4,5},{5,4},{6,7},{7,6},{8,9},{9,8},{10,11... | collective-permute-start | bytes 1081352 | tf_op jit(solution)/shard_map/ppermute | solution.py:64
  172.7 7.7 %collective-permute-start.9 = (bf16[704,128]{1,0:T(8,128)(2,1)S(1)}, bf16[704,128]{1,0:T(8,128)(2,1)S(1)}, u32[]{:S(2)}, u32[]{:S(2)}) collective-permute-start(bf16[704,128]{1,0:T(8,128)(2,1)S(1)} %select_convert_fusion.1), channel_id=1, source_target_pairs={{0,2},{1,3},{2,0},{3,1},{4,6},{5,7},{6,4},{7,5},{8,10},{9,11},{10,... | collective-permute-start | bytes 540680 | tf_op jit(solution)/shard_map/ppermute | solution.py:68
  180.5 6.7 %collective-permute-start.10 = (bf16[704,128]{1,0:T(8,128)(2,1)S(1)}, bf16[704,128]{1,0:T(8,128)(2,1)S(1)}, u32[]{:S(2)}, u32[]{:S(2)}) collective-permute-start(bf16[704,128]{1,0:T(8,128)(2,1)S(1)} %add_convert_fusion), channel_id=1, source_target_pairs={{0,2},{1,3},{2,0},{3,1},{4,6},{5,7},{6,4},{7,5},{8,10},{9,11},{10,... | collective-permute-start | bytes 540680 | tf_op jit(solution)/shard_map/ppermute | solution.py:70
  187.3 5.3 %collective-permute-start.11 = (bf16[1408,128]{1,0:T(8,128)(2,1)S(1)}, bf16[1408,128]{1,0:T(8,128)(2,1)S(1)}, u32[]{:S(2)}, u32[]{:S(2)}) collective-permute-start(bf16[1408,128]{1,0:T(8,128)(2,1)S(1)} %maximum_select_fusion.1), channel_id=1, source_target_pairs={{0,1},{1,0},{2,3},{3,2},{4,5},{5,4},{6,7},{7,6},{8,9},{9,8},{10,11... | collective-permute-start | bytes 1081352 | tf_op jit(solution)/shard_map/ppermute | solution.py:74
  (31 other events, 151.3 us)

commit v3 on v1

--- a/solution.py
+++ b/solution.py
@@ -20,6 +20,13 @@
     devices = range(lax.axis_size(axis))
     route = [((i - distance) % len(devices), i) for i in devices]
     return lax.ppermute(block, axis, route)
+
+
+def shifted_pair(block, extra, axis, distance):
+    width = block.shape[1]
+    padded = jnp.pad(extra, ((0, block.shape[0] - extra.shape[0]), (0, 0)))
+    both = shifted(jnp.concatenate([block, padded], axis=1), axis, distance)
+    return both[:, :width], both[: extra.shape[0], width:]
 
 
 def extended_2(block, sides, width):
@@ -240,18 +247,6 @@
         "bsc,bsx->cx", selector_mask.astype(jnp.float32), returned_flat, precision=HIGHEST
     )
     outgoing = outgoing.reshape(2 * WIN + 1, tok_rows, 2 * features)
-    collected = outgoing[WIN]
-    for distance in range(-WIN, WIN + 1):
-        if distance != 0:
-            collected = collected + shifted(
-                outgoing[distance + WIN].astype(jnp.bfloat16), "seq", distance
-            ).astype(jnp.float32)
-    token_grads = [
-        dquery.reshape(tok_rows, features).astype(jnp.bfloat16),
-        collected[:, :features].astype(jnp.bfloat16),
-        collected[:, features:].astype(jnp.bfloat16),
-        grad_gate,
-    ]
     w_atom_all, w_atom_out_all, atom_bias_all = (w_atom, w_atom_out, atom_bias)
     atom_rows = atoms.shape[0]
     heads_atom = w_atom_all.shape[2] // DA
@@ -350,7 +345,28 @@
         )
     ext_grad = ext_grad.reshape(atom_rows + 2 * halo_rows, 2 * atom_feat)
     rims = jnp.concatenate([ext_grad[:halo_rows], ext_grad[atom_rows + halo_rows :]], axis=0)
-    edges = extended_2(rims.astype(jnp.bfloat16), (("seq", 0),), halo_rows).astype(rims.dtype)
+    collected = outgoing[WIN]
+    for distance in range(-WIN, WIN + 1):
+        if abs(distance) > 1:
+            collected = collected + shifted(
+                outgoing[distance + WIN].astype(jnp.bfloat16), "seq", distance
+            ).astype(jnp.float32)
+    came_low, edge_low = shifted_pair(
+        outgoing[WIN + 1].astype(jnp.bfloat16), rims[halo_rows:].astype(jnp.bfloat16), "seq", 1
+    )
+    came_high, edge_high = shifted_pair(
+        outgoing[WIN - 1].astype(jnp.bfloat16), rims[:halo_rows].astype(jnp.bfloat16), "seq", -1
+    )
+    collected = collected + came_low.astype(jnp.float32) + came_high.astype(jnp.float32)
+    edges = jnp.concatenate(
+        [edge_low, rims.astype(jnp.bfloat16), edge_high], axis=0
+    ).astype(rims.dtype)
+    token_grads = [
+        dquery.reshape(tok_rows, features).astype(jnp.bfloat16),
+        collected[:, :features].astype(jnp.bfloat16),
+        collected[:, features:].astype(jnp.bfloat16),
+        grad_gate,
+    ]
     own_grad = ext_grad[halo_rows : halo_rows + atom_rows]
     own_grad = jnp.concatenate(
         [

time: 154 us -> 163 us (1.058)
  other arithmetic: 12.5 us -> 21.4 us
  local copies, waits for them, and re-layouts: 19.6 us -> 26.9 us
  starting transfers between devices: 70.9 us -> 65.2 us
  waiting for transfers between devices: 18.6 us -> 15 us
    ppermute x2 -> x1, waiting for transfers between devices: 6.3 us -> 0.01 us  [extended_2(): lax.ppermute(lax.slice_in_dim(block, block.shape[dim] - width, None, axis...]
    sub x1, other arithmetic: 1.01 us -> 5.4 us  [attend_local(): exponent = jnp.exp(scores - row_max)]
    ppermute x8, waiting for transfers between devices: 0.02 us -> 2.74 us  [shifted(): return lax.ppermute(block, axis, route)]
    convert_element_type x2, local copies, waits for them, and re-layouts: 0.38 us -> 2.67 us  [body(): aquery_grad.reshape(atom_rows, atom_feat).astype(jnp.bfloat16)]
    ppermute x2 -> x1, starting transfers between devices: 11.2 us -> 9.09 us  [extended_2(): lax.ppermute(lax.slice_in_dim(block, 0, width, axis=dim), axis, backward)]
    dot_general x3, matrix products: 1.31 us -> 3.43 us  [body(): jnp.dot(atom_grads[which], w_atom_all[which].T, preferred_element_type=jn...]
    ppermute x2 -> x1, starting transfers between devices: 3.84 us -> 1.91 us  [extended_2(): lax.ppermute(lax.slice_in_dim(block, block.shape[dim] - width, None, axis...]
    dot_general x1, matrix products: 0.25 us -> 1.89 us  [body(): jnp.dot(atom_grads[0], w_atom_all[0].T, preferred_element_type=jnp.float32)]
  transfers between devices with their start and end apart: 16 -> 14, of which waited for: 6 -> 5; matrix products, arithmetic and copies ran while one was open for 26% -> 30% of each run, Pallas kernels for 0% -> 0%
where the time goes in v3:
time: 163 us; the launch traced here: 162 us
  starting transfers between devices  65.2 us (40%)
  matrix products  30.3 us (19%)
  local copies, waits for them, and re-layouts  26.9 us (17%)
  other arithmetic  21.4 us (13%)
  waiting for transfers between devices  15 us (9%)
  between operations  2.73 us (2%)
    ppermute x8, starting transfers between devices, shifted(): return lax.ppermute(block, axis, route)  40.4 us
    ppermute x1, starting transfers between devices, extended_2(): lax.ppermute(lax.slice_in_dim(block, 0, width, axis=dim), axis, backward)  9.09 us
    sub x1, other arithmetic, attend_local(): exponent = jnp.exp(scores - row_max)  5.4 us
    ppermute x1, waiting for transfers between devices, head_sum(): got = lax.ppermute(give.astype(jnp.bfloat16), axis, pair_far)  5.35 us
    ppermute x1, starting transfers between devices, head_sum(): got = lax.ppermute(give.astype(jnp.bfloat16), axis, pair_near)  5.13 us
    ppermute x1, waiting for transfers between devices, head_sum(): got = lax.ppermute(own, axis, pair_far)  4.42 us
    ppermute x1, starting transfers between devices, head_sum(): got = lax.ppermute(half, axis, pair_near)  4.03 us
    dot_general x4, matrix products, body(): jnp.dot(normed_low, w_token[which], preferred_element_type=jnp.float32)  3.7 us
  transfers between devices with their start and end apart: 14, of which 5 were waited for; matrix products, arithmetic and copies ran while one was open for 30% of the time, Pallas kernels for 0%

profile of v3, /device:TPU:1, one launch (start us, length us, event | category | flops | bytes accessed | tf_op | source)
XLA Modules:
  0.0 161.6 jit_solution(6967920720988341495)
XLA Ops:
  7.2 5.5 %collective-permute-start = (bf16[128,192]{0,1:T(8,128)(2,1)}, bf16[128,192]{0,1:T(8,128)(2,1)}, u32[]{:S(2)}, u32[]{:S(2)}) collective-permute-start(bf16[128,192]{0,1:T(8,128)(2,1)} %pad_maximum_fusion.7), channel_id=1, source_target_pairs={{504,0},{508,4},{0,8},{4,12},{8,16},{12,20},{16,24},{20,28},{24,32... | collective-permute-start | bytes 147464 | tf_op jit(solution)/shard_map/ppermute | solution.py:22
  12.6 2.2 %collective-permute-start.1 = (bf16[128,192]{0,1:T(8,128)(2,1)}, bf16[128,192]{0,1:T(8,128)(2,1)}, u32[]{:S(2)}, u32[]{:S(2)}) collective-permute-start(bf16[128,192]{0,1:T(8,128)(2,1)} %pad_maximum_fusion.7), channel_id=1, source_target_pairs={{508,0},{0,4},{4,8},{8,12},{12,16},{16,20},{20,24},{24,28},{28,32}... | collective-permute-start | bytes 147464 | tf_op jit(solution)/shard_map/ppermute | solution.py:22
  14.9 12.9 %collective-permute-start.2 = (bf16[128,192]{0,1:T(8,128)(2,1)}, bf16[128,192]{0,1:T(8,128)(2,1)}, u32[]{:S(2)}, u32[]{:S(2)}) collective-permute-start(bf16[128,192]{0,1:T(8,128)(2,1)} %pad_maximum_fusion.7), channel_id=1, source_target_pairs={{4,0},{8,4},{12,8},{16,12},{20,16},{24,20},{28,24},{32,28},{36,32}... | collective-permute-start | bytes 147464 | tf_op jit(solution)/shard_map/ppermute | solution.py:22
  34.5 1.9 %collective-permute-start.4 = (bf16[64,64]{0,1:T(8,128)(2,1)S(1)}, bf16[64,64]{0,1:T(8,128)(2,1)S(1)}, u32[]{:S(2)}, u32[]{:S(2)}) collective-permute-start(bf16[64,64]{0,1:T(8,128)(2,1)S(1)} %get-tuple-element.50), channel_id=1, source_target_pairs={{0,4},{4,8},{8,12},{12,16},{16,20},{20,24},{24,28},{28,32},{32,36}... | collective-permute-start | bytes 24584 | tf_op jit(solution)/shard_map/ppermute | solution.py:38
  36.4 9.1 %collective-permute-start.5 = (bf16[64,64]{0,1:T(8,128)(2,1)S(1)}, bf16[64,64]{0,1:T(8,128)(2,1)S(1)}, u32[]{:S(2)}, u32[]{:S(2)}) collective-permute-start(bf16[64,64]{0,1:T(8,128)(2,1)S(1)} %get-tuple-element.49), channel_id=1, source_target_pairs={{4,0},{8,4},{12,8},{16,12},{20,16},{24,20},{28,24},{32,28},{36,32}... | collective-permute-start | bytes 24584 | tf_op jit(solution)/shard_map/ppermute | solution.py:41
  51.8 2.1 %collective-permute-start.3 = (bf16[128,192]{0,1:T(8,128)(2,1)}, bf16[128,192]{0,1:T(8,128)(2,1)}, u32[]{:S(2)}, u32[]{:S(2)}) collective-permute-start(bf16[128,192]{0,1:T(8,128)(2,1)} %pad_maximum_fusion.7), channel_id=1, source_target_pairs={{8,0},{12,4},{16,8},{20,12},{24,16},{28,20},{32,24},{36,28},{40,32... | collective-permute-start | bytes 147464 | tf_op jit(solution)/shard_map/ppermute | solution.py:22
  56.1 2.2 %concatenate.69 = bf16[32,160,64]{1,2,0:T(8,128)(2,1)} concatenate(bf16[32,32,64]{1,2,0:T(8,128)(2,1)S(1)} %copy.91, bf16[32,32,64]{1,2,0:T(8,128)(2,1)S(1)} %copy.92, bf16[32,32,64]{1,2,0:T(8,128)(2,1)S(1)} %copy.93, bf16[32,32,64]{1,2,0:T(8,128)(2,1)S(1)} %copy.94, bf16[32,32,64]{1,2,0:T(8,128)(2,1)S(1)} %copy.95), dimensions={1} | concatenate | bytes 1310720 | tf_op jit(solution)/shard_map/concatenate | solution.py:281
  58.3 1.8 %fusion.11 = bf16[32,128,64]{1,2,0:T(8,128)(2,1)S(1)} fusion(bf16[32,160,64]{1,2,0:T(8,128)(2,1)} %concatenate.69, s32[32,128]{1,0:T(8,128)S(1)} %iota_add_fusion), kind=kOutput, calls=%fused_computation.15 | convolution fusion | flops 84803584 | bytes 1196032 | tf_op jit(solution)/shard_map/wrs,wsf->wrf/dot_general | solution.py:289
  60.5 5.4 %fusion.145 = (f32[32,32]{1,0:T(8,128)S(1)}, f32[32,32,128]{2,1,0:T(8,128)S(1)}) fusion(f32[32,32,128]{2,1,0:T(8,128)S(1)} %fusion.17), kind=kOutput, calls=%fused_computation.246 | output fusion | flops 262271 | bytes 1052672 | tf_op jit(solution)/shard_map/sub | solution.py:118
  65.9 1.8 %convolution_bitcast_fusion.1 = f32[32,32,1,32]{1,3,0,2:T(8,128)S(1)} fusion(bf16[32,128,64]{1,2,0:T(8,128)(2,1)S(1)} %fusion.11, f32[32,32]{1,0:T(8,128)S(1)} %get-tuple-element.54, f32[32,32,128]{2,1,0:T(8,128)S(1)} %fusion.17), kind=kOutput, calls=%fused_computation.23 | convolution fusion | flops 8782975 | bytes 1458176 | tf_op jit(solution)/shard_map/bhqk,bkhd->bqhd/dot_general | solution.py:121
  76.8 1.9 %convert_element_type.217 = bf16[1024,32]{0,1:T(8,128)(2,1)} reshape(bf16[32,32,1,32]{1,0,3,2:T(8,128)(2,1)} %copy.99) | data formatting | bytes 131072 | tf_op jit(solution)/shard_map/convert_element_type | solution.py:380
  78.7 1.9 %fusion.107 = f32[1024,128]{1,0:T(8,128)} fusion(bf16[1024,32]{0,1:T(8,128)(2,1)} %convert_element_type.217, bf16[4,128,32]{1,2,0:T(8,128)(2,1)} %param.24), kind=kOutput, calls=%fused_computation.194 | convolution fusion | flops 8388608 | bytes 598016 | tf_op jit(solution)/shard_map/dot_general | solution.py:385
  85.4 2.2 %stack.23 = bf16[5,24576]{1,0:T(8,128)(2,1)S(1)} concatenate(bf16[1,24576]{1,0:T(2,128)(2,1)S(1)} %stack.18, bf16[1,24576]{1,0:T(2,128)(2,1)S(1)} %stack.19, bf16[1,24576]{1,0:T(2,128)(2,1)} %stack.20, bf16[1,24576]{1,0:T(2,128)(2,1)S(1)} %stack.21, bf16[1,24576]{1,0:T(2,128)(2,1)S(1)} %stack.22), dimensions={0} | concatenate | bytes 491520 | tf_op jit(solution)/shard_map/stack | solution.py:192
  96.7 2.5 %collective-permute-start.6 = (bf16[128,256]{1,0:T(8,128)(2,1)}, bf16[128,256]{1,0:T(8,128)(2,1)S(1)}, u32[]{:S(2)}, u32[]{:S(2)}) collective-permute-start(bf16[128,256]{1,0:T(8,128)(2,1)} %fusion.86), channel_id=1, source_target_pairs={{508,0},{0,4},{4,8},{8,12},{12,16},{16,20},{20,24},{24,28},{28,32}... | collective-permute-start | bytes 196616 | tf_op jit(solution)/shard_map/ppermute | solution.py:22
  100.0 8.5 %collective-permute-start.7 = (bf16[128,256]{1,0:T(8,128)(2,1)}, bf16[128,256]{1,0:T(8,128)(2,1)S(1)}, u32[]{:S(2)}, u32[]{:S(2)}) collective-permute-start(bf16[128,256]{1,0:T(8,128)(2,1)} %fusion.87), channel_id=1, source_target_pairs={{4,0},{8,4},{12,8},{16,12},{20,16},{24,20},{28,24},{32,28},{36,32}... | collective-permute-start | bytes 196616 | tf_op jit(solution)/shard_map/ppermute | solution.py:22
  109.2 1.9 %collective-permute-start.8 = (bf16[128,192]{1,0:T(8,128)(2,1)}, bf16[128,192]{1,0:T(8,128)(2,1)S(1)}, u32[]{:S(2)}, u32[]{:S(2)}) collective-permute-start(bf16[128,192]{1,0:T(8,128)(2,1)} %convert_element_type.230), channel_id=1, source_target_pairs={{8,0},{12,4},{16,8},{20,12},{24,16},{28,20},{32,24},{36,28},{40,32... | collective-permute-start | bytes 147464 | tf_op jit(solution)/shard_map/ppermute | solution.py:22
  111.9 4.9 %collective-permute-start.9 = (bf16[128,192]{1,0:T(8,128)(2,1)}, bf16[128,192]{1,0:T(8,128)(2,1)}, u32[]{:S(2)}, u32[]{:S(2)}) collective-permute-start(bf16[128,192]{1,0:T(8,128)(2,1)} %convert_element_type.232), channel_id=1, source_target_pairs={{504,0},{508,4},{0,8},{4,12},{8,16},{12,20},{16,24},{20,28},{24,32... | collective-permute-start | bytes 147464 | tf_op jit(solution)/shard_map/ppermute | solution.py:22
  120.5 2.7 %collective-permute-done.9 = bf16[128,192]{1,0:T(8,128)(2,1)} collective-permute-done((bf16[128,192]{1,0:T(8,128)(2,1)}, bf16[128,192]{1,0:T(8,128)(2,1)}, u32[]{:S(2)}, u32[]{:S(2)}) %collective-permute-start.9) | collective-permute-done | bytes 49184 | tf_op jit(solution)/shard_map/ppermute | solution.py:22
  132.8 5.1 %collective-permute-start.10 = (bf16[1408,128]{1,0:T(8,128)(2,1)S(1)}, bf16[1408,128]{1,0:T(8,128)(2,1)S(1)}, u32[]{:S(2)}, u32[]{:S(2)}) collective-permute-start(bf16[1408,128]{1,0:T(8,128)(2,1)S(1)} %select_convert_fusion), channel_id=1, source_target_pairs={{0,1},{1,0},{2,3},{3,2},{4,5},{5,4},{6,7},{7,6},{8,9},{9,8},{10,11... | collective-permute-start | bytes 1081352 | tf_op jit(solution)/shard_map/ppermute | solution.py:64
  139.3 2.3 %collective-permute-start.11 = (bf16[704,128]{1,0:T(8,128)(2,1)S(1)}, bf16[704,128]{1,0:T(8,128)(2,1)S(1)}, u32[]{:S(2)}, u32[]{:S(2)}) collective-permute-start(bf16[704,128]{1,0:T(8,128)(2,1)S(1)} %select_convert_fusion.1), channel_id=1, source_target_pairs={{0,2},{1,3},{2,0},{3,1},{4,6},{5,7},{6,4},{7,5},{8,10},{9,11},{10,... | collective-permute-start | bytes 540680 | tf_op jit(solution)/shard_map/ppermute | solution.py:68
  141.6 5.3 %collective-permute-done.11 = bf16[704,128]{1,0:T(8,128)(2,1)S(1)} collective-permute-done((bf16[704,128]{1,0:T(8,128)(2,1)S(1)}, bf16[704,128]{1,0:T(8,128)(2,1)S(1)}, u32[]{:S(2)}, u32[]{:S(2)}) %collective-permute-start.11) | collective-permute-done | bytes 180256 | tf_op jit(solution)/shard_map/ppermute | solution.py:68
  147.1 2.3 %collective-permute-start.12 = (bf16[704,128]{1,0:T(8,128)(2,1)S(1)}, bf16[704,128]{1,0:T(8,128)(2,1)S(1)}, u32[]{:S(2)}, u32[]{:S(2)}) collective-permute-start(bf16[704,128]{1,0:T(8,128)(2,1)S(1)} %add_convert_fusion), channel_id=1, source_target_pairs={{0,2},{1,3},{2,0},{3,1},{4,6},{5,7},{6,4},{7,5},{8,10},{9,11},{10,... | collective-permute-start | bytes 540680 | tf_op jit(solution)/shard_map/ppermute | solution.py:70
  149.4 4.4 %collective-permute-done.12 = bf16[704,128]{1,0:T(8,128)(2,1)S(1)} collective-permute-done((bf16[704,128]{1,0:T(8,128)(2,1)S(1)}, bf16[704,128]{1,0:T(8,128)(2,1)S(1)}, u32[]{:S(2)}, u32[]{:S(2)}) %collective-permute-start.12) | collective-permute-done | bytes 180256 | tf_op jit(solution)/shard_map/ppermute | solution.py:70
  153.9 4.0 %collective-permute-start.13 = (bf16[1408,128]{1,0:T(8,128)(2,1)S(1)}, bf16[1408,128]{1,0:T(8,128)(2,1)S(1)}, u32[]{:S(2)}, u32[]{:S(2)}) collective-permute-start(bf16[1408,128]{1,0:T(8,128)(2,1)S(1)} %maximum_select_fusion.1), channel_id=1, source_target_pairs={{0,1},{1,0},{2,3},{3,2},{4,5},{5,4},{6,7},{7,6},{8,9},{9,8},{10,11... | collective-permute-start | bytes 1081352 | tf_op jit(solution)/shard_map/ppermute | solution.py:74
  (237 shorter events, 63.8 us)
Async XLA Ops:
  0.6 67.7 %copy-start = (bf16[1024,128]{1,0:T(8,128)(2,1)S(1)}, bf16[1024,128]{1,0:T(8,128)(2,1)}, u32[]{:S(2)}) copy-start(bf16[1024,128]{1,0:T(8,128)(2,1)} %param.33) | copy-start | bytes 786436
  0.6 45.3 %copy-start.9 = (bf16[4,384,96]{1,2,0:T(8,128)(2,1)S(1)}, bf16[4,384,96]{1,2,0:T(8,128)(2,1)}, u32[]{:S(2)}) copy-start(bf16[4,384,96]{1,2,0:T(8,128)(2,1)} %param.21) | copy-start | bytes 884740
  0.7 33.4 %copy-start.20 = (bf16[4,128,32]{1,2,0:T(8,128)(2,1)S(1)}, bf16[4,128,32]{1,2,0:T(8,128)(2,1)}, u32[]{:S(2)}) copy-start(bf16[4,128,32]{1,2,0:T(8,128)(2,1)} %param.24) | copy-start | bytes 98308
  0.7 46.9 %copy-start.41 = (s32[32]{0:T(128)S(1)}, s32[32]{0:T(128)}, u32[]{:S(2)}) copy-start(s32[32]{0:T(128)} %param.31) | copy-start | bytes 388
  1.7 47.2 %copy-start.42 = (s32[1,4]{1,0:T(1,128)S(1)}, s32[1,4]{1,0:T(1,128)}, u32[]{:S(2)}) copy-start(s32[1,4]{1,0:T(1,128)} %param.28) | copy-start | bytes 52
  7.2 74.0 %collective-permute-start = (bf16[128,192]{0,1:T(8,128)(2,1)}, bf16[128,192]{0,1:T(8,128)(2,1)}, u32[]{:S(2)}, u32[]{:S(2)}) collective-permute-start(bf16[128,192]{0,1:T(8,128)(2,1)} %pad_maximum_fusion.7), channel_id=1, source_target_pairs={{504,0},{508,4},{0,8},{4,12},{8,16},{12,20},{16,24},{20,28},{24,32... | collective-permute-start | bytes 147464 | tf_op jit(solution)/shard_map/ppermute | solution.py:22
  12.6 69.7 %collective-permute-start.1 = (bf16[128,192]{0,1:T(8,128)(2,1)}, bf16[128,192]{0,1:T(8,128)(2,1)}, u32[]{:S(2)}, u32[]{:S(2)}) collective-permute-start(bf16[128,192]{0,1:T(8,128)(2,1)} %pad_maximum_fusion.7), channel_id=1, source_target_pairs={{508,0},{0,4},{4,8},{8,12},{12,16},{16,20},{20,24},{24,28},{28,32}... | collective-permute-start | bytes 147464 | tf_op jit(solution)/shard_map/ppermute | solution.py:22
  14.9 68.5 %collective-permute-start.2 = (bf16[128,192]{0,1:T(8,128)(2,1)}, bf16[128,192]{0,1:T(8,128)(2,1)}, u32[]{:S(2)}, u32[]{:S(2)}) collective-permute-start(bf16[128,192]{0,1:T(8,128)(2,1)} %pad_maximum_fusion.7), channel_id=1, source_target_pairs={{4,0},{8,4},{12,8},{16,12},{20,16},{24,20},{28,24},{32,28},{36,32}... | collective-permute-start | bytes 147464 | tf_op jit(solution)/shard_map/ppermute | solution.py:22
  30.0 20.6 %copy-start.23 = (f32[1024]{0:T(1024)}, f32[1024]{0:T(1024)S(1)}, u32[]{:S(2)}) copy-start(f32[1024]{0:T(1024)S(1)} %broadcast_multiply_fusion.2) | copy-start | bytes 12292
  34.5 17.3 %collective-permute-start.4 = (bf16[64,64]{0,1:T(8,128)(2,1)S(1)}, bf16[64,64]{0,1:T(8,128)(2,1)S(1)}, u32[]{:S(2)}, u32[]{:S(2)}) collective-permute-start(bf16[64,64]{0,1:T(8,128)(2,1)S(1)} %get-tuple-element.50), channel_id=1, source_target_pairs={{0,4},{4,8},{8,12},{12,16},{16,20},{20,24},{24,28},{28,32},{32,36}... | collective-permute-start | bytes 24584 | tf_op jit(solution)/shard_map/ppermute | solution.py:38
  36.4 17.5 %collective-permute-start.5 = (bf16[64,64]{0,1:T(8,128)(2,1)S(1)}, bf16[64,64]{0,1:T(8,128)(2,1)S(1)}, u32[]{:S(2)}, u32[]{:S(2)}) collective-permute-start(bf16[64,64]{0,1:T(8,128)(2,1)S(1)} %get-tuple-element.49), channel_id=1, source_target_pairs={{4,0},{8,4},{12,8},{16,12},{20,16},{24,20},{28,24},{32,28},{36,32}... | collective-permute-start | bytes 24584 | tf_op jit(solution)/shard_map/ppermute | solution.py:41
  46.0 22.4 %copy-start.5 = (f32[1024,32]{0,1:T(8,128)}, f32[1024,32]{0,1:T(8,128)S(1)}, u32[]{:S(2)}) copy-start(f32[1024,32]{0,1:T(8,128)S(1)} %fusion.29) | copy-start | bytes 393220
  51.8 32.6 %collective-permute-start.3 = (bf16[128,192]{0,1:T(8,128)(2,1)}, bf16[128,192]{0,1:T(8,128)(2,1)}, u32[]{:S(2)}, u32[]{:S(2)}) collective-permute-start(bf16[128,192]{0,1:T(8,128)(2,1)} %pad_maximum_fusion.7), channel_id=1, source_target_pairs={{8,0},{12,4},{16,8},{20,12},{24,16},{28,20},{32,24},{36,28},{40,32... | collective-permute-start | bytes 147464 | tf_op jit(solution)/shard_map/ppermute | solution.py:22
  92.6 24.1 %copy-start.10 = (bf16[4,384,96]{1,2,0:T(8,128)(2,1)S(1)}, bf16[4,384,96]{1,2,0:T(8,128)(2,1)}, u32[]{:S(2)}) copy-start(bf16[4,384,96]{1,2,0:T(8,128)(2,1)} %param.21) | copy-start | bytes 884740
  93.3 33.7 %slice-start = ((bf16[36,32,64]{2,1,0:T(8,128)(2,1)}), bf16[28,32,64]{2,1,0:T(8,128)(2,1)S(1)}, s32[]{:S(2)}) async-start(bf16[36,32,64]{2,1,0:T(8,128)(2,1)} %pad_add_fusion), calls=%async_computation | async-start | bytes 458752 | tf_op jit(solution)/shard_map/slice | solution.py:374
  94.8 32.3 %copy-start.4 = (f32[1024,128]{1,0:T(8,128)S(1)}, f32[1024,128]{1,0:T(8,128)}, u32[]{:S(2)}) copy-start(f32[1024,128]{1,0:T(8,128)} %fusion.107) | copy-start | bytes 1572868
  96.7 26.5 %collective-permute-start.6 = (bf16[128,256]{1,0:T(8,128)(2,1)}, bf16[128,256]{1,0:T(8,128)(2,1)S(1)}, u32[]{:S(2)}, u32[]{:S(2)}) collective-permute-start(bf16[128,256]{1,0:T(8,128)(2,1)} %fusion.86), channel_id=1, source_target_pairs={{508,0},{0,4},{4,8},{8,12},{12,16},{16,20},{20,24},{24,28},{28,32}... | collective-permute-start | bytes 196616 | tf_op jit(solution)/shard_map/ppermute | solution.py:22
  100.0 23.2 %collective-permute-start.7 = (bf16[128,256]{1,0:T(8,128)(2,1)}, bf16[128,256]{1,0:T(8,128)(2,1)S(1)}, u32[]{:S(2)}, u32[]{:S(2)}) collective-permute-start(bf16[128,256]{1,0:T(8,128)(2,1)} %fusion.87), channel_id=1, source_target_pairs={{4,0},{8,4},{12,8},{16,12},{20,16},{24,20},{28,24},{32,28},{36,32}... | collective-permute-start | bytes 196616 | tf_op jit(solution)/shard_map/ppermute | solution.py:22
  109.2 11.2 %collective-permute-start.8 = (bf16[128,192]{1,0:T(8,128)(2,1)}, bf16[128,192]{1,0:T(8,128)(2,1)S(1)}, u32[]{:S(2)}, u32[]{:S(2)}) collective-permute-start(bf16[128,192]{1,0:T(8,128)(2,1)} %convert_element_type.230), channel_id=1, source_target_pairs={{8,0},{12,4},{16,8},{20,12},{24,16},{28,20},{32,24},{36,28},{40,32... | collective-permute-start | bytes 147464 | tf_op jit(solution)/shard_map/ppermute | solution.py:22
  111.9 11.3 %collective-permute-start.9 = (bf16[128,192]{1,0:T(8,128)(2,1)}, bf16[128,192]{1,0:T(8,128)(2,1)}, u32[]{:S(2)}, u32[]{:S(2)}) collective-permute-start(bf16[128,192]{1,0:T(8,128)(2,1)} %convert_element_type.232), channel_id=1, source_target_pairs={{504,0},{508,4},{0,8},{4,12},{8,16},{12,20},{16,24},{20,28},{24,32... | collective-permute-start | bytes 147464 | tf_op jit(solution)/shard_map/ppermute | solution.py:22
  132.8 6.4 %collective-permute-start.10 = (bf16[1408,128]{1,0:T(8,128)(2,1)S(1)}, bf16[1408,128]{1,0:T(8,128)(2,1)S(1)}, u32[]{:S(2)}, u32[]{:S(2)}) collective-permute-start(bf16[1408,128]{1,0:T(8,128)(2,1)S(1)} %select_convert_fusion), channel_id=1, source_target_pairs={{0,1},{1,0},{2,3},{3,2},{4,5},{5,4},{6,7},{7,6},{8,9},{9,8},{10,11... | collective-permute-start | bytes 1081352 | tf_op jit(solution)/shard_map/ppermute | solution.py:64
  139.3 7.7 %collective-permute-start.11 = (bf16[704,128]{1,0:T(8,128)(2,1)S(1)}, bf16[704,128]{1,0:T(8,128)(2,1)S(1)}, u32[]{:S(2)}, u32[]{:S(2)}) collective-permute-start(bf16[704,128]{1,0:T(8,128)(2,1)S(1)} %select_convert_fusion.1), channel_id=1, source_target_pairs={{0,2},{1,3},{2,0},{3,1},{4,6},{5,7},{6,4},{7,5},{8,10},{9,11},{10,... | collective-permute-start | bytes 540680 | tf_op jit(solution)/shard_map/ppermute | solution.py:68
  147.1 6.7 %collective-permute-start.12 = (bf16[704,128]{1,0:T(8,128)(2,1)S(1)}, bf16[704,128]{1,0:T(8,128)(2,1)S(1)}, u32[]{:S(2)}, u32[]{:S(2)}) collective-permute-start(bf16[704,128]{1,0:T(8,128)(2,1)S(1)} %add_convert_fusion), channel_id=1, source_target_pairs={{0,2},{1,3},{2,0},{3,1},{4,6},{5,7},{6,4},{7,5},{8,10},{9,11},{10,... | collective-permute-start | bytes 540680 | tf_op jit(solution)/shard_map/ppermute | solution.py:70
  153.9 5.3 %collective-permute-start.13 = (bf16[1408,128]{1,0:T(8,128)(2,1)S(1)}, bf16[1408,128]{1,0:T(8,128)(2,1)S(1)}, u32[]{:S(2)}, u32[]{:S(2)}) collective-permute-start(bf16[1408,128]{1,0:T(8,128)(2,1)S(1)} %maximum_select_fusion.1), channel_id=1, source_target_pairs={{0,1},{1,0},{2,3},{3,2},{4,5},{5,4},{6,7},{7,6},{8,9},{9,8},{10,11... | collective-permute-start | bytes 1081352 | tf_op jit(solution)/shard_map/ppermute | solution.py:74
  (35 other events, 183.4 us)

commit v4 on v1

--- a/solution.py
+++ b/solution.py
@@ -13,7 +13,7 @@
 
 
 EPSILON = 1e-05
-HIGHEST = lax.Precision.HIGHEST
+ONE_HOT_PRECISION = lax.Precision.HIGH
 
 
 def shifted(block, axis, distance):
@@ -166,9 +166,14 @@
     features = local_heads * DH
     scaling = DH ** (-0.5)
     normed_low = norm_rows(single.astype(jnp.float32), gain_single).astype(jnp.bfloat16)
+    token_width = w_token.shape[2]
+    projected_all = jnp.dot(
+        normed_low,
+        w_token.transpose(1, 0, 2).reshape(w_token.shape[1], 4 * token_width),
+        preferred_element_type=jnp.float32,
+    )
     projected = [
-        jnp.dot(normed_low, w_token[which], preferred_element_type=jnp.float32)
-        for which in range(4)
+        projected_all[:, which * token_width : (which + 1) * token_width] for which in range(4)
     ]
     queries = projected[0].astype(jnp.bfloat16)
     gate_act = jax.nn.sigmoid(projected[3])
@@ -237,7 +242,7 @@
     )
     returned_flat = returned.reshape(blocks_here, S, BLK * 2 * features)
     outgoing = jnp.einsum(
-        "bsc,bsx->cx", selector_mask.astype(jnp.float32), returned_flat, precision=HIGHEST
+        "bsc,bsx->cx", selector_mask.astype(jnp.float32), returned_flat, precision=ONE_HOT_PRECISION
     )
     outgoing = outgoing.reshape(2 * WIN + 1, tok_rows, 2 * features)
     collected = outgoing[WIN]
@@ -270,12 +275,17 @@
         jnp.float32
     )
     condition = jnp.dot(normed_low, w_cond, preferred_element_type=jnp.float32)
-    atom_input = (normed_atoms + jnp.dot(token_pick, condition, precision=HIGHEST)).astype(
+    atom_input = (normed_atoms + jnp.dot(token_pick, condition, precision=ONE_HOT_PRECISION)).astype(
         jnp.bfloat16
     )
+    atom_width = w_atom_all.shape[2]
+    atom_proj_all = jnp.dot(
+        atom_input,
+        w_atom_all.transpose(1, 0, 2).reshape(w_atom_all.shape[1], 4 * atom_width),
+        preferred_element_type=jnp.float32,
+    )
     atom_proj = [
-        jnp.dot(atom_input, w_atom_all[which], preferred_element_type=jnp.float32)
-        for which in range(4)
+        atom_proj_all[:, which * atom_width : (which + 1) * atom_width] for which in range(4)
     ]
     atom_gate = jax.nn.sigmoid(atom_proj[3])
     atom_kv = jnp.concatenate(
@@ -340,7 +350,7 @@
         axis=-1,
     )
     slab_grads = jnp.einsum(
-        "wrs,wrf->wsf", placer_mask.astype(jnp.float32), spread_grads, precision=HIGHEST
+        "wrs,wrf->wsf", placer_mask.astype(jnp.float32), spread_grads, precision=ONE_HOT_PRECISION
     )
     slab_grads = slab_grads.reshape(windows_here, group_span, AQ, 2 * atom_feat)
     ext_grad = jnp.pad(slab_grads[:, 0], ((0, group_span - 1), (0, 0), (0, 0)))
@@ -366,19 +376,19 @@
         own_grad[:, atom_feat:].astype(jnp.bfloat16),
         agrad_gate,
     ]
-    agrad_input = jnp.dot(atom_grads[0], w_atom_all[0].T, preferred_element_type=jnp.float32)
-    for which in range(1, 4):
-        agrad_input = agrad_input + jnp.dot(
-            atom_grads[which], w_atom_all[which].T, preferred_element_type=jnp.float32
-        )
+    agrad_input = jnp.dot(
+        jnp.concatenate(atom_grads, axis=1),
+        w_atom_all.transpose(0, 2, 1).reshape(4 * atom_width, w_atom_all.shape[1]),
+        preferred_element_type=jnp.float32,
+    )
     atoms_part = norm_back(atoms.astype(jnp.float32), gain_atom, agrad_input)
-    cond_grad = jnp.dot(token_pick.T, agrad_input, precision=HIGHEST)
-    cond_term = jnp.dot(cond_grad, w_cond.astype(jnp.float32).T, precision=HIGHEST)
-    grad_normed = cond_term
-    for which in range(4):
-        grad_normed = grad_normed + jnp.dot(
-            token_grads[which], w_token[which].T, preferred_element_type=jnp.float32
-        )
+    cond_grad = jnp.dot(token_pick.T, agrad_input, precision=ONE_HOT_PRECISION)
+    cond_term = jnp.dot(cond_grad, w_cond.astype(jnp.float32).T, precision=ONE_HOT_PRECISION)
+    grad_normed = cond_term + jnp.dot(
+        jnp.concatenate(token_grads, axis=1),
+        w_token.transpose(0, 2, 1).reshape(4 * token_width, w_token.shape[1]),
+        preferred_element_type=jnp.float32,
+    )
     single_part = norm_back(single.astype(jnp.float32), gain_single, grad_normed)
     token_total, atom_total, single_total, atoms_total = head_sum(
         [token_part, atom_part, single_part, atoms_part], "head"

time: 154 us -> 159 us (1.032)
  matrix products: 28.7 us -> 24.4 us
  other arithmetic: 12.5 us -> 16.6 us
  local copies, waits for them, and re-layouts: 19.6 us -> 23.1 us
  waiting for transfers between devices: 18.6 us -> 20.6 us
    dot_general x19 -> x7, matrix products: 11.8 us -> 5.29 us  [the longest x1 1.46 us: body(): jnp.dot(token_pick, condition, precision=ONE_HOT_PRECISION)]
    sub x1, other arithmetic: 1.01 us -> 5.4 us  [attend_local(): exponent = jnp.exp(scores - row_max)]
    ppermute x4 -> x0, local copies, waits for them, and re-layouts: 2.79 us -> none  [shifted(): return lax.ppermute(block, axis, route)]
    another operation x6, local copies, waits for them, and re-layouts: 2.08 us -> 4.79 us  [body(): window = jnp.stack(pieces)]
    dot_general x1, matrix products: 0.21 us -> 2.4 us  [body(): jnp.dot(grad_atom, w_atom_out_all.T, preferred_element_type=jnp.float32)]
  transfers between devices with their start and end apart: 16 -> 16, of which waited for: 6 -> 7; matrix products, arithmetic and copies ran while one was open for 26% -> 30% of each run, Pallas kernels for 0% -> 0%
where the time goes in v4:
time: 159 us; the launch traced here: 158 us
  starting transfers between devices  70.6 us (44%)
  matrix products  24.4 us (15%)
  local copies, waits for them, and re-layouts  23.1 us (15%)
  waiting for transfers between devices  20.6 us (13%)
  other arithmetic  16.6 us (10%)
  between operations  2.59 us (2%)
    ppermute x8, starting transfers between devices, shifted(): return lax.ppermute(block, axis, route)  41.9 us
    ppermute x2, starting transfers between devices, extended_2(): lax.ppermute(lax.slice_in_dim(block, 0, width, axis=dim), axis, backward)  10 us
    ppermute x2, waiting for transfers between devices, extended_2(): lax.ppermute(lax.slice_in_dim(block, block.shape[dim] - width, None, axis...  6.89 us
    ppermute x1, starting transfers between devices, head_sum(): got = lax.ppermute(give.astype(jnp.bfloat16), axis, pair_near)  6.24 us
    sub x1, other arithmetic, attend_local(): exponent = jnp.exp(scores - row_max)  5.4 us
    ppermute x1, waiting for transfers between devices, head_sum(): got = lax.ppermute(give.astype(jnp.bfloat16), axis, pair_far)  5.34 us
    another operation x6, local copies, waits for them, and re-layouts, body(): window = jnp.stack(pieces)  4.79 us
    ppermute x1, waiting for transfers between devices, head_sum(): got = lax.ppermute(own, axis, pair_far)  4.42 us
  transfers between devices with their start and end apart: 16, of which 7 were waited for; matrix products, arithmetic and copies ran while one was open for 30% of the time, Pallas kernels for 0%

profile of v4, /device:TPU:1, one launch (start us, length us, event | category | flops | bytes accessed | tf_op | source)
XLA Modules:
  0.0 157.9 jit_solution(1122881748940593031)
XLA Ops:
  4.7 5.5 %collective-permute-start = (bf16[128,192]{1,0:T(8,128)(2,1)}, bf16[128,192]{1,0:T(8,128)(2,1)}, u32[]{:S(2)}, u32[]{:S(2)}) collective-permute-start(bf16[128,192]{1,0:T(8,128)(2,1)} %slice.311), channel_id=1, source_target_pairs={{504,0},{508,4},{0,8},{4,12},{8,16},{12,20},{16,24},{20,28},{24,32... | collective-permute-start | bytes 147464 | tf_op jit(solution)/shard_map/ppermute | solution.py:22
  10.2 2.2 %collective-permute-start.1 = (bf16[128,192]{1,0:T(8,128)(2,1)}, bf16[128,192]{1,0:T(8,128)(2,1)}, u32[]{:S(2)}, u32[]{:S(2)}) collective-permute-start(bf16[128,192]{1,0:T(8,128)(2,1)} %slice.311), channel_id=1, source_target_pairs={{508,0},{0,4},{4,8},{8,12},{12,16},{16,20},{20,24},{24,28},{28,32}... | collective-permute-start | bytes 147464 | tf_op jit(solution)/shard_map/ppermute | solution.py:22
  12.4 12.9 %collective-permute-start.2 = (bf16[128,192]{1,0:T(8,128)(2,1)}, bf16[128,192]{1,0:T(8,128)(2,1)}, u32[]{:S(2)}, u32[]{:S(2)}) collective-permute-start(bf16[128,192]{1,0:T(8,128)(2,1)} %slice.311), channel_id=1, source_target_pairs={{4,0},{8,4},{12,8},{16,12},{20,16},{24,20},{28,24},{32,28},{36,32}... | collective-permute-start | bytes 147464 | tf_op jit(solution)/shard_map/ppermute | solution.py:22
  32.9 3.4 %collective-permute-start.5 = (bf16[64,64]{0,1:T(8,128)(2,1)S(1)}, bf16[64,64]{0,1:T(8,128)(2,1)S(1)}, u32[]{:S(2)}, u32[]{:S(2)}) collective-permute-start(bf16[64,64]{0,1:T(8,128)(2,1)S(1)} %get-tuple-element.40), channel_id=1, source_target_pairs={{4,0},{8,4},{12,8},{16,12},{20,16},{24,20},{28,24},{32,28},{36,32}... | collective-permute-start | bytes 24584 | tf_op jit(solution)/shard_map/ppermute | solution.py:34
  36.2 1.9 %collective-permute-start.4 = (bf16[64,64]{0,1:T(8,128)(2,1)S(1)}, bf16[64,64]{0,1:T(8,128)(2,1)S(1)}, u32[]{:S(2)}, u32[]{:S(2)}) collective-permute-start(bf16[64,64]{0,1:T(8,128)(2,1)S(1)} %get-tuple-element.41), channel_id=1, source_target_pairs={{0,4},{4,8},{8,12},{12,16},{16,20},{20,24},{24,28},{28,32},{32,36}... | collective-permute-start | bytes 24584 | tf_op jit(solution)/shard_map/ppermute | solution.py:31
  43.9 2.6 %collective-permute-done.4 = bf16[64,64]{0,1:T(8,128)(2,1)S(1)} collective-permute-done((bf16[64,64]{0,1:T(8,128)(2,1)S(1)}, bf16[64,64]{0,1:T(8,128)(2,1)S(1)}, u32[]{:S(2)}, u32[]{:S(2)}) %collective-permute-start.4) | collective-permute-done | bytes 8224 | tf_op jit(solution)/shard_map/ppermute | solution.py:31
  48.5 2.3 %concatenate.69 = bf16[32,160,64]{1,2,0:T(8,128)(2,1)} concatenate(bf16[32,32,64]{1,2,0:T(8,128)(2,1)S(1)} %copy.136, bf16[32,32,64]{1,2,0:T(8,128)(2,1)S(1)} %copy.137, bf16[32,32,64]{1,2,0:T(8,128)(2,1)S(1)} %copy.138, bf16[32,32,64]{1,2,0:T(8,128)(2,1)S(1)} %copy.139, bf16[32,32,64]{1,2,0:T(8,128)(2,1)S(1)} %copy.140), dimensions={1} | concatenate | bytes 1310720 | tf_op jit(solution)/shard_map/concatenate | solution.py:296
  53.0 5.4 %fusion.116 = (f32[32,32]{1,0:T(8,128)S(1)}, f32[32,32,128]{2,1,0:T(8,128)S(1)}) fusion(f32[32,32,128]{2,1,0:T(8,128)S(1)} %fusion.17), kind=kOutput, calls=%fused_computation.197 | output fusion | flops 262271 | bytes 1052672 | tf_op jit(solution)/shard_map/sub | solution.py:111
  58.4 2.6 %convolution_bitcast_fusion.1 = f32[32,32,1,32]{1,3,0,2:T(8,128)} fusion(bf16[32,128,64]{1,2,0:T(8,128)(2,1)S(1)} %fusion.11, f32[32,32]{1,0:T(8,128)S(1)} %get-tuple-element.60, f32[32,32,128]{2,1,0:T(8,128)S(1)} %fusion.17), kind=kOutput, calls=%fused_computation.20 | convolution fusion | flops 8782975 | bytes 1458176 | tf_op jit(solution)/shard_map/bhqk,bkhd->bqhd/dot_general | solution.py:114
  62.9 2.4 %multiply_reduce_fusion.1 = (f32[1024]{0:T(1024)}, bf16[1024,32]{0,1:T(8,128)(2,1)}, bf16[1024,32]{0,1:T(8,128)(2,1)}) fusion(f32[1024,32]{0,1:T(8,128)S(1)} %reshape.443, f32[1024,128]{0,1:T(8,128)S(1)} %copy-done.5, bf16[1024,128]{1,0:T(8,128)(2,1)} %param.33, bf16[32,128]{1,0:T(8,128)(2,1)S(1)} %copy-done.18), kind=kOutput, calls=%fused_computation.122 | convolution fusion | flops 8813568 | bytes 667648 | tf_op jit(solution)/shard_map/dot_general | solution.py:325
  66.4 2.5 %convolution_bitcast_fusion = f32[32,128,32]{1,2,0:T(8,128)S(1)} fusion(bf16[32,32,32]{1,0,2:T(8,128)(2,1)S(1)} %reshape.444, f32[32,32]{1,0:T(8,128)} %copy-done.17, f32[32,32,128]{2,1,0:T(8,128)S(1)} %fusion.17), kind=kOutput, calls=%fused_computation.19 | convolution fusion | flops 8782975 | bytes 1118208 | tf_op jit(solution)/shard_map/bhqk,bqhd->bkhd/dot_general | solution.py:136
  72.9 6.6 %collective-permute-start.7 = (bf16[64,64]{1,0:T(8,128)(2,1)S(1)}, bf16[64,64]{1,0:T(8,128)(2,1)S(1)}, u32[]{:S(2)}, u32[]{:S(2)}) collective-permute-start(bf16[64,64]{1,0:T(8,128)(2,1)S(1)} %bitcast.194), channel_id=1, source_target_pairs={{4,0},{8,4},{12,8},{16,12},{20,16},{24,20},{28,24},{32,28},{36,32}... | collective-permute-start | bytes 24584 | tf_op jit(solution)/shard_map/ppermute | solution.py:34
  79.6 1.9 %collective-permute-start.6 = (bf16[64,64]{1,0:T(8,128)(2,1)S(1)}, bf16[64,64]{1,0:T(8,128)(2,1)S(1)}, u32[]{:S(2)}, u32[]{:S(2)}) collective-permute-start(bf16[64,64]{1,0:T(8,128)(2,1)S(1)} %bitcast.192), channel_id=1, source_target_pairs={{0,4},{4,8},{8,12},{12,16},{16,20},{20,24},{24,28},{28,32},{32,36}... | collective-permute-start | bytes 24584 | tf_op jit(solution)/shard_map/ppermute | solution.py:31
  82.2 3.3 %collective-permute-start.3 = (bf16[128,192]{1,0:T(8,128)(2,1)}, bf16[128,192]{1,0:T(8,128)(2,1)S(1)}, u32[]{:S(2)}, u32[]{:S(2)}) collective-permute-start(bf16[128,192]{1,0:T(8,128)(2,1)} %slice.311), channel_id=1, source_target_pairs={{8,0},{12,4},{16,8},{20,12},{24,16},{28,20},{32,24},{36,28},{40,32... | collective-permute-start | bytes 147464 | tf_op jit(solution)/shard_map/ppermute | solution.py:22
  85.5 4.3 %collective-permute-done.6 = bf16[64,64]{1,0:T(8,128)(2,1)S(1)} collective-permute-done((bf16[64,64]{1,0:T(8,128)(2,1)S(1)}, bf16[64,64]{1,0:T(8,128)(2,1)S(1)}, u32[]{:S(2)}, u32[]{:S(2)}) %collective-permute-start.6) | collective-permute-done | bytes 8224 | tf_op jit(solution)/shard_map/ppermute | solution.py:31
  107.3 4.2 %collective-permute-start.10 = (bf16[128,192]{1,0:T(8,128)(2,1)S(1)}, bf16[128,192]{1,0:T(8,128)(2,1)S(1)}, u32[]{:S(2)}, u32[]{:S(2)}) collective-permute-start(bf16[128,192]{1,0:T(8,128)(2,1)S(1)} %convert_element_type.206), channel_id=1, source_target_pairs={{508,0},{0,4},{4,8},{8,12},{12,16},{16,20},{20,24},{24,28},{28,32}... | collective-permute-start | bytes 147464 | tf_op jit(solution)/shard_map/ppermute | solution.py:22
  111.6 8.8 %collective-permute-start.9 = (bf16[128,192]{1,0:T(8,128)(2,1)S(1)}, bf16[128,192]{1,0:T(8,128)(2,1)S(1)}, u32[]{:S(2)}, u32[]{:S(2)}) collective-permute-start(bf16[128,192]{1,0:T(8,128)(2,1)S(1)} %convert_element_type.204), channel_id=1, source_target_pairs={{4,0},{8,4},{12,8},{16,12},{20,16},{24,20},{28,24},{32,28},{36,32}... | collective-permute-start | bytes 147464 | tf_op jit(solution)/shard_map/ppermute | solution.py:22
  120.5 3.1 %collective-permute-start.8 = (bf16[128,192]{1,0:T(8,128)(2,1)S(1)}, bf16[128,192]{1,0:T(8,128)(2,1)S(1)}, u32[]{:S(2)}, u32[]{:S(2)}) collective-permute-start(bf16[128,192]{1,0:T(8,128)(2,1)S(1)} %convert_element_type.202), channel_id=1, source_target_pairs={{8,0},{12,4},{16,8},{20,12},{24,16},{28,20},{32,24},{36,28},{40,32... | collective-permute-start | bytes 147464 | tf_op jit(solution)/shard_map/ppermute | solution.py:22
  128.0 6.2 %collective-permute-start.12 = (bf16[1408,128]{1,0:T(8,128)(2,1)S(1)}, bf16[1408,128]{1,0:T(8,128)(2,1)S(1)}, u32[]{:S(2)}, u32[]{:S(2)}) collective-permute-start(bf16[1408,128]{1,0:T(8,128)(2,1)S(1)} %select_convert_fusion), channel_id=1, source_target_pairs={{0,1},{1,0},{2,3},{3,2},{4,5},{5,4},{6,7},{7,6},{8,9},{9,8},{10,11... | collective-permute-start | bytes 1081352 | tf_op jit(solution)/shard_map/ppermute | solution.py:57
  135.6 2.3 %collective-permute-start.13 = (bf16[704,128]{1,0:T(8,128)(2,1)S(1)}, bf16[704,128]{1,0:T(8,128)(2,1)S(1)}, u32[]{:S(2)}, u32[]{:S(2)}) collective-permute-start(bf16[704,128]{1,0:T(8,128)(2,1)S(1)} %select_convert_fusion.1), channel_id=1, source_target_pairs={{0,2},{1,3},{2,0},{3,1},{4,6},{5,7},{6,4},{7,5},{8,10},{9,11},{10,... | collective-permute-start | bytes 540680 | tf_op jit(solution)/shard_map/ppermute | solution.py:61
  138.0 5.3 %collective-permute-done.13 = bf16[704,128]{1,0:T(8,128)(2,1)S(1)} collective-permute-done((bf16[704,128]{1,0:T(8,128)(2,1)S(1)}, bf16[704,128]{1,0:T(8,128)(2,1)S(1)}, u32[]{:S(2)}, u32[]{:S(2)}) %collective-permute-start.13) | collective-permute-done | bytes 180256 | tf_op jit(solution)/shard_map/ppermute | solution.py:61
  143.4 2.3 %collective-permute-start.14 = (bf16[704,128]{1,0:T(8,128)(2,1)S(1)}, bf16[704,128]{1,0:T(8,128)(2,1)S(1)}, u32[]{:S(2)}, u32[]{:S(2)}) collective-permute-start(bf16[704,128]{1,0:T(8,128)(2,1)S(1)} %add_convert_fusion), channel_id=1, source_target_pairs={{0,2},{1,3},{2,0},{3,1},{4,6},{5,7},{6,4},{7,5},{8,10},{9,11},{10,... | collective-permute-start | bytes 540680 | tf_op jit(solution)/shard_map/ppermute | solution.py:63
  145.7 4.4 %collective-permute-done.14 = bf16[704,128]{1,0:T(8,128)(2,1)S(1)} collective-permute-done((bf16[704,128]{1,0:T(8,128)(2,1)S(1)}, bf16[704,128]{1,0:T(8,128)(2,1)S(1)}, u32[]{:S(2)}, u32[]{:S(2)}) %collective-permute-start.14) | collective-permute-done | bytes 180256 | tf_op jit(solution)/shard_map/ppermute | solution.py:63
  150.2 4.0 %collective-permute-start.15 = (bf16[1408,128]{1,0:T(8,128)(2,1)S(1)}, bf16[1408,128]{1,0:T(8,128)(2,1)S(1)}, u32[]{:S(2)}, u32[]{:S(2)}) collective-permute-start(bf16[1408,128]{1,0:T(8,128)(2,1)S(1)} %maximum_select_fusion.1), channel_id=1, source_target_pairs={{0,1},{1,0},{2,3},{3,2},{4,5},{5,4},{6,7},{7,6},{8,9},{9,8},{10,11... | collective-permute-start | bytes 1081352 | tf_op jit(solution)/shard_map/ppermute | solution.py:67
  (196 shorter events, 54.7 us)
Async XLA Ops:
  0.6 31.1 %copy-start.7 = (bf16[4,128,32]{1,2,0:T(8,128)(2,1)S(1)}, bf16[4,128,32]{1,2,0:T(8,128)(2,1)}, u32[]{:S(2)}) copy-start(bf16[4,128,32]{1,2,0:T(8,128)(2,1)} %param.24) | copy-start | bytes 98308
  0.7 37.5 %copy-start.27 = (s32[32]{0:T(128)S(1)}, s32[32]{0:T(128)}, u32[]{:S(2)}) copy-start(s32[32]{0:T(128)} %param.31) | copy-start | bytes 388
  0.7 39.5 %copy-start.28 = (s32[1,4]{1,0:T(1,128)S(1)}, s32[1,4]{1,0:T(1,128)}, u32[]{:S(2)}) copy-start(s32[1,4]{1,0:T(1,128)} %param.28) | copy-start | bytes 52
  2.8 26.1 %copy-start.20 = (f32[128]{0:T(128)}, f32[128]{0:T(128)S(1)}, u32[]{:S(2)}) copy-start(f32[128]{0:T(128)S(1)} %add_rsqrt_fusion.1) | copy-start | bytes 1540
  4.7 87.7 %collective-permute-start = (bf16[128,192]{1,0:T(8,128)(2,1)}, bf16[128,192]{1,0:T(8,128)(2,1)}, u32[]{:S(2)}, u32[]{:S(2)}) collective-permute-start(bf16[128,192]{1,0:T(8,128)(2,1)} %slice.311), channel_id=1, source_target_pairs={{504,0},{508,4},{0,8},{4,12},{8,16},{12,20},{16,24},{20,28},{24,32... | collective-permute-start | bytes 147464 | tf_op jit(solution)/shard_map/ppermute | solution.py:22
  10.2 83.2 %collective-permute-start.1 = (bf16[128,192]{1,0:T(8,128)(2,1)}, bf16[128,192]{1,0:T(8,128)(2,1)}, u32[]{:S(2)}, u32[]{:S(2)}) collective-permute-start(bf16[128,192]{1,0:T(8,128)(2,1)} %slice.311), channel_id=1, source_target_pairs={{508,0},{0,4},{4,8},{8,12},{12,16},{16,20},{20,24},{24,28},{28,32}... | collective-permute-start | bytes 147464 | tf_op jit(solution)/shard_map/ppermute | solution.py:22
  12.4 82.0 %collective-permute-start.2 = (bf16[128,192]{1,0:T(8,128)(2,1)}, bf16[128,192]{1,0:T(8,128)(2,1)}, u32[]{:S(2)}, u32[]{:S(2)}) collective-permute-start(bf16[128,192]{1,0:T(8,128)(2,1)} %slice.311), channel_id=1, source_target_pairs={{4,0},{8,4},{12,8},{16,12},{20,16},{24,20},{28,24},{32,28},{36,32}... | collective-permute-start | bytes 147464 | tf_op jit(solution)/shard_map/ppermute | solution.py:22
  32.9 11.0 %collective-permute-start.5 = (bf16[64,64]{0,1:T(8,128)(2,1)S(1)}, bf16[64,64]{0,1:T(8,128)(2,1)S(1)}, u32[]{:S(2)}, u32[]{:S(2)}) collective-permute-start(bf16[64,64]{0,1:T(8,128)(2,1)S(1)} %get-tuple-element.40), channel_id=1, source_target_pairs={{4,0},{8,4},{12,8},{16,12},{20,16},{24,20},{28,24},{32,28},{36,32}... | collective-permute-start | bytes 24584 | tf_op jit(solution)/shard_map/ppermute | solution.py:34
  36.2 10.2 %collective-permute-start.4 = (bf16[64,64]{0,1:T(8,128)(2,1)S(1)}, bf16[64,64]{0,1:T(8,128)(2,1)S(1)}, u32[]{:S(2)}, u32[]{:S(2)}) collective-permute-start(bf16[64,64]{0,1:T(8,128)(2,1)S(1)} %get-tuple-element.41), channel_id=1, source_target_pairs={{0,4},{4,8},{8,12},{12,16},{16,20},{20,24},{24,28},{28,32},{32,36}... | collective-permute-start | bytes 24584 | tf_op jit(solution)/shard_map/ppermute | solution.py:31
  72.9 9.3 %collective-permute-start.7 = (bf16[64,64]{1,0:T(8,128)(2,1)S(1)}, bf16[64,64]{1,0:T(8,128)(2,1)S(1)}, u32[]{:S(2)}, u32[]{:S(2)}) collective-permute-start(bf16[64,64]{1,0:T(8,128)(2,1)S(1)} %bitcast.194), channel_id=1, source_target_pairs={{4,0},{8,4},{12,8},{16,12},{20,16},{24,20},{28,24},{32,28},{36,32}... | collective-permute-start | bytes 24584 | tf_op jit(solution)/shard_map/ppermute | solution.py:34
  79.6 10.2 %collective-permute-start.6 = (bf16[64,64]{1,0:T(8,128)(2,1)S(1)}, bf16[64,64]{1,0:T(8,128)(2,1)S(1)}, u32[]{:S(2)}, u32[]{:S(2)}) collective-permute-start(bf16[64,64]{1,0:T(8,128)(2,1)S(1)} %bitcast.192), channel_id=1, source_target_pairs={{0,4},{4,8},{8,12},{12,16},{16,20},{20,24},{24,28},{28,32},{32,36}... | collective-permute-start | bytes 24584 | tf_op jit(solution)/shard_map/ppermute | solution.py:31
  82.2 13.2 %collective-permute-start.3 = (bf16[128,192]{1,0:T(8,128)(2,1)}, bf16[128,192]{1,0:T(8,128)(2,1)S(1)}, u32[]{:S(2)}, u32[]{:S(2)}) collective-permute-start(bf16[128,192]{1,0:T(8,128)(2,1)} %slice.311), channel_id=1, source_target_pairs={{8,0},{12,4},{16,8},{20,12},{24,16},{28,20},{32,24},{36,28},{40,32... | collective-permute-start | bytes 147464 | tf_op jit(solution)/shard_map/ppermute | solution.py:22
  102.7 24.7 %copy-start.2 = (bf16[128,384]{1,0:T(8,128)(2,1)S(1)}, bf16[128,384]{1,0:T(8,128)(2,1)}, u32[]{:S(2)}) copy-start(bf16[128,384]{1,0:T(8,128)(2,1)} %param.17) | copy-start | bytes 294916
  102.7 24.7 %copy-start.10 = (bf16[384,128]{1,0:T(8,128)(2,1)S(1)}, bf16[384,128]{1,0:T(8,128)(2,1)}, u32[]{:S(2)}) copy-start(bf16[384,128]{1,0:T(8,128)(2,1)} %param.23) | copy-start | bytes 294916
  102.7 24.7 %copy-start.19 = (f32[384]{0:T(512)S(1)}, f32[384]{0:T(512)}, u32[]{:S(2)}) copy-start(f32[384]{0:T(512)} %param.19) | copy-start | bytes 4612
  102.7 24.7 %copy-start.21 = (f32[128]{0:T(128)S(1)}, f32[128]{0:T(128)}, u32[]{:S(2)}) copy-start(f32[128]{0:T(128)} %copy-done.20) | copy-start | bytes 1540
  105.2 20.4 %collective-permute-start.11 = (bf16[128,192]{1,0:T(8,128)(2,1)S(1)}, bf16[128,192]{1,0:T(8,128)(2,1)S(1)}, u32[]{:S(2)}, u32[]{:S(2)}) collective-permute-start(bf16[128,192]{1,0:T(8,128)(2,1)S(1)} %convert_element_type.208), channel_id=1, source_target_pairs={{504,0},{508,4},{0,8},{4,12},{8,16},{12,20},{16,24},{20,28},{24,32... | collective-permute-start | bytes 147464 | tf_op jit(solution)/shard_map/ppermute | solution.py:22
  107.3 18.3 %collective-permute-start.10 = (bf16[128,192]{1,0:T(8,128)(2,1)S(1)}, bf16[128,192]{1,0:T(8,128)(2,1)S(1)}, u32[]{:S(2)}, u32[]{:S(2)}) collective-permute-start(bf16[128,192]{1,0:T(8,128)(2,1)S(1)} %convert_element_type.206), channel_id=1, source_target_pairs={{508,0},{0,4},{4,8},{8,12},{12,16},{16,20},{20,24},{24,28},{28,32}... | collective-permute-start | bytes 147464 | tf_op jit(solution)/shard_map/ppermute | solution.py:22
  111.6 14.1 %collective-permute-start.9 = (bf16[128,192]{1,0:T(8,128)(2,1)S(1)}, bf16[128,192]{1,0:T(8,128)(2,1)S(1)}, u32[]{:S(2)}, u32[]{:S(2)}) collective-permute-start(bf16[128,192]{1,0:T(8,128)(2,1)S(1)} %convert_element_type.204), channel_id=1, source_target_pairs={{4,0},{8,4},{12,8},{16,12},{20,16},{24,20},{28,24},{32,28},{36,32}... | collective-permute-start | bytes 147464 | tf_op jit(solution)/shard_map/ppermute | solution.py:22
  120.5 6.5 %collective-permute-start.8 = (bf16[128,192]{1,0:T(8,128)(2,1)S(1)}, bf16[128,192]{1,0:T(8,128)(2,1)S(1)}, u32[]{:S(2)}, u32[]{:S(2)}) collective-permute-start(bf16[128,192]{1,0:T(8,128)(2,1)S(1)} %convert_element_type.202), channel_id=1, source_target_pairs={{8,0},{12,4},{16,8},{20,12},{24,16},{28,20},{32,24},{36,28},{40,32... | collective-permute-start | bytes 147464 | tf_op jit(solution)/shard_map/ppermute | solution.py:22
  128.0 7.5 %collective-permute-start.12 = (bf16[1408,128]{1,0:T(8,128)(2,1)S(1)}, bf16[1408,128]{1,0:T(8,128)(2,1)S(1)}, u32[]{:S(2)}, u32[]{:S(2)}) collective-permute-start(bf16[1408,128]{1,0:T(8,128)(2,1)S(1)} %select_convert_fusion), channel_id=1, source_target_pairs={{0,1},{1,0},{2,3},{3,2},{4,5},{5,4},{6,7},{7,6},{8,9},{9,8},{10,11... | collective-permute-start | bytes 1081352 | tf_op jit(solution)/shard_map/ppermute | solution.py:57
  135.6 7.7 %collective-permute-start.13 = (bf16[704,128]{1,0:T(8,128)(2,1)S(1)}, bf16[704,128]{1,0:T(8,128)(2,1)S(1)}, u32[]{:S(2)}, u32[]{:S(2)}) collective-permute-start(bf16[704,128]{1,0:T(8,128)(2,1)S(1)} %select_convert_fusion.1), channel_id=1, source_target_pairs={{0,2},{1,3},{2,0},{3,1},{4,6},{5,7},{6,4},{7,5},{8,10},{9,11},{10,... | collective-permute-start | bytes 540680 | tf_op jit(solution)/shard_map/ppermute | solution.py:61
  143.4 6.7 %collective-permute-start.14 = (bf16[704,128]{1,0:T(8,128)(2,1)S(1)}, bf16[704,128]{1,0:T(8,128)(2,1)S(1)}, u32[]{:S(2)}, u32[]{:S(2)}) collective-permute-start(bf16[704,128]{1,0:T(8,128)(2,1)S(1)} %add_convert_fusion), channel_id=1, source_target_pairs={{0,2},{1,3},{2,0},{3,1},{4,6},{5,7},{6,4},{7,5},{8,10},{9,11},{10,... | collective-permute-start | bytes 540680 | tf_op jit(solution)/shard_map/ppermute | solution.py:63
  150.2 5.3 %collective-permute-start.15 = (bf16[1408,128]{1,0:T(8,128)(2,1)S(1)}, bf16[1408,128]{1,0:T(8,128)(2,1)S(1)}, u32[]{:S(2)}, u32[]{:S(2)}) collective-permute-start(bf16[1408,128]{1,0:T(8,128)(2,1)S(1)} %maximum_select_fusion.1), channel_id=1, source_target_pairs={{0,1},{1,0},{2,3},{3,2},{4,5},{5,4},{6,7},{7,6},{8,9},{9,8},{10,11... | collective-permute-start | bytes 1081352 | tf_op jit(solution)/shard_map/ppermute | solution.py:67
  (22 other events, 180.7 us)

commit v5 on v2

--- a/solution.py
+++ b/solution.py
@@ -23,10 +23,10 @@
 
 
 def shifted_pair(block, extra, axis, distance):
-    width = block.shape[1]
-    padded = jnp.pad(extra, ((0, block.shape[0] - extra.shape[0]), (0, 0)))
-    both = shifted(jnp.concatenate([block, padded], axis=1), axis, distance)
-    return both[:, :width], both[: extra.shape[0], width:]
+    rows = block.shape[0]
+    padded = jnp.pad(extra, ((0, 0), (0, block.shape[1] - extra.shape[1])))
+    both = shifted(jnp.concatenate([block, padded], axis=0), axis, distance)
+    return both[:rows], both[rows:, : extra.shape[1]]
 
 
 def extended_2(block, sides, width):

time: 198 us -> 198 us (level)
  no operation moved by 1% of the time
where the time goes in v5:
time: 198 us; the launch traced here: 195 us
  starting transfers between devices  61.1 us (31%)
  local copies, waits for them, and re-layouts  46.6 us (24%)
  matrix products  46.3 us (23%)
  other arithmetic  26.2 us (13%)
  waiting for transfers between devices  12.3 us (6%)
  between operations  2.53 us (1%)
    ppermute x8, starting transfers between devices, shifted(): return lax.ppermute(block, axis, route)  47.9 us
    dot_general x4, matrix products, body(): jnp.dot(token_grads[which], w_token[which].T, preferred_element_type=jnp....  5.74 us
    sub x1, other arithmetic, attend_local(): exponent = jnp.exp(scores - row_max)  5.4 us
    ppermute x1, waiting for transfers between devices, head_sum(): got = lax.ppermute(give.astype(jnp.bfloat16), axis, pair_far)  5.35 us
    another operation x6, local copies, waits for them, and re-layouts, body(): window = jnp.stack(pieces)  5.31 us
    ppermute x1, starting transfers between devices, head_sum(): got = lax.ppermute(give.astype(jnp.bfloat16), axis, pair_near)  4.55 us
    ppermute x1, waiting for transfers between devices, head_sum(): got = lax.ppermute(own, axis, pair_far)  4.42 us
    ppermute x1, starting transfers between devices, head_sum(): got = lax.ppermute(half, axis, pair_near)  4.03 us
  transfers between devices with their start and end apart: 12, of which 4 were waited for; matrix products, arithmetic and copies ran while one was open for 18% of the time, Pallas kernels for 0%

profile of v5, /device:TPU:1, one launch (start us, length us, event | category | flops | bytes accessed | tf_op | source)
XLA Modules:
  0.0 195.0 jit_solution(13011396392355444981)
XLA Ops:
  6.0 5.5 %collective-permute-start = (bf16[128,192]{0,1:T(8,128)(2,1)S(1)}, bf16[128,192]{0,1:T(8,128)(2,1)S(1)}, u32[]{:S(2)}, u32[]{:S(2)}) collective-permute-start(bf16[128,192]{0,1:T(8,128)(2,1)S(1)} %pad_maximum_fusion.8), channel_id=1, source_target_pairs={{504,0},{508,4},{0,8},{4,12},{8,16},{12,20},{16,24},{20,28},{24,32... | collective-permute-start | bytes 147464 | tf_op jit(solution)/shard_map/ppermute | solution.py:22
  11.5 13.5 %collective-permute-start.3 = (bf16[128,192]{0,1:T(8,128)(2,1)S(1)}, bf16[128,192]{0,1:T(8,128)(2,1)S(1)}, u32[]{:S(2)}, u32[]{:S(2)}) collective-permute-start(bf16[128,192]{0,1:T(8,128)(2,1)S(1)} %pad_maximum_fusion.8), channel_id=1, source_target_pairs={{8,0},{12,4},{16,8},{20,12},{24,16},{28,20},{32,24},{36,28},{40,32... | collective-permute-start | bytes 147464 | tf_op jit(solution)/shard_map/ppermute | solution.py:22
  31.8 2.2 %collective-permute-start.1 = (bf16[192,192]{0,1:T(8,128)(2,1)S(1)}, bf16[192,192]{0,1:T(8,128)(2,1)S(1)}, u32[]{:S(2)}, u32[]{:S(2)}) collective-permute-start(bf16[192,192]{0,1:T(8,128)(2,1)S(1)} %get-tuple-element.55), channel_id=1, source_target_pairs={{508,0},{0,4},{4,8},{8,12},{12,16},{16,20},{20,24},{24,28},{28,32}... | collective-permute-start | bytes 221192 | tf_op jit(solution)/shard_map/ppermute | solution.py:22
  34.0 8.8 %collective-permute-start.2 = (bf16[192,192]{0,1:T(8,128)(2,1)S(1)}, bf16[192,192]{0,1:T(8,128)(2,1)S(1)}, u32[]{:S(2)}, u32[]{:S(2)}) collective-permute-start(bf16[192,192]{0,1:T(8,128)(2,1)S(1)} %get-tuple-element.54), channel_id=1, source_target_pairs={{4,0},{8,4},{12,8},{16,12},{20,16},{24,20},{28,24},{32,28},{36,32}... | collective-permute-start | bytes 221192 | tf_op jit(solution)/shard_map/ppermute | solution.py:22
  54.4 2.4 %concatenate.77 = bf16[32,160,64]{1,2,0:T(8,128)(2,1)} concatenate(bf16[32,32,64]{1,2,0:T(8,128)(2,1)S(1)} %copy.91, bf16[32,32,64]{1,2,0:T(8,128)(2,1)S(1)} %copy.92, bf16[32,32,64]{1,2,0:T(8,128)(2,1)S(1)} %copy.93, bf16[32,32,64]{1,2,0:T(8,128)(2,1)S(1)} %copy.94, bf16[32,32,64]{1,2,0:T(8,128)(2,1)S(1)} %copy.95), dimensions={1} | concatenate | bytes 1310720 | tf_op jit(solution)/shard_map/concatenate | solution.py:285
  60.1 5.4 %fusion.149 = (f32[32,32]{1,0:T(8,128)S(1)}, f32[32,32,128]{2,1,0:T(8,128)S(1)}) fusion(f32[32,32,128]{2,1,0:T(8,128)S(1)} %fusion.17), kind=kOutput, calls=%fused_computation.252 | output fusion | flops 262271 | bytes 1052672 | tf_op jit(solution)/shard_map/sub | solution.py:118
  77.4 2.1 %stack.23 = bf16[5,24576]{1,0:T(8,128)(2,1)S(1)} concatenate(bf16[1,24576]{1,0:T(2,128)(2,1)} %stack.18, bf16[1,24576]{1,0:T(2,128)(2,1)S(1)} %stack.19, bf16[1,24576]{1,0:T(2,128)(2,1)} %stack.20, bf16[1,24576]{1,0:T(2,128)(2,1)} %stack.21, bf16[1,24576]{1,0:T(2,128)(2,1)} %stack.22), dimensions={0} | concatenate | bytes 491520 | tf_op jit(solution)/shard_map/stack | solution.py:225
  83.4 3.1 %fusion.150 = (f32[4,128]{1,0:T(4,128)}, f32[4,128,512]{2,1,0:T(8,128)}) fusion(bf16[128,4,24]{0,2,1:T(8,128)(2,1)} %bitcast.229, bf16[512,4,24]{0,2,1:T(8,128)(2,1)S(1)} %reshape.424, bf16[4,128,512]{2,1,0:T(8,128)(2,1)} %param.26, pred[512]{0:T(512)(128)(4,1)} %broadcast_bitcast_fusion), kind=kOutput, calls=%fused_computation.253 | convolution fusion | flops 14156287 | bytes 1698304 | tf_op jit(solution)/shard_map/sub | solution.py:118
  105.3 2.0 %pad_maximum_fusion.2 = f32[1,4,128,192]{3,2,1,0:T(8,128)} fusion(f32[1,4,128,96]{3,2,1,0:T(8,128)} %copy.108, f32[1,4,128,96]{3,2,1,0:T(8,128)} %copy.107), kind=kLoop, calls=%fused_computation.85 | loop fusion | flops 98304 | bytes 786432 | tf_op jit(solution)/shard_map/concatenate | solution.py:271
  107.3 2.1 %reshape.436 = f32[4,24576]{1,0:T(4,128)} reshape(f32[1,4,128,192]{3,2,1,0:T(8,128)} %pad_maximum_fusion.2) | data formatting | bytes 786432 | tf_op jit(solution)/shard_map/reshape.94
  109.4 2.5 %fusion.151 = (bf16[5,24576]{1,0:T(8,128)(2,1)S(1)}, f32[5,24576]{1,0:T(8,128)}) fusion(f32[4,24576]{1,0:T(4,128)} %reshape.436, s32[4]{0:T(128)} %fusion.133), kind=kOutput, calls=%fused_computation.254 | convolution fusion | flops 6021140 | bytes 1130512 | tf_op jit(solution)/shard_map/bsc,bsx->cx/dot_general | solution.py:279
  116.7 2.1 %collective-permute-start.4 = (bf16[192,192]{1,0:T(8,128)(2,1)}, bf16[192,192]{1,0:T(8,128)(2,1)}, u32[]{:S(2)}, u32[]{:S(2)}) collective-permute-start(bf16[192,192]{1,0:T(8,128)(2,1)} %fusion.77), channel_id=1, source_target_pairs={{508,0},{0,4},{4,8},{8,12},{12,16},{16,20},{20,24},{24,28},{28,32}... | collective-permute-start | bytes 221192 | tf_op jit(solution)/shard_map/ppermute | solution.py:22
  121.9 9.1 %collective-permute-start.5 = (bf16[192,192]{1,0:T(8,128)(2,1)}, bf16[192,192]{1,0:T(8,128)(2,1)}, u32[]{:S(2)}, u32[]{:S(2)}) collective-permute-start(bf16[192,192]{1,0:T(8,128)(2,1)} %fusion.78), channel_id=1, source_target_pairs={{4,0},{8,4},{12,8},{16,12},{20,16},{24,20},{28,24},{32,28},{36,32}... | collective-permute-start | bytes 221192 | tf_op jit(solution)/shard_map/ppermute | solution.py:22
  132.5 1.9 collective-permute-start.6
  135.9 4.9 %collective-permute-start.7 = (bf16[128,192]{1,0:T(8,128)(2,1)}, bf16[128,192]{1,0:T(8,128)(2,1)}, u32[]{:S(2)}, u32[]{:S(2)}) collective-permute-start(bf16[128,192]{1,0:T(8,128)(2,1)} %convert_element_type.234), channel_id=1, source_target_pairs={{504,0},{508,4},{0,8},{4,12},{8,16},{12,20},{16,24},{20,28},{24,32... | collective-permute-start | bytes 147464 | tf_op jit(solution)/shard_map/ppermute | solution.py:22
  140.8 2.1 %slice_reduce_fusion.2 = f32[24576]{0:T(1024)} fusion(f32[5,24576]{1,0:T(8,128)} %get-tuple-element.62), kind=kLoop, calls=%fused_computation.147 | loop fusion | bytes 196608 | tf_op jit(solution)/shard_map/slice | solution.py:352
  144.6 1.9 convert_element_type.219
  146.5 1.9 fusion.111
  166.8 4.5 %collective-permute-start.8 = (bf16[1408,128]{1,0:T(8,128)(2,1)S(1)}, bf16[1408,128]{1,0:T(8,128)(2,1)S(1)}, u32[]{:S(2)}, u32[]{:S(2)}) collective-permute-start(bf16[1408,128]{1,0:T(8,128)(2,1)S(1)} %select_convert_fusion), channel_id=1, source_target_pairs={{0,1},{1,0},{2,3},{3,2},{4,5},{5,4},{6,7},{7,6},{8,9},{9,8},{10,11... | collective-permute-start | bytes 1081352 | tf_op jit(solution)/shard_map/ppermute | solution.py:64
  172.8 2.3 %collective-permute-start.9 = (bf16[704,128]{1,0:T(8,128)(2,1)S(1)}, bf16[704,128]{1,0:T(8,128)(2,1)S(1)}, u32[]{:S(2)}, u32[]{:S(2)}) collective-permute-start(bf16[704,128]{1,0:T(8,128)(2,1)S(1)} %select_convert_fusion.1), channel_id=1, source_target_pairs={{0,2},{1,3},{2,0},{3,1},{4,6},{5,7},{6,4},{7,5},{8,10},{9,11},{10,... | collective-permute-start | bytes 540680 | tf_op jit(solution)/shard_map/ppermute | solution.py:68
  175.1 5.3 %collective-permute-done.9 = bf16[704,128]{1,0:T(8,128)(2,1)S(1)} collective-permute-done((bf16[704,128]{1,0:T(8,128)(2,1)S(1)}, bf16[704,128]{1,0:T(8,128)(2,1)S(1)}, u32[]{:S(2)}, u32[]{:S(2)}) %collective-permute-start.9) | collective-permute-done | bytes 180256 | tf_op jit(solution)/shard_map/ppermute | solution.py:68
  180.5 2.3 %collective-permute-start.10 = (bf16[704,128]{1,0:T(8,128)(2,1)S(1)}, bf16[704,128]{1,0:T(8,128)(2,1)S(1)}, u32[]{:S(2)}, u32[]{:S(2)}) collective-permute-start(bf16[704,128]{1,0:T(8,128)(2,1)S(1)} %add_convert_fusion), channel_id=1, source_target_pairs={{0,2},{1,3},{2,0},{3,1},{4,6},{5,7},{6,4},{7,5},{8,10},{9,11},{10,... | collective-permute-start | bytes 540680 | tf_op jit(solution)/shard_map/ppermute | solution.py:70
  182.8 4.4 %collective-permute-done.10 = bf16[704,128]{1,0:T(8,128)(2,1)S(1)} collective-permute-done((bf16[704,128]{1,0:T(8,128)(2,1)S(1)}, bf16[704,128]{1,0:T(8,128)(2,1)S(1)}, u32[]{:S(2)}, u32[]{:S(2)}) %collective-permute-start.10) | collective-permute-done | bytes 180256 | tf_op jit(solution)/shard_map/ppermute | solution.py:70
  187.4 4.0 %collective-permute-start.11 = (bf16[1408,128]{1,0:T(8,128)(2,1)S(1)}, bf16[1408,128]{1,0:T(8,128)(2,1)S(1)}, u32[]{:S(2)}, u32[]{:S(2)}) collective-permute-start(bf16[1408,128]{1,0:T(8,128)(2,1)S(1)} %maximum_select_fusion.1), channel_id=1, source_target_pairs={{0,1},{1,0},{2,3},{3,2},{4,5},{5,4},{6,7},{7,6},{8,9},{9,8},{10,11... | collective-permute-start | bytes 1081352 | tf_op jit(solution)/shard_map/ppermute | solution.py:74
  (233 shorter events, 96.1 us)
Async XLA Ops:
  0.6 67.3 %copy-start = (bf16[1024,128]{1,0:T(8,128)(2,1)S(1)}, bf16[1024,128]{1,0:T(8,128)(2,1)}, u32[]{:S(2)}) copy-start(bf16[1024,128]{1,0:T(8,128)(2,1)} %param.33) | copy-start | bytes 786436
  0.6 42.6 %copy-start.9 = (bf16[4,384,96]{1,2,0:T(8,128)(2,1)S(1)}, bf16[4,384,96]{1,2,0:T(8,128)(2,1)}, u32[]{:S(2)}) copy-start(bf16[4,384,96]{1,2,0:T(8,128)(2,1)} %param.21) | copy-start | bytes 884740
  0.7 30.6 %copy-start.20 = (bf16[4,128,32]{1,2,0:T(8,128)(2,1)S(1)}, bf16[4,128,32]{1,2,0:T(8,128)(2,1)}, u32[]{:S(2)}) copy-start(bf16[4,128,32]{1,2,0:T(8,128)(2,1)} %param.24) | copy-start | bytes 98308
  1.7 26.8 %copy-start.34 = (f32[128]{0:T(128)}, f32[128]{0:T(128)S(1)}, u32[]{:S(2)}) copy-start(f32[128]{0:T(128)S(1)} %broadcast_multiply_fusion.5) | copy-start | bytes 1540
  2.8 25.7 %copy-start.37 = (f32[128]{0:T(128)}, f32[128]{0:T(128)S(1)}, u32[]{:S(2)}) copy-start(f32[128]{0:T(128)S(1)} %add_rsqrt_fusion.1) | copy-start | bytes 1540
  3.9 41.0 %copy-start.40 = (s32[32]{0:T(128)S(1)}, s32[32]{0:T(128)}, u32[]{:S(2)}) copy-start(s32[32]{0:T(128)} %param.31) | copy-start | bytes 388
  3.9 42.4 %copy-start.41 = (s32[1,4]{1,0:T(1,128)S(1)}, s32[1,4]{1,0:T(1,128)}, u32[]{:S(2)}) copy-start(s32[1,4]{1,0:T(1,128)} %param.28) | copy-start | bytes 52
  6.0 42.3 %collective-permute-start = (bf16[128,192]{0,1:T(8,128)(2,1)S(1)}, bf16[128,192]{0,1:T(8,128)(2,1)S(1)}, u32[]{:S(2)}, u32[]{:S(2)}) collective-permute-start(bf16[128,192]{0,1:T(8,128)(2,1)S(1)} %pad_maximum_fusion.8), channel_id=1, source_target_pairs={{504,0},{508,4},{0,8},{4,12},{8,16},{12,20},{16,24},{20,28},{24,32... | collective-permute-start | bytes 147464 | tf_op jit(solution)/shard_map/ppermute | solution.py:22
  11.5 37.7 %collective-permute-start.3 = (bf16[128,192]{0,1:T(8,128)(2,1)S(1)}, bf16[128,192]{0,1:T(8,128)(2,1)S(1)}, u32[]{:S(2)}, u32[]{:S(2)}) collective-permute-start(bf16[128,192]{0,1:T(8,128)(2,1)S(1)} %pad_maximum_fusion.8), channel_id=1, source_target_pairs={{8,0},{12,4},{16,8},{20,12},{24,16},{28,20},{32,24},{36,28},{40,32... | collective-permute-start | bytes 147464 | tf_op jit(solution)/shard_map/ppermute | solution.py:22
  27.2 15.6 %copy-start.23 = (f32[1024]{0:T(1024)}, f32[1024]{0:T(1024)S(1)}, u32[]{:S(2)}) copy-start(f32[1024]{0:T(1024)S(1)} %broadcast_multiply_fusion.2) | copy-start | bytes 12292
  28.5 14.3 %copy-start.28 = (f32[1024]{0:T(1024)}, f32[1024]{0:T(1024)S(1)}, u32[]{:S(2)}) copy-start(f32[1024]{0:T(1024)S(1)} %add_rsqrt_fusion) | copy-start | bytes 12292
  31.8 18.3 %collective-permute-start.1 = (bf16[192,192]{0,1:T(8,128)(2,1)S(1)}, bf16[192,192]{0,1:T(8,128)(2,1)S(1)}, u32[]{:S(2)}, u32[]{:S(2)}) collective-permute-start(bf16[192,192]{0,1:T(8,128)(2,1)S(1)} %get-tuple-element.55), channel_id=1, source_target_pairs={{508,0},{0,4},{4,8},{8,12},{12,16},{16,20},{20,24},{24,28},{28,32}... | collective-permute-start | bytes 221192 | tf_op jit(solution)/shard_map/ppermute | solution.py:22
  34.0 16.1 %collective-permute-start.2 = (bf16[192,192]{0,1:T(8,128)(2,1)S(1)}, bf16[192,192]{0,1:T(8,128)(2,1)S(1)}, u32[]{:S(2)}, u32[]{:S(2)}) collective-permute-start(bf16[192,192]{0,1:T(8,128)(2,1)S(1)} %get-tuple-element.54), channel_id=1, source_target_pairs={{4,0},{8,4},{12,8},{16,12},{20,16},{24,20},{28,24},{32,28},{36,32}... | collective-permute-start | bytes 221192 | tf_op jit(solution)/shard_map/ppermute | solution.py:22
  43.3 24.7 %copy-start.5 = (f32[1024,32]{0,1:T(8,128)}, f32[1024,32]{0,1:T(8,128)S(1)}, u32[]{:S(2)}) copy-start(f32[1024,32]{0,1:T(8,128)S(1)} %fusion.29) | copy-start | bytes 393220
  58.7 12.3 %copy-start.15 = (bf16[32,128,64]{1,2,0:T(8,128)(2,1)}, bf16[32,128,64]{1,2,0:T(8,128)(2,1)S(1)}, u32[]{:S(2)}) copy-start(bf16[32,128,64]{1,2,0:T(8,128)(2,1)S(1)} %fusion.11) | copy-start | bytes 1572868
  116.7 40.2 %collective-permute-start.4 = (bf16[192,192]{1,0:T(8,128)(2,1)}, bf16[192,192]{1,0:T(8,128)(2,1)}, u32[]{:S(2)}, u32[]{:S(2)}) collective-permute-start(bf16[192,192]{1,0:T(8,128)(2,1)} %fusion.77), channel_id=1, source_target_pairs={{508,0},{0,4},{4,8},{8,12},{12,16},{16,20},{20,24},{24,28},{28,32}... | collective-permute-start | bytes 221192 | tf_op jit(solution)/shard_map/ppermute | solution.py:22
  121.9 35.0 %collective-permute-start.5 = (bf16[192,192]{1,0:T(8,128)(2,1)}, bf16[192,192]{1,0:T(8,128)(2,1)}, u32[]{:S(2)}, u32[]{:S(2)}) collective-permute-start(bf16[192,192]{1,0:T(8,128)(2,1)} %fusion.78), channel_id=1, source_target_pairs={{4,0},{8,4},{12,8},{16,12},{20,16},{24,20},{28,24},{32,28},{36,32}... | collective-permute-start | bytes 221192 | tf_op jit(solution)/shard_map/ppermute | solution.py:22
  132.5 24.3 %collective-permute-start.6 = (bf16[128,192]{1,0:T(8,128)(2,1)}, bf16[128,192]{1,0:T(8,128)(2,1)}, u32[]{:S(2)}, u32[]{:S(2)}) collective-permute-start(bf16[128,192]{1,0:T(8,128)(2,1)} %convert_element_type.232), channel_id=1, source_target_pairs={{8,0},{12,4},{16,8},{20,12},{24,16},{28,20},{32,24},{36,28},{40,32... | collective-permute-start | bytes 147464 | tf_op jit(solution)/shard_map/ppermute | solution.py:22
  135.9 20.9 %collective-permute-start.7 = (bf16[128,192]{1,0:T(8,128)(2,1)}, bf16[128,192]{1,0:T(8,128)(2,1)}, u32[]{:S(2)}, u32[]{:S(2)}) collective-permute-start(bf16[128,192]{1,0:T(8,128)(2,1)} %convert_element_type.234), channel_id=1, source_target_pairs={{504,0},{508,4},{0,8},{4,12},{8,16},{12,20},{16,24},{20,28},{24,32... | collective-permute-start | bytes 147464 | tf_op jit(solution)/shard_map/ppermute | solution.py:22
  154.7 9.0 %copy-start.17 = (f32[1024,32]{0,1:T(8,128)S(1)}, f32[1024,32]{0,1:T(8,128)}, u32[]{:S(2)}) copy-start(f32[1024,32]{0,1:T(8,128)} %get-tuple-element.58) | copy-start | bytes 393220
  166.8 5.8 %collective-permute-start.8 = (bf16[1408,128]{1,0:T(8,128)(2,1)S(1)}, bf16[1408,128]{1,0:T(8,128)(2,1)S(1)}, u32[]{:S(2)}, u32[]{:S(2)}) collective-permute-start(bf16[1408,128]{1,0:T(8,128)(2,1)S(1)} %select_convert_fusion), channel_id=1, source_target_pairs={{0,1},{1,0},{2,3},{3,2},{4,5},{5,4},{6,7},{7,6},{8,9},{9,8},{10,11... | collective-permute-start | bytes 1081352 | tf_op jit(solution)/shard_map/ppermute | solution.py:64
  172.8 7.7 %collective-permute-start.9 = (bf16[704,128]{1,0:T(8,128)(2,1)S(1)}, bf16[704,128]{1,0:T(8,128)(2,1)S(1)}, u32[]{:S(2)}, u32[]{:S(2)}) collective-permute-start(bf16[704,128]{1,0:T(8,128)(2,1)S(1)} %select_convert_fusion.1), channel_id=1, source_target_pairs={{0,2},{1,3},{2,0},{3,1},{4,6},{5,7},{6,4},{7,5},{8,10},{9,11},{10,... | collective-permute-start | bytes 540680 | tf_op jit(solution)/shard_map/ppermute | solution.py:68
  180.5 6.7 %collective-permute-start.10 = (bf16[704,128]{1,0:T(8,128)(2,1)S(1)}, bf16[704,128]{1,0:T(8,128)(2,1)S(1)}, u32[]{:S(2)}, u32[]{:S(2)}) collective-permute-start(bf16[704,128]{1,0:T(8,128)(2,1)S(1)} %add_convert_fusion), channel_id=1, source_target_pairs={{0,2},{1,3},{2,0},{3,1},{4,6},{5,7},{6,4},{7,5},{8,10},{9,11},{10,... | collective-permute-start | bytes 540680 | tf_op jit(solution)/shard_map/ppermute | solution.py:70
  187.4 5.3 %collective-permute-start.11 = (bf16[1408,128]{1,0:T(8,128)(2,1)S(1)}, bf16[1408,128]{1,0:T(8,128)(2,1)S(1)}, u32[]{:S(2)}, u32[]{:S(2)}) collective-permute-start(bf16[1408,128]{1,0:T(8,128)(2,1)S(1)} %maximum_select_fusion.1), channel_id=1, source_target_pairs={{0,1},{1,0},{2,3},{3,2},{4,5},{5,4},{6,7},{7,6},{8,9},{9,8},{10,11... | collective-permute-start | bytes 1081352 | tf_op jit(solution)/shard_map/ppermute | solution.py:74
  (30 other events, 133.0 us)

commit v6 on v1

--- a/solution.py
+++ b/solution.py
@@ -77,6 +77,17 @@
         start += width * rows_here
         outs.append(jnp.concatenate(cols, axis=1) if width > 1 else cols[0])
     return outs
+
+
+def head_sum_small(part, axis):
+    count = lax.axis_size(axis)
+    low = part.astype(jnp.bfloat16)
+    if count != 4:
+        return lax.psum(low, axis)
+    got = lax.ppermute(low, axis, [(i, i ^ 1) for i in range(count)])
+    low = (low.astype(jnp.float32) + got.astype(jnp.float32)).astype(jnp.bfloat16)
+    got = lax.ppermute(low, axis, [(i, i ^ 2) for i in range(count)])
+    return low.astype(jnp.float32) + got.astype(jnp.float32)
 
 
 def norm_rows(inputs, gains):
@@ -380,9 +391,8 @@
             token_grads[which], w_token[which].T, preferred_element_type=jnp.float32
         )
     single_part = norm_back(single.astype(jnp.float32), gain_single, grad_normed)
-    token_total, atom_total, single_total, atoms_total = head_sum(
-        [token_part, atom_part, single_part, atoms_part], "head"
-    )
+    token_total, atom_total, atoms_total = head_sum([token_part, atom_part, atoms_part], "head")
+    single_total = head_sum_small(single_part, "head")
     return (
         token_total.astype(jnp.bfloat16),
         atom_total.astype(jnp.bfloat16),

time: 154 us -> 154 us (level)
  waiting for transfers between devices: 18.6 us -> 1.2 us
  starting transfers between devices: 70.9 us -> 84.5 us
  other arithmetic: 12.5 us -> 14.1 us
    ppermute x2, starting transfers between devices: 11.2 us -> 18.5 us  [extended_2(): lax.ppermute(lax.slice_in_dim(block, 0, width, axis=dim), axis, backward)]
    ppermute x0 -> x2, starting transfers between devices: none -> 6.53 us  [the longest x1 4.23 us: head_sum_small(): got = lax.ppermute(low, axis, [(i, i ^ 1) for i in range(count)])]
    ppermute x2, waiting for transfers between devices: 6.3 us -> 0.01 us  [extended_2(): lax.ppermute(lax.slice_in_dim(block, block.shape[dim] - width, None, axis...]
    ppermute x1, waiting for transfers between devices: 5.35 us -> 0.01 us  [head_sum(): got = lax.ppermute(give.astype(jnp.bfloat16), axis, pair_far)]
    ppermute x1, waiting for transfers between devices: 4.42 us -> 0.63 us  [head_sum(): got = lax.ppermute(own, axis, pair_far)]
    ppermute x8, starting transfers between devices: 41.3 us -> 38.1 us  [shifted(): return lax.ppermute(block, axis, route)]
    ppermute x1, starting transfers between devices: 4.03 us -> 6.57 us  [head_sum(): got = lax.ppermute(half, axis, pair_near)]
    convert_element_type x4, local copies, waits for them, and re-layouts: 0.41 us -> 2.92 us  [body(): outgoing[distance + WIN].astype(jnp.bfloat16)]
  transfers between devices with their start and end apart: 16 -> 18, of which waited for: 6 -> 2; matrix products, arithmetic and copies ran while one was open for 26% -> 30% of each run, Pallas kernels for 0% -> 0%
where the time goes in v6:
time: 154 us; the launch traced here: 152 us
  starting transfers between devices  84.5 us (55%)
  matrix products  28.9 us (19%)
  local copies, waits for them, and re-layouts  20.9 us (14%)
  other arithmetic  14.1 us (9%)
  between operations  2.64 us (2%)
    ppermute x8, starting transfers between devices, shifted(): return lax.ppermute(block, axis, route)  38.1 us
    ppermute x2, starting transfers between devices, extended_2(): lax.ppermute(lax.slice_in_dim(block, 0, width, axis=dim), axis, backward)  18.5 us
    ppermute x1, starting transfers between devices, head_sum(): got = lax.ppermute(half, axis, pair_near)  6.57 us
    ppermute x1, starting transfers between devices, head_sum(): got = lax.ppermute(give.astype(jnp.bfloat16), axis, pair_near)  5.67 us
    ppermute x1, starting transfers between devices, head_sum_small(): got = lax.ppermute(low, axis, [(i, i ^ 1) for i in range(count)])  4.23 us
    ppermute x2, starting transfers between devices, extended_2(): lax.ppermute(lax.slice_in_dim(block, block.shape[dim] - width, None, axis...  3.83 us
    dot_general x4, matrix products, body(): jnp.dot(normed_low, w_token[which], preferred_element_type=jnp.float32)  3.71 us
  transfers between devices with their start and end apart: 18, of which 2 were waited for; matrix products, arithmetic and copies ran while one was open for 30% of the time, Pallas kernels for 0%

profile of v6, /device:TPU:1, one launch (start us, length us, event | category | flops | bytes accessed | tf_op | source)
XLA Modules:
  0.0 152.3 jit_solution(3134587085635308727)
XLA Ops:
  7.2 5.5 %collective-permute-start = (bf16[128,192]{0,1:T(8,128)(2,1)}, bf16[128,192]{0,1:T(8,128)(2,1)}, u32[]{:S(2)}, u32[]{:S(2)}) collective-permute-start(bf16[128,192]{0,1:T(8,128)(2,1)} %pad_maximum_fusion.8), channel_id=1, source_target_pairs={{504,0},{508,4},{0,8},{4,12},{8,16},{12,20},{16,24},{20,28},{24,32... | collective-permute-start | bytes 147464 | tf_op jit(solution)/shard_map/ppermute | solution.py:22
  12.6 2.2 %collective-permute-start.1 = (bf16[128,192]{0,1:T(8,128)(2,1)}, bf16[128,192]{0,1:T(8,128)(2,1)}, u32[]{:S(2)}, u32[]{:S(2)}) collective-permute-start(bf16[128,192]{0,1:T(8,128)(2,1)} %pad_maximum_fusion.8), channel_id=1, source_target_pairs={{508,0},{0,4},{4,8},{8,12},{12,16},{16,20},{20,24},{24,28},{28,32}... | collective-permute-start | bytes 147464 | tf_op jit(solution)/shard_map/ppermute | solution.py:22
  14.9 12.9 %collective-permute-start.2 = (bf16[128,192]{0,1:T(8,128)(2,1)}, bf16[128,192]{0,1:T(8,128)(2,1)}, u32[]{:S(2)}, u32[]{:S(2)}) collective-permute-start(bf16[128,192]{0,1:T(8,128)(2,1)} %pad_maximum_fusion.8), channel_id=1, source_target_pairs={{4,0},{8,4},{12,8},{16,12},{20,16},{24,20},{28,24},{32,28},{36,32}... | collective-permute-start | bytes 147464 | tf_op jit(solution)/shard_map/ppermute | solution.py:22
  34.5 1.9 %collective-permute-start.4 = (bf16[64,64]{0,1:T(8,128)(2,1)S(1)}, bf16[64,64]{0,1:T(8,128)(2,1)S(1)}, u32[]{:S(2)}, u32[]{:S(2)}) collective-permute-start(bf16[64,64]{0,1:T(8,128)(2,1)S(1)} %get-tuple-element.47), channel_id=1, source_target_pairs={{0,4},{4,8},{8,12},{12,16},{16,20},{20,24},{24,28},{28,32},{32,36}... | collective-permute-start | bytes 24584 | tf_op jit(solution)/shard_map/ppermute | solution.py:31
  36.4 9.1 %collective-permute-start.5 = (bf16[64,64]{0,1:T(8,128)(2,1)S(1)}, bf16[64,64]{0,1:T(8,128)(2,1)S(1)}, u32[]{:S(2)}, u32[]{:S(2)}) collective-permute-start(bf16[64,64]{0,1:T(8,128)(2,1)S(1)} %get-tuple-element.46), channel_id=1, source_target_pairs={{4,0},{8,4},{12,8},{16,12},{20,16},{24,20},{28,24},{32,28},{36,32}... | collective-permute-start | bytes 24584 | tf_op jit(solution)/shard_map/ppermute | solution.py:34
  54.6 2.3 %concatenate.60 = bf16[32,160,64]{1,2,0:T(8,128)(2,1)} concatenate(bf16[32,32,64]{1,2,0:T(8,128)(2,1)S(1)} %copy.91, bf16[32,32,64]{1,2,0:T(8,128)(2,1)S(1)} %copy.92, bf16[32,32,64]{1,2,0:T(8,128)(2,1)S(1)} %copy.93, bf16[32,32,64]{1,2,0:T(8,128)(2,1)S(1)} %copy.94, bf16[32,32,64]{1,2,0:T(8,128)(2,1)S(1)} %copy.95), dimensions={1} | concatenate | bytes 1310720 | tf_op jit(solution)/shard_map/concatenate | solution.py:297
  56.9 1.9 %fusion.11 = bf16[32,128,64]{1,2,0:T(8,128)(2,1)S(1)} fusion(bf16[32,160,64]{1,2,0:T(8,128)(2,1)} %concatenate.60, s32[32,128]{1,0:T(8,128)} %iota_add_fusion), kind=kOutput, calls=%fused_computation.15 | convolution fusion | flops 84803584 | bytes 1196032 | tf_op jit(solution)/shard_map/wrs,wsf->wrf/dot_general | solution.py:305
  60.1 1.8 %convolution_bitcast_fusion.1 = f32[32,32,1,32]{1,3,0,2:T(8,128)S(1)} fusion(bf16[32,128,64]{1,2,0:T(8,128)(2,1)S(1)} %fusion.11, f32[32,32]{1,0:T(8,128)S(1)} %get-tuple-element.51, f32[32,32,128]{2,1,0:T(8,128)S(1)} %fusion.17), kind=kOutput, calls=%fused_computation.23 | convolution fusion | flops 8782975 | bytes 1458176 | tf_op jit(solution)/shard_map/bhqk,bkhd->bqhd/dot_general | solution.py:125
  62.9 1.8 %convolution_bitcast_fusion = f32[32,128,32]{1,2,0:T(8,128)S(1)} fusion(bf16[32,32,32]{1,0,2:T(8,128)(2,1)S(1)} %reshape.430, f32[32,32]{1,0:T(8,128)S(1)} %get-tuple-element.51, f32[32,32,128]{2,1,0:T(8,128)S(1)} %fusion.17), kind=kOutput, calls=%fused_computation.22 | convolution fusion | flops 8782975 | bytes 1118208 | tf_op jit(solution)/shard_map/bhqk,bqhd->bkhd/dot_general | solution.py:147
  64.8 1.5 fusion.18
  69.2 1.9 %collective-permute-start.6 = (bf16[64,64]{1,0:T(8,128)(2,1)S(1)}, bf16[64,64]{1,0:T(8,128)(2,1)S(1)}, u32[]{:S(2)}, u32[]{:S(2)}) collective-permute-start(bf16[64,64]{1,0:T(8,128)(2,1)S(1)} %bitcast.232), channel_id=1, source_target_pairs={{0,4},{4,8},{8,12},{12,16},{16,20},{20,24},{24,28},{28,32},{32,36}... | collective-permute-start | bytes 24584 | tf_op jit(solution)/shard_map/ppermute | solution.py:31
  71.2 9.4 %collective-permute-start.7 = (bf16[64,64]{1,0:T(8,128)(2,1)S(1)}, bf16[64,64]{1,0:T(8,128)(2,1)S(1)}, u32[]{:S(2)}, u32[]{:S(2)}) collective-permute-start(bf16[64,64]{1,0:T(8,128)(2,1)S(1)} %bitcast.234), channel_id=1, source_target_pairs={{4,0},{8,4},{12,8},{16,12},{20,16},{24,20},{28,24},{32,28},{36,32}... | collective-permute-start | bytes 24584 | tf_op jit(solution)/shard_map/ppermute | solution.py:34
  81.3 1.9 %collective-permute-start.3 = (bf16[128,192]{0,1:T(8,128)(2,1)}, bf16[128,192]{0,1:T(8,128)(2,1)S(1)}, u32[]{:S(2)}, u32[]{:S(2)}) collective-permute-start(bf16[128,192]{0,1:T(8,128)(2,1)} %pad_maximum_fusion.8), channel_id=1, source_target_pairs={{8,0},{12,4},{16,8},{20,12},{24,16},{28,20},{32,24},{36,28},{40,32... | collective-permute-start | bytes 147464 | tf_op jit(solution)/shard_map/ppermute | solution.py:22
  92.1 1.6 %fusion.139 = (f32[4,128]{1,0:T(4,128)S(1)}, f32[4,128,512]{2,1,0:T(8,128)S(1)}) fusion(bf16[128,4,24]{0,2,1:T(8,128)(2,1)S(1)} %bitcast.227, bf16[512,4,24]{0,2,1:T(8,128)(2,1)S(1)} %reshape.424, bf16[4,128,512]{2,1,0:T(8,128)(2,1)} %param.26, pred[512]{0:T(512)(128)(4,1)S(1)} %copy-done.27), kind=kOutput, calls=%fused_computation.241 | convolution fusion | flops 14156287 | bytes 1698304 | tf_op jit(solution)/shard_map/sub | solution.py:122
  100.0 4.4 %collective-permute-start.12 = (bf16[128,192]{1,0:T(8,128)(2,1)}, bf16[128,192]{1,0:T(8,128)(2,1)}, u32[]{:S(2)}, u32[]{:S(2)}) collective-permute-start(bf16[128,192]{1,0:T(8,128)(2,1)} %convert_element_type.246), channel_id=1, source_target_pairs={{8,0},{12,4},{16,8},{20,12},{24,16},{28,20},{32,24},{36,28},{40,32... | collective-permute-start | bytes 147464 | tf_op jit(solution)/shard_map/ppermute | solution.py:22
  105.2 5.0 %collective-permute-start.13 = (bf16[128,192]{1,0:T(8,128)(2,1)}, bf16[128,192]{1,0:T(8,128)(2,1)}, u32[]{:S(2)}, u32[]{:S(2)}) collective-permute-start(bf16[128,192]{1,0:T(8,128)(2,1)} %convert_element_type.248), channel_id=1, source_target_pairs={{4,0},{8,4},{12,8},{16,12},{20,16},{24,20},{28,24},{32,28},{36,32}... | collective-permute-start | bytes 147464 | tf_op jit(solution)/shard_map/ppermute | solution.py:22
  110.9 2.5 %collective-permute-start.14 = (bf16[128,192]{1,0:T(8,128)(2,1)}, bf16[128,192]{1,0:T(8,128)(2,1)}, u32[]{:S(2)}, u32[]{:S(2)}) collective-permute-start(bf16[128,192]{1,0:T(8,128)(2,1)} %convert_element_type.250), channel_id=1, source_target_pairs={{508,0},{0,4},{4,8},{8,12},{12,16},{16,20},{20,24},{24,28},{28,32}... | collective-permute-start | bytes 147464 | tf_op jit(solution)/shard_map/ppermute | solution.py:22
  114.1 3.7 %collective-permute-start.15 = (bf16[128,192]{1,0:T(8,128)(2,1)}, bf16[128,192]{1,0:T(8,128)(2,1)}, u32[]{:S(2)}, u32[]{:S(2)}) collective-permute-start(bf16[128,192]{1,0:T(8,128)(2,1)} %convert_element_type.252), channel_id=1, source_target_pairs={{504,0},{508,4},{0,8},{4,12},{8,16},{12,20},{16,24},{20,28},{24,32... | collective-permute-start | bytes 147464 | tf_op jit(solution)/shard_map/ppermute | solution.py:22
  120.9 5.7 %collective-permute-start.8 = (bf16[1216,128]{1,0:T(8,128)(2,1)}, bf16[1216,128]{1,0:T(8,128)(2,1)S(1)}, u32[]{:S(2)}, u32[]{:S(2)}) collective-permute-start(bf16[1216,128]{1,0:T(8,128)(2,1)} %select_convert_fusion), channel_id=1, source_target_pairs={{0,1},{1,0},{2,3},{3,2},{4,5},{5,4},{6,7},{7,6},{8,9},{9,8},{10,11... | collective-permute-start | bytes 933896 | tf_op jit(solution)/shard_map/ppermute | solution.py:57
  130.0 2.3 %collective-permute-start.9 = (bf16[608,128]{1,0:T(8,128)(2,1)S(1)}, bf16[608,128]{1,0:T(8,128)(2,1)S(1)}, u32[]{:S(2)}, u32[]{:S(2)}) collective-permute-start(bf16[608,128]{1,0:T(8,128)(2,1)S(1)} %select_convert_fusion.1), channel_id=1, source_target_pairs={{0,2},{1,3},{2,0},{3,1},{4,6},{5,7},{6,4},{7,5},{8,10},{9,11},{10,... | collective-permute-start | bytes 466952 | tf_op jit(solution)/shard_map/ppermute | solution.py:61
  132.4 4.2 %collective-permute-start.16 = (bf16[128,384]{1,0:T(8,128)(2,1)S(1)}, bf16[128,384]{1,0:T(8,128)(2,1)S(1)}, u32[]{:S(2)}, u32[]{:S(2)}) collective-permute-start(bf16[128,384]{1,0:T(8,128)(2,1)S(1)} %fusion.67), channel_id=1, source_target_pairs={{0,1},{1,0},{2,3},{3,2},{4,5},{5,4},{6,7},{7,6},{8,9},{9,8},{10,11... | collective-permute-start | bytes 294920 | tf_op jit(solution)/shard_map/ppermute | solution.py:87
  136.7 3.0 %collective-permute-start.10 = (bf16[608,128]{1,0:T(8,128)(2,1)S(1)}, bf16[608,128]{1,0:T(8,128)(2,1)S(1)}, u32[]{:S(2)}, u32[]{:S(2)}) collective-permute-start(bf16[608,128]{1,0:T(8,128)(2,1)S(1)} %add_convert_fusion), channel_id=1, source_target_pairs={{0,2},{1,3},{2,0},{3,1},{4,6},{5,7},{6,4},{7,5},{8,10},{9,11},{10,... | collective-permute-start | bytes 466952 | tf_op jit(solution)/shard_map/ppermute | solution.py:63
  139.8 2.3 %collective-permute-start.17 = (bf16[128,384]{1,0:T(8,128)(2,1)S(1)}, bf16[128,384]{1,0:T(8,128)(2,1)S(1)}, u32[]{:S(2)}, u32[]{:S(2)}) collective-permute-start(bf16[128,384]{1,0:T(8,128)(2,1)S(1)} %add_convert_fusion.2), channel_id=1, source_target_pairs={{0,2},{1,3},{2,0},{3,1},{4,6},{5,7},{6,4},{7,5},{8,10},{9,11},{10,... | collective-permute-start | bytes 294920 | tf_op jit(solution)/shard_map/ppermute | solution.py:89
  142.8 6.6 %collective-permute-start.11 = (bf16[1216,128]{1,0:T(8,128)(2,1)S(1)}, bf16[1216,128]{1,0:T(8,128)(2,1)S(1)}, u32[]{:S(2)}, u32[]{:S(2)}) collective-permute-start(bf16[1216,128]{1,0:T(8,128)(2,1)S(1)} %maximum_select_fusion.1), channel_id=1, source_target_pairs={{0,1},{1,0},{2,3},{3,2},{4,5},{5,4},{6,7},{7,6},{8,9},{9,8},{10,11... | collective-permute-start | bytes 933896 | tf_op jit(solution)/shard_map/ppermute | solution.py:67
  (208 shorter events, 54.2 us)
Async XLA Ops:
  0.6 61.9 %copy-start = (bf16[1024,128]{1,0:T(8,128)(2,1)S(1)}, bf16[1024,128]{1,0:T(8,128)(2,1)}, u32[]{:S(2)}) copy-start(bf16[1024,128]{1,0:T(8,128)(2,1)} %param.33) | copy-start | bytes 786436
  0.6 44.9 %copy-start.5 = (bf16[4,384,96]{1,2,0:T(8,128)(2,1)S(1)}, bf16[4,384,96]{1,2,0:T(8,128)(2,1)}, u32[]{:S(2)}) copy-start(bf16[4,384,96]{1,2,0:T(8,128)(2,1)} %param.21) | copy-start | bytes 884740
  0.7 33.4 %copy-start.11 = (bf16[4,128,32]{1,2,0:T(8,128)(2,1)S(1)}, bf16[4,128,32]{1,2,0:T(8,128)(2,1)}, u32[]{:S(2)}) copy-start(bf16[4,128,32]{1,2,0:T(8,128)(2,1)} %param.24) | copy-start | bytes 98308
  1.7 47.1 %copy-start.25 = (s32[32]{0:T(128)S(1)}, s32[32]{0:T(128)}, u32[]{:S(2)}) copy-start(s32[32]{0:T(128)} %param.31) | copy-start | bytes 388
  1.7 47.8 %copy-start.26 = (s32[1,4]{1,0:T(1,128)S(1)}, s32[1,4]{1,0:T(1,128)}, u32[]{:S(2)}) copy-start(s32[1,4]{1,0:T(1,128)} %param.28) | copy-start | bytes 52
  7.2 79.6 %collective-permute-start = (bf16[128,192]{0,1:T(8,128)(2,1)}, bf16[128,192]{0,1:T(8,128)(2,1)}, u32[]{:S(2)}, u32[]{:S(2)}) collective-permute-start(bf16[128,192]{0,1:T(8,128)(2,1)} %pad_maximum_fusion.8), channel_id=1, source_target_pairs={{504,0},{508,4},{0,8},{4,12},{8,16},{12,20},{16,24},{20,28},{24,32... | collective-permute-start | bytes 147464 | tf_op jit(solution)/shard_map/ppermute | solution.py:22
  12.6 75.2 %collective-permute-start.1 = (bf16[128,192]{0,1:T(8,128)(2,1)}, bf16[128,192]{0,1:T(8,128)(2,1)}, u32[]{:S(2)}, u32[]{:S(2)}) collective-permute-start(bf16[128,192]{0,1:T(8,128)(2,1)} %pad_maximum_fusion.8), channel_id=1, source_target_pairs={{508,0},{0,4},{4,8},{8,12},{12,16},{16,20},{20,24},{24,28},{28,32}... | collective-permute-start | bytes 147464 | tf_op jit(solution)/shard_map/ppermute | solution.py:22
  14.9 74.0 %collective-permute-start.2 = (bf16[128,192]{0,1:T(8,128)(2,1)}, bf16[128,192]{0,1:T(8,128)(2,1)}, u32[]{:S(2)}, u32[]{:S(2)}) collective-permute-start(bf16[128,192]{0,1:T(8,128)(2,1)} %pad_maximum_fusion.8), channel_id=1, source_target_pairs={{4,0},{8,4},{12,8},{16,12},{20,16},{24,20},{28,24},{32,28},{36,32}... | collective-permute-start | bytes 147464 | tf_op jit(solution)/shard_map/ppermute | solution.py:22
  34.5 18.0 %collective-permute-start.4 = (bf16[64,64]{0,1:T(8,128)(2,1)S(1)}, bf16[64,64]{0,1:T(8,128)(2,1)S(1)}, u32[]{:S(2)}, u32[]{:S(2)}) collective-permute-start(bf16[64,64]{0,1:T(8,128)(2,1)S(1)} %get-tuple-element.47), channel_id=1, source_target_pairs={{0,4},{4,8},{8,12},{12,16},{16,20},{20,24},{24,28},{28,32},{32,36}... | collective-permute-start | bytes 24584 | tf_op jit(solution)/shard_map/ppermute | solution.py:31
  36.4 16.0 %collective-permute-start.5 = (bf16[64,64]{0,1:T(8,128)(2,1)S(1)}, bf16[64,64]{0,1:T(8,128)(2,1)S(1)}, u32[]{:S(2)}, u32[]{:S(2)}) collective-permute-start(bf16[64,64]{0,1:T(8,128)(2,1)S(1)} %get-tuple-element.46), channel_id=1, source_target_pairs={{4,0},{8,4},{12,8},{16,12},{20,16},{24,20},{28,24},{32,28},{36,32}... | collective-permute-start | bytes 24584 | tf_op jit(solution)/shard_map/ppermute | solution.py:34
  69.2 12.1 %collective-permute-start.6 = (bf16[64,64]{1,0:T(8,128)(2,1)S(1)}, bf16[64,64]{1,0:T(8,128)(2,1)S(1)}, u32[]{:S(2)}, u32[]{:S(2)}) collective-permute-start(bf16[64,64]{1,0:T(8,128)(2,1)S(1)} %bitcast.232), channel_id=1, source_target_pairs={{0,4},{4,8},{8,12},{12,16},{16,20},{20,24},{24,28},{28,32},{32,36}... | collective-permute-start | bytes 24584 | tf_op jit(solution)/shard_map/ppermute | solution.py:31
  71.2 12.1 %collective-permute-start.7 = (bf16[64,64]{1,0:T(8,128)(2,1)S(1)}, bf16[64,64]{1,0:T(8,128)(2,1)S(1)}, u32[]{:S(2)}, u32[]{:S(2)}) collective-permute-start(bf16[64,64]{1,0:T(8,128)(2,1)S(1)} %bitcast.234), channel_id=1, source_target_pairs={{4,0},{8,4},{12,8},{16,12},{20,16},{24,20},{28,24},{32,28},{36,32}... | collective-permute-start | bytes 24584 | tf_op jit(solution)/shard_map/ppermute | solution.py:34
  81.3 8.6 %collective-permute-start.3 = (bf16[128,192]{0,1:T(8,128)(2,1)}, bf16[128,192]{0,1:T(8,128)(2,1)S(1)}, u32[]{:S(2)}, u32[]{:S(2)}) collective-permute-start(bf16[128,192]{0,1:T(8,128)(2,1)} %pad_maximum_fusion.8), channel_id=1, source_target_pairs={{8,0},{12,4},{16,8},{20,12},{24,16},{28,20},{32,24},{36,28},{40,32... | collective-permute-start | bytes 147464 | tf_op jit(solution)/shard_map/ppermute | solution.py:22
  98.2 30.8 %copy-start.6 = (bf16[4,384,96]{1,2,0:T(8,128)(2,1)S(1)}, bf16[4,384,96]{1,2,0:T(8,128)(2,1)}, u32[]{:S(2)}) copy-start(bf16[4,384,96]{1,2,0:T(8,128)(2,1)} %param.21) | copy-start | bytes 884740
  100.0 28.0 %collective-permute-start.12 = (bf16[128,192]{1,0:T(8,128)(2,1)}, bf16[128,192]{1,0:T(8,128)(2,1)}, u32[]{:S(2)}, u32[]{:S(2)}) collective-permute-start(bf16[128,192]{1,0:T(8,128)(2,1)} %convert_element_type.246), channel_id=1, source_target_pairs={{8,0},{12,4},{16,8},{20,12},{24,16},{28,20},{32,24},{36,28},{40,32... | collective-permute-start | bytes 147464 | tf_op jit(solution)/shard_map/ppermute | solution.py:22
  105.2 22.9 %collective-permute-start.13 = (bf16[128,192]{1,0:T(8,128)(2,1)}, bf16[128,192]{1,0:T(8,128)(2,1)}, u32[]{:S(2)}, u32[]{:S(2)}) collective-permute-start(bf16[128,192]{1,0:T(8,128)(2,1)} %convert_element_type.248), channel_id=1, source_target_pairs={{4,0},{8,4},{12,8},{16,12},{20,16},{24,20},{28,24},{32,28},{36,32}... | collective-permute-start | bytes 147464 | tf_op jit(solution)/shard_map/ppermute | solution.py:22
  110.9 17.1 %collective-permute-start.14 = (bf16[128,192]{1,0:T(8,128)(2,1)}, bf16[128,192]{1,0:T(8,128)(2,1)}, u32[]{:S(2)}, u32[]{:S(2)}) collective-permute-start(bf16[128,192]{1,0:T(8,128)(2,1)} %convert_element_type.250), channel_id=1, source_target_pairs={{508,0},{0,4},{4,8},{8,12},{12,16},{16,20},{20,24},{24,28},{28,32}... | collective-permute-start | bytes 147464 | tf_op jit(solution)/shard_map/ppermute | solution.py:22
  114.1 13.9 %collective-permute-start.15 = (bf16[128,192]{1,0:T(8,128)(2,1)}, bf16[128,192]{1,0:T(8,128)(2,1)}, u32[]{:S(2)}, u32[]{:S(2)}) collective-permute-start(bf16[128,192]{1,0:T(8,128)(2,1)} %convert_element_type.252), channel_id=1, source_target_pairs={{504,0},{508,4},{0,8},{4,12},{8,16},{12,20},{16,24},{20,28},{24,32... | collective-permute-start | bytes 147464 | tf_op jit(solution)/shard_map/ppermute | solution.py:22
  120.9 9.0 %collective-permute-start.8 = (bf16[1216,128]{1,0:T(8,128)(2,1)}, bf16[1216,128]{1,0:T(8,128)(2,1)S(1)}, u32[]{:S(2)}, u32[]{:S(2)}) collective-permute-start(bf16[1216,128]{1,0:T(8,128)(2,1)} %select_convert_fusion), channel_id=1, source_target_pairs={{0,1},{1,0},{2,3},{3,2},{4,5},{5,4},{6,7},{7,6},{8,9},{9,8},{10,11... | collective-permute-start | bytes 933896 | tf_op jit(solution)/shard_map/ppermute | solution.py:57
  130.0 6.7 %collective-permute-start.9 = (bf16[608,128]{1,0:T(8,128)(2,1)S(1)}, bf16[608,128]{1,0:T(8,128)(2,1)S(1)}, u32[]{:S(2)}, u32[]{:S(2)}) collective-permute-start(bf16[608,128]{1,0:T(8,128)(2,1)S(1)} %select_convert_fusion.1), channel_id=1, source_target_pairs={{0,2},{1,3},{2,0},{3,1},{4,6},{5,7},{6,4},{7,5},{8,10},{9,11},{10,... | collective-permute-start | bytes 466952 | tf_op jit(solution)/shard_map/ppermute | solution.py:61
  132.4 7.3 %collective-permute-start.16 = (bf16[128,384]{1,0:T(8,128)(2,1)S(1)}, bf16[128,384]{1,0:T(8,128)(2,1)S(1)}, u32[]{:S(2)}, u32[]{:S(2)}) collective-permute-start(bf16[128,384]{1,0:T(8,128)(2,1)S(1)} %fusion.67), channel_id=1, source_target_pairs={{0,1},{1,0},{2,3},{3,2},{4,5},{5,4},{6,7},{7,6},{8,9},{9,8},{10,11... | collective-permute-start | bytes 294920 | tf_op jit(solution)/shard_map/ppermute | solution.py:87
  136.7 6.0 %collective-permute-start.10 = (bf16[608,128]{1,0:T(8,128)(2,1)S(1)}, bf16[608,128]{1,0:T(8,128)(2,1)S(1)}, u32[]{:S(2)}, u32[]{:S(2)}) collective-permute-start(bf16[608,128]{1,0:T(8,128)(2,1)S(1)} %add_convert_fusion), channel_id=1, source_target_pairs={{0,2},{1,3},{2,0},{3,1},{4,6},{5,7},{6,4},{7,5},{8,10},{9,11},{10,... | collective-permute-start | bytes 466952 | tf_op jit(solution)/shard_map/ppermute | solution.py:63
  139.8 9.6 %collective-permute-start.17 = (bf16[128,384]{1,0:T(8,128)(2,1)S(1)}, bf16[128,384]{1,0:T(8,128)(2,1)S(1)}, u32[]{:S(2)}, u32[]{:S(2)}) collective-permute-start(bf16[128,384]{1,0:T(8,128)(2,1)S(1)} %add_convert_fusion.2), channel_id=1, source_target_pairs={{0,2},{1,3},{2,0},{3,1},{4,6},{5,7},{6,4},{7,5},{8,10},{9,11},{10,... | collective-permute-start | bytes 294920 | tf_op jit(solution)/shard_map/ppermute | solution.py:89
  142.8 7.8 %collective-permute-start.11 = (bf16[1216,128]{1,0:T(8,128)(2,1)S(1)}, bf16[1216,128]{1,0:T(8,128)(2,1)S(1)}, u32[]{:S(2)}, u32[]{:S(2)}) collective-permute-start(bf16[1216,128]{1,0:T(8,128)(2,1)S(1)} %maximum_select_fusion.1), channel_id=1, source_target_pairs={{0,1},{1,0},{2,3},{3,2},{4,5},{5,4},{6,7},{7,6},{8,9},{9,8},{10,11... | collective-permute-start | bytes 933896 | tf_op jit(solution)/shard_map/ppermute | solution.py:67
  (22 other events, 214.8 us)

commit v7 on v1

--- a/solution.py
+++ b/solution.py
@@ -13,7 +13,7 @@
 
 
 EPSILON = 1e-05
-HIGHEST = lax.Precision.HIGHEST
+ONE_HOT_PRECISION = lax.Precision.HIGH
 
 
 def shifted(block, axis, distance):
@@ -237,7 +237,7 @@
     )
     returned_flat = returned.reshape(blocks_here, S, BLK * 2 * features)
     outgoing = jnp.einsum(
-        "bsc,bsx->cx", selector_mask.astype(jnp.float32), returned_flat, precision=HIGHEST
+        "bsc,bsx->cx", selector_mask.astype(jnp.float32), returned_flat, precision=ONE_HOT_PRECISION
     )
     outgoing = outgoing.reshape(2 * WIN + 1, tok_rows, 2 * features)
     collected = outgoing[WIN]
@@ -270,7 +270,7 @@
         jnp.float32
     )
     condition = jnp.dot(normed_low, w_cond, preferred_element_type=jnp.float32)
-    atom_input = (normed_atoms + jnp.dot(token_pick, condition, precision=HIGHEST)).astype(
+    atom_input = (normed_atoms + jnp.dot(token_pick, condition, precision=ONE_HOT_PRECISION)).astype(
         jnp.bfloat16
     )
     atom_proj = [
@@ -340,7 +340,7 @@
         axis=-1,
     )
     slab_grads = jnp.einsum(
-        "wrs,wrf->wsf", placer_mask.astype(jnp.float32), spread_grads, precision=HIGHEST
+        "wrs,wrf->wsf", placer_mask.astype(jnp.float32), spread_grads, precision=ONE_HOT_PRECISION
     )
     slab_grads = slab_grads.reshape(windows_here, group_span, AQ, 2 * atom_feat)
     ext_grad = jnp.pad(slab_grads[:, 0], ((0, group_span - 1), (0, 0), (0, 0)))
@@ -372,8 +372,8 @@
             atom_grads[which], w_atom_all[which].T, preferred_element_type=jnp.float32
         )
     atoms_part = norm_back(atoms.astype(jnp.float32), gain_atom, agrad_input)
-    cond_grad = jnp.dot(token_pick.T, agrad_input, precision=HIGHEST)
-    cond_term = jnp.dot(cond_grad, w_cond.astype(jnp.float32).T, precision=HIGHEST)
+    cond_grad = jnp.dot(token_pick.T, agrad_input, precision=ONE_HOT_PRECISION)
+    cond_term = jnp.dot(cond_grad, w_cond.astype(jnp.float32).T, precision=ONE_HOT_PRECISION)
     grad_normed = cond_term
     for which in range(4):
         grad_normed = grad_normed + jnp.dot(

time: 154 us -> 154 us (level)
  no operation moved by 1% of the time
where the time goes in v7:
time: 154 us; the launch traced here: 152 us
  starting transfers between devices  71 us (46%)
  matrix products  28 us (18%)
  local copies, waits for them, and re-layouts  19.6 us (13%)
  waiting for transfers between devices  18.6 us (12%)
  other arithmetic  12.5 us (8%)
  between operations  2.57 us (2%)
    ppermute x8, starting transfers between devices, shifted(): return lax.ppermute(block, axis, route)  41.3 us
    ppermute x2, starting transfers between devices, extended_2(): lax.ppermute(lax.slice_in_dim(block, 0, width, axis=dim), axis, backward)  11.2 us
    ppermute x2, waiting for transfers between devices, extended_2(): lax.ppermute(lax.slice_in_dim(block, block.shape[dim] - width, None, axis...  6.3 us
    ppermute x1, starting transfers between devices, head_sum(): got = lax.ppermute(give.astype(jnp.bfloat16), axis, pair_near)  6.01 us
    ppermute x1, waiting for transfers between devices, head_sum(): got = lax.ppermute(give.astype(jnp.bfloat16), axis, pair_far)  5.34 us
    ppermute x1, waiting for transfers between devices, head_sum(): got = lax.ppermute(own, axis, pair_far)  4.42 us
    ppermute x1, starting transfers between devices, head_sum(): got = lax.ppermute(half, axis, pair_near)  4.03 us
    ppermute x2, starting transfers between devices, extended_2(): lax.ppermute(lax.slice_in_dim(block, block.shape[dim] - width, None, axis...  3.84 us
  transfers between devices with their start and end apart: 16, of which 6 were waited for; matrix products, arithmetic and copies ran while one was open for 26% of the time, Pallas kernels for 0%

profile of v7, /device:TPU:1, one launch (start us, length us, event | category | flops | bytes accessed | tf_op | source)
XLA Modules:
  0.0 152.3 jit_solution(14851550710830765029)
XLA Ops:
  7.1 5.5 %collective-permute-start = (bf16[128,192]{0,1:T(8,128)(2,1)}, bf16[128,192]{0,1:T(8,128)(2,1)}, u32[]{:S(2)}, u32[]{:S(2)}) collective-permute-start(bf16[128,192]{0,1:T(8,128)(2,1)} %pad_maximum_fusion.7), channel_id=1, source_target_pairs={{504,0},{508,4},{0,8},{4,12},{8,16},{12,20},{16,24},{20,28},{24,32... | collective-permute-start | bytes 147464 | tf_op jit(solution)/shard_map/ppermute | solution.py:22
  12.6 2.2 %collective-permute-start.1 = (bf16[128,192]{0,1:T(8,128)(2,1)}, bf16[128,192]{0,1:T(8,128)(2,1)}, u32[]{:S(2)}, u32[]{:S(2)}) collective-permute-start(bf16[128,192]{0,1:T(8,128)(2,1)} %pad_maximum_fusion.7), channel_id=1, source_target_pairs={{508,0},{0,4},{4,8},{8,12},{12,16},{16,20},{20,24},{24,28},{28,32}... | collective-permute-start | bytes 147464 | tf_op jit(solution)/shard_map/ppermute | solution.py:22
  14.9 12.9 %collective-permute-start.2 = (bf16[128,192]{0,1:T(8,128)(2,1)}, bf16[128,192]{0,1:T(8,128)(2,1)}, u32[]{:S(2)}, u32[]{:S(2)}) collective-permute-start(bf16[128,192]{0,1:T(8,128)(2,1)} %pad_maximum_fusion.7), channel_id=1, source_target_pairs={{4,0},{8,4},{12,8},{16,12},{20,16},{24,20},{28,24},{32,28},{36,32}... | collective-permute-start | bytes 147464 | tf_op jit(solution)/shard_map/ppermute | solution.py:22
  34.5 3.4 %collective-permute-start.5 = (bf16[64,64]{0,1:T(8,128)(2,1)S(1)}, bf16[64,64]{0,1:T(8,128)(2,1)S(1)}, u32[]{:S(2)}, u32[]{:S(2)}) collective-permute-start(bf16[64,64]{0,1:T(8,128)(2,1)S(1)} %get-tuple-element.52), channel_id=1, source_target_pairs={{4,0},{8,4},{12,8},{16,12},{20,16},{24,20},{28,24},{32,28},{36,32}... | collective-permute-start | bytes 24584 | tf_op jit(solution)/shard_map/ppermute | solution.py:34
  37.9 1.9 %collective-permute-start.4 = (bf16[64,64]{0,1:T(8,128)(2,1)S(1)}, bf16[64,64]{0,1:T(8,128)(2,1)S(1)}, u32[]{:S(2)}, u32[]{:S(2)}) collective-permute-start(bf16[64,64]{0,1:T(8,128)(2,1)S(1)} %get-tuple-element.53), channel_id=1, source_target_pairs={{0,4},{4,8},{8,12},{12,16},{16,20},{20,24},{24,28},{28,32},{32,36}... | collective-permute-start | bytes 24584 | tf_op jit(solution)/shard_map/ppermute | solution.py:31
  50.3 2.3 %concatenate.63 = bf16[32,160,64]{1,2,0:T(8,128)(2,1)} concatenate(bf16[32,32,64]{1,2,0:T(8,128)(2,1)S(1)} %copy.91, bf16[32,32,64]{1,2,0:T(8,128)(2,1)S(1)} %copy.92, bf16[32,32,64]{1,2,0:T(8,128)(2,1)S(1)} %copy.93, bf16[32,32,64]{1,2,0:T(8,128)(2,1)S(1)} %copy.94, bf16[32,32,64]{1,2,0:T(8,128)(2,1)S(1)} %copy.95), dimensions={1} | concatenate | bytes 1310720 | tf_op jit(solution)/shard_map/concatenate | solution.py:286
  52.5 1.9 %fusion.11 = bf16[32,128,64]{1,2,0:T(8,128)(2,1)S(1)} fusion(bf16[32,160,64]{1,2,0:T(8,128)(2,1)} %concatenate.63, s32[32,128]{1,0:T(8,128)} %iota_add_fusion), kind=kOutput, calls=%fused_computation.15 | convolution fusion | flops 84803584 | bytes 1196032 | tf_op jit(solution)/shard_map/wrs,wsf->wrf/dot_general | solution.py:294
  55.7 1.8 %convolution_bitcast_fusion.1 = f32[32,32,1,32]{1,3,0,2:T(8,128)S(1)} fusion(bf16[32,128,64]{1,2,0:T(8,128)(2,1)S(1)} %fusion.11, f32[32,32]{1,0:T(8,128)S(1)} %get-tuple-element.57, f32[32,32,128]{2,1,0:T(8,128)S(1)} %fusion.17), kind=kOutput, calls=%fused_computation.23 | convolution fusion | flops 8782975 | bytes 1458176 | tf_op jit(solution)/shard_map/bhqk,bkhd->bqhd/dot_general | solution.py:114
  58.6 1.8 %convolution_bitcast_fusion = f32[32,128,32]{1,2,0:T(8,128)S(1)} fusion(bf16[32,32,32]{1,0,2:T(8,128)(2,1)S(1)} %reshape.430, f32[32,32]{1,0:T(8,128)S(1)} %get-tuple-element.57, f32[32,32,128]{2,1,0:T(8,128)S(1)} %fusion.17), kind=kOutput, calls=%fused_computation.22 | convolution fusion | flops 8782975 | bytes 1118208 | tf_op jit(solution)/shard_map/bhqk,bqhd->bkhd/dot_general | solution.py:136
  65.1 7.8 %collective-permute-start.7 = (bf16[64,64]{1,0:T(8,128)(2,1)S(1)}, bf16[64,64]{1,0:T(8,128)(2,1)S(1)}, u32[]{:S(2)}, u32[]{:S(2)}) collective-permute-start(bf16[64,64]{1,0:T(8,128)(2,1)S(1)} %bitcast.234), channel_id=1, source_target_pairs={{4,0},{8,4},{12,8},{16,12},{20,16},{24,20},{28,24},{32,28},{36,32}... | collective-permute-start | bytes 24584 | tf_op jit(solution)/shard_map/ppermute | solution.py:34
  73.0 1.9 %collective-permute-start.6 = (bf16[64,64]{1,0:T(8,128)(2,1)S(1)}, bf16[64,64]{1,0:T(8,128)(2,1)S(1)}, u32[]{:S(2)}, u32[]{:S(2)}) collective-permute-start(bf16[64,64]{1,0:T(8,128)(2,1)S(1)} %bitcast.232), channel_id=1, source_target_pairs={{0,4},{4,8},{8,12},{12,16},{16,20},{20,24},{24,28},{28,32},{32,36}... | collective-permute-start | bytes 24584 | tf_op jit(solution)/shard_map/ppermute | solution.py:31
  75.0 3.3 %collective-permute-start.3 = (bf16[128,192]{0,1:T(8,128)(2,1)}, bf16[128,192]{0,1:T(8,128)(2,1)S(1)}, u32[]{:S(2)}, u32[]{:S(2)}) collective-permute-start(bf16[128,192]{0,1:T(8,128)(2,1)} %pad_maximum_fusion.7), channel_id=1, source_target_pairs={{8,0},{12,4},{16,8},{20,12},{24,16},{28,20},{32,24},{36,28},{40,32... | collective-permute-start | bytes 147464 | tf_op jit(solution)/shard_map/ppermute | solution.py:22
  78.3 4.9 %collective-permute-done.6 = bf16[64,64]{1,0:T(8,128)(2,1)S(1)} collective-permute-done((bf16[64,64]{1,0:T(8,128)(2,1)S(1)}, bf16[64,64]{1,0:T(8,128)(2,1)S(1)}, u32[]{:S(2)}, u32[]{:S(2)}) %collective-permute-start.6) | collective-permute-done | bytes 8224 | tf_op jit(solution)/shard_map/ppermute | solution.py:31
  96.9 2.0 %fusion.140 = (bf16[5,24576]{1,0:T(8,128)(2,1)S(1)}, f32[5,24576]{1,0:T(8,128)}) fusion(f32[4,24576]{1,0:T(4,128)S(1)} %reshape.438, s32[4]{0:T(128)} %fusion.119), kind=kOutput, calls=%fused_computation.239 | convolution fusion | flops 3072020 | bytes 1130512 | tf_op jit(solution)/shard_map/bsc,bsx->cx/dot_general | solution.py:239
  100.1 1.9 %collective-permute-start.11 = (bf16[128,192]{1,0:T(8,128)(2,1)S(1)}, bf16[128,192]{1,0:T(8,128)(2,1)S(1)}, u32[]{:S(2)}, u32[]{:S(2)}) collective-permute-start(bf16[128,192]{1,0:T(8,128)(2,1)S(1)} %convert_element_type.226), channel_id=1, source_target_pairs={{504,0},{508,4},{0,8},{4,12},{8,16},{12,20},{16,24},{20,28},{24,32... | collective-permute-start | bytes 147464 | tf_op jit(solution)/shard_map/ppermute | solution.py:22
  102.1 3.6 %collective-permute-start.10 = (bf16[128,192]{1,0:T(8,128)(2,1)S(1)}, bf16[128,192]{1,0:T(8,128)(2,1)S(1)}, u32[]{:S(2)}, u32[]{:S(2)}) collective-permute-start(bf16[128,192]{1,0:T(8,128)(2,1)S(1)} %convert_element_type.224), channel_id=1, source_target_pairs={{508,0},{0,4},{4,8},{8,12},{12,16},{16,20},{20,24},{24,28},{28,32}... | collective-permute-start | bytes 147464 | tf_op jit(solution)/shard_map/ppermute | solution.py:22
  105.8 8.8 %collective-permute-start.9 = (bf16[128,192]{1,0:T(8,128)(2,1)S(1)}, bf16[128,192]{1,0:T(8,128)(2,1)S(1)}, u32[]{:S(2)}, u32[]{:S(2)}) collective-permute-start(bf16[128,192]{1,0:T(8,128)(2,1)S(1)} %convert_element_type.222), channel_id=1, source_target_pairs={{4,0},{8,4},{12,8},{16,12},{20,16},{24,20},{28,24},{32,28},{36,32}... | collective-permute-start | bytes 147464 | tf_op jit(solution)/shard_map/ppermute | solution.py:22
  114.7 3.1 %collective-permute-start.8 = (bf16[128,192]{1,0:T(8,128)(2,1)S(1)}, bf16[128,192]{1,0:T(8,128)(2,1)S(1)}, u32[]{:S(2)}, u32[]{:S(2)}) collective-permute-start(bf16[128,192]{1,0:T(8,128)(2,1)S(1)} %convert_element_type.220), channel_id=1, source_target_pairs={{8,0},{12,4},{16,8},{20,12},{24,16},{28,20},{32,24},{36,28},{40,32... | collective-permute-start | bytes 147464 | tf_op jit(solution)/shard_map/ppermute | solution.py:22
  122.6 6.0 %collective-permute-start.12 = (bf16[1408,128]{1,0:T(8,128)(2,1)S(1)}, bf16[1408,128]{1,0:T(8,128)(2,1)S(1)}, u32[]{:S(2)}, u32[]{:S(2)}) collective-permute-start(bf16[1408,128]{1,0:T(8,128)(2,1)S(1)} %select_convert_fusion), channel_id=1, source_target_pairs={{0,1},{1,0},{2,3},{3,2},{4,5},{5,4},{6,7},{7,6},{8,9},{9,8},{10,11... | collective-permute-start | bytes 1081352 | tf_op jit(solution)/shard_map/ppermute | solution.py:57
  130.0 2.3 %collective-permute-start.13 = (bf16[704,128]{1,0:T(8,128)(2,1)S(1)}, bf16[704,128]{1,0:T(8,128)(2,1)S(1)}, u32[]{:S(2)}, u32[]{:S(2)}) collective-permute-start(bf16[704,128]{1,0:T(8,128)(2,1)S(1)} %select_convert_fusion.1), channel_id=1, source_target_pairs={{0,2},{1,3},{2,0},{3,1},{4,6},{5,7},{6,4},{7,5},{8,10},{9,11},{10,... | collective-permute-start | bytes 540680 | tf_op jit(solution)/shard_map/ppermute | solution.py:61
  132.3 5.3 %collective-permute-done.13 = bf16[704,128]{1,0:T(8,128)(2,1)S(1)} collective-permute-done((bf16[704,128]{1,0:T(8,128)(2,1)S(1)}, bf16[704,128]{1,0:T(8,128)(2,1)S(1)}, u32[]{:S(2)}, u32[]{:S(2)}) %collective-permute-start.13) | collective-permute-done | bytes 180256 | tf_op jit(solution)/shard_map/ppermute | solution.py:61
  137.7 2.3 %collective-permute-start.14 = (bf16[704,128]{1,0:T(8,128)(2,1)S(1)}, bf16[704,128]{1,0:T(8,128)(2,1)S(1)}, u32[]{:S(2)}, u32[]{:S(2)}) collective-permute-start(bf16[704,128]{1,0:T(8,128)(2,1)S(1)} %add_convert_fusion), channel_id=1, source_target_pairs={{0,2},{1,3},{2,0},{3,1},{4,6},{5,7},{6,4},{7,5},{8,10},{9,11},{10,... | collective-permute-start | bytes 540680 | tf_op jit(solution)/shard_map/ppermute | solution.py:63
  140.0 4.4 %collective-permute-done.14 = bf16[704,128]{1,0:T(8,128)(2,1)S(1)} collective-permute-done((bf16[704,128]{1,0:T(8,128)(2,1)S(1)}, bf16[704,128]{1,0:T(8,128)(2,1)S(1)}, u32[]{:S(2)}, u32[]{:S(2)}) %collective-permute-start.14) | collective-permute-done | bytes 180256 | tf_op jit(solution)/shard_map/ppermute | solution.py:63
  144.6 4.0 %collective-permute-start.15 = (bf16[1408,128]{1,0:T(8,128)(2,1)S(1)}, bf16[1408,128]{1,0:T(8,128)(2,1)S(1)}, u32[]{:S(2)}, u32[]{:S(2)}) collective-permute-start(bf16[1408,128]{1,0:T(8,128)(2,1)S(1)} %maximum_select_fusion.1), channel_id=1, source_target_pairs={{0,1},{1,0},{2,3},{3,2},{4,5},{5,4},{6,7},{7,6},{8,9},{9,8},{10,11... | collective-permute-start | bytes 1081352 | tf_op jit(solution)/shard_map/ppermute | solution.py:67
  (204 shorter events, 54.2 us)
Async XLA Ops:
  0.6 57.5 %copy-start = (bf16[1024,128]{1,0:T(8,128)(2,1)S(1)}, bf16[1024,128]{1,0:T(8,128)(2,1)}, u32[]{:S(2)}) copy-start(bf16[1024,128]{1,0:T(8,128)(2,1)} %param.33) | copy-start | bytes 786436
  0.6 39.6 %copy-start.5 = (bf16[4,384,96]{1,2,0:T(8,128)(2,1)S(1)}, bf16[4,384,96]{1,2,0:T(8,128)(2,1)}, u32[]{:S(2)}) copy-start(bf16[4,384,96]{1,2,0:T(8,128)(2,1)} %param.21) | copy-start | bytes 884740
  0.7 33.4 %copy-start.11 = (bf16[4,128,32]{1,2,0:T(8,128)(2,1)S(1)}, bf16[4,128,32]{1,2,0:T(8,128)(2,1)}, u32[]{:S(2)}) copy-start(bf16[4,128,32]{1,2,0:T(8,128)(2,1)} %param.24) | copy-start | bytes 98308
  0.7 41.2 %copy-start.25 = (s32[32]{0:T(128)S(1)}, s32[32]{0:T(128)}, u32[]{:S(2)}) copy-start(s32[32]{0:T(128)} %param.31) | copy-start | bytes 388
  1.7 42.1 %copy-start.26 = (s32[1,4]{1,0:T(1,128)S(1)}, s32[1,4]{1,0:T(1,128)}, u32[]{:S(2)}) copy-start(s32[1,4]{1,0:T(1,128)} %param.28) | copy-start | bytes 52
  7.1 79.4 %collective-permute-start = (bf16[128,192]{0,1:T(8,128)(2,1)}, bf16[128,192]{0,1:T(8,128)(2,1)}, u32[]{:S(2)}, u32[]{:S(2)}) collective-permute-start(bf16[128,192]{0,1:T(8,128)(2,1)} %pad_maximum_fusion.7), channel_id=1, source_target_pairs={{504,0},{508,4},{0,8},{4,12},{8,16},{12,20},{16,24},{20,28},{24,32... | collective-permute-start | bytes 147464 | tf_op jit(solution)/shard_map/ppermute | solution.py:22
  12.6 75.0 %collective-permute-start.1 = (bf16[128,192]{0,1:T(8,128)(2,1)}, bf16[128,192]{0,1:T(8,128)(2,1)}, u32[]{:S(2)}, u32[]{:S(2)}) collective-permute-start(bf16[128,192]{0,1:T(8,128)(2,1)} %pad_maximum_fusion.7), channel_id=1, source_target_pairs={{508,0},{0,4},{4,8},{8,12},{12,16},{16,20},{20,24},{24,28},{28,32}... | collective-permute-start | bytes 147464 | tf_op jit(solution)/shard_map/ppermute | solution.py:22
  14.9 73.8 %collective-permute-start.2 = (bf16[128,192]{0,1:T(8,128)(2,1)}, bf16[128,192]{0,1:T(8,128)(2,1)}, u32[]{:S(2)}, u32[]{:S(2)}) collective-permute-start(bf16[128,192]{0,1:T(8,128)(2,1)} %pad_maximum_fusion.7), channel_id=1, source_target_pairs={{4,0},{8,4},{12,8},{16,12},{20,16},{24,20},{28,24},{32,28},{36,32}... | collective-permute-start | bytes 147464 | tf_op jit(solution)/shard_map/ppermute | solution.py:22
  34.5 12.2 %collective-permute-start.5 = (bf16[64,64]{0,1:T(8,128)(2,1)S(1)}, bf16[64,64]{0,1:T(8,128)(2,1)S(1)}, u32[]{:S(2)}, u32[]{:S(2)}) collective-permute-start(bf16[64,64]{0,1:T(8,128)(2,1)S(1)} %get-tuple-element.52), channel_id=1, source_target_pairs={{4,0},{8,4},{12,8},{16,12},{20,16},{24,20},{28,24},{32,28},{36,32}... | collective-permute-start | bytes 24584 | tf_op jit(solution)/shard_map/ppermute | solution.py:34
  37.9 10.2 %collective-permute-start.4 = (bf16[64,64]{0,1:T(8,128)(2,1)S(1)}, bf16[64,64]{0,1:T(8,128)(2,1)S(1)}, u32[]{:S(2)}, u32[]{:S(2)}) collective-permute-start(bf16[64,64]{0,1:T(8,128)(2,1)S(1)} %get-tuple-element.53), channel_id=1, source_target_pairs={{0,4},{4,8},{8,12},{12,16},{16,20},{20,24},{24,28},{28,32},{32,36}... | collective-permute-start | bytes 24584 | tf_op jit(solution)/shard_map/ppermute | solution.py:31
  65.1 9.8 %collective-permute-start.7 = (bf16[64,64]{1,0:T(8,128)(2,1)S(1)}, bf16[64,64]{1,0:T(8,128)(2,1)S(1)}, u32[]{:S(2)}, u32[]{:S(2)}) collective-permute-start(bf16[64,64]{1,0:T(8,128)(2,1)S(1)} %bitcast.234), channel_id=1, source_target_pairs={{4,0},{8,4},{12,8},{16,12},{20,16},{24,20},{28,24},{32,28},{36,32}... | collective-permute-start | bytes 24584 | tf_op jit(solution)/shard_map/ppermute | solution.py:34
  73.0 10.2 %collective-permute-start.6 = (bf16[64,64]{1,0:T(8,128)(2,1)S(1)}, bf16[64,64]{1,0:T(8,128)(2,1)S(1)}, u32[]{:S(2)}, u32[]{:S(2)}) collective-permute-start(bf16[64,64]{1,0:T(8,128)(2,1)S(1)} %bitcast.232), channel_id=1, source_target_pairs={{0,4},{4,8},{8,12},{12,16},{16,20},{20,24},{24,28},{28,32},{32,36}... | collective-permute-start | bytes 24584 | tf_op jit(solution)/shard_map/ppermute | solution.py:31
  75.0 14.7 %collective-permute-start.3 = (bf16[128,192]{0,1:T(8,128)(2,1)}, bf16[128,192]{0,1:T(8,128)(2,1)S(1)}, u32[]{:S(2)}, u32[]{:S(2)}) collective-permute-start(bf16[128,192]{0,1:T(8,128)(2,1)} %pad_maximum_fusion.7), channel_id=1, source_target_pairs={{8,0},{12,4},{16,8},{20,12},{24,16},{28,20},{32,24},{36,28},{40,32... | collective-permute-start | bytes 147464 | tf_op jit(solution)/shard_map/ppermute | solution.py:22
  96.9 24.7 %copy-start.6 = (bf16[4,384,96]{1,2,0:T(8,128)(2,1)S(1)}, bf16[4,384,96]{1,2,0:T(8,128)(2,1)}, u32[]{:S(2)}) copy-start(bf16[4,384,96]{1,2,0:T(8,128)(2,1)} %param.21) | copy-start | bytes 884740
  96.9 25.1 %copy-start.2 = (bf16[128,384]{1,0:T(8,128)(2,1)S(1)}, bf16[128,384]{1,0:T(8,128)(2,1)}, u32[]{:S(2)}) copy-start(bf16[128,384]{1,0:T(8,128)(2,1)} %param.17) | copy-start | bytes 294916
  96.9 25.1 %copy-start.19 = (f32[384]{0:T(512)S(1)}, f32[384]{0:T(512)}, u32[]{:S(2)}) copy-start(f32[384]{0:T(512)} %param.19) | copy-start | bytes 4612
  100.1 21.4 %collective-permute-start.11 = (bf16[128,192]{1,0:T(8,128)(2,1)S(1)}, bf16[128,192]{1,0:T(8,128)(2,1)S(1)}, u32[]{:S(2)}, u32[]{:S(2)}) collective-permute-start(bf16[128,192]{1,0:T(8,128)(2,1)S(1)} %convert_element_type.226), channel_id=1, source_target_pairs={{504,0},{508,4},{0,8},{4,12},{8,16},{12,20},{16,24},{20,28},{24,32... | collective-permute-start | bytes 147464 | tf_op jit(solution)/shard_map/ppermute | solution.py:22
  102.1 19.3 %collective-permute-start.10 = (bf16[128,192]{1,0:T(8,128)(2,1)S(1)}, bf16[128,192]{1,0:T(8,128)(2,1)S(1)}, u32[]{:S(2)}, u32[]{:S(2)}) collective-permute-start(bf16[128,192]{1,0:T(8,128)(2,1)S(1)} %convert_element_type.224), channel_id=1, source_target_pairs={{508,0},{0,4},{4,8},{8,12},{12,16},{16,20},{20,24},{24,28},{28,32}... | collective-permute-start | bytes 147464 | tf_op jit(solution)/shard_map/ppermute | solution.py:22
  105.8 15.7 %collective-permute-start.9 = (bf16[128,192]{1,0:T(8,128)(2,1)S(1)}, bf16[128,192]{1,0:T(8,128)(2,1)S(1)}, u32[]{:S(2)}, u32[]{:S(2)}) collective-permute-start(bf16[128,192]{1,0:T(8,128)(2,1)S(1)} %convert_element_type.222), channel_id=1, source_target_pairs={{4,0},{8,4},{12,8},{16,12},{20,16},{24,20},{28,24},{32,28},{36,32}... | collective-permute-start | bytes 147464 | tf_op jit(solution)/shard_map/ppermute | solution.py:22
  114.7 6.7 %collective-permute-start.8 = (bf16[128,192]{1,0:T(8,128)(2,1)S(1)}, bf16[128,192]{1,0:T(8,128)(2,1)S(1)}, u32[]{:S(2)}, u32[]{:S(2)}) collective-permute-start(bf16[128,192]{1,0:T(8,128)(2,1)S(1)} %convert_element_type.220), channel_id=1, source_target_pairs={{8,0},{12,4},{16,8},{20,12},{24,16},{28,20},{32,24},{36,28},{40,32... | collective-permute-start | bytes 147464 | tf_op jit(solution)/shard_map/ppermute | solution.py:22
  122.6 7.3 %collective-permute-start.12 = (bf16[1408,128]{1,0:T(8,128)(2,1)S(1)}, bf16[1408,128]{1,0:T(8,128)(2,1)S(1)}, u32[]{:S(2)}, u32[]{:S(2)}) collective-permute-start(bf16[1408,128]{1,0:T(8,128)(2,1)S(1)} %select_convert_fusion), channel_id=1, source_target_pairs={{0,1},{1,0},{2,3},{3,2},{4,5},{5,4},{6,7},{7,6},{8,9},{9,8},{10,11... | collective-permute-start | bytes 1081352 | tf_op jit(solution)/shard_map/ppermute | solution.py:57
  130.0 7.7 %collective-permute-start.13 = (bf16[704,128]{1,0:T(8,128)(2,1)S(1)}, bf16[704,128]{1,0:T(8,128)(2,1)S(1)}, u32[]{:S(2)}, u32[]{:S(2)}) collective-permute-start(bf16[704,128]{1,0:T(8,128)(2,1)S(1)} %select_convert_fusion.1), channel_id=1, source_target_pairs={{0,2},{1,3},{2,0},{3,1},{4,6},{5,7},{6,4},{7,5},{8,10},{9,11},{10,... | collective-permute-start | bytes 540680 | tf_op jit(solution)/shard_map/ppermute | solution.py:61
  137.7 6.7 %collective-permute-start.14 = (bf16[704,128]{1,0:T(8,128)(2,1)S(1)}, bf16[704,128]{1,0:T(8,128)(2,1)S(1)}, u32[]{:S(2)}, u32[]{:S(2)}) collective-permute-start(bf16[704,128]{1,0:T(8,128)(2,1)S(1)} %add_convert_fusion), channel_id=1, source_target_pairs={{0,2},{1,3},{2,0},{3,1},{4,6},{5,7},{6,4},{7,5},{8,10},{9,11},{10,... | collective-permute-start | bytes 540680 | tf_op jit(solution)/shard_map/ppermute | solution.py:63
  144.6 5.3 %collective-permute-start.15 = (bf16[1408,128]{1,0:T(8,128)(2,1)S(1)}, bf16[1408,128]{1,0:T(8,128)(2,1)S(1)}, u32[]{:S(2)}, u32[]{:S(2)}) collective-permute-start(bf16[1408,128]{1,0:T(8,128)(2,1)S(1)} %maximum_select_fusion.1), channel_id=1, source_target_pairs={{0,1},{1,0},{2,3},{3,2},{4,5},{5,4},{6,7},{7,6},{8,9},{9,8},{10,11... | collective-permute-start | bytes 1081352 | tf_op jit(solution)/shard_map/ppermute | solution.py:67
  (20 other events, 160.4 us)

commit v8 on v5

--- a/solution.py
+++ b/solution.py
@@ -20,13 +20,6 @@
     devices = range(lax.axis_size(axis))
     route = [((i - distance) % len(devices), i) for i in devices]
     return lax.ppermute(block, axis, route)
-
-
-def shifted_pair(block, extra, axis, distance):
-    rows = block.shape[0]
-    padded = jnp.pad(extra, ((0, 0), (0, block.shape[1] - extra.shape[1])))
-    both = shifted(jnp.concatenate([block, padded], axis=0), axis, distance)
-    return both[:rows], both[rows:, : extra.shape[1]]
 
 
 def extended_2(block, sides, width):
@@ -211,17 +204,15 @@
     atom_kv = jnp.concatenate(
         [atom_proj[1].astype(jnp.bfloat16), atom_proj[2].astype(jnp.bfloat16)], axis=1
     )
+    extended = extended_2(atom_kv, (("seq", 0),), halo_rows)
+    key_value, extended = lax.optimization_barrier((key_value, extended))
     owner_dev = used_blocks // blocks_here
     relative = jnp.mod(owner_dev - device, shards)
     relative = jnp.where(relative > shards // 2, relative - shards, relative)
     pieces = [key_value for distance in range(-WIN, WIN + 1)]
     for distance in range(-WIN, WIN + 1):
-        if abs(distance) > 1:
+        if distance != 0:
             pieces[distance + WIN] = shifted(key_value, "seq", -distance)
-    pieces[WIN - 1], halo_low = shifted_pair(
-        key_value, atom_kv[atom_kv.shape[0] - AK // 2 :], "seq", 1
-    )
-    pieces[WIN + 1], halo_high = shifted_pair(key_value, atom_kv[: AK // 2], "seq", -1)
     window = jnp.stack(pieces)
     candidates = (2 * WIN + 1) * blocks_here
     window_flat = window.reshape(candidates, BLK * 2 * features)
@@ -280,7 +271,18 @@
         "bsc,bsx->cx", selector_mask.astype(jnp.float32), returned_flat, precision=HIGHEST
     )
     outgoing = outgoing.reshape(2 * WIN + 1, tok_rows, 2 * features)
-    extended = jnp.concatenate([halo_low, atom_kv, halo_high], axis=0)
+    collected = outgoing[WIN]
+    for distance in range(-WIN, WIN + 1):
+        if distance != 0:
+            collected = collected + shifted(
+                outgoing[distance + WIN].astype(jnp.bfloat16), "seq", distance
+            ).astype(jnp.float32)
+    token_grads = [
+        dquery.reshape(tok_rows, features).astype(jnp.bfloat16),
+        collected[:, :features].astype(jnp.bfloat16),
+        collected[:, features:].astype(jnp.bfloat16),
+        grad_gate,
+    ]
     ext_groups = extended.reshape(windows_here + AK // AQ, AQ, 2 * atom_feat)
     slabs = jnp.concatenate(
         [ext_groups[step : step + windows_here] for step in range(group_span)], axis=1
@@ -349,28 +351,7 @@
         )
     ext_grad = ext_grad.reshape(atom_rows + 2 * halo_rows, 2 * atom_feat)
     rims = jnp.concatenate([ext_grad[:halo_rows], ext_grad[atom_rows + halo_rows :]], axis=0)
-    collected = outgoing[WIN]
-    for distance in range(-WIN, WIN + 1):
-        if abs(distance) > 1:
-            collected = collected + shifted(
-                outgoing[distance + WIN].astype(jnp.bfloat16), "seq", distance
-            ).astype(jnp.float32)
-    came_low, edge_low = shifted_pair(
-        outgoing[WIN + 1].astype(jnp.bfloat16), rims[halo_rows:].astype(jnp.bfloat16), "seq", 1
-    )
-    came_high, edge_high = shifted_pair(
-        outgoing[WIN - 1].astype(jnp.bfloat16), rims[:halo_rows].astype(jnp.bfloat16), "seq", -1
-    )
-    collected = collected + came_low.astype(jnp.float32) + came_high.astype(jnp.float32)
-    edges = jnp.concatenate(
-        [edge_low, rims.astype(jnp.bfloat16), edge_high], axis=0
-    ).astype(rims.dtype)
-    token_grads = [
-        dquery.reshape(tok_rows, features).astype(jnp.bfloat16),
-        collected[:, :features].astype(jnp.bfloat16),
-        collected[:, features:].astype(jnp.bfloat16),
-        grad_gate,
-    ]
+    edges = extended_2(rims.astype(jnp.bfloat16), (("seq", 0),), halo_rows).astype(rims.dtype)
     own_grad = ext_grad[halo_rows : halo_rows + atom_rows]
     own_grad = jnp.concatenate(
         [

time: 198 us -> 150 us (0.76); the launches traced: 195 us -> 149 us
  local copies, waits for them, and re-layouts: 46.6 us -> 16.1 us
  matrix products: 46.3 us -> 29.4 us
  other arithmetic: 26.2 us -> 12.5 us
  starting transfers between devices: 61.1 us -> 73.3 us
  waiting for transfers between devices: 12.3 us -> 15.1 us
    ppermute x0 -> x4, starting transfers between devices: none -> 24.1 us  [the longest x2 17.4 us: extended_2(): lax.ppermute(lax.slice_in_dim(block, 0, width, axis=dim), axis, backward)]
    ppermute x8, starting transfers between devices: 47.9 us -> 34.8 us  [shifted(): return lax.ppermute(block, axis, route)]
    sub x1, other arithmetic: 5.4 us -> 1.01 us  [attend_local(): exponent = jnp.exp(scores - row_max)]
    dot_general x4, matrix products: 5.74 us -> 1.79 us  [body(): jnp.dot(token_grads[which], w_token[which].T, preferred_element_type=jnp....]
    another operation x6, local copies, waits for them, and re-layouts: 5.31 us -> 1.44 us  [body(): window = jnp.stack(pieces)]
    convert_element_type x2, local copies, waits for them, and re-layouts: 3.62 us -> 0.38 us  [body(): aquery_grad.reshape(atom_rows, atom_feat).astype(jnp.bfloat16)]
    reshape x2, local copies, waits for them, and re-layouts: 3.43 us -> 0.2 us  [body(): key_grad.reshape(blocks_here, S, BLK, features)]
    reshape x2, local copies, waits for them, and re-layouts: 3.42 us -> 0.2 us  [body(): dvalue.reshape(blocks_here, S, BLK, features)]
  transfers between devices with their start and end apart: 12 -> 16, of which waited for: 4 -> 5; matrix products, arithmetic and copies ran while one was open for 18% -> 12% of each run, Pallas kernels for 0% -> 0%
where the time goes in v8:
time: 150 us; the launch traced here: 149 us
  starting transfers between devices  73.3 us (49%)
  matrix products  29.4 us (20%)
  local copies, waits for them, and re-layouts  16.1 us (11%)
  waiting for transfers between devices  15.1 us (10%)
  other arithmetic  12.5 us (8%)
  between operations  2.65 us (2%)
    ppermute x8, starting transfers between devices, shifted(): return lax.ppermute(block, axis, route)  34.8 us
    ppermute x2, starting transfers between devices, extended_2(): lax.ppermute(lax.slice_in_dim(block, 0, width, axis=dim), axis, backward)  17.4 us
    ppermute x2, starting transfers between devices, extended_2(): lax.ppermute(lax.slice_in_dim(block, block.shape[dim] - width, None, axis...  6.74 us
    ppermute x1, starting transfers between devices, head_sum(): got = lax.ppermute(give.astype(jnp.bfloat16), axis, pair_near)  5.69 us
    ppermute x1, waiting for transfers between devices, head_sum(): got = lax.ppermute(give.astype(jnp.bfloat16), axis, pair_far)  5.35 us
    ppermute x1, waiting for transfers between devices, head_sum(): got = lax.ppermute(own, axis, pair_far)  4.43 us
    ppermute x1, starting transfers between devices, head_sum(): got = lax.ppermute(half, axis, pair_near)  4.03 us
  transfers between devices with their start and end apart: 16, of which 5 were waited for; matrix products, arithmetic and copies ran while one was open for 12% of the time, Pallas kernels for 0%

profile of v8, /device:TPU:1, one launch (start us, length us, event | category | flops | bytes accessed | tf_op | source)
XLA Modules:
  0.0 149.0 jit_solution(1292354703894161001)
XLA Ops:
  11.3 3.9 %collective-permute-start = (bf16[64,64]{0,1:T(8,128)(2,1)S(1)}, bf16[64,64]{0,1:T(8,128)(2,1)S(1)}, u32[]{:S(2)}, u32[]{:S(2)}) collective-permute-start(bf16[64,64]{0,1:T(8,128)(2,1)S(1)} %get-tuple-element.56), channel_id=1, source_target_pairs={{0,4},{4,8},{8,12},{12,16},{16,20},{20,24},{24,28},{28,32},{32,36}... | collective-permute-start | bytes 24584 | tf_op jit(solution)/shard_map/ppermute | solution.py:31
  15.3 14.8 %collective-permute-start.1 = (bf16[64,64]{0,1:T(8,128)(2,1)S(1)}, bf16[64,64]{0,1:T(8,128)(2,1)S(1)}, u32[]{:S(2)}, u32[]{:S(2)}) collective-permute-start(bf16[64,64]{0,1:T(8,128)(2,1)S(1)} %get-tuple-element.55), channel_id=1, source_target_pairs={{4,0},{8,4},{12,8},{16,12},{20,16},{24,20},{28,24},{32,28},{36,32}... | collective-permute-start | bytes 24584 | tf_op jit(solution)/shard_map/ppermute | solution.py:34
  38.5 2.3 %concatenate.56 = bf16[32,160,64]{1,2,0:T(8,128)(2,1)} concatenate(bf16[32,32,64]{1,2,0:T(8,128)(2,1)S(1)} %copy.91, bf16[32,32,64]{1,2,0:T(8,128)(2,1)S(1)} %copy.92, bf16[32,32,64]{1,2,0:T(8,128)(2,1)S(1)} %copy.93, bf16[32,32,64]{1,2,0:T(8,128)(2,1)S(1)} %copy.94, bf16[32,32,64]{1,2,0:T(8,128)(2,1)S(1)} %copy.95), dimensions={1} | concatenate | bytes 1310720 | tf_op jit(solution)/shard_map/concatenate | solution.py:287
  40.7 1.9 %fusion.11 = bf16[32,128,64]{1,2,0:T(8,128)(2,1)S(1)} fusion(bf16[32,160,64]{1,2,0:T(8,128)(2,1)} %concatenate.56, s32[32,128]{1,0:T(8,128)} %iota_add_fusion), kind=kOutput, calls=%fused_computation.15 | convolution fusion | flops 84803584 | bytes 1196032 | tf_op jit(solution)/shard_map/wrs,wsf->wrf/dot_general | solution.py:295
  43.9 1.8 %convolution_bitcast_fusion.1 = f32[32,32,1,32]{1,3,0,2:T(8,128)S(1)} fusion(bf16[32,128,64]{1,2,0:T(8,128)(2,1)S(1)} %fusion.11, f32[32,32]{1,0:T(8,128)S(1)} %get-tuple-element.60, f32[32,32,128]{2,1,0:T(8,128)S(1)} %fusion.17), kind=kOutput, calls=%fused_computation.23 | convolution fusion | flops 8782975 | bytes 1458176 | tf_op jit(solution)/shard_map/bhqk,bkhd->bqhd/dot_general | solution.py:114
  46.8 1.8 %convolution_bitcast_fusion = f32[32,128,32]{1,2,0:T(8,128)S(1)} fusion(bf16[32,32,32]{1,0,2:T(8,128)(2,1)S(1)} %reshape.430, f32[32,32]{1,0:T(8,128)S(1)} %get-tuple-element.60, f32[32,32,128]{2,1,0:T(8,128)S(1)} %fusion.17), kind=kOutput, calls=%fused_computation.22 | convolution fusion | flops 8782975 | bytes 1118208 | tf_op jit(solution)/shard_map/bhqk,bqhd->bkhd/dot_general | solution.py:136
  50.7 1.9 %collective-permute-start.2 = (bf16[128,192]{0,1:T(8,128)(2,1)}, bf16[128,192]{0,1:T(8,128)(2,1)S(1)}, u32[]{:S(2)}, u32[]{:S(2)}) collective-permute-start(bf16[128,192]{0,1:T(8,128)(2,1)} %pad_maximum_fusion.6), channel_id=1, source_target_pairs={{504,0},{508,4},{0,8},{4,12},{8,16},{12,20},{16,24},{20,28},{24,32... | collective-permute-start | bytes 147464 | tf_op jit(solution)/shard_map/ppermute | solution.py:22
  52.6 1.9 %collective-permute-start.3 = (bf16[128,192]{0,1:T(8,128)(2,1)}, bf16[128,192]{0,1:T(8,128)(2,1)S(1)}, u32[]{:S(2)}, u32[]{:S(2)}) collective-permute-start(bf16[128,192]{0,1:T(8,128)(2,1)} %pad_maximum_fusion.6), channel_id=1, source_target_pairs={{508,0},{0,4},{4,8},{8,12},{12,16},{16,20},{20,24},{24,28},{28,32}... | collective-permute-start | bytes 147464 | tf_op jit(solution)/shard_map/ppermute | solution.py:22
  54.5 9.3 %collective-permute-start.4 = (bf16[128,192]{0,1:T(8,128)(2,1)}, bf16[128,192]{0,1:T(8,128)(2,1)S(1)}, u32[]{:S(2)}, u32[]{:S(2)}) collective-permute-start(bf16[128,192]{0,1:T(8,128)(2,1)} %pad_maximum_fusion.6), channel_id=1, source_target_pairs={{4,0},{8,4},{12,8},{16,12},{20,16},{24,20},{28,24},{32,28},{36,32}... | collective-permute-start | bytes 147464 | tf_op jit(solution)/shard_map/ppermute | solution.py:22
  67.6 2.6 %collective-permute-start.7 = (bf16[64,64]{1,0:T(8,128)(2,1)S(1)}, bf16[64,64]{1,0:T(8,128)(2,1)S(1)}, u32[]{:S(2)}, u32[]{:S(2)}) collective-permute-start(bf16[64,64]{1,0:T(8,128)(2,1)S(1)} %bitcast.234), channel_id=1, source_target_pairs={{4,0},{8,4},{12,8},{16,12},{20,16},{24,20},{28,24},{32,28},{36,32}... | collective-permute-start | bytes 24584 | tf_op jit(solution)/shard_map/ppermute | solution.py:34
  70.2 2.8 %collective-permute-start.6 = (bf16[64,64]{1,0:T(8,128)(2,1)S(1)}, bf16[64,64]{1,0:T(8,128)(2,1)S(1)}, u32[]{:S(2)}, u32[]{:S(2)}) collective-permute-start(bf16[64,64]{1,0:T(8,128)(2,1)S(1)} %bitcast.232), channel_id=1, source_target_pairs={{0,4},{4,8},{8,12},{12,16},{16,20},{20,24},{24,28},{28,32},{32,36}... | collective-permute-start | bytes 24584 | tf_op jit(solution)/shard_map/ppermute | solution.py:31
  74.1 3.7 %collective-permute-start.5 = (bf16[128,192]{0,1:T(8,128)(2,1)}, bf16[128,192]{0,1:T(8,128)(2,1)S(1)}, u32[]{:S(2)}, u32[]{:S(2)}) collective-permute-start(bf16[128,192]{0,1:T(8,128)(2,1)} %pad_maximum_fusion.6), channel_id=1, source_target_pairs={{8,0},{12,4},{16,8},{20,12},{24,16},{28,20},{32,24},{36,28},{40,32... | collective-permute-start | bytes 147464 | tf_op jit(solution)/shard_map/ppermute | solution.py:22
  77.8 2.8 %collective-permute-done.6 = bf16[64,64]{1,0:T(8,128)(2,1)S(1)} collective-permute-done((bf16[64,64]{1,0:T(8,128)(2,1)S(1)}, bf16[64,64]{1,0:T(8,128)(2,1)S(1)}, u32[]{:S(2)}, u32[]{:S(2)}) %collective-permute-start.6) | collective-permute-done | bytes 8224 | tf_op jit(solution)/shard_map/ppermute | solution.py:31
  93.1 2.2 %fusion.139 = (bf16[5,24576]{1,0:T(8,128)(2,1)S(1)}, f32[5,24576]{1,0:T(8,128)}) fusion(f32[4,24576]{1,0:T(4,128)S(1)} %reshape.438, s32[4]{0:T(128)} %fusion.119), kind=kOutput, calls=%fused_computation.236 | convolution fusion | flops 6021140 | bytes 1130512 | tf_op jit(solution)/shard_map/bsc,bsx->cx/dot_general | solution.py:270
  96.5 1.9 %collective-permute-start.11 = (bf16[128,192]{1,0:T(8,128)(2,1)S(1)}, bf16[128,192]{1,0:T(8,128)(2,1)S(1)}, u32[]{:S(2)}, u32[]{:S(2)}) collective-permute-start(bf16[128,192]{1,0:T(8,128)(2,1)S(1)} %convert_element_type.226), channel_id=1, source_target_pairs={{504,0},{508,4},{0,8},{4,12},{8,16},{12,20},{16,24},{20,28},{24,32... | collective-permute-start | bytes 147464 | tf_op jit(solution)/shard_map/ppermute | solution.py:22
  98.5 4.3 %collective-permute-start.10 = (bf16[128,192]{1,0:T(8,128)(2,1)S(1)}, bf16[128,192]{1,0:T(8,128)(2,1)S(1)}, u32[]{:S(2)}, u32[]{:S(2)}) collective-permute-start(bf16[128,192]{1,0:T(8,128)(2,1)S(1)} %convert_element_type.224), channel_id=1, source_target_pairs={{508,0},{0,4},{4,8},{8,12},{12,16},{16,20},{20,24},{24,28},{28,32}... | collective-permute-start | bytes 147464 | tf_op jit(solution)/shard_map/ppermute | solution.py:22
  102.9 8.8 %collective-permute-start.9 = (bf16[128,192]{1,0:T(8,128)(2,1)S(1)}, bf16[128,192]{1,0:T(8,128)(2,1)S(1)}, u32[]{:S(2)}, u32[]{:S(2)}) collective-permute-start(bf16[128,192]{1,0:T(8,128)(2,1)S(1)} %convert_element_type.222), channel_id=1, source_target_pairs={{4,0},{8,4},{12,8},{16,12},{20,16},{24,20},{28,24},{32,28},{36,32}... | collective-permute-start | bytes 147464 | tf_op jit(solution)/shard_map/ppermute | solution.py:22
  111.8 3.1 %collective-permute-start.8 = (bf16[128,192]{1,0:T(8,128)(2,1)S(1)}, bf16[128,192]{1,0:T(8,128)(2,1)S(1)}, u32[]{:S(2)}, u32[]{:S(2)}) collective-permute-start(bf16[128,192]{1,0:T(8,128)(2,1)S(1)} %convert_element_type.220), channel_id=1, source_target_pairs={{8,0},{12,4},{16,8},{20,12},{24,16},{28,20},{32,24},{36,28},{40,32... | collective-permute-start | bytes 147464 | tf_op jit(solution)/shard_map/ppermute | solution.py:22
  119.7 5.7 %collective-permute-start.12 = (bf16[1408,128]{1,0:T(8,128)(2,1)S(1)}, bf16[1408,128]{1,0:T(8,128)(2,1)S(1)}, u32[]{:S(2)}, u32[]{:S(2)}) collective-permute-start(bf16[1408,128]{1,0:T(8,128)(2,1)S(1)} %select_convert_fusion), channel_id=1, source_target_pairs={{0,1},{1,0},{2,3},{3,2},{4,5},{5,4},{6,7},{7,6},{8,9},{9,8},{10,11... | collective-permute-start | bytes 1081352 | tf_op jit(solution)/shard_map/ppermute | solution.py:57
  126.8 2.3 %collective-permute-start.13 = (bf16[704,128]{1,0:T(8,128)(2,1)S(1)}, bf16[704,128]{1,0:T(8,128)(2,1)S(1)}, u32[]{:S(2)}, u32[]{:S(2)}) collective-permute-start(bf16[704,128]{1,0:T(8,128)(2,1)S(1)} %select_convert_fusion.1), channel_id=1, source_target_pairs={{0,2},{1,3},{2,0},{3,1},{4,6},{5,7},{6,4},{7,5},{8,10},{9,11},{10,... | collective-permute-start | bytes 540680 | tf_op jit(solution)/shard_map/ppermute | solution.py:61
  129.1 5.4 %collective-permute-done.13 = bf16[704,128]{1,0:T(8,128)(2,1)S(1)} collective-permute-done((bf16[704,128]{1,0:T(8,128)(2,1)S(1)}, bf16[704,128]{1,0:T(8,128)(2,1)S(1)}, u32[]{:S(2)}, u32[]{:S(2)}) %collective-permute-start.13) | collective-permute-done | bytes 180256 | tf_op jit(solution)/shard_map/ppermute | solution.py:61
  134.5 2.3 %collective-permute-start.14 = (bf16[704,128]{1,0:T(8,128)(2,1)S(1)}, bf16[704,128]{1,0:T(8,128)(2,1)S(1)}, u32[]{:S(2)}, u32[]{:S(2)}) collective-permute-start(bf16[704,128]{1,0:T(8,128)(2,1)S(1)} %add_convert_fusion), channel_id=1, source_target_pairs={{0,2},{1,3},{2,0},{3,1},{4,6},{5,7},{6,4},{7,5},{8,10},{9,11},{10,... | collective-permute-start | bytes 540680 | tf_op jit(solution)/shard_map/ppermute | solution.py:63
  136.8 4.4 %collective-permute-done.14 = bf16[704,128]{1,0:T(8,128)(2,1)S(1)} collective-permute-done((bf16[704,128]{1,0:T(8,128)(2,1)S(1)}, bf16[704,128]{1,0:T(8,128)(2,1)S(1)}, u32[]{:S(2)}, u32[]{:S(2)}) %collective-permute-start.14) | collective-permute-done | bytes 180256 | tf_op jit(solution)/shard_map/ppermute | solution.py:63
  141.4 4.0 %collective-permute-start.15 = (bf16[1408,128]{1,0:T(8,128)(2,1)S(1)}, bf16[1408,128]{1,0:T(8,128)(2,1)S(1)}, u32[]{:S(2)}, u32[]{:S(2)}) collective-permute-start(bf16[1408,128]{1,0:T(8,128)(2,1)S(1)} %maximum_select_fusion.1), channel_id=1, source_target_pairs={{0,1},{1,0},{2,3},{3,2},{4,5},{5,4},{6,7},{7,6},{8,9},{9,8},{10,11... | collective-permute-start | bytes 1081352 | tf_op jit(solution)/shard_map/ppermute | solution.py:67
  (206 shorter events, 50.5 us)
Async XLA Ops:
  0.6 45.7 %copy-start = (bf16[1024,128]{1,0:T(8,128)(2,1)S(1)}, bf16[1024,128]{1,0:T(8,128)(2,1)}, u32[]{:S(2)}) copy-start(bf16[1024,128]{1,0:T(8,128)(2,1)} %param.33) | copy-start | bytes 786436
  0.7 29.4 %copy-start.5 = (bf16[4,384,96]{1,2,0:T(8,128)(2,1)S(1)}, bf16[4,384,96]{1,2,0:T(8,128)(2,1)}, u32[]{:S(2)}) copy-start(bf16[4,384,96]{1,2,0:T(8,128)(2,1)} %param.21) | copy-start | bytes 884740
  1.8 30.6 %copy-start.27 = (s32[32]{0:T(128)S(1)}, s32[32]{0:T(128)}, u32[]{:S(2)}) copy-start(s32[32]{0:T(128)} %param.31) | copy-start | bytes 388
  1.8 32.5 %copy-start.28 = (s32[1,4]{1,0:T(1,128)S(1)}, s32[1,4]{1,0:T(1,128)}, u32[]{:S(2)}) copy-start(s32[1,4]{1,0:T(1,128)} %param.28) | copy-start | bytes 52
  11.3 24.5 %collective-permute-start = (bf16[64,64]{0,1:T(8,128)(2,1)S(1)}, bf16[64,64]{0,1:T(8,128)(2,1)S(1)}, u32[]{:S(2)}, u32[]{:S(2)}) collective-permute-start(bf16[64,64]{0,1:T(8,128)(2,1)S(1)} %get-tuple-element.56), channel_id=1, source_target_pairs={{0,4},{4,8},{8,12},{12,16},{16,20},{20,24},{24,28},{28,32},{32,36}... | collective-permute-start | bytes 24584 | tf_op jit(solution)/shard_map/ppermute | solution.py:31
  15.3 20.5 %collective-permute-start.1 = (bf16[64,64]{0,1:T(8,128)(2,1)S(1)}, bf16[64,64]{0,1:T(8,128)(2,1)S(1)}, u32[]{:S(2)}, u32[]{:S(2)}) collective-permute-start(bf16[64,64]{0,1:T(8,128)(2,1)S(1)} %get-tuple-element.55), channel_id=1, source_target_pairs={{4,0},{8,4},{12,8},{16,12},{20,16},{24,20},{28,24},{32,28},{36,32}... | collective-permute-start | bytes 24584 | tf_op jit(solution)/shard_map/ppermute | solution.py:34
  50.7 33.4 %collective-permute-start.2 = (bf16[128,192]{0,1:T(8,128)(2,1)}, bf16[128,192]{0,1:T(8,128)(2,1)S(1)}, u32[]{:S(2)}, u32[]{:S(2)}) collective-permute-start(bf16[128,192]{0,1:T(8,128)(2,1)} %pad_maximum_fusion.6), channel_id=1, source_target_pairs={{504,0},{508,4},{0,8},{4,12},{8,16},{12,20},{16,24},{20,28},{24,32... | collective-permute-start | bytes 147464 | tf_op jit(solution)/shard_map/ppermute | solution.py:22
  52.6 31.7 %collective-permute-start.3 = (bf16[128,192]{0,1:T(8,128)(2,1)}, bf16[128,192]{0,1:T(8,128)(2,1)S(1)}, u32[]{:S(2)}, u32[]{:S(2)}) collective-permute-start(bf16[128,192]{0,1:T(8,128)(2,1)} %pad_maximum_fusion.6), channel_id=1, source_target_pairs={{508,0},{0,4},{4,8},{8,12},{12,16},{16,20},{20,24},{24,28},{28,32}... | collective-permute-start | bytes 147464 | tf_op jit(solution)/shard_map/ppermute | solution.py:22
  54.5 30.1 %collective-permute-start.4 = (bf16[128,192]{0,1:T(8,128)(2,1)}, bf16[128,192]{0,1:T(8,128)(2,1)S(1)}, u32[]{:S(2)}, u32[]{:S(2)}) collective-permute-start(bf16[128,192]{0,1:T(8,128)(2,1)} %pad_maximum_fusion.6), channel_id=1, source_target_pairs={{4,0},{8,4},{12,8},{16,12},{20,16},{24,20},{28,24},{32,28},{36,32}... | collective-permute-start | bytes 147464 | tf_op jit(solution)/shard_map/ppermute | solution.py:22
  67.6 6.5 %collective-permute-start.7 = (bf16[64,64]{1,0:T(8,128)(2,1)S(1)}, bf16[64,64]{1,0:T(8,128)(2,1)S(1)}, u32[]{:S(2)}, u32[]{:S(2)}) collective-permute-start(bf16[64,64]{1,0:T(8,128)(2,1)S(1)} %bitcast.234), channel_id=1, source_target_pairs={{4,0},{8,4},{12,8},{16,12},{20,16},{24,20},{28,24},{32,28},{36,32}... | collective-permute-start | bytes 24584 | tf_op jit(solution)/shard_map/ppermute | solution.py:34
  70.2 10.4 %collective-permute-start.6 = (bf16[64,64]{1,0:T(8,128)(2,1)S(1)}, bf16[64,64]{1,0:T(8,128)(2,1)S(1)}, u32[]{:S(2)}, u32[]{:S(2)}) collective-permute-start(bf16[64,64]{1,0:T(8,128)(2,1)S(1)} %bitcast.232), channel_id=1, source_target_pairs={{0,4},{4,8},{8,12},{12,16},{16,20},{20,24},{24,28},{28,32},{32,36}... | collective-permute-start | bytes 24584 | tf_op jit(solution)/shard_map/ppermute | solution.py:31
  74.1 10.7 %collective-permute-start.5 = (bf16[128,192]{0,1:T(8,128)(2,1)}, bf16[128,192]{0,1:T(8,128)(2,1)S(1)}, u32[]{:S(2)}, u32[]{:S(2)}) collective-permute-start(bf16[128,192]{0,1:T(8,128)(2,1)} %pad_maximum_fusion.6), channel_id=1, source_target_pairs={{8,0},{12,4},{16,8},{20,12},{24,16},{28,20},{32,24},{36,28},{40,32... | collective-permute-start | bytes 147464 | tf_op jit(solution)/shard_map/ppermute | solution.py:22
  93.0 25.6 %copy-start.6 = (bf16[4,384,96]{1,2,0:T(8,128)(2,1)S(1)}, bf16[4,384,96]{1,2,0:T(8,128)(2,1)}, u32[]{:S(2)}) copy-start(bf16[4,384,96]{1,2,0:T(8,128)(2,1)} %param.21) | copy-start | bytes 884740
  93.1 26.0 %copy-start.2 = (bf16[128,384]{1,0:T(8,128)(2,1)S(1)}, bf16[128,384]{1,0:T(8,128)(2,1)}, u32[]{:S(2)}) copy-start(bf16[128,384]{1,0:T(8,128)(2,1)} %param.17) | copy-start | bytes 294916
  93.1 26.0 %copy-start.20 = (f32[384]{0:T(512)S(1)}, f32[384]{0:T(512)}, u32[]{:S(2)}) copy-start(f32[384]{0:T(512)} %param.19) | copy-start | bytes 4612
  93.1 26.0 %copy-start.22 = (f32[128]{0:T(128)S(1)}, f32[128]{0:T(128)}, u32[]{:S(2)}) copy-start(f32[128]{0:T(128)} %copy-done.21) | copy-start | bytes 1540
  96.5 22.1 %collective-permute-start.11 = (bf16[128,192]{1,0:T(8,128)(2,1)S(1)}, bf16[128,192]{1,0:T(8,128)(2,1)S(1)}, u32[]{:S(2)}, u32[]{:S(2)}) collective-permute-start(bf16[128,192]{1,0:T(8,128)(2,1)S(1)} %convert_element_type.226), channel_id=1, source_target_pairs={{504,0},{508,4},{0,8},{4,12},{8,16},{12,20},{16,24},{20,28},{24,32... | collective-permute-start | bytes 147464 | tf_op jit(solution)/shard_map/ppermute | solution.py:22
  98.5 20.1 %collective-permute-start.10 = (bf16[128,192]{1,0:T(8,128)(2,1)S(1)}, bf16[128,192]{1,0:T(8,128)(2,1)S(1)}, u32[]{:S(2)}, u32[]{:S(2)}) collective-permute-start(bf16[128,192]{1,0:T(8,128)(2,1)S(1)} %convert_element_type.224), channel_id=1, source_target_pairs={{508,0},{0,4},{4,8},{8,12},{12,16},{16,20},{20,24},{24,28},{28,32}... | collective-permute-start | bytes 147464 | tf_op jit(solution)/shard_map/ppermute | solution.py:22
  102.9 15.7 %collective-permute-start.9 = (bf16[128,192]{1,0:T(8,128)(2,1)S(1)}, bf16[128,192]{1,0:T(8,128)(2,1)S(1)}, u32[]{:S(2)}, u32[]{:S(2)}) collective-permute-start(bf16[128,192]{1,0:T(8,128)(2,1)S(1)} %convert_element_type.222), channel_id=1, source_target_pairs={{4,0},{8,4},{12,8},{16,12},{20,16},{24,20},{28,24},{32,28},{36,32}... | collective-permute-start | bytes 147464 | tf_op jit(solution)/shard_map/ppermute | solution.py:22
  111.8 6.8 %collective-permute-start.8 = (bf16[128,192]{1,0:T(8,128)(2,1)S(1)}, bf16[128,192]{1,0:T(8,128)(2,1)S(1)}, u32[]{:S(2)}, u32[]{:S(2)}) collective-permute-start(bf16[128,192]{1,0:T(8,128)(2,1)S(1)} %convert_element_type.220), channel_id=1, source_target_pairs={{8,0},{12,4},{16,8},{20,12},{24,16},{28,20},{32,24},{36,28},{40,32... | collective-permute-start | bytes 147464 | tf_op jit(solution)/shard_map/ppermute | solution.py:22
  119.7 7.0 %collective-permute-start.12 = (bf16[1408,128]{1,0:T(8,128)(2,1)S(1)}, bf16[1408,128]{1,0:T(8,128)(2,1)S(1)}, u32[]{:S(2)}, u32[]{:S(2)}) collective-permute-start(bf16[1408,128]{1,0:T(8,128)(2,1)S(1)} %select_convert_fusion), channel_id=1, source_target_pairs={{0,1},{1,0},{2,3},{3,2},{4,5},{5,4},{6,7},{7,6},{8,9},{9,8},{10,11... | collective-permute-start | bytes 1081352 | tf_op jit(solution)/shard_map/ppermute | solution.py:57
  126.8 7.7 %collective-permute-start.13 = (bf16[704,128]{1,0:T(8,128)(2,1)S(1)}, bf16[704,128]{1,0:T(8,128)(2,1)S(1)}, u32[]{:S(2)}, u32[]{:S(2)}) collective-permute-start(bf16[704,128]{1,0:T(8,128)(2,1)S(1)} %select_convert_fusion.1), channel_id=1, source_target_pairs={{0,2},{1,3},{2,0},{3,1},{4,6},{5,7},{6,4},{7,5},{8,10},{9,11},{10,... | collective-permute-start | bytes 540680 | tf_op jit(solution)/shard_map/ppermute | solution.py:61
  134.5 6.7 %collective-permute-start.14 = (bf16[704,128]{1,0:T(8,128)(2,1)S(1)}, bf16[704,128]{1,0:T(8,128)(2,1)S(1)}, u32[]{:S(2)}, u32[]{:S(2)}) collective-permute-start(bf16[704,128]{1,0:T(8,128)(2,1)S(1)} %add_convert_fusion), channel_id=1, source_target_pairs={{0,2},{1,3},{2,0},{3,1},{4,6},{5,7},{6,4},{7,5},{8,10},{9,11},{10,... | collective-permute-start | bytes 540680 | tf_op jit(solution)/shard_map/ppermute | solution.py:63
  141.4 5.3 %collective-permute-start.15 = (bf16[1408,128]{1,0:T(8,128)(2,1)S(1)}, bf16[1408,128]{1,0:T(8,128)(2,1)S(1)}, u32[]{:S(2)}, u32[]{:S(2)}) collective-permute-start(bf16[1408,128]{1,0:T(8,128)(2,1)S(1)} %maximum_select_fusion.1), channel_id=1, source_target_pairs={{0,1},{1,0},{2,3},{3,2},{4,5},{5,4},{6,7},{7,6},{8,9},{9,8},{10,11... | collective-permute-start | bytes 1081352 | tf_op jit(solution)/shard_map/ppermute | solution.py:67
  (22 other events, 207.7 us)

commit v9 on v8

--- a/solution.py
+++ b/solution.py
@@ -271,18 +271,6 @@
         "bsc,bsx->cx", selector_mask.astype(jnp.float32), returned_flat, precision=HIGHEST
     )
     outgoing = outgoing.reshape(2 * WIN + 1, tok_rows, 2 * features)
-    collected = outgoing[WIN]
-    for distance in range(-WIN, WIN + 1):
-        if distance != 0:
-            collected = collected + shifted(
-                outgoing[distance + WIN].astype(jnp.bfloat16), "seq", distance
-            ).astype(jnp.float32)
-    token_grads = [
-        dquery.reshape(tok_rows, features).astype(jnp.bfloat16),
-        collected[:, :features].astype(jnp.bfloat16),
-        collected[:, features:].astype(jnp.bfloat16),
-        grad_gate,
-    ]
     ext_groups = extended.reshape(windows_here + AK // AQ, AQ, 2 * atom_feat)
     slabs = jnp.concatenate(
         [ext_groups[step : step + windows_here] for step in range(group_span)], axis=1
@@ -351,7 +339,20 @@
         )
     ext_grad = ext_grad.reshape(atom_rows + 2 * halo_rows, 2 * atom_feat)
     rims = jnp.concatenate([ext_grad[:halo_rows], ext_grad[atom_rows + halo_rows :]], axis=0)
+    outgoing, rims = lax.optimization_barrier((outgoing, rims))
     edges = extended_2(rims.astype(jnp.bfloat16), (("seq", 0),), halo_rows).astype(rims.dtype)
+    collected = outgoing[WIN]
+    for distance in range(-WIN, WIN + 1):
+        if distance != 0:
+            collected = collected + shifted(
+                outgoing[distance + WIN].astype(jnp.bfloat16), "seq", distance
+            ).astype(jnp.float32)
+    token_grads = [
+        dquery.reshape(tok_rows, features).astype(jnp.bfloat16),
+        collected[:, :features].astype(jnp.bfloat16),
+        collected[:, features:].astype(jnp.bfloat16),
+        grad_gate,
+    ]
     own_grad = ext_grad[halo_rows : halo_rows + atom_rows]
     own_grad = jnp.concatenate(
         [

time: 150 us -> 160 us (1.067)
  other arithmetic: 12.5 us -> 18.2 us
  starting transfers between devices: 73.3 us -> 76.3 us
  waiting for transfers between devices: 15.1 us -> 12.3 us
  local copies, waits for them, and re-layouts: 16.1 us -> 18.9 us
    ppermute x2, starting transfers between devices: 17.4 us -> 23 us  [extended_2(): lax.ppermute(lax.slice_in_dim(block, 0, width, axis=dim), axis, backward)]
    sub x1, other arithmetic: 1.01 us -> 5.4 us  [attend_local(): exponent = jnp.exp(scores - row_max)]
    ppermute x4, local copies, waits for them, and re-layouts: 0.42 us -> 3.59 us  [shifted(): return lax.ppermute(block, axis, route)]
    ppermute x8, starting transfers between devices: 34.8 us -> 32 us  [shifted(): return lax.ppermute(block, axis, route)]
    ppermute x2, waiting for transfers between devices: 2.8 us -> 0.01 us  [extended_2(): lax.ppermute(lax.slice_in_dim(block, block.shape[dim] - width, None, axis...]
  transfers between devices with their start and end apart: 16 -> 16, of which waited for: 5 -> 4; matrix products, arithmetic and copies ran while one was open for 12% -> 25% of each run, Pallas kernels for 0% -> 0%
where the time goes in v9:
time: 160 us; the launch traced here: 159 us
  starting transfers between devices  76.3 us (48%)
  matrix products  30.2 us (19%)
  local copies, waits for them, and re-layouts  18.9 us (12%)
  other arithmetic  18.2 us (11%)
  waiting for transfers between devices  12.3 us (8%)
  between operations  2.85 us (2%)
    ppermute x8, starting transfers between devices, shifted(): return lax.ppermute(block, axis, route)  32 us
    ppermute x2, starting transfers between devices, extended_2(): lax.ppermute(lax.slice_in_dim(block, 0, width, axis=dim), axis, backward)  23 us
    ppermute x2, starting transfers between devices, extended_2(): lax.ppermute(lax.slice_in_dim(block, block.shape[dim] - width, None, axis...  6.74 us
    ppermute x1, starting transfers between devices, head_sum(): got = lax.ppermute(give.astype(jnp.bfloat16), axis, pair_near)  5.89 us
    sub x1, other arithmetic, attend_local(): exponent = jnp.exp(scores - row_max)  5.4 us
    ppermute x1, waiting for transfers between devices, head_sum(): got = lax.ppermute(give.astype(jnp.bfloat16), axis, pair_far)  5.35 us
    ppermute x1, waiting for transfers between devices, head_sum(): got = lax.ppermute(own, axis, pair_far)  4.42 us
    ppermute x1, starting transfers between devices, head_sum(): got = lax.ppermute(half, axis, pair_near)  4.03 us
  transfers between devices with their start and end apart: 16, of which 4 were waited for; matrix products, arithmetic and copies ran while one was open for 25% of the time, Pallas kernels for 0%

profile of v9, /device:TPU:1, one launch (start us, length us, event | category | flops | bytes accessed | tf_op | source)
XLA Modules:
  0.0 158.8 jit_solution(14755386774583596668)
XLA Ops:
  11.3 3.9 %collective-permute-start = (bf16[64,64]{0,1:T(8,128)(2,1)S(1)}, bf16[64,64]{0,1:T(8,128)(2,1)S(1)}, u32[]{:S(2)}, u32[]{:S(2)}) collective-permute-start(bf16[64,64]{0,1:T(8,128)(2,1)S(1)} %get-tuple-element.58), channel_id=1, source_target_pairs={{0,4},{4,8},{8,12},{12,16},{16,20},{20,24},{24,28},{28,32},{32,36}... | collective-permute-start | bytes 24584 | tf_op jit(solution)/shard_map/ppermute | solution.py:31
  15.2 14.7 %collective-permute-start.1 = (bf16[64,64]{0,1:T(8,128)(2,1)S(1)}, bf16[64,64]{0,1:T(8,128)(2,1)S(1)}, u32[]{:S(2)}, u32[]{:S(2)}) collective-permute-start(bf16[64,64]{0,1:T(8,128)(2,1)S(1)} %get-tuple-element.57), channel_id=1, source_target_pairs={{4,0},{8,4},{12,8},{16,12},{20,16},{24,20},{28,24},{32,28},{36,32}... | collective-permute-start | bytes 24584 | tf_op jit(solution)/shard_map/ppermute | solution.py:34
  36.0 1.9 %collective-permute-start.2 = (bf16[128,192]{0,1:T(8,128)(2,1)}, bf16[128,192]{0,1:T(8,128)(2,1)}, u32[]{:S(2)}, u32[]{:S(2)}) collective-permute-start(bf16[128,192]{0,1:T(8,128)(2,1)} %pad_maximum_fusion.7), channel_id=1, source_target_pairs={{504,0},{508,4},{0,8},{4,12},{8,16},{12,20},{16,24},{20,28},{24,32... | collective-permute-start | bytes 147464 | tf_op jit(solution)/shard_map/ppermute | solution.py:22
  37.9 1.9 %collective-permute-start.3 = (bf16[128,192]{0,1:T(8,128)(2,1)}, bf16[128,192]{0,1:T(8,128)(2,1)}, u32[]{:S(2)}, u32[]{:S(2)}) collective-permute-start(bf16[128,192]{0,1:T(8,128)(2,1)} %pad_maximum_fusion.7), channel_id=1, source_target_pairs={{508,0},{0,4},{4,8},{8,12},{12,16},{16,20},{20,24},{24,28},{28,32}... | collective-permute-start | bytes 147464 | tf_op jit(solution)/shard_map/ppermute | solution.py:22
  39.9 9.1 %collective-permute-start.4 = (bf16[128,192]{0,1:T(8,128)(2,1)}, bf16[128,192]{0,1:T(8,128)(2,1)}, u32[]{:S(2)}, u32[]{:S(2)}) collective-permute-start(bf16[128,192]{0,1:T(8,128)(2,1)} %pad_maximum_fusion.7), channel_id=1, source_target_pairs={{4,0},{8,4},{12,8},{16,12},{20,16},{24,20},{28,24},{32,28},{36,32}... | collective-permute-start | bytes 147464 | tf_op jit(solution)/shard_map/ppermute | solution.py:22
  49.0 3.8 %collective-permute-start.5 = (bf16[128,192]{0,1:T(8,128)(2,1)}, bf16[128,192]{0,1:T(8,128)(2,1)}, u32[]{:S(2)}, u32[]{:S(2)}) collective-permute-start(bf16[128,192]{0,1:T(8,128)(2,1)} %pad_maximum_fusion.7), channel_id=1, source_target_pairs={{8,0},{12,4},{16,8},{20,12},{24,16},{28,20},{32,24},{36,28},{40,32... | collective-permute-start | bytes 147464 | tf_op jit(solution)/shard_map/ppermute | solution.py:22
  55.3 2.2 %concatenate.56 = bf16[32,160,64]{1,2,0:T(8,128)(2,1)} concatenate(bf16[32,32,64]{1,2,0:T(8,128)(2,1)S(1)} %copy.210, bf16[32,32,64]{1,2,0:T(8,128)(2,1)S(1)} %copy.211, bf16[32,32,64]{1,2,0:T(8,128)(2,1)S(1)} %copy.212, bf16[32,32,64]{1,2,0:T(8,128)(2,1)S(1)} %copy.213, bf16[32,32,64]{1,2,0:T(8,128)(2,1)S(1)} %copy.214), dimensions={1} | concatenate | bytes 1310720 | tf_op jit(solution)/shard_map/concatenate | solution.py:275
  57.6 1.9 %fusion.11 = bf16[32,128,64]{1,2,0:T(8,128)(2,1)S(1)} fusion(bf16[32,160,64]{1,2,0:T(8,128)(2,1)} %concatenate.56, s32[32,128]{1,0:T(8,128)} %iota_add_fusion), kind=kOutput, calls=%fused_computation.15 | convolution fusion | flops 84803584 | bytes 1196032 | tf_op jit(solution)/shard_map/wrs,wsf->wrf/dot_general | solution.py:283
  59.7 5.4 %fusion.136 = (f32[32,32]{1,0:T(8,128)S(1)}, f32[32,32,128]{2,1,0:T(8,128)S(1)}) fusion(f32[32,32,128]{2,1,0:T(8,128)S(1)} %fusion.17), kind=kOutput, calls=%fused_computation.236 | output fusion | flops 262271 | bytes 1052672 | tf_op jit(solution)/shard_map/sub | solution.py:111
  65.2 2.6 %convolution_bitcast_fusion.1 = f32[32,32,1,32]{1,3,0,2:T(8,128)} fusion(bf16[32,128,64]{1,2,0:T(8,128)(2,1)S(1)} %fusion.11, f32[32,32]{1,0:T(8,128)S(1)} %get-tuple-element.64, f32[32,32,128]{2,1,0:T(8,128)S(1)} %fusion.17), kind=kOutput, calls=%fused_computation.23 | convolution fusion | flops 8782975 | bytes 1458176 | tf_op jit(solution)/shard_map/bhqk,bkhd->bqhd/dot_general | solution.py:114
  69.8 1.8 %convolution_bitcast_fusion = f32[32,128,32]{1,2,0:T(8,128)S(1)} fusion(bf16[32,32,32]{1,0,2:T(8,128)(2,1)S(1)} %reshape.419, f32[32,32]{1,0:T(8,128)S(1)} %get-tuple-element.64, f32[32,32,128]{2,1,0:T(8,128)S(1)} %fusion.17), kind=kOutput, calls=%fused_computation.22 | convolution fusion | flops 8782975 | bytes 1118208 | tf_op jit(solution)/shard_map/bhqk,bqhd->bkhd/dot_general | solution.py:136
  92.8 1.8 %fusion.30 = bf16[4,24,128]{2,1,0:T(8,128)(2,1)} fusion(bf16[512,4,24]{0,2,1:T(8,128)(2,1)} %copy-done.8, bf16[4,128,512]{2,1,0:T(8,128)(2,1)S(1)} %fusion.12), kind=kOutput, calls=%fused_computation.56 | convolution fusion | flops 12607488 | bytes 647168 | tf_op jit(solution)/shard_map/bhqk,bkhd->bqhd/dot_general | solution.py:129
  97.2 2.1 %collective-permute-start.10 = (bf16[128,192]{0,1:T(8,128)(2,1)S(1)}, bf16[128,192]{0,1:T(8,128)(2,1)S(1)}, u32[]{:S(2)}, u32[]{:S(2)}) collective-permute-start(bf16[128,192]{0,1:T(8,128)(2,1)S(1)} %bitcast.252), channel_id=1, source_target_pairs={{508,0},{0,4},{4,8},{8,12},{12,16},{16,20},{20,24},{24,28},{28,32}... | collective-permute-start | bytes 147464 | tf_op jit(solution)/shard_map/ppermute | solution.py:22
  99.2 3.1 %collective-permute-start.11 = (bf16[128,192]{0,1:T(8,128)(2,1)S(1)}, bf16[128,192]{0,1:T(8,128)(2,1)S(1)}, u32[]{:S(2)}, u32[]{:S(2)}) collective-permute-start(bf16[128,192]{0,1:T(8,128)(2,1)S(1)} %bitcast.253), channel_id=1, source_target_pairs={{504,0},{508,4},{0,8},{4,12},{8,16},{12,20},{16,24},{20,28},{24,32... | collective-permute-start | bytes 147464 | tf_op jit(solution)/shard_map/ppermute | solution.py:22
  102.4 8.2 %collective-permute-start.8 = (bf16[128,192]{0,1:T(8,128)(2,1)S(1)}, bf16[128,192]{0,1:T(8,128)(2,1)S(1)}, u32[]{:S(2)}, u32[]{:S(2)}) collective-permute-start(bf16[128,192]{0,1:T(8,128)(2,1)S(1)} %bitcast.254), channel_id=1, source_target_pairs={{8,0},{12,4},{16,8},{20,12},{24,16},{28,20},{32,24},{36,28},{40,32... | collective-permute-start | bytes 147464 | tf_op jit(solution)/shard_map/ppermute | solution.py:22
  111.6 2.8 %collective-permute-start.6 = (bf16[64,64]{1,0:T(8,128)(2,1)S(1)}, bf16[64,64]{1,0:T(8,128)(2,1)S(1)}, u32[]{:S(2)}, u32[]{:S(2)}) collective-permute-start(bf16[64,64]{1,0:T(8,128)(2,1)S(1)} %get-tuple-element.62), channel_id=1, source_target_pairs={{0,4},{4,8},{8,12},{12,16},{16,20},{20,24},{24,28},{28,32},{32,36}... | collective-permute-start | bytes 24584 | tf_op jit(solution)/shard_map/ppermute | solution.py:31
  114.4 8.2 %collective-permute-start.7 = (bf16[64,64]{1,0:T(8,128)(2,1)S(1)}, bf16[64,64]{1,0:T(8,128)(2,1)S(1)}, u32[]{:S(2)}, u32[]{:S(2)}) collective-permute-start(bf16[64,64]{1,0:T(8,128)(2,1)S(1)} %get-tuple-element.63), channel_id=1, source_target_pairs={{4,0},{8,4},{12,8},{16,12},{20,16},{24,20},{28,24},{32,28},{36,32}... | collective-permute-start | bytes 24584 | tf_op jit(solution)/shard_map/ppermute | solution.py:34
  123.0 1.9 %collective-permute-start.9 = (bf16[128,192]{0,1:T(8,128)(2,1)S(1)}, bf16[128,192]{0,1:T(8,128)(2,1)S(1)}, u32[]{:S(2)}, u32[]{:S(2)}) collective-permute-start(bf16[128,192]{0,1:T(8,128)(2,1)S(1)} %bitcast.255), channel_id=1, source_target_pairs={{4,0},{8,4},{12,8},{16,12},{20,16},{24,20},{28,24},{32,28},{36,32}... | collective-permute-start | bytes 147464 | tf_op jit(solution)/shard_map/ppermute | solution.py:22
  129.3 5.9 %collective-permute-start.12 = (bf16[1408,128]{1,0:T(8,128)(2,1)S(1)}, bf16[1408,128]{1,0:T(8,128)(2,1)S(1)}, u32[]{:S(2)}, u32[]{:S(2)}) collective-permute-start(bf16[1408,128]{1,0:T(8,128)(2,1)S(1)} %select_convert_fusion), channel_id=1, source_target_pairs={{0,1},{1,0},{2,3},{3,2},{4,5},{5,4},{6,7},{7,6},{8,9},{9,8},{10,11... | collective-permute-start | bytes 1081352 | tf_op jit(solution)/shard_map/ppermute | solution.py:57
  136.6 2.3 %collective-permute-start.13 = (bf16[704,128]{1,0:T(8,128)(2,1)S(1)}, bf16[704,128]{1,0:T(8,128)(2,1)S(1)}, u32[]{:S(2)}, u32[]{:S(2)}) collective-permute-start(bf16[704,128]{1,0:T(8,128)(2,1)S(1)} %select_convert_fusion.1), channel_id=1, source_target_pairs={{0,2},{1,3},{2,0},{3,1},{4,6},{5,7},{6,4},{7,5},{8,10},{9,11},{10,... | collective-permute-start | bytes 540680 | tf_op jit(solution)/shard_map/ppermute | solution.py:61
  138.9 5.3 %collective-permute-done.13 = bf16[704,128]{1,0:T(8,128)(2,1)S(1)} collective-permute-done((bf16[704,128]{1,0:T(8,128)(2,1)S(1)}, bf16[704,128]{1,0:T(8,128)(2,1)S(1)}, u32[]{:S(2)}, u32[]{:S(2)}) %collective-permute-start.13) | collective-permute-done | bytes 180256 | tf_op jit(solution)/shard_map/ppermute | solution.py:61
  144.3 2.3 %collective-permute-start.14 = (bf16[704,128]{1,0:T(8,128)(2,1)S(1)}, bf16[704,128]{1,0:T(8,128)(2,1)S(1)}, u32[]{:S(2)}, u32[]{:S(2)}) collective-permute-start(bf16[704,128]{1,0:T(8,128)(2,1)S(1)} %add_convert_fusion), channel_id=1, source_target_pairs={{0,2},{1,3},{2,0},{3,1},{4,6},{5,7},{6,4},{7,5},{8,10},{9,11},{10,... | collective-permute-start | bytes 540680 | tf_op jit(solution)/shard_map/ppermute | solution.py:63
  146.6 4.4 %collective-permute-done.14 = bf16[704,128]{1,0:T(8,128)(2,1)S(1)} collective-permute-done((bf16[704,128]{1,0:T(8,128)(2,1)S(1)}, bf16[704,128]{1,0:T(8,128)(2,1)S(1)}, u32[]{:S(2)}, u32[]{:S(2)}) %collective-permute-start.14) | collective-permute-done | bytes 180256 | tf_op jit(solution)/shard_map/ppermute | solution.py:63
  151.1 4.0 %collective-permute-start.15 = (bf16[1408,128]{1,0:T(8,128)(2,1)S(1)}, bf16[1408,128]{1,0:T(8,128)(2,1)S(1)}, u32[]{:S(2)}, u32[]{:S(2)}) collective-permute-start(bf16[1408,128]{1,0:T(8,128)(2,1)S(1)} %maximum_select_fusion.1), channel_id=1, source_target_pairs={{0,1},{1,0},{2,3},{3,2},{4,5},{5,4},{6,7},{7,6},{8,9},{9,8},{10,11... | collective-permute-start | bytes 1081352 | tf_op jit(solution)/shard_map/ppermute | solution.py:67
  (229 shorter events, 54.2 us)
Async XLA Ops:
  0.6 68.8 %copy-start = (bf16[1024,128]{1,0:T(8,128)(2,1)S(1)}, bf16[1024,128]{1,0:T(8,128)(2,1)}, u32[]{:S(2)}) copy-start(bf16[1024,128]{1,0:T(8,128)(2,1)} %param.33) | copy-start | bytes 786436
  0.7 29.4 %copy-start.6 = (bf16[4,384,96]{1,2,0:T(8,128)(2,1)S(1)}, bf16[4,384,96]{1,2,0:T(8,128)(2,1)}, u32[]{:S(2)}) copy-start(bf16[4,384,96]{1,2,0:T(8,128)(2,1)} %param.21) | copy-start | bytes 884740
  2.8 29.6 %copy-start.36 = (s32[32]{0:T(128)S(1)}, s32[32]{0:T(128)}, u32[]{:S(2)}) copy-start(s32[32]{0:T(128)} %param.31) | copy-start | bytes 388
  2.9 31.6 %copy-start.37 = (s32[1,4]{1,0:T(1,128)S(1)}, s32[1,4]{1,0:T(1,128)}, u32[]{:S(2)}) copy-start(s32[1,4]{1,0:T(1,128)} %param.28) | copy-start | bytes 52
  11.3 24.5 %collective-permute-start = (bf16[64,64]{0,1:T(8,128)(2,1)S(1)}, bf16[64,64]{0,1:T(8,128)(2,1)S(1)}, u32[]{:S(2)}, u32[]{:S(2)}) collective-permute-start(bf16[64,64]{0,1:T(8,128)(2,1)S(1)} %get-tuple-element.58), channel_id=1, source_target_pairs={{0,4},{4,8},{8,12},{12,16},{16,20},{20,24},{24,28},{28,32},{32,36}... | collective-permute-start | bytes 24584 | tf_op jit(solution)/shard_map/ppermute | solution.py:31
  15.2 20.6 %collective-permute-start.1 = (bf16[64,64]{0,1:T(8,128)(2,1)S(1)}, bf16[64,64]{0,1:T(8,128)(2,1)S(1)}, u32[]{:S(2)}, u32[]{:S(2)}) collective-permute-start(bf16[64,64]{0,1:T(8,128)(2,1)S(1)} %get-tuple-element.57), channel_id=1, source_target_pairs={{4,0},{8,4},{12,8},{16,12},{20,16},{24,20},{28,24},{32,28},{36,32}... | collective-permute-start | bytes 24584 | tf_op jit(solution)/shard_map/ppermute | solution.py:34
  36.0 43.8 %collective-permute-start.2 = (bf16[128,192]{0,1:T(8,128)(2,1)}, bf16[128,192]{0,1:T(8,128)(2,1)}, u32[]{:S(2)}, u32[]{:S(2)}) collective-permute-start(bf16[128,192]{0,1:T(8,128)(2,1)} %pad_maximum_fusion.7), channel_id=1, source_target_pairs={{504,0},{508,4},{0,8},{4,12},{8,16},{12,20},{16,24},{20,28},{24,32... | collective-permute-start | bytes 147464 | tf_op jit(solution)/shard_map/ppermute | solution.py:22
  37.9 42.9 %collective-permute-start.3 = (bf16[128,192]{0,1:T(8,128)(2,1)}, bf16[128,192]{0,1:T(8,128)(2,1)}, u32[]{:S(2)}, u32[]{:S(2)}) collective-permute-start(bf16[128,192]{0,1:T(8,128)(2,1)} %pad_maximum_fusion.7), channel_id=1, source_target_pairs={{508,0},{0,4},{4,8},{8,12},{12,16},{16,20},{20,24},{24,28},{28,32}... | collective-permute-start | bytes 147464 | tf_op jit(solution)/shard_map/ppermute | solution.py:22
  39.9 42.0 %collective-permute-start.4 = (bf16[128,192]{0,1:T(8,128)(2,1)}, bf16[128,192]{0,1:T(8,128)(2,1)}, u32[]{:S(2)}, u32[]{:S(2)}) collective-permute-start(bf16[128,192]{0,1:T(8,128)(2,1)} %pad_maximum_fusion.7), channel_id=1, source_target_pairs={{4,0},{8,4},{12,8},{16,12},{20,16},{24,20},{28,24},{32,28},{36,32}... | collective-permute-start | bytes 147464 | tf_op jit(solution)/shard_map/ppermute | solution.py:22
  49.0 34.0 %collective-permute-start.5 = (bf16[128,192]{0,1:T(8,128)(2,1)}, bf16[128,192]{0,1:T(8,128)(2,1)}, u32[]{:S(2)}, u32[]{:S(2)}) collective-permute-start(bf16[128,192]{0,1:T(8,128)(2,1)} %pad_maximum_fusion.7), channel_id=1, source_target_pairs={{8,0},{12,4},{16,8},{20,12},{24,16},{28,20},{32,24},{36,28},{40,32... | collective-permute-start | bytes 147464 | tf_op jit(solution)/shard_map/ppermute | solution.py:22
  96.1 28.8 %copy-start.16 = (f32[2,32,64]{2,1,0:T(8,128)S(1)}, f32[2,32,64]{2,1,0:T(8,128)}, u32[]{:S(2)}) copy-start(f32[2,32,64]{2,1,0:T(8,128)} %get-tuple-element.22) | copy-start | bytes 49156
  96.1 28.8 %copy-start.17 = (f32[2,32,64]{2,1,0:T(8,128)S(1)}, f32[2,32,64]{2,1,0:T(8,128)}, u32[]{:S(2)}) copy-start(f32[2,32,64]{2,1,0:T(8,128)} %get-tuple-element.23) | copy-start | bytes 49156
  96.1 28.9 %slice-start = ((bf16[36,32,64]{2,1,0:T(8,128)(2,1)}), bf16[28,32,64]{2,1,0:T(8,128)(2,1)S(1)}, s32[]{:S(2)}) async-start(bf16[36,32,64]{2,1,0:T(8,128)(2,1)} %copy-done.5), calls=%async_computation | async-start | bytes 458752 | tf_op jit(solution)/shard_map/slice | solution.py:360
  96.1 28.9 %copy-start.19 = (bf16[4,128,32]{1,2,0:T(8,128)(2,1)S(1)}, bf16[4,128,32]{1,2,0:T(8,128)(2,1)}, u32[]{:S(2)}) copy-start(bf16[4,128,32]{1,2,0:T(8,128)(2,1)} %param.24) | copy-start | bytes 98308
  97.2 31.0 %collective-permute-start.10 = (bf16[128,192]{0,1:T(8,128)(2,1)S(1)}, bf16[128,192]{0,1:T(8,128)(2,1)S(1)}, u32[]{:S(2)}, u32[]{:S(2)}) collective-permute-start(bf16[128,192]{0,1:T(8,128)(2,1)S(1)} %bitcast.252), channel_id=1, source_target_pairs={{508,0},{0,4},{4,8},{8,12},{12,16},{16,20},{20,24},{24,28},{28,32}... | collective-permute-start | bytes 147464 | tf_op jit(solution)/shard_map/ppermute | solution.py:22
  99.2 28.9 %collective-permute-start.11 = (bf16[128,192]{0,1:T(8,128)(2,1)S(1)}, bf16[128,192]{0,1:T(8,128)(2,1)S(1)}, u32[]{:S(2)}, u32[]{:S(2)}) collective-permute-start(bf16[128,192]{0,1:T(8,128)(2,1)S(1)} %bitcast.253), channel_id=1, source_target_pairs={{504,0},{508,4},{0,8},{4,12},{8,16},{12,20},{16,24},{20,28},{24,32... | collective-permute-start | bytes 147464 | tf_op jit(solution)/shard_map/ppermute | solution.py:22
  102.4 25.8 %collective-permute-start.8 = (bf16[128,192]{0,1:T(8,128)(2,1)S(1)}, bf16[128,192]{0,1:T(8,128)(2,1)S(1)}, u32[]{:S(2)}, u32[]{:S(2)}) collective-permute-start(bf16[128,192]{0,1:T(8,128)(2,1)S(1)} %bitcast.254), channel_id=1, source_target_pairs={{8,0},{12,4},{16,8},{20,12},{24,16},{28,20},{32,24},{36,28},{40,32... | collective-permute-start | bytes 147464 | tf_op jit(solution)/shard_map/ppermute | solution.py:22
  111.6 11.4 %collective-permute-start.6 = (bf16[64,64]{1,0:T(8,128)(2,1)S(1)}, bf16[64,64]{1,0:T(8,128)(2,1)S(1)}, u32[]{:S(2)}, u32[]{:S(2)}) collective-permute-start(bf16[64,64]{1,0:T(8,128)(2,1)S(1)} %get-tuple-element.62), channel_id=1, source_target_pairs={{0,4},{4,8},{8,12},{12,16},{16,20},{20,24},{24,28},{28,32},{32,36}... | collective-permute-start | bytes 24584 | tf_op jit(solution)/shard_map/ppermute | solution.py:31
  114.4 10.6 %collective-permute-start.7 = (bf16[64,64]{1,0:T(8,128)(2,1)S(1)}, bf16[64,64]{1,0:T(8,128)(2,1)S(1)}, u32[]{:S(2)}, u32[]{:S(2)}) collective-permute-start(bf16[64,64]{1,0:T(8,128)(2,1)S(1)} %get-tuple-element.63), channel_id=1, source_target_pairs={{4,0},{8,4},{12,8},{16,12},{20,16},{24,20},{28,24},{32,28},{36,32}... | collective-permute-start | bytes 24584 | tf_op jit(solution)/shard_map/ppermute | solution.py:34
  123.0 5.2 %collective-permute-start.9 = (bf16[128,192]{0,1:T(8,128)(2,1)S(1)}, bf16[128,192]{0,1:T(8,128)(2,1)S(1)}, u32[]{:S(2)}, u32[]{:S(2)}) collective-permute-start(bf16[128,192]{0,1:T(8,128)(2,1)S(1)} %bitcast.255), channel_id=1, source_target_pairs={{4,0},{8,4},{12,8},{16,12},{20,16},{24,20},{28,24},{32,28},{36,32}... | collective-permute-start | bytes 147464 | tf_op jit(solution)/shard_map/ppermute | solution.py:22
  129.3 7.2 %collective-permute-start.12 = (bf16[1408,128]{1,0:T(8,128)(2,1)S(1)}, bf16[1408,128]{1,0:T(8,128)(2,1)S(1)}, u32[]{:S(2)}, u32[]{:S(2)}) collective-permute-start(bf16[1408,128]{1,0:T(8,128)(2,1)S(1)} %select_convert_fusion), channel_id=1, source_target_pairs={{0,1},{1,0},{2,3},{3,2},{4,5},{5,4},{6,7},{7,6},{8,9},{9,8},{10,11... | collective-permute-start | bytes 1081352 | tf_op jit(solution)/shard_map/ppermute | solution.py:57
  136.6 7.7 %collective-permute-start.13 = (bf16[704,128]{1,0:T(8,128)(2,1)S(1)}, bf16[704,128]{1,0:T(8,128)(2,1)S(1)}, u32[]{:S(2)}, u32[]{:S(2)}) collective-permute-start(bf16[704,128]{1,0:T(8,128)(2,1)S(1)} %select_convert_fusion.1), channel_id=1, source_target_pairs={{0,2},{1,3},{2,0},{3,1},{4,6},{5,7},{6,4},{7,5},{8,10},{9,11},{10,... | collective-permute-start | bytes 540680 | tf_op jit(solution)/shard_map/ppermute | solution.py:61
  144.3 6.7 %collective-permute-start.14 = (bf16[704,128]{1,0:T(8,128)(2,1)S(1)}, bf16[704,128]{1,0:T(8,128)(2,1)S(1)}, u32[]{:S(2)}, u32[]{:S(2)}) collective-permute-start(bf16[704,128]{1,0:T(8,128)(2,1)S(1)} %add_convert_fusion), channel_id=1, source_target_pairs={{0,2},{1,3},{2,0},{3,1},{4,6},{5,7},{6,4},{7,5},{8,10},{9,11},{10,... | collective-permute-start | bytes 540680 | tf_op jit(solution)/shard_map/ppermute | solution.py:63
  151.1 5.3 %collective-permute-start.15 = (bf16[1408,128]{1,0:T(8,128)(2,1)S(1)}, bf16[1408,128]{1,0:T(8,128)(2,1)S(1)}, u32[]{:S(2)}, u32[]{:S(2)}) collective-permute-start(bf16[1408,128]{1,0:T(8,128)(2,1)S(1)} %maximum_select_fusion.1), channel_id=1, source_target_pairs={{0,1},{1,0},{2,3},{3,2},{4,5},{5,4},{6,7},{7,6},{8,9},{9,8},{10,11... | collective-permute-start | bytes 1081352 | tf_op jit(solution)/shard_map/ppermute | solution.py:67
  (32 other events, 319.8 us)

commit v10 on v9

--- a/solution.py
+++ b/solution.py
@@ -206,6 +206,75 @@
     )
     extended = extended_2(atom_kv, (("seq", 0),), halo_rows)
     key_value, extended = lax.optimization_barrier((key_value, extended))
+    ext_groups = extended.reshape(windows_here + AK // AQ, AQ, 2 * atom_feat)
+    slabs = jnp.concatenate(
+        [ext_groups[step : step + windows_here] for step in range(group_span)], axis=1
+    )
+    shift_here = key_offset + halo_rows
+    placer_mask = (
+        jnp.arange(slab_rows, dtype=jnp.int32)[None, None, :]
+        == jnp.arange(AK, dtype=jnp.int32)[None, :, None] + shift_here[:, None, None]
+    )
+    window_kv = jnp.einsum(
+        "wrs,wsf->wrf", placer_mask.astype(jnp.bfloat16), slabs, preferred_element_type=jnp.float32
+    ).astype(jnp.bfloat16)
+    atom_keys = window_kv[..., :atom_feat].reshape(windows_here, AK, heads_atom, DA)
+    atom_values = window_kv[..., atom_feat:].reshape(windows_here, AK, heads_atom, DA)
+    atom_queries = atom_proj[0].astype(jnp.bfloat16).reshape(windows_here, AQ, heads_atom, DA)
+    atom_bias_blocks = (
+        atom_bias_all.reshape(heads_atom, windows_here, AQ, AK)
+        .transpose(1, 0, 2, 3)
+        .astype(jnp.float32)
+    )
+    all_valid = jnp.ones((windows_here, AK), dtype=bool)
+    aweights, aweights_low, atom_attended = attend_local(
+        atom_queries, atom_keys, atom_values, atom_bias_blocks, all_valid, atom_scaling
+    )
+    atom_attended = atom_attended.reshape(atom_rows, atom_feat)
+    atom_part = jnp.dot(
+        (atom_attended * atom_gate).astype(jnp.bfloat16),
+        w_atom_out_all,
+        preferred_element_type=jnp.float32,
+    )
+    agrad_gated = jnp.dot(grad_atom, w_atom_out_all.T, preferred_element_type=jnp.float32)
+    agrad_attended = (agrad_gated * atom_gate).astype(jnp.bfloat16)
+    agrad_gate = (agrad_gated * atom_attended * atom_gate * (1.0 - atom_gate)).astype(jnp.bfloat16)
+    atom_delta = jnp.sum(
+        (agrad_attended.astype(jnp.float32) * atom_attended).reshape(
+            windows_here, AQ, heads_atom, DA
+        ),
+        axis=-1,
+    ).transpose(0, 2, 1)
+    ascore_low, aquery_grad, akey_grad, avalue_grad = attend_grads(
+        aweights,
+        aweights_low,
+        atom_queries,
+        atom_keys,
+        atom_values,
+        agrad_attended.reshape(windows_here, AQ, heads_atom, DA),
+        atom_delta,
+        atom_scaling,
+    )
+    grad_abias = ascore_low.transpose(1, 0, 2, 3).reshape(heads_atom, atom_rows, AK)
+    spread_grads = jnp.concatenate(
+        [
+            akey_grad.reshape(windows_here, AK, atom_feat),
+            avalue_grad.reshape(windows_here, AK, atom_feat),
+        ],
+        axis=-1,
+    )
+    slab_grads = jnp.einsum(
+        "wrs,wrf->wsf", placer_mask.astype(jnp.float32), spread_grads, precision=HIGHEST
+    )
+    slab_grads = slab_grads.reshape(windows_here, group_span, AQ, 2 * atom_feat)
+    ext_grad = jnp.pad(slab_grads[:, 0], ((0, group_span - 1), (0, 0), (0, 0)))
+    for step in range(1, group_span):
+        ext_grad = ext_grad + jnp.pad(
+            slab_grads[:, step], ((step, group_span - 1 - step), (0, 0), (0, 0))
+        )
+    ext_grad = ext_grad.reshape(atom_rows + 2 * halo_rows, 2 * atom_feat)
+    rims = jnp.concatenate([ext_grad[:halo_rows], ext_grad[atom_rows + halo_rows :]], axis=0)
+    key_value, rims = lax.optimization_barrier((key_value, rims))
     owner_dev = used_blocks // blocks_here
     relative = jnp.mod(owner_dev - device, shards)
     relative = jnp.where(relative > shards // 2, relative - shards, relative)
@@ -271,76 +340,6 @@
         "bsc,bsx->cx", selector_mask.astype(jnp.float32), returned_flat, precision=HIGHEST
     )
     outgoing = outgoing.reshape(2 * WIN + 1, tok_rows, 2 * features)
-    ext_groups = extended.reshape(windows_here + AK // AQ, AQ, 2 * atom_feat)
-    slabs = jnp.concatenate(
-        [ext_groups[step : step + windows_here] for step in range(group_span)], axis=1
-    )
-    shift_here = key_offset + halo_rows
-    placer_mask = (
-        jnp.arange(slab_rows, dtype=jnp.int32)[None, None, :]
-        == jnp.arange(AK, dtype=jnp.int32)[None, :, None] + shift_here[:, None, None]
-    )
-    window_kv = jnp.einsum(
-        "wrs,wsf->wrf", placer_mask.astype(jnp.bfloat16), slabs, preferred_element_type=jnp.float32
-    ).astype(jnp.bfloat16)
-    atom_keys = window_kv[..., :atom_feat].reshape(windows_here, AK, heads_atom, DA)
-    atom_values = window_kv[..., atom_feat:].reshape(windows_here, AK, heads_atom, DA)
-    atom_queries = atom_proj[0].astype(jnp.bfloat16).reshape(windows_here, AQ, heads_atom, DA)
-    atom_bias_blocks = (
-        atom_bias_all.reshape(heads_atom, windows_here, AQ, AK)
-        .transpose(1, 0, 2, 3)
-        .astype(jnp.float32)
-    )
-    all_valid = jnp.ones((windows_here, AK), dtype=bool)
-    aweights, aweights_low, atom_attended = attend_local(
-        atom_queries, atom_keys, atom_values, atom_bias_blocks, all_valid, atom_scaling
-    )
-    atom_attended = atom_attended.reshape(atom_rows, atom_feat)
-    atom_part = jnp.dot(
-        (atom_attended * atom_gate).astype(jnp.bfloat16),
-        w_atom_out_all,
-        preferred_element_type=jnp.float32,
-    )
-    agrad_gated = jnp.dot(grad_atom, w_atom_out_all.T, preferred_element_type=jnp.float32)
-    agrad_attended = (agrad_gated * atom_gate).astype(jnp.bfloat16)
-    agrad_gate = (agrad_gated * atom_attended * atom_gate * (1.0 - atom_gate)).astype(jnp.bfloat16)
-    atom_delta = jnp.sum(
-        (agrad_attended.astype(jnp.float32) * atom_attended).reshape(
-            windows_here, AQ, heads_atom, DA
-        ),
-        axis=-1,
-    ).transpose(0, 2, 1)
-    ascore_low, aquery_grad, akey_grad, avalue_grad = attend_grads(
-        aweights,
-        aweights_low,
-        atom_queries,
-        atom_keys,
-        atom_values,
-        agrad_attended.reshape(windows_here, AQ, heads_atom, DA),
-        atom_delta,
-        atom_scaling,
-    )
-    grad_abias = ascore_low.transpose(1, 0, 2, 3).reshape(heads_atom, atom_rows, AK)
-    spread_grads = jnp.concatenate(
-        [
-            akey_grad.reshape(windows_here, AK, atom_feat),
-            avalue_grad.reshape(windows_here, AK, atom_feat),
-        ],
-        axis=-1,
-    )
-    slab_grads = jnp.einsum(
-        "wrs,wrf->wsf", placer_mask.astype(jnp.float32), spread_grads, precision=HIGHEST
-    )
-    slab_grads = slab_grads.reshape(windows_here, group_span, AQ, 2 * atom_feat)
-    ext_grad = jnp.pad(slab_grads[:, 0], ((0, group_span - 1), (0, 0), (0, 0)))
-    for step in range(1, group_span):
-        ext_grad = ext_grad + jnp.pad(
-            slab_grads[:, step], ((step, group_span - 1 - step), (0, 0), (0, 0))
-        )
-    ext_grad = ext_grad.reshape(atom_rows + 2 * halo_rows, 2 * atom_feat)
-    rims = jnp.concatenate([ext_grad[:halo_rows], ext_grad[atom_rows + halo_rows :]], axis=0)
-    outgoing, rims = lax.optimization_barrier((outgoing, rims))
-    edges = extended_2(rims.astype(jnp.bfloat16), (("seq", 0),), halo_rows).astype(rims.dtype)
     collected = outgoing[WIN]
     for distance in range(-WIN, WIN + 1):
         if distance != 0:
@@ -353,6 +352,7 @@
         collected[:, features:].astype(jnp.bfloat16),
         grad_gate,
     ]
+    edges = extended_2(rims.astype(jnp.bfloat16), (("seq", 0),), halo_rows).astype(rims.dtype)
     own_grad = ext_grad[halo_rows : halo_rows + atom_rows]
     own_grad = jnp.concatenate(
         [

time: 160 us -> 163 us (1.019)
  local copies, waits for them, and re-layouts: 18.9 us -> 22.7 us
  matrix products: 30.2 us -> 28.5 us
    convert_element_type x2, local copies, waits for them, and re-layouts: 0.38 us -> 2.67 us  [body(): aquery_grad.reshape(atom_rows, atom_feat).astype(jnp.bfloat16)]
  transfers between devices with their start and end apart: 16 -> 16, of which waited for: 4 -> 4; matrix products, arithmetic and copies ran while one was open for 25% -> 16% of each run, Pallas kernels for 0% -> 0%
where the time goes in v10:
time: 163 us; the launch traced here: 162 us
  starting transfers between devices  76.4 us (47%)
  matrix products  28.5 us (17%)
  local copies, waits for them, and re-layouts  22.7 us (14%)
  other arithmetic  19.1 us (12%)
  waiting for transfers between devices  12.3 us (8%)
  between operations  2.72 us (2%)
    ppermute x8, starting transfers between devices, shifted(): return lax.ppermute(block, axis, route)  32.8 us
    ppermute x2, starting transfers between devices, extended_2(): lax.ppermute(lax.slice_in_dim(block, 0, width, axis=dim), axis, backward)  24 us
    ppermute x2, starting transfers between devices, extended_2(): lax.ppermute(lax.slice_in_dim(block, block.shape[dim] - width, None, axis...  5.85 us
    sub x1, other arithmetic, attend_local(): exponent = jnp.exp(scores - row_max)  5.4 us
    ppermute x1, waiting for transfers between devices, head_sum(): got = lax.ppermute(give.astype(jnp.bfloat16), axis, pair_far)  5.35 us
    ppermute x1, starting transfers between devices, head_sum(): got = lax.ppermute(give.astype(jnp.bfloat16), axis, pair_near)  5.11 us
    ppermute x1, waiting for transfers between devices, head_sum(): got = lax.ppermute(own, axis, pair_far)  4.42 us
    ppermute x1, starting transfers between devices, head_sum(): got = lax.ppermute(half, axis, pair_near)  4.03 us
  transfers between devices with their start and end apart: 16, of which 4 were waited for; matrix products, arithmetic and copies ran while one was open for 16% of the time, Pallas kernels for 0%

profile of v10, /device:TPU:1, one launch (start us, length us, event | category | flops | bytes accessed | tf_op | source)
XLA Modules:
  0.0 161.7 jit_solution(8911626169840869897)
XLA Ops:
  11.3 3.9 %collective-permute-start = (bf16[64,64]{0,1:T(8,128)(2,1)S(1)}, bf16[64,64]{0,1:T(8,128)(2,1)S(1)}, u32[]{:S(2)}, u32[]{:S(2)}) collective-permute-start(bf16[64,64]{0,1:T(8,128)(2,1)S(1)} %get-tuple-element.58), channel_id=1, source_target_pairs={{0,4},{4,8},{8,12},{12,16},{16,20},{20,24},{24,28},{28,32},{32,36}... | collective-permute-start | bytes 24584 | tf_op jit(solution)/shard_map/ppermute | solution.py:31
  15.3 14.7 %collective-permute-start.1 = (bf16[64,64]{0,1:T(8,128)(2,1)S(1)}, bf16[64,64]{0,1:T(8,128)(2,1)S(1)}, u32[]{:S(2)}, u32[]{:S(2)}) collective-permute-start(bf16[64,64]{0,1:T(8,128)(2,1)S(1)} %get-tuple-element.57), channel_id=1, source_target_pairs={{4,0},{8,4},{12,8},{16,12},{20,16},{24,20},{28,24},{32,28},{36,32}... | collective-permute-start | bytes 24584 | tf_op jit(solution)/shard_map/ppermute | solution.py:34
  38.5 2.3 %concatenate.56 = bf16[32,160,64]{1,2,0:T(8,128)(2,1)} concatenate(bf16[32,32,64]{1,2,0:T(8,128)(2,1)S(1)} %copy.85, bf16[32,32,64]{1,2,0:T(8,128)(2,1)S(1)} %copy.86, bf16[32,32,64]{1,2,0:T(8,128)(2,1)S(1)} %copy.87, bf16[32,32,64]{1,2,0:T(8,128)(2,1)S(1)} %copy.88, bf16[32,32,64]{1,2,0:T(8,128)(2,1)S(1)} %copy.89), dimensions={1} | concatenate | bytes 1310720 | tf_op jit(solution)/shard_map/concatenate | solution.py:210
  40.7 1.9 %fusion.11 = bf16[32,128,64]{1,2,0:T(8,128)(2,1)S(1)} fusion(bf16[32,160,64]{1,2,0:T(8,128)(2,1)} %concatenate.56, s32[32,128]{1,0:T(8,128)} %iota_add_fusion), kind=kOutput, calls=%fused_computation.15 | convolution fusion | flops 84803584 | bytes 1196032 | tf_op jit(solution)/shard_map/wrs,wsf->wrf/dot_general | solution.py:218
  42.9 5.4 %fusion.135 = (f32[32,32]{1,0:T(8,128)S(1)}, f32[32,32,128]{2,1,0:T(8,128)S(1)}) fusion(f32[32,32,128]{2,1,0:T(8,128)S(1)} %fusion.17), kind=kOutput, calls=%fused_computation.236 | output fusion | flops 262271 | bytes 1052672 | tf_op jit(solution)/shard_map/sub | solution.py:111
  48.3 1.8 %convolution_bitcast_fusion.1 = f32[32,32,1,32]{1,3,0,2:T(8,128)S(1)} fusion(bf16[32,128,64]{1,2,0:T(8,128)(2,1)S(1)} %fusion.11, f32[32,32]{1,0:T(8,128)S(1)} %get-tuple-element.64, f32[32,32,128]{2,1,0:T(8,128)S(1)} %fusion.17), kind=kOutput, calls=%fused_computation.23 | convolution fusion | flops 8782975 | bytes 1458176 | tf_op jit(solution)/shard_map/bhqk,bkhd->bqhd/dot_general | solution.py:114
  56.3 2.1 %collective-permute-start.2 = (bf16[128,192]{0,1:T(8,128)(2,1)}, bf16[128,192]{0,1:T(8,128)(2,1)}, u32[]{:S(2)}, u32[]{:S(2)}) collective-permute-start(bf16[128,192]{0,1:T(8,128)(2,1)} %pad_maximum_fusion.7), channel_id=1, source_target_pairs={{504,0},{508,4},{0,8},{4,12},{8,16},{12,20},{16,24},{20,28},{24,32... | collective-permute-start | bytes 147464 | tf_op jit(solution)/shard_map/ppermute | solution.py:22
  58.3 1.9 %collective-permute-start.3 = (bf16[128,192]{0,1:T(8,128)(2,1)}, bf16[128,192]{0,1:T(8,128)(2,1)}, u32[]{:S(2)}, u32[]{:S(2)}) collective-permute-start(bf16[128,192]{0,1:T(8,128)(2,1)} %pad_maximum_fusion.7), channel_id=1, source_target_pairs={{508,0},{0,4},{4,8},{8,12},{12,16},{16,20},{20,24},{24,28},{28,32}... | collective-permute-start | bytes 147464 | tf_op jit(solution)/shard_map/ppermute | solution.py:22
  60.3 9.1 %collective-permute-start.4 = (bf16[128,192]{0,1:T(8,128)(2,1)}, bf16[128,192]{0,1:T(8,128)(2,1)}, u32[]{:S(2)}, u32[]{:S(2)}) collective-permute-start(bf16[128,192]{0,1:T(8,128)(2,1)} %pad_maximum_fusion.7), channel_id=1, source_target_pairs={{4,0},{8,4},{12,8},{16,12},{20,16},{24,20},{28,24},{32,28},{36,32}... | collective-permute-start | bytes 147464 | tf_op jit(solution)/shard_map/ppermute | solution.py:22
  71.6 1.9 %collective-permute-start.6 = (bf16[64,64]{1,0:T(8,128)(2,1)}, bf16[64,64]{1,0:T(8,128)(2,1)}, u32[]{:S(2)}, u32[]{:S(2)}) collective-permute-start(bf16[64,64]{1,0:T(8,128)(2,1)} %get-tuple-element.62), channel_id=1, source_target_pairs={{0,4},{4,8},{8,12},{12,16},{16,20},{20,24},{24,28},{28,32},{32,36}... | collective-permute-start | bytes 24584 | tf_op jit(solution)/shard_map/ppermute | solution.py:31
  73.5 9.3 %collective-permute-start.7 = (bf16[64,64]{1,0:T(8,128)(2,1)}, bf16[64,64]{1,0:T(8,128)(2,1)}, u32[]{:S(2)}, u32[]{:S(2)}) collective-permute-start(bf16[64,64]{1,0:T(8,128)(2,1)} %get-tuple-element.63), channel_id=1, source_target_pairs={{4,0},{8,4},{12,8},{16,12},{20,16},{24,20},{28,24},{32,28},{36,32}... | collective-permute-start | bytes 24584 | tf_op jit(solution)/shard_map/ppermute | solution.py:34
  83.6 1.9 %convert_element_type.212 = bf16[1024,32]{0,1:T(8,128)(2,1)} reshape(bf16[32,32,1,32]{1,0,3,2:T(8,128)(2,1)} %copy.107) | data formatting | bytes 131072 | tf_op jit(solution)/shard_map/convert_element_type | solution.py:366
  85.4 1.9 %fusion.97 = f32[1024,128]{1,0:T(8,128)} fusion(bf16[1024,32]{0,1:T(8,128)(2,1)} %convert_element_type.212, bf16[4,128,32]{1,2,0:T(8,128)(2,1)} %param.24), kind=kOutput, calls=%fused_computation.184 | convolution fusion | flops 8388608 | bytes 598016 | tf_op jit(solution)/shard_map/dot_general | solution.py:371
  90.1 1.9 %collective-permute-start.5 = (bf16[128,192]{0,1:T(8,128)(2,1)}, bf16[128,192]{0,1:T(8,128)(2,1)S(1)}, u32[]{:S(2)}, u32[]{:S(2)}) collective-permute-start(bf16[128,192]{0,1:T(8,128)(2,1)} %pad_maximum_fusion.7), channel_id=1, source_target_pairs={{8,0},{12,4},{16,8},{20,12},{24,16},{28,20},{32,24},{36,28},{40,32... | collective-permute-start | bytes 147464 | tf_op jit(solution)/shard_map/ppermute | solution.py:22
  109.8 2.5 %collective-permute-start.10 = (bf16[128,192]{1,0:T(8,128)(2,1)S(1)}, bf16[128,192]{1,0:T(8,128)(2,1)S(1)}, u32[]{:S(2)}, u32[]{:S(2)}) collective-permute-start(bf16[128,192]{1,0:T(8,128)(2,1)S(1)} %convert_element_type.227), channel_id=1, source_target_pairs={{508,0},{0,4},{4,8},{8,12},{12,16},{16,20},{20,24},{24,28},{28,32}... | collective-permute-start | bytes 147464 | tf_op jit(solution)/shard_map/ppermute | solution.py:22
  112.4 4.3 %collective-permute-start.11 = (bf16[128,192]{1,0:T(8,128)(2,1)S(1)}, bf16[128,192]{1,0:T(8,128)(2,1)S(1)}, u32[]{:S(2)}, u32[]{:S(2)}) collective-permute-start(bf16[128,192]{1,0:T(8,128)(2,1)S(1)} %convert_element_type.229), channel_id=1, source_target_pairs={{504,0},{508,4},{0,8},{4,12},{8,16},{12,20},{16,24},{20,28},{24,32... | collective-permute-start | bytes 147464 | tf_op jit(solution)/shard_map/ppermute | solution.py:22
  116.9 7.0 %collective-permute-start.8 = (bf16[128,192]{1,0:T(8,128)(2,1)S(1)}, bf16[128,192]{1,0:T(8,128)(2,1)S(1)}, u32[]{:S(2)}, u32[]{:S(2)}) collective-permute-start(bf16[128,192]{1,0:T(8,128)(2,1)S(1)} %convert_element_type.223), channel_id=1, source_target_pairs={{8,0},{12,4},{16,8},{20,12},{24,16},{28,20},{32,24},{36,28},{40,32... | collective-permute-start | bytes 147464 | tf_op jit(solution)/shard_map/ppermute | solution.py:22
  124.0 4.0 %collective-permute-start.9 = (bf16[128,192]{1,0:T(8,128)(2,1)S(1)}, bf16[128,192]{1,0:T(8,128)(2,1)S(1)}, u32[]{:S(2)}, u32[]{:S(2)}) collective-permute-start(bf16[128,192]{1,0:T(8,128)(2,1)S(1)} %convert_element_type.225), channel_id=1, source_target_pairs={{4,0},{8,4},{12,8},{16,12},{20,16},{24,20},{28,24},{32,28},{36,32}... | collective-permute-start | bytes 147464 | tf_op jit(solution)/shard_map/ppermute | solution.py:22
  133.0 5.1 %collective-permute-start.12 = (bf16[1408,128]{1,0:T(8,128)(2,1)S(1)}, bf16[1408,128]{1,0:T(8,128)(2,1)S(1)}, u32[]{:S(2)}, u32[]{:S(2)}) collective-permute-start(bf16[1408,128]{1,0:T(8,128)(2,1)S(1)} %select_convert_fusion), channel_id=1, source_target_pairs={{0,1},{1,0},{2,3},{3,2},{4,5},{5,4},{6,7},{7,6},{8,9},{9,8},{10,11... | collective-permute-start | bytes 1081352 | tf_op jit(solution)/shard_map/ppermute | solution.py:57
  139.5 2.3 %collective-permute-start.13 = (bf16[704,128]{1,0:T(8,128)(2,1)S(1)}, bf16[704,128]{1,0:T(8,128)(2,1)S(1)}, u32[]{:S(2)}, u32[]{:S(2)}) collective-permute-start(bf16[704,128]{1,0:T(8,128)(2,1)S(1)} %select_convert_fusion.1), channel_id=1, source_target_pairs={{0,2},{1,3},{2,0},{3,1},{4,6},{5,7},{6,4},{7,5},{8,10},{9,11},{10,... | collective-permute-start | bytes 540680 | tf_op jit(solution)/shard_map/ppermute | solution.py:61
  141.8 5.3 %collective-permute-done.13 = bf16[704,128]{1,0:T(8,128)(2,1)S(1)} collective-permute-done((bf16[704,128]{1,0:T(8,128)(2,1)S(1)}, bf16[704,128]{1,0:T(8,128)(2,1)S(1)}, u32[]{:S(2)}, u32[]{:S(2)}) %collective-permute-start.13) | collective-permute-done | bytes 180256 | tf_op jit(solution)/shard_map/ppermute | solution.py:61
  147.2 2.3 %collective-permute-start.14 = (bf16[704,128]{1,0:T(8,128)(2,1)S(1)}, bf16[704,128]{1,0:T(8,128)(2,1)S(1)}, u32[]{:S(2)}, u32[]{:S(2)}) collective-permute-start(bf16[704,128]{1,0:T(8,128)(2,1)S(1)} %add_convert_fusion), channel_id=1, source_target_pairs={{0,2},{1,3},{2,0},{3,1},{4,6},{5,7},{6,4},{7,5},{8,10},{9,11},{10,... | collective-permute-start | bytes 540680 | tf_op jit(solution)/shard_map/ppermute | solution.py:63
  149.5 4.4 %collective-permute-done.14 = bf16[704,128]{1,0:T(8,128)(2,1)S(1)} collective-permute-done((bf16[704,128]{1,0:T(8,128)(2,1)S(1)}, bf16[704,128]{1,0:T(8,128)(2,1)S(1)}, u32[]{:S(2)}, u32[]{:S(2)}) %collective-permute-start.14) | collective-permute-done | bytes 180256 | tf_op jit(solution)/shard_map/ppermute | solution.py:63
  154.1 4.0 %collective-permute-start.15 = (bf16[1408,128]{1,0:T(8,128)(2,1)S(1)}, bf16[1408,128]{1,0:T(8,128)(2,1)S(1)}, u32[]{:S(2)}, u32[]{:S(2)}) collective-permute-start(bf16[1408,128]{1,0:T(8,128)(2,1)S(1)} %maximum_select_fusion.1), channel_id=1, source_target_pairs={{0,1},{1,0},{2,3},{3,2},{4,5},{5,4},{6,7},{7,6},{8,9},{9,8},{10,11... | collective-permute-start | bytes 1081352 | tf_op jit(solution)/shard_map/ppermute | solution.py:67
  (226 shorter events, 57.7 us)
Async XLA Ops:
  0.6 50.1 %copy-start = (bf16[1024,128]{1,0:T(8,128)(2,1)S(1)}, bf16[1024,128]{1,0:T(8,128)(2,1)}, u32[]{:S(2)}) copy-start(bf16[1024,128]{1,0:T(8,128)(2,1)} %param.33) | copy-start | bytes 786436
  0.7 29.4 %copy-start.8 = (bf16[4,384,96]{1,2,0:T(8,128)(2,1)S(1)}, bf16[4,384,96]{1,2,0:T(8,128)(2,1)}, u32[]{:S(2)}) copy-start(bf16[4,384,96]{1,2,0:T(8,128)(2,1)} %param.21) | copy-start | bytes 884740
  2.8 29.6 %copy-start.36 = (s32[32]{0:T(128)S(1)}, s32[32]{0:T(128)}, u32[]{:S(2)}) copy-start(s32[32]{0:T(128)} %param.31) | copy-start | bytes 388
  2.9 31.5 %copy-start.37 = (s32[1,4]{1,0:T(1,128)S(1)}, s32[1,4]{1,0:T(1,128)}, u32[]{:S(2)}) copy-start(s32[1,4]{1,0:T(1,128)} %param.28) | copy-start | bytes 52
  6.6 29.2 %copy-start.26 = (s32[1024]{0:T(1024)}, s32[1024]{0:T(1024)S(1)}, u32[]{:S(2)}) copy-start(s32[1024]{0:T(1024)S(1)} %convert_reduce_fusion.1) | copy-start | bytes 12292
  11.3 24.5 %collective-permute-start = (bf16[64,64]{0,1:T(8,128)(2,1)S(1)}, bf16[64,64]{0,1:T(8,128)(2,1)S(1)}, u32[]{:S(2)}, u32[]{:S(2)}) collective-permute-start(bf16[64,64]{0,1:T(8,128)(2,1)S(1)} %get-tuple-element.58), channel_id=1, source_target_pairs={{0,4},{4,8},{8,12},{12,16},{16,20},{20,24},{24,28},{28,32},{32,36}... | collective-permute-start | bytes 24584 | tf_op jit(solution)/shard_map/ppermute | solution.py:31
  15.3 20.5 %collective-permute-start.1 = (bf16[64,64]{0,1:T(8,128)(2,1)S(1)}, bf16[64,64]{0,1:T(8,128)(2,1)S(1)}, u32[]{:S(2)}, u32[]{:S(2)}) collective-permute-start(bf16[64,64]{0,1:T(8,128)(2,1)S(1)} %get-tuple-element.57), channel_id=1, source_target_pairs={{4,0},{8,4},{12,8},{16,12},{20,16},{24,20},{28,24},{32,28},{36,32}... | collective-permute-start | bytes 24584 | tf_op jit(solution)/shard_map/ppermute | solution.py:34
  56.3 40.5 %collective-permute-start.2 = (bf16[128,192]{0,1:T(8,128)(2,1)}, bf16[128,192]{0,1:T(8,128)(2,1)}, u32[]{:S(2)}, u32[]{:S(2)}) collective-permute-start(bf16[128,192]{0,1:T(8,128)(2,1)} %pad_maximum_fusion.7), channel_id=1, source_target_pairs={{504,0},{508,4},{0,8},{4,12},{8,16},{12,20},{16,24},{20,28},{24,32... | collective-permute-start | bytes 147464 | tf_op jit(solution)/shard_map/ppermute | solution.py:22
  58.3 39.5 %collective-permute-start.3 = (bf16[128,192]{0,1:T(8,128)(2,1)}, bf16[128,192]{0,1:T(8,128)(2,1)}, u32[]{:S(2)}, u32[]{:S(2)}) collective-permute-start(bf16[128,192]{0,1:T(8,128)(2,1)} %pad_maximum_fusion.7), channel_id=1, source_target_pairs={{508,0},{0,4},{4,8},{8,12},{12,16},{16,20},{20,24},{24,28},{28,32}... | collective-permute-start | bytes 147464 | tf_op jit(solution)/shard_map/ppermute | solution.py:22
  60.3 38.6 %collective-permute-start.4 = (bf16[128,192]{0,1:T(8,128)(2,1)}, bf16[128,192]{0,1:T(8,128)(2,1)}, u32[]{:S(2)}, u32[]{:S(2)}) collective-permute-start(bf16[128,192]{0,1:T(8,128)(2,1)} %pad_maximum_fusion.7), channel_id=1, source_target_pairs={{4,0},{8,4},{12,8},{16,12},{20,16},{24,20},{28,24},{32,28},{36,32}... | collective-permute-start | bytes 147464 | tf_op jit(solution)/shard_map/ppermute | solution.py:22
  71.6 18.5 %collective-permute-start.6 = (bf16[64,64]{1,0:T(8,128)(2,1)}, bf16[64,64]{1,0:T(8,128)(2,1)}, u32[]{:S(2)}, u32[]{:S(2)}) collective-permute-start(bf16[64,64]{1,0:T(8,128)(2,1)} %get-tuple-element.62), channel_id=1, source_target_pairs={{0,4},{4,8},{8,12},{12,16},{16,20},{20,24},{24,28},{28,32},{32,36}... | collective-permute-start | bytes 24584 | tf_op jit(solution)/shard_map/ppermute | solution.py:31
  73.5 18.5 %collective-permute-start.7 = (bf16[64,64]{1,0:T(8,128)(2,1)}, bf16[64,64]{1,0:T(8,128)(2,1)}, u32[]{:S(2)}, u32[]{:S(2)}) collective-permute-start(bf16[64,64]{1,0:T(8,128)(2,1)} %get-tuple-element.63), channel_id=1, source_target_pairs={{4,0},{8,4},{12,8},{16,12},{20,16},{24,20},{28,24},{32,28},{36,32}... | collective-permute-start | bytes 24584 | tf_op jit(solution)/shard_map/ppermute | solution.py:34
  90.1 9.9 %collective-permute-start.5 = (bf16[128,192]{0,1:T(8,128)(2,1)}, bf16[128,192]{0,1:T(8,128)(2,1)S(1)}, u32[]{:S(2)}, u32[]{:S(2)}) collective-permute-start(bf16[128,192]{0,1:T(8,128)(2,1)} %pad_maximum_fusion.7), channel_id=1, source_target_pairs={{8,0},{12,4},{16,8},{20,12},{24,16},{28,20},{32,24},{36,28},{40,32... | collective-permute-start | bytes 147464 | tf_op jit(solution)/shard_map/ppermute | solution.py:22
  107.1 24.8 %copy-start.9 = (bf16[4,384,96]{1,2,0:T(8,128)(2,1)S(1)}, bf16[4,384,96]{1,2,0:T(8,128)(2,1)}, u32[]{:S(2)}) copy-start(bf16[4,384,96]{1,2,0:T(8,128)(2,1)} %param.21) | copy-start | bytes 884740
  108.6 23.7 %copy-start.30 = (f32[128]{0:T(128)S(1)}, f32[128]{0:T(128)}, u32[]{:S(2)}) copy-start(f32[128]{0:T(128)} %copy-done.29) | copy-start | bytes 1540
  108.7 23.7 %copy-start.32 = (f32[128]{0:T(128)S(1)}, f32[128]{0:T(128)}, u32[]{:S(2)}) copy-start(f32[128]{0:T(128)} %copy-done.31) | copy-start | bytes 1540
  109.8 22.0 %collective-permute-start.10 = (bf16[128,192]{1,0:T(8,128)(2,1)S(1)}, bf16[128,192]{1,0:T(8,128)(2,1)S(1)}, u32[]{:S(2)}, u32[]{:S(2)}) collective-permute-start(bf16[128,192]{1,0:T(8,128)(2,1)S(1)} %convert_element_type.227), channel_id=1, source_target_pairs={{508,0},{0,4},{4,8},{8,12},{12,16},{16,20},{20,24},{24,28},{28,32}... | collective-permute-start | bytes 147464 | tf_op jit(solution)/shard_map/ppermute | solution.py:22
  112.4 19.4 %collective-permute-start.11 = (bf16[128,192]{1,0:T(8,128)(2,1)S(1)}, bf16[128,192]{1,0:T(8,128)(2,1)S(1)}, u32[]{:S(2)}, u32[]{:S(2)}) collective-permute-start(bf16[128,192]{1,0:T(8,128)(2,1)S(1)} %convert_element_type.229), channel_id=1, source_target_pairs={{504,0},{508,4},{0,8},{4,12},{8,16},{12,20},{16,24},{20,28},{24,32... | collective-permute-start | bytes 147464 | tf_op jit(solution)/shard_map/ppermute | solution.py:22
  116.9 15.0 %collective-permute-start.8 = (bf16[128,192]{1,0:T(8,128)(2,1)S(1)}, bf16[128,192]{1,0:T(8,128)(2,1)S(1)}, u32[]{:S(2)}, u32[]{:S(2)}) collective-permute-start(bf16[128,192]{1,0:T(8,128)(2,1)S(1)} %convert_element_type.223), channel_id=1, source_target_pairs={{8,0},{12,4},{16,8},{20,12},{24,16},{28,20},{32,24},{36,28},{40,32... | collective-permute-start | bytes 147464 | tf_op jit(solution)/shard_map/ppermute | solution.py:22
  124.0 7.9 %collective-permute-start.9 = (bf16[128,192]{1,0:T(8,128)(2,1)S(1)}, bf16[128,192]{1,0:T(8,128)(2,1)S(1)}, u32[]{:S(2)}, u32[]{:S(2)}) collective-permute-start(bf16[128,192]{1,0:T(8,128)(2,1)S(1)} %convert_element_type.225), channel_id=1, source_target_pairs={{4,0},{8,4},{12,8},{16,12},{20,16},{24,20},{28,24},{32,28},{36,32}... | collective-permute-start | bytes 147464 | tf_op jit(solution)/shard_map/ppermute | solution.py:22
  133.0 6.4 %collective-permute-start.12 = (bf16[1408,128]{1,0:T(8,128)(2,1)S(1)}, bf16[1408,128]{1,0:T(8,128)(2,1)S(1)}, u32[]{:S(2)}, u32[]{:S(2)}) collective-permute-start(bf16[1408,128]{1,0:T(8,128)(2,1)S(1)} %select_convert_fusion), channel_id=1, source_target_pairs={{0,1},{1,0},{2,3},{3,2},{4,5},{5,4},{6,7},{7,6},{8,9},{9,8},{10,11... | collective-permute-start | bytes 1081352 | tf_op jit(solution)/shard_map/ppermute | solution.py:57
  139.5 7.7 %collective-permute-start.13 = (bf16[704,128]{1,0:T(8,128)(2,1)S(1)}, bf16[704,128]{1,0:T(8,128)(2,1)S(1)}, u32[]{:S(2)}, u32[]{:S(2)}) collective-permute-start(bf16[704,128]{1,0:T(8,128)(2,1)S(1)} %select_convert_fusion.1), channel_id=1, source_target_pairs={{0,2},{1,3},{2,0},{3,1},{4,6},{5,7},{6,4},{7,5},{8,10},{9,11},{10,... | collective-permute-start | bytes 540680 | tf_op jit(solution)/shard_map/ppermute | solution.py:61
  147.2 6.7 %collective-permute-start.14 = (bf16[704,128]{1,0:T(8,128)(2,1)S(1)}, bf16[704,128]{1,0:T(8,128)(2,1)S(1)}, u32[]{:S(2)}, u32[]{:S(2)}) collective-permute-start(bf16[704,128]{1,0:T(8,128)(2,1)S(1)} %add_convert_fusion), channel_id=1, source_target_pairs={{0,2},{1,3},{2,0},{3,1},{4,6},{5,7},{6,4},{7,5},{8,10},{9,11},{10,... | collective-permute-start | bytes 540680 | tf_op jit(solution)/shard_map/ppermute | solution.py:63
  154.1 5.3 %collective-permute-start.15 = (bf16[1408,128]{1,0:T(8,128)(2,1)S(1)}, bf16[1408,128]{1,0:T(8,128)(2,1)S(1)}, u32[]{:S(2)}, u32[]{:S(2)}) collective-permute-start(bf16[1408,128]{1,0:T(8,128)(2,1)S(1)} %maximum_select_fusion.1), channel_id=1, source_target_pairs={{0,1},{1,0},{2,3},{3,2},{4,5},{5,4},{6,7},{7,6},{8,9},{9,8},{10,11... | collective-permute-start | bytes 1081352 | tf_op jit(solution)/shard_map/ppermute | solution.py:67
  (31 other events, 286.7 us)

commit v11 on v8

--- a/solution.py
+++ b/solution.py
@@ -13,7 +13,7 @@
 
 
 EPSILON = 1e-05
-HIGHEST = lax.Precision.HIGHEST
+ONE_HOT_PRECISION = lax.Precision.HIGH
 
 
 def shifted(block, axis, distance):
@@ -193,7 +193,7 @@
         jnp.float32
     )
     condition = jnp.dot(normed_low, w_cond, preferred_element_type=jnp.float32)
-    atom_input = (normed_atoms + jnp.dot(token_pick, condition, precision=HIGHEST)).astype(
+    atom_input = (normed_atoms + jnp.dot(token_pick, condition, precision=ONE_HOT_PRECISION)).astype(
         jnp.bfloat16
     )
     atom_proj = [
@@ -268,7 +268,7 @@
     )
     returned_flat = returned.reshape(blocks_here, S, BLK * 2 * features)
     outgoing = jnp.einsum(
-        "bsc,bsx->cx", selector_mask.astype(jnp.float32), returned_flat, precision=HIGHEST
+        "bsc,bsx->cx", selector_mask.astype(jnp.float32), returned_flat, precision=ONE_HOT_PRECISION
     )
     outgoing = outgoing.reshape(2 * WIN + 1, tok_rows, 2 * features)
     collected = outgoing[WIN]
@@ -341,7 +341,7 @@
         axis=-1,
     )
     slab_grads = jnp.einsum(
-        "wrs,wrf->wsf", placer_mask.astype(jnp.float32), spread_grads, precision=HIGHEST
+        "wrs,wrf->wsf", placer_mask.astype(jnp.float32), spread_grads, precision=ONE_HOT_PRECISION
     )
     slab_grads = slab_grads.reshape(windows_here, group_span, AQ, 2 * atom_feat)
     ext_grad = jnp.pad(slab_grads[:, 0], ((0, group_span - 1), (0, 0), (0, 0)))
@@ -373,8 +373,8 @@
             atom_grads[which], w_atom_all[which].T, preferred_element_type=jnp.float32
         )
     atoms_part = norm_back(atoms.astype(jnp.float32), gain_atom, agrad_input)
-    cond_grad = jnp.dot(token_pick.T, agrad_input, precision=HIGHEST)
-    cond_term = jnp.dot(cond_grad, w_cond.astype(jnp.float32).T, precision=HIGHEST)
+    cond_grad = jnp.dot(token_pick.T, agrad_input, precision=ONE_HOT_PRECISION)
+    cond_term = jnp.dot(cond_grad, w_cond.astype(jnp.float32).T, precision=ONE_HOT_PRECISION)
     grad_normed = cond_term
     for which in range(4):
         grad_normed = grad_normed + jnp.dot(

time: 150 us -> 150 us (level)
  no operation moved by 1% of the time
where the time goes in v11:
time: 150 us; the launch traced here: 148 us
  starting transfers between devices  73.5 us (49%)
  matrix products  28.7 us (19%)
  local copies, waits for them, and re-layouts  16.1 us (11%)
  waiting for transfers between devices  15 us (10%)
  other arithmetic  12.5 us (8%)
  between operations  2.65 us (2%)
    ppermute x8, starting transfers between devices, shifted(): return lax.ppermute(block, axis, route)  35 us
    ppermute x2, starting transfers between devices, extended_2(): lax.ppermute(lax.slice_in_dim(block, 0, width, axis=dim), axis, backward)  17.4 us
    ppermute x2, starting transfers between devices, extended_2(): lax.ppermute(lax.slice_in_dim(block, block.shape[dim] - width, None, axis...  6.74 us
    ppermute x1, starting transfers between devices, head_sum(): got = lax.ppermute(give.astype(jnp.bfloat16), axis, pair_near)  5.73 us
    ppermute x1, waiting for transfers between devices, head_sum(): got = lax.ppermute(give.astype(jnp.bfloat16), axis, pair_far)  5.35 us
    ppermute x1, waiting for transfers between devices, head_sum(): got = lax.ppermute(own, axis, pair_far)  4.42 us
    ppermute x1, starting transfers between devices, head_sum(): got = lax.ppermute(half, axis, pair_near)  4.03 us
  transfers between devices with their start and end apart: 16, of which 5 were waited for; matrix products, arithmetic and copies ran while one was open for 12% of the time, Pallas kernels for 0%

profile of v11, /device:TPU:1, one launch (start us, length us, event | category | flops | bytes accessed | tf_op | source)
XLA Modules:
  0.0 148.4 jit_solution(11001082355623145260)
XLA Ops:
  11.3 3.9 %collective-permute-start = (bf16[64,64]{0,1:T(8,128)(2,1)S(1)}, bf16[64,64]{0,1:T(8,128)(2,1)S(1)}, u32[]{:S(2)}, u32[]{:S(2)}) collective-permute-start(bf16[64,64]{0,1:T(8,128)(2,1)S(1)} %get-tuple-element.56), channel_id=1, source_target_pairs={{0,4},{4,8},{8,12},{12,16},{16,20},{20,24},{24,28},{28,32},{32,36}... | collective-permute-start | bytes 24584 | tf_op jit(solution)/shard_map/ppermute | solution.py:31
  15.3 14.8 %collective-permute-start.1 = (bf16[64,64]{0,1:T(8,128)(2,1)S(1)}, bf16[64,64]{0,1:T(8,128)(2,1)S(1)}, u32[]{:S(2)}, u32[]{:S(2)}) collective-permute-start(bf16[64,64]{0,1:T(8,128)(2,1)S(1)} %get-tuple-element.55), channel_id=1, source_target_pairs={{4,0},{8,4},{12,8},{16,12},{20,16},{24,20},{28,24},{32,28},{36,32}... | collective-permute-start | bytes 24584 | tf_op jit(solution)/shard_map/ppermute | solution.py:34
  38.5 2.3 %concatenate.56 = bf16[32,160,64]{1,2,0:T(8,128)(2,1)} concatenate(bf16[32,32,64]{1,2,0:T(8,128)(2,1)S(1)} %copy.91, bf16[32,32,64]{1,2,0:T(8,128)(2,1)S(1)} %copy.92, bf16[32,32,64]{1,2,0:T(8,128)(2,1)S(1)} %copy.93, bf16[32,32,64]{1,2,0:T(8,128)(2,1)S(1)} %copy.94, bf16[32,32,64]{1,2,0:T(8,128)(2,1)S(1)} %copy.95), dimensions={1} | concatenate | bytes 1310720 | tf_op jit(solution)/shard_map/concatenate | solution.py:287
  40.7 1.9 %fusion.11 = bf16[32,128,64]{1,2,0:T(8,128)(2,1)S(1)} fusion(bf16[32,160,64]{1,2,0:T(8,128)(2,1)} %concatenate.56, s32[32,128]{1,0:T(8,128)} %iota_add_fusion), kind=kOutput, calls=%fused_computation.15 | convolution fusion | flops 84803584 | bytes 1196032 | tf_op jit(solution)/shard_map/wrs,wsf->wrf/dot_general | solution.py:295
  43.9 1.8 %convolution_bitcast_fusion.1 = f32[32,32,1,32]{1,3,0,2:T(8,128)S(1)} fusion(bf16[32,128,64]{1,2,0:T(8,128)(2,1)S(1)} %fusion.11, f32[32,32]{1,0:T(8,128)S(1)} %get-tuple-element.60, f32[32,32,128]{2,1,0:T(8,128)S(1)} %fusion.17), kind=kOutput, calls=%fused_computation.23 | convolution fusion | flops 8782975 | bytes 1458176 | tf_op jit(solution)/shard_map/bhqk,bkhd->bqhd/dot_general | solution.py:114
  46.8 1.8 %convolution_bitcast_fusion = f32[32,128,32]{1,2,0:T(8,128)S(1)} fusion(bf16[32,32,32]{1,0,2:T(8,128)(2,1)S(1)} %reshape.430, f32[32,32]{1,0:T(8,128)S(1)} %get-tuple-element.60, f32[32,32,128]{2,1,0:T(8,128)S(1)} %fusion.17), kind=kOutput, calls=%fused_computation.22 | convolution fusion | flops 8782975 | bytes 1118208 | tf_op jit(solution)/shard_map/bhqk,bqhd->bkhd/dot_general | solution.py:136
  50.7 1.9 %collective-permute-start.2 = (bf16[128,192]{0,1:T(8,128)(2,1)}, bf16[128,192]{0,1:T(8,128)(2,1)S(1)}, u32[]{:S(2)}, u32[]{:S(2)}) collective-permute-start(bf16[128,192]{0,1:T(8,128)(2,1)} %pad_maximum_fusion.6), channel_id=1, source_target_pairs={{504,0},{508,4},{0,8},{4,12},{8,16},{12,20},{16,24},{20,28},{24,32... | collective-permute-start | bytes 147464 | tf_op jit(solution)/shard_map/ppermute | solution.py:22
  52.6 1.9 %collective-permute-start.3 = (bf16[128,192]{0,1:T(8,128)(2,1)}, bf16[128,192]{0,1:T(8,128)(2,1)S(1)}, u32[]{:S(2)}, u32[]{:S(2)}) collective-permute-start(bf16[128,192]{0,1:T(8,128)(2,1)} %pad_maximum_fusion.6), channel_id=1, source_target_pairs={{508,0},{0,4},{4,8},{8,12},{12,16},{16,20},{20,24},{24,28},{28,32}... | collective-permute-start | bytes 147464 | tf_op jit(solution)/shard_map/ppermute | solution.py:22
  54.5 9.1 %collective-permute-start.4 = (bf16[128,192]{0,1:T(8,128)(2,1)}, bf16[128,192]{0,1:T(8,128)(2,1)S(1)}, u32[]{:S(2)}, u32[]{:S(2)}) collective-permute-start(bf16[128,192]{0,1:T(8,128)(2,1)} %pad_maximum_fusion.6), channel_id=1, source_target_pairs={{4,0},{8,4},{12,8},{16,12},{20,16},{24,20},{28,24},{32,28},{36,32}... | collective-permute-start | bytes 147464 | tf_op jit(solution)/shard_map/ppermute | solution.py:22
  67.0 2.6 %collective-permute-start.7 = (bf16[64,64]{1,0:T(8,128)(2,1)S(1)}, bf16[64,64]{1,0:T(8,128)(2,1)S(1)}, u32[]{:S(2)}, u32[]{:S(2)}) collective-permute-start(bf16[64,64]{1,0:T(8,128)(2,1)S(1)} %bitcast.234), channel_id=1, source_target_pairs={{4,0},{8,4},{12,8},{16,12},{20,16},{24,20},{28,24},{32,28},{36,32}... | collective-permute-start | bytes 24584 | tf_op jit(solution)/shard_map/ppermute | solution.py:34
  69.6 2.8 %collective-permute-start.6 = (bf16[64,64]{1,0:T(8,128)(2,1)S(1)}, bf16[64,64]{1,0:T(8,128)(2,1)S(1)}, u32[]{:S(2)}, u32[]{:S(2)}) collective-permute-start(bf16[64,64]{1,0:T(8,128)(2,1)S(1)} %bitcast.232), channel_id=1, source_target_pairs={{0,4},{4,8},{8,12},{12,16},{16,20},{20,24},{24,28},{28,32},{32,36}... | collective-permute-start | bytes 24584 | tf_op jit(solution)/shard_map/ppermute | solution.py:31
  73.5 3.8 %collective-permute-start.5 = (bf16[128,192]{0,1:T(8,128)(2,1)}, bf16[128,192]{0,1:T(8,128)(2,1)S(1)}, u32[]{:S(2)}, u32[]{:S(2)}) collective-permute-start(bf16[128,192]{0,1:T(8,128)(2,1)} %pad_maximum_fusion.6), channel_id=1, source_target_pairs={{8,0},{12,4},{16,8},{20,12},{24,16},{28,20},{32,24},{36,28},{40,32... | collective-permute-start | bytes 147464 | tf_op jit(solution)/shard_map/ppermute | solution.py:22
  77.4 2.6 %collective-permute-done.6 = bf16[64,64]{1,0:T(8,128)(2,1)S(1)} collective-permute-done((bf16[64,64]{1,0:T(8,128)(2,1)S(1)}, bf16[64,64]{1,0:T(8,128)(2,1)S(1)}, u32[]{:S(2)}, u32[]{:S(2)}) %collective-permute-start.6) | collective-permute-done | bytes 8224 | tf_op jit(solution)/shard_map/ppermute | solution.py:31
  92.4 2.1 %fusion.139 = (bf16[5,24576]{1,0:T(8,128)(2,1)S(1)}, f32[5,24576]{1,0:T(8,128)}) fusion(f32[4,24576]{1,0:T(4,128)S(1)} %reshape.438, s32[4]{0:T(128)} %fusion.119), kind=kOutput, calls=%fused_computation.236 | convolution fusion | flops 3072020 | bytes 1130512 | tf_op jit(solution)/shard_map/bsc,bsx->cx/dot_general | solution.py:270
  95.6 1.9 %collective-permute-start.11 = (bf16[128,192]{1,0:T(8,128)(2,1)S(1)}, bf16[128,192]{1,0:T(8,128)(2,1)S(1)}, u32[]{:S(2)}, u32[]{:S(2)}) collective-permute-start(bf16[128,192]{1,0:T(8,128)(2,1)S(1)} %convert_element_type.226), channel_id=1, source_target_pairs={{504,0},{508,4},{0,8},{4,12},{8,16},{12,20},{16,24},{20,28},{24,32... | collective-permute-start | bytes 147464 | tf_op jit(solution)/shard_map/ppermute | solution.py:22
  97.7 4.4 %collective-permute-start.10 = (bf16[128,192]{1,0:T(8,128)(2,1)S(1)}, bf16[128,192]{1,0:T(8,128)(2,1)S(1)}, u32[]{:S(2)}, u32[]{:S(2)}) collective-permute-start(bf16[128,192]{1,0:T(8,128)(2,1)S(1)} %convert_element_type.224), channel_id=1, source_target_pairs={{508,0},{0,4},{4,8},{8,12},{12,16},{16,20},{20,24},{24,28},{28,32}... | collective-permute-start | bytes 147464 | tf_op jit(solution)/shard_map/ppermute | solution.py:22
  102.2 8.8 %collective-permute-start.9 = (bf16[128,192]{1,0:T(8,128)(2,1)S(1)}, bf16[128,192]{1,0:T(8,128)(2,1)S(1)}, u32[]{:S(2)}, u32[]{:S(2)}) collective-permute-start(bf16[128,192]{1,0:T(8,128)(2,1)S(1)} %convert_element_type.222), channel_id=1, source_target_pairs={{4,0},{8,4},{12,8},{16,12},{20,16},{24,20},{28,24},{32,28},{36,32}... | collective-permute-start | bytes 147464 | tf_op jit(solution)/shard_map/ppermute | solution.py:22
  111.1 3.1 %collective-permute-start.8 = (bf16[128,192]{1,0:T(8,128)(2,1)S(1)}, bf16[128,192]{1,0:T(8,128)(2,1)S(1)}, u32[]{:S(2)}, u32[]{:S(2)}) collective-permute-start(bf16[128,192]{1,0:T(8,128)(2,1)S(1)} %convert_element_type.220), channel_id=1, source_target_pairs={{8,0},{12,4},{16,8},{20,12},{24,16},{28,20},{32,24},{36,28},{40,32... | collective-permute-start | bytes 147464 | tf_op jit(solution)/shard_map/ppermute | solution.py:22
  119.0 5.7 %collective-permute-start.12 = (bf16[1408,128]{1,0:T(8,128)(2,1)S(1)}, bf16[1408,128]{1,0:T(8,128)(2,1)S(1)}, u32[]{:S(2)}, u32[]{:S(2)}) collective-permute-start(bf16[1408,128]{1,0:T(8,128)(2,1)S(1)} %select_convert_fusion), channel_id=1, source_target_pairs={{0,1},{1,0},{2,3},{3,2},{4,5},{5,4},{6,7},{7,6},{8,9},{9,8},{10,11... | collective-permute-start | bytes 1081352 | tf_op jit(solution)/shard_map/ppermute | solution.py:57
  126.1 2.3 %collective-permute-start.13 = (bf16[704,128]{1,0:T(8,128)(2,1)S(1)}, bf16[704,128]{1,0:T(8,128)(2,1)S(1)}, u32[]{:S(2)}, u32[]{:S(2)}) collective-permute-start(bf16[704,128]{1,0:T(8,128)(2,1)S(1)} %select_convert_fusion.1), channel_id=1, source_target_pairs={{0,2},{1,3},{2,0},{3,1},{4,6},{5,7},{6,4},{7,5},{8,10},{9,11},{10,... | collective-permute-start | bytes 540680 | tf_op jit(solution)/shard_map/ppermute | solution.py:61
  128.4 5.3 %collective-permute-done.13 = bf16[704,128]{1,0:T(8,128)(2,1)S(1)} collective-permute-done((bf16[704,128]{1,0:T(8,128)(2,1)S(1)}, bf16[704,128]{1,0:T(8,128)(2,1)S(1)}, u32[]{:S(2)}, u32[]{:S(2)}) %collective-permute-start.13) | collective-permute-done | bytes 180256 | tf_op jit(solution)/shard_map/ppermute | solution.py:61
  133.9 2.3 %collective-permute-start.14 = (bf16[704,128]{1,0:T(8,128)(2,1)S(1)}, bf16[704,128]{1,0:T(8,128)(2,1)S(1)}, u32[]{:S(2)}, u32[]{:S(2)}) collective-permute-start(bf16[704,128]{1,0:T(8,128)(2,1)S(1)} %add_convert_fusion), channel_id=1, source_target_pairs={{0,2},{1,3},{2,0},{3,1},{4,6},{5,7},{6,4},{7,5},{8,10},{9,11},{10,... | collective-permute-start | bytes 540680 | tf_op jit(solution)/shard_map/ppermute | solution.py:63
  136.2 4.4 %collective-permute-done.14 = bf16[704,128]{1,0:T(8,128)(2,1)S(1)} collective-permute-done((bf16[704,128]{1,0:T(8,128)(2,1)S(1)}, bf16[704,128]{1,0:T(8,128)(2,1)S(1)}, u32[]{:S(2)}, u32[]{:S(2)}) %collective-permute-start.14) | collective-permute-done | bytes 180256 | tf_op jit(solution)/shard_map/ppermute | solution.py:63
  140.7 4.0 %collective-permute-start.15 = (bf16[1408,128]{1,0:T(8,128)(2,1)S(1)}, bf16[1408,128]{1,0:T(8,128)(2,1)S(1)}, u32[]{:S(2)}, u32[]{:S(2)}) collective-permute-start(bf16[1408,128]{1,0:T(8,128)(2,1)S(1)} %maximum_select_fusion.1), channel_id=1, source_target_pairs={{0,1},{1,0},{2,3},{3,2},{4,5},{5,4},{6,7},{7,6},{8,9},{9,8},{10,11... | collective-permute-start | bytes 1081352 | tf_op jit(solution)/shard_map/ppermute | solution.py:67
  (206 shorter events, 50.0 us)
Async XLA Ops:
  0.6 45.7 %copy-start = (bf16[1024,128]{1,0:T(8,128)(2,1)S(1)}, bf16[1024,128]{1,0:T(8,128)(2,1)}, u32[]{:S(2)}) copy-start(bf16[1024,128]{1,0:T(8,128)(2,1)} %param.33) | copy-start | bytes 786436
  0.7 29.4 %copy-start.5 = (bf16[4,384,96]{1,2,0:T(8,128)(2,1)S(1)}, bf16[4,384,96]{1,2,0:T(8,128)(2,1)}, u32[]{:S(2)}) copy-start(bf16[4,384,96]{1,2,0:T(8,128)(2,1)} %param.21) | copy-start | bytes 884740
  1.8 30.6 %copy-start.27 = (s32[32]{0:T(128)S(1)}, s32[32]{0:T(128)}, u32[]{:S(2)}) copy-start(s32[32]{0:T(128)} %param.31) | copy-start | bytes 388
  1.8 32.5 %copy-start.28 = (s32[1,4]{1,0:T(1,128)S(1)}, s32[1,4]{1,0:T(1,128)}, u32[]{:S(2)}) copy-start(s32[1,4]{1,0:T(1,128)} %param.28) | copy-start | bytes 52
  11.3 24.5 %collective-permute-start = (bf16[64,64]{0,1:T(8,128)(2,1)S(1)}, bf16[64,64]{0,1:T(8,128)(2,1)S(1)}, u32[]{:S(2)}, u32[]{:S(2)}) collective-permute-start(bf16[64,64]{0,1:T(8,128)(2,1)S(1)} %get-tuple-element.56), channel_id=1, source_target_pairs={{0,4},{4,8},{8,12},{12,16},{16,20},{20,24},{24,28},{28,32},{32,36}... | collective-permute-start | bytes 24584 | tf_op jit(solution)/shard_map/ppermute | solution.py:31
  15.3 20.5 %collective-permute-start.1 = (bf16[64,64]{0,1:T(8,128)(2,1)S(1)}, bf16[64,64]{0,1:T(8,128)(2,1)S(1)}, u32[]{:S(2)}, u32[]{:S(2)}) collective-permute-start(bf16[64,64]{0,1:T(8,128)(2,1)S(1)} %get-tuple-element.55), channel_id=1, source_target_pairs={{4,0},{8,4},{12,8},{16,12},{20,16},{24,20},{28,24},{32,28},{36,32}... | collective-permute-start | bytes 24584 | tf_op jit(solution)/shard_map/ppermute | solution.py:34
  50.7 32.7 %collective-permute-start.2 = (bf16[128,192]{0,1:T(8,128)(2,1)}, bf16[128,192]{0,1:T(8,128)(2,1)S(1)}, u32[]{:S(2)}, u32[]{:S(2)}) collective-permute-start(bf16[128,192]{0,1:T(8,128)(2,1)} %pad_maximum_fusion.6), channel_id=1, source_target_pairs={{504,0},{508,4},{0,8},{4,12},{8,16},{12,20},{16,24},{20,28},{24,32... | collective-permute-start | bytes 147464 | tf_op jit(solution)/shard_map/ppermute | solution.py:22
  52.6 31.0 %collective-permute-start.3 = (bf16[128,192]{0,1:T(8,128)(2,1)}, bf16[128,192]{0,1:T(8,128)(2,1)S(1)}, u32[]{:S(2)}, u32[]{:S(2)}) collective-permute-start(bf16[128,192]{0,1:T(8,128)(2,1)} %pad_maximum_fusion.6), channel_id=1, source_target_pairs={{508,0},{0,4},{4,8},{8,12},{12,16},{16,20},{20,24},{24,28},{28,32}... | collective-permute-start | bytes 147464 | tf_op jit(solution)/shard_map/ppermute | solution.py:22
  54.5 29.3 %collective-permute-start.4 = (bf16[128,192]{0,1:T(8,128)(2,1)}, bf16[128,192]{0,1:T(8,128)(2,1)S(1)}, u32[]{:S(2)}, u32[]{:S(2)}) collective-permute-start(bf16[128,192]{0,1:T(8,128)(2,1)} %pad_maximum_fusion.6), channel_id=1, source_target_pairs={{4,0},{8,4},{12,8},{16,12},{20,16},{24,20},{28,24},{32,28},{36,32}... | collective-permute-start | bytes 147464 | tf_op jit(solution)/shard_map/ppermute | solution.py:22
  67.0 6.5 %collective-permute-start.7 = (bf16[64,64]{1,0:T(8,128)(2,1)S(1)}, bf16[64,64]{1,0:T(8,128)(2,1)S(1)}, u32[]{:S(2)}, u32[]{:S(2)}) collective-permute-start(bf16[64,64]{1,0:T(8,128)(2,1)S(1)} %bitcast.234), channel_id=1, source_target_pairs={{4,0},{8,4},{12,8},{16,12},{20,16},{24,20},{28,24},{32,28},{36,32}... | collective-permute-start | bytes 24584 | tf_op jit(solution)/shard_map/ppermute | solution.py:34
  69.6 10.4 %collective-permute-start.6 = (bf16[64,64]{1,0:T(8,128)(2,1)S(1)}, bf16[64,64]{1,0:T(8,128)(2,1)S(1)}, u32[]{:S(2)}, u32[]{:S(2)}) collective-permute-start(bf16[64,64]{1,0:T(8,128)(2,1)S(1)} %bitcast.232), channel_id=1, source_target_pairs={{0,4},{4,8},{8,12},{12,16},{16,20},{20,24},{24,28},{28,32},{32,36}... | collective-permute-start | bytes 24584 | tf_op jit(solution)/shard_map/ppermute | solution.py:31
  73.5 10.6 %collective-permute-start.5 = (bf16[128,192]{0,1:T(8,128)(2,1)}, bf16[128,192]{0,1:T(8,128)(2,1)S(1)}, u32[]{:S(2)}, u32[]{:S(2)}) collective-permute-start(bf16[128,192]{0,1:T(8,128)(2,1)} %pad_maximum_fusion.6), channel_id=1, source_target_pairs={{8,0},{12,4},{16,8},{20,12},{24,16},{28,20},{32,24},{36,28},{40,32... | collective-permute-start | bytes 147464 | tf_op jit(solution)/shard_map/ppermute | solution.py:22
  92.3 25.6 %copy-start.6 = (bf16[4,384,96]{1,2,0:T(8,128)(2,1)S(1)}, bf16[4,384,96]{1,2,0:T(8,128)(2,1)}, u32[]{:S(2)}) copy-start(bf16[4,384,96]{1,2,0:T(8,128)(2,1)} %param.21) | copy-start | bytes 884740
  92.3 26.0 %copy-start.2 = (bf16[128,384]{1,0:T(8,128)(2,1)S(1)}, bf16[128,384]{1,0:T(8,128)(2,1)}, u32[]{:S(2)}) copy-start(bf16[128,384]{1,0:T(8,128)(2,1)} %param.17) | copy-start | bytes 294916
  92.4 26.0 %copy-start.20 = (f32[384]{0:T(512)S(1)}, f32[384]{0:T(512)}, u32[]{:S(2)}) copy-start(f32[384]{0:T(512)} %param.19) | copy-start | bytes 4612
  92.4 26.0 %copy-start.22 = (f32[128]{0:T(128)S(1)}, f32[128]{0:T(128)}, u32[]{:S(2)}) copy-start(f32[128]{0:T(128)} %copy-done.21) | copy-start | bytes 1540
  95.6 22.2 %collective-permute-start.11 = (bf16[128,192]{1,0:T(8,128)(2,1)S(1)}, bf16[128,192]{1,0:T(8,128)(2,1)S(1)}, u32[]{:S(2)}, u32[]{:S(2)}) collective-permute-start(bf16[128,192]{1,0:T(8,128)(2,1)S(1)} %convert_element_type.226), channel_id=1, source_target_pairs={{504,0},{508,4},{0,8},{4,12},{8,16},{12,20},{16,24},{20,28},{24,32... | collective-permute-start | bytes 147464 | tf_op jit(solution)/shard_map/ppermute | solution.py:22
  97.7 20.2 %collective-permute-start.10 = (bf16[128,192]{1,0:T(8,128)(2,1)S(1)}, bf16[128,192]{1,0:T(8,128)(2,1)S(1)}, u32[]{:S(2)}, u32[]{:S(2)}) collective-permute-start(bf16[128,192]{1,0:T(8,128)(2,1)S(1)} %convert_element_type.224), channel_id=1, source_target_pairs={{508,0},{0,4},{4,8},{8,12},{12,16},{16,20},{20,24},{24,28},{28,32}... | collective-permute-start | bytes 147464 | tf_op jit(solution)/shard_map/ppermute | solution.py:22
  102.2 15.7 %collective-permute-start.9 = (bf16[128,192]{1,0:T(8,128)(2,1)S(1)}, bf16[128,192]{1,0:T(8,128)(2,1)S(1)}, u32[]{:S(2)}, u32[]{:S(2)}) collective-permute-start(bf16[128,192]{1,0:T(8,128)(2,1)S(1)} %convert_element_type.222), channel_id=1, source_target_pairs={{4,0},{8,4},{12,8},{16,12},{20,16},{24,20},{28,24},{32,28},{36,32}... | collective-permute-start | bytes 147464 | tf_op jit(solution)/shard_map/ppermute | solution.py:22
  111.1 6.7 %collective-permute-start.8 = (bf16[128,192]{1,0:T(8,128)(2,1)S(1)}, bf16[128,192]{1,0:T(8,128)(2,1)S(1)}, u32[]{:S(2)}, u32[]{:S(2)}) collective-permute-start(bf16[128,192]{1,0:T(8,128)(2,1)S(1)} %convert_element_type.220), channel_id=1, source_target_pairs={{8,0},{12,4},{16,8},{20,12},{24,16},{28,20},{32,24},{36,28},{40,32... | collective-permute-start | bytes 147464 | tf_op jit(solution)/shard_map/ppermute | solution.py:22
  119.0 7.0 %collective-permute-start.12 = (bf16[1408,128]{1,0:T(8,128)(2,1)S(1)}, bf16[1408,128]{1,0:T(8,128)(2,1)S(1)}, u32[]{:S(2)}, u32[]{:S(2)}) collective-permute-start(bf16[1408,128]{1,0:T(8,128)(2,1)S(1)} %select_convert_fusion), channel_id=1, source_target_pairs={{0,1},{1,0},{2,3},{3,2},{4,5},{5,4},{6,7},{7,6},{8,9},{9,8},{10,11... | collective-permute-start | bytes 1081352 | tf_op jit(solution)/shard_map/ppermute | solution.py:57
  126.1 7.7 %collective-permute-start.13 = (bf16[704,128]{1,0:T(8,128)(2,1)S(1)}, bf16[704,128]{1,0:T(8,128)(2,1)S(1)}, u32[]{:S(2)}, u32[]{:S(2)}) collective-permute-start(bf16[704,128]{1,0:T(8,128)(2,1)S(1)} %select_convert_fusion.1), channel_id=1, source_target_pairs={{0,2},{1,3},{2,0},{3,1},{4,6},{5,7},{6,4},{7,5},{8,10},{9,11},{10,... | collective-permute-start | bytes 540680 | tf_op jit(solution)/shard_map/ppermute | solution.py:61
  133.9 6.7 %collective-permute-start.14 = (bf16[704,128]{1,0:T(8,128)(2,1)S(1)}, bf16[704,128]{1,0:T(8,128)(2,1)S(1)}, u32[]{:S(2)}, u32[]{:S(2)}) collective-permute-start(bf16[704,128]{1,0:T(8,128)(2,1)S(1)} %add_convert_fusion), channel_id=1, source_target_pairs={{0,2},{1,3},{2,0},{3,1},{4,6},{5,7},{6,4},{7,5},{8,10},{9,11},{10,... | collective-permute-start | bytes 540680 | tf_op jit(solution)/shard_map/ppermute | solution.py:63
  140.7 5.3 %collective-permute-start.15 = (bf16[1408,128]{1,0:T(8,128)(2,1)S(1)}, bf16[1408,128]{1,0:T(8,128)(2,1)S(1)}, u32[]{:S(2)}, u32[]{:S(2)}) collective-permute-start(bf16[1408,128]{1,0:T(8,128)(2,1)S(1)} %maximum_select_fusion.1), channel_id=1, source_target_pairs={{0,1},{1,0},{2,3},{3,2},{4,5},{5,4},{6,7},{7,6},{8,9},{9,8},{10,11... | collective-permute-start | bytes 1081352 | tf_op jit(solution)/shard_map/ppermute | solution.py:67
  (22 other events, 207.0 us)

commit v12 on v11

--- a/solution.py
+++ b/solution.py
@@ -77,6 +77,17 @@
         start += width * rows_here
         outs.append(jnp.concatenate(cols, axis=1) if width > 1 else cols[0])
     return outs
+
+
+def head_sum_small(part, axis):
+    count = lax.axis_size(axis)
+    low = part.astype(jnp.bfloat16)
+    if count != 4:
+        return lax.psum(low, axis)
+    got = lax.ppermute(low, axis, [(i, i ^ 1) for i in range(count)])
+    low = (low.astype(jnp.float32) + got.astype(jnp.float32)).astype(jnp.bfloat16)
+    got = lax.ppermute(low, axis, [(i, i ^ 2) for i in range(count)])
+    return low.astype(jnp.float32) + got.astype(jnp.float32)
 
 
 def norm_rows(inputs, gains):
@@ -381,9 +392,8 @@
             token_grads[which], w_token[which].T, preferred_element_type=jnp.float32
         )
     single_part = norm_back(single.astype(jnp.float32), gain_single, grad_normed)
-    token_total, atom_total, single_total, atoms_total = head_sum(
-        [token_part, atom_part, single_part, atoms_part], "head"
-    )
+    token_total, atom_total, atoms_total = head_sum([token_part, atom_part, atoms_part], "head")
+    single_total = head_sum_small(single_part, "head")
     return (
         token_total.astype(jnp.bfloat16),
         atom_total.astype(jnp.bfloat16),

time: 150 us -> 155 us (1.033)
  waiting for transfers between devices: 15 us -> 1.2 us
  starting transfers between devices: 73.5 us -> 84.2 us
  other arithmetic: 12.5 us -> 19.4 us
  local copies, waits for them, and re-layouts: 16.1 us -> 21.2 us
  matrix products: 28.7 us -> 25 us
    ppermute x0 -> x2, starting transfers between devices: none -> 7.46 us  [the longest x1 5.17 us: head_sum_small(): got = lax.ppermute(low, axis, [(i, i ^ 1) for i in range(count)])]
    ppermute x2, starting transfers between devices: 17.4 us -> 23.8 us  [extended_2(): lax.ppermute(lax.slice_in_dim(block, 0, width, axis=dim), axis, backward)]
    ppermute x8, starting transfers between devices: 35 us -> 29.5 us  [shifted(): return lax.ppermute(block, axis, route)]
    ppermute x1, waiting for transfers between devices: 5.35 us -> 0.01 us  [head_sum(): got = lax.ppermute(give.astype(jnp.bfloat16), axis, pair_far)]
    sub x1, other arithmetic: 1.01 us -> 5.4 us  [attend_local(): exponent = jnp.exp(scores - row_max)]
    ppermute x1, waiting for transfers between devices: 4.42 us -> 0.63 us  [head_sum(): got = lax.ppermute(own, axis, pair_far)]
    ppermute x2, waiting for transfers between devices: 2.63 us -> 0.01 us  [extended_2(): lax.ppermute(lax.slice_in_dim(block, block.shape[dim] - width, None, axis...]
    ppermute x1, starting transfers between devices: 4.03 us -> 6.58 us  [head_sum(): got = lax.ppermute(half, axis, pair_near)]
  transfers between devices with their start and end apart: 16 -> 18, of which waited for: 5 -> 2; matrix products, arithmetic and copies ran while one was open for 12% -> 27% of each run, Pallas kernels for 0% -> 0%
where the time goes in v12:
time: 155 us; the launch traced here: 154 us
  starting transfers between devices  84.2 us (54%)
  matrix products  25 us (16%)
  local copies, waits for them, and re-layouts  21.2 us (14%)
  other arithmetic  19.4 us (13%)
  between operations  2.68 us (2%)
    ppermute x8, starting transfers between devices, shifted(): return lax.ppermute(block, axis, route)  29.5 us
    ppermute x2, starting transfers between devices, extended_2(): lax.ppermute(lax.slice_in_dim(block, 0, width, axis=dim), axis, backward)  23.8 us
    ppermute x1, starting transfers between devices, head_sum(): got = lax.ppermute(half, axis, pair_near)  6.58 us
    ppermute x2, starting transfers between devices, extended_2(): lax.ppermute(lax.slice_in_dim(block, block.shape[dim] - width, None, axis...  5.86 us
    ppermute x1, starting transfers between devices, head_sum(): got = lax.ppermute(give.astype(jnp.bfloat16), axis, pair_near)  5.7 us
    sub x1, other arithmetic, attend_local(): exponent = jnp.exp(scores - row_max)  5.4 us
    ppermute x1, starting transfers between devices, head_sum_small(): got = lax.ppermute(low, axis, [(i, i ^ 1) for i in range(count)])  5.17 us
  transfers between devices with their start and end apart: 18, of which 2 were waited for; matrix products, arithmetic and copies ran while one was open for 27% of the time, Pallas kernels for 0%

profile of v12, /device:TPU:1, one launch (start us, length us, event | category | flops | bytes accessed | tf_op | source)
XLA Modules:
  0.0 153.8 jit_solution(4375896616743903992)
XLA Ops:
  8.7 1.5 fusion.19
  11.3 3.9 %collective-permute-start = (bf16[64,64]{0,1:T(8,128)(2,1)S(1)}, bf16[64,64]{0,1:T(8,128)(2,1)S(1)}, u32[]{:S(2)}, u32[]{:S(2)}) collective-permute-start(bf16[64,64]{0,1:T(8,128)(2,1)S(1)} %get-tuple-element.50), channel_id=1, source_target_pairs={{0,4},{4,8},{8,12},{12,16},{16,20},{20,24},{24,28},{28,32},{32,36}... | collective-permute-start | bytes 24584 | tf_op jit(solution)/shard_map/ppermute | solution.py:31
  15.3 14.8 %collective-permute-start.1 = (bf16[64,64]{0,1:T(8,128)(2,1)S(1)}, bf16[64,64]{0,1:T(8,128)(2,1)S(1)}, u32[]{:S(2)}, u32[]{:S(2)}) collective-permute-start(bf16[64,64]{0,1:T(8,128)(2,1)S(1)} %get-tuple-element.49), channel_id=1, source_target_pairs={{4,0},{8,4},{12,8},{16,12},{20,16},{24,20},{28,24},{32,28},{36,32}... | collective-permute-start | bytes 24584 | tf_op jit(solution)/shard_map/ppermute | solution.py:34
  36.0 1.9 %collective-permute-start.2 = (bf16[128,192]{0,1:T(8,128)(2,1)}, bf16[128,192]{0,1:T(8,128)(2,1)}, u32[]{:S(2)}, u32[]{:S(2)}) collective-permute-start(bf16[128,192]{0,1:T(8,128)(2,1)} %pad_maximum_fusion.7), channel_id=1, source_target_pairs={{504,0},{508,4},{0,8},{4,12},{8,16},{12,20},{16,24},{20,28},{24,32... | collective-permute-start | bytes 147464 | tf_op jit(solution)/shard_map/ppermute | solution.py:22
  38.0 1.9 %collective-permute-start.3 = (bf16[128,192]{0,1:T(8,128)(2,1)}, bf16[128,192]{0,1:T(8,128)(2,1)}, u32[]{:S(2)}, u32[]{:S(2)}) collective-permute-start(bf16[128,192]{0,1:T(8,128)(2,1)} %pad_maximum_fusion.7), channel_id=1, source_target_pairs={{508,0},{0,4},{4,8},{8,12},{12,16},{16,20},{20,24},{24,28},{28,32}... | collective-permute-start | bytes 147464 | tf_op jit(solution)/shard_map/ppermute | solution.py:22
  39.9 9.1 %collective-permute-start.4 = (bf16[128,192]{0,1:T(8,128)(2,1)}, bf16[128,192]{0,1:T(8,128)(2,1)}, u32[]{:S(2)}, u32[]{:S(2)}) collective-permute-start(bf16[128,192]{0,1:T(8,128)(2,1)} %pad_maximum_fusion.7), channel_id=1, source_target_pairs={{4,0},{8,4},{12,8},{16,12},{20,16},{24,20},{28,24},{32,28},{36,32}... | collective-permute-start | bytes 147464 | tf_op jit(solution)/shard_map/ppermute | solution.py:22
  51.5 2.3 %concatenate.53 = bf16[32,160,64]{1,2,0:T(8,128)(2,1)} concatenate(bf16[32,32,64]{1,2,0:T(8,128)(2,1)S(1)} %copy.91, bf16[32,32,64]{1,2,0:T(8,128)(2,1)S(1)} %copy.92, bf16[32,32,64]{1,2,0:T(8,128)(2,1)S(1)} %copy.93, bf16[32,32,64]{1,2,0:T(8,128)(2,1)S(1)} %copy.94, bf16[32,32,64]{1,2,0:T(8,128)(2,1)S(1)} %copy.95), dimensions={1} | concatenate | bytes 1310720 | tf_op jit(solution)/shard_map/concatenate | solution.py:298
  53.7 1.9 %fusion.11 = bf16[32,128,64]{1,2,0:T(8,128)(2,1)S(1)} fusion(bf16[32,160,64]{1,2,0:T(8,128)(2,1)} %concatenate.53, s32[32,128]{1,0:T(8,128)} %iota_add_fusion), kind=kOutput, calls=%fused_computation.15 | convolution fusion | flops 84803584 | bytes 1196032 | tf_op jit(solution)/shard_map/wrs,wsf->wrf/dot_general | solution.py:306
  55.9 5.4 %fusion.137 = (f32[32,32]{1,0:T(8,128)S(1)}, f32[32,32,128]{2,1,0:T(8,128)S(1)}) fusion(f32[32,32,128]{2,1,0:T(8,128)S(1)} %fusion.17), kind=kOutput, calls=%fused_computation.237 | output fusion | flops 262271 | bytes 1052672 | tf_op jit(solution)/shard_map/sub | solution.py:122
  61.3 2.6 %convolution_bitcast_fusion.1 = f32[32,32,1,32]{1,3,0,2:T(8,128)} fusion(bf16[32,128,64]{1,2,0:T(8,128)(2,1)S(1)} %fusion.11, f32[32,32]{1,0:T(8,128)S(1)} %get-tuple-element.54, f32[32,32,128]{2,1,0:T(8,128)S(1)} %fusion.17), kind=kOutput, calls=%fused_computation.23 | convolution fusion | flops 8782975 | bytes 1458176 | tf_op jit(solution)/shard_map/bhqk,bkhd->bqhd/dot_general | solution.py:125
  66.0 1.8 %convolution_bitcast_fusion = f32[32,128,32]{1,2,0:T(8,128)S(1)} fusion(bf16[32,32,32]{1,0,2:T(8,128)(2,1)S(1)} %reshape.430, f32[32,32]{1,0:T(8,128)S(1)} %get-tuple-element.54, f32[32,32,128]{2,1,0:T(8,128)S(1)} %fusion.17), kind=kOutput, calls=%fused_computation.22 | convolution fusion | flops 8782975 | bytes 1118208 | tf_op jit(solution)/shard_map/bhqk,bqhd->bkhd/dot_general | solution.py:147
  70.9 1.9 %collective-permute-start.6 = (bf16[64,64]{1,0:T(8,128)(2,1)S(1)}, bf16[64,64]{1,0:T(8,128)(2,1)S(1)}, u32[]{:S(2)}, u32[]{:S(2)}) collective-permute-start(bf16[64,64]{1,0:T(8,128)(2,1)S(1)} %bitcast.232), channel_id=1, source_target_pairs={{0,4},{4,8},{8,12},{12,16},{16,20},{20,24},{24,28},{28,32},{32,36}... | collective-permute-start | bytes 24584 | tf_op jit(solution)/shard_map/ppermute | solution.py:31
  72.8 9.1 %collective-permute-start.7 = (bf16[64,64]{1,0:T(8,128)(2,1)S(1)}, bf16[64,64]{1,0:T(8,128)(2,1)S(1)}, u32[]{:S(2)}, u32[]{:S(2)}) collective-permute-start(bf16[64,64]{1,0:T(8,128)(2,1)S(1)} %bitcast.234), channel_id=1, source_target_pairs={{4,0},{8,4},{12,8},{16,12},{20,16},{24,20},{28,24},{32,28},{36,32}... | collective-permute-start | bytes 24584 | tf_op jit(solution)/shard_map/ppermute | solution.py:34
  83.7 2.1 %collective-permute-start.5 = (bf16[128,192]{0,1:T(8,128)(2,1)}, bf16[128,192]{0,1:T(8,128)(2,1)S(1)}, u32[]{:S(2)}, u32[]{:S(2)}) collective-permute-start(bf16[128,192]{0,1:T(8,128)(2,1)} %pad_maximum_fusion.7), channel_id=1, source_target_pairs={{8,0},{12,4},{16,8},{20,12},{24,16},{28,20},{32,24},{36,28},{40,32... | collective-permute-start | bytes 147464 | tf_op jit(solution)/shard_map/ppermute | solution.py:22
  101.8 5.0 %collective-permute-start.12 = (bf16[128,192]{1,0:T(8,128)(2,1)}, bf16[128,192]{1,0:T(8,128)(2,1)}, u32[]{:S(2)}, u32[]{:S(2)}) collective-permute-start(bf16[128,192]{1,0:T(8,128)(2,1)} %convert_element_type.246), channel_id=1, source_target_pairs={{8,0},{12,4},{16,8},{20,12},{24,16},{28,20},{32,24},{36,28},{40,32... | collective-permute-start | bytes 147464 | tf_op jit(solution)/shard_map/ppermute | solution.py:22
  107.5 3.4 %collective-permute-start.13 = (bf16[128,192]{1,0:T(8,128)(2,1)}, bf16[128,192]{1,0:T(8,128)(2,1)}, u32[]{:S(2)}, u32[]{:S(2)}) collective-permute-start(bf16[128,192]{1,0:T(8,128)(2,1)} %convert_element_type.248), channel_id=1, source_target_pairs={{4,0},{8,4},{12,8},{16,12},{20,16},{24,20},{28,24},{32,28},{36,32}... | collective-permute-start | bytes 147464 | tf_op jit(solution)/shard_map/ppermute | solution.py:22
  111.6 2.5 %collective-permute-start.14 = (bf16[128,192]{1,0:T(8,128)(2,1)}, bf16[128,192]{1,0:T(8,128)(2,1)}, u32[]{:S(2)}, u32[]{:S(2)}) collective-permute-start(bf16[128,192]{1,0:T(8,128)(2,1)} %convert_element_type.250), channel_id=1, source_target_pairs={{508,0},{0,4},{4,8},{8,12},{12,16},{16,20},{20,24},{24,28},{28,32}... | collective-permute-start | bytes 147464 | tf_op jit(solution)/shard_map/ppermute | solution.py:22
  114.8 3.7 %collective-permute-start.15 = (bf16[128,192]{1,0:T(8,128)(2,1)}, bf16[128,192]{1,0:T(8,128)(2,1)S(1)}, u32[]{:S(2)}, u32[]{:S(2)}) collective-permute-start(bf16[128,192]{1,0:T(8,128)(2,1)} %convert_element_type.252), channel_id=1, source_target_pairs={{504,0},{508,4},{0,8},{4,12},{8,16},{12,20},{16,24},{20,28},{24,32... | collective-permute-start | bytes 147464 | tf_op jit(solution)/shard_map/ppermute | solution.py:22
  121.4 5.7 %collective-permute-start.8 = (bf16[1216,128]{1,0:T(8,128)(2,1)}, bf16[1216,128]{1,0:T(8,128)(2,1)}, u32[]{:S(2)}, u32[]{:S(2)}) collective-permute-start(bf16[1216,128]{1,0:T(8,128)(2,1)} %select_convert_fusion), channel_id=1, source_target_pairs={{0,1},{1,0},{2,3},{3,2},{4,5},{5,4},{6,7},{7,6},{8,9},{9,8},{10,11... | collective-permute-start | bytes 933896 | tf_op jit(solution)/shard_map/ppermute | solution.py:57
  130.6 2.3 %collective-permute-start.9 = (bf16[608,128]{1,0:T(8,128)(2,1)S(1)}, bf16[608,128]{1,0:T(8,128)(2,1)S(1)}, u32[]{:S(2)}, u32[]{:S(2)}) collective-permute-start(bf16[608,128]{1,0:T(8,128)(2,1)S(1)} %select_convert_fusion.1), channel_id=1, source_target_pairs={{0,2},{1,3},{2,0},{3,1},{4,6},{5,7},{6,4},{7,5},{8,10},{9,11},{10,... | collective-permute-start | bytes 466952 | tf_op jit(solution)/shard_map/ppermute | solution.py:61
  133.0 5.2 %collective-permute-start.16 = (bf16[128,384]{1,0:T(8,128)(2,1)S(1)}, bf16[128,384]{1,0:T(8,128)(2,1)S(1)}, u32[]{:S(2)}, u32[]{:S(2)}) collective-permute-start(bf16[128,384]{1,0:T(8,128)(2,1)S(1)} %fusion.67), channel_id=1, source_target_pairs={{0,1},{1,0},{2,3},{3,2},{4,5},{5,4},{6,7},{7,6},{8,9},{9,8},{10,11... | collective-permute-start | bytes 294920 | tf_op jit(solution)/shard_map/ppermute | solution.py:87
  138.2 3.0 %collective-permute-start.10 = (bf16[608,128]{1,0:T(8,128)(2,1)S(1)}, bf16[608,128]{1,0:T(8,128)(2,1)S(1)}, u32[]{:S(2)}, u32[]{:S(2)}) collective-permute-start(bf16[608,128]{1,0:T(8,128)(2,1)S(1)} %add_convert_fusion), channel_id=1, source_target_pairs={{0,2},{1,3},{2,0},{3,1},{4,6},{5,7},{6,4},{7,5},{8,10},{9,11},{10,... | collective-permute-start | bytes 466952 | tf_op jit(solution)/shard_map/ppermute | solution.py:63
  141.3 2.3 %collective-permute-start.17 = (bf16[128,384]{1,0:T(8,128)(2,1)S(1)}, bf16[128,384]{1,0:T(8,128)(2,1)S(1)}, u32[]{:S(2)}, u32[]{:S(2)}) collective-permute-start(bf16[128,384]{1,0:T(8,128)(2,1)S(1)} %add_convert_fusion.2), channel_id=1, source_target_pairs={{0,2},{1,3},{2,0},{3,1},{4,6},{5,7},{6,4},{7,5},{8,10},{9,11},{10,... | collective-permute-start | bytes 294920 | tf_op jit(solution)/shard_map/ppermute | solution.py:89
  144.3 6.6 %collective-permute-start.11 = (bf16[1216,128]{1,0:T(8,128)(2,1)S(1)}, bf16[1216,128]{1,0:T(8,128)(2,1)S(1)}, u32[]{:S(2)}, u32[]{:S(2)}) collective-permute-start(bf16[1216,128]{1,0:T(8,128)(2,1)S(1)} %maximum_select_fusion.1), channel_id=1, source_target_pairs={{0,1},{1,0},{2,3},{3,2},{4,5},{5,4},{6,7},{7,6},{8,9},{9,8},{10,11... | collective-permute-start | bytes 933896 | tf_op jit(solution)/shard_map/ppermute | solution.py:67
  (214 shorter events, 51.4 us)
Async XLA Ops:
  0.6 65.0 %copy-start = (bf16[1024,128]{1,0:T(8,128)(2,1)S(1)}, bf16[1024,128]{1,0:T(8,128)(2,1)}, u32[]{:S(2)}) copy-start(bf16[1024,128]{1,0:T(8,128)(2,1)} %param.33) | copy-start | bytes 786436
  0.7 29.4 %copy-start.5 = (bf16[4,384,96]{1,2,0:T(8,128)(2,1)S(1)}, bf16[4,384,96]{1,2,0:T(8,128)(2,1)}, u32[]{:S(2)}) copy-start(bf16[4,384,96]{1,2,0:T(8,128)(2,1)} %param.21) | copy-start | bytes 884740
  2.8 30.9 %copy-start.29 = (s32[32]{0:T(128)S(1)}, s32[32]{0:T(128)}, u32[]{:S(2)}) copy-start(s32[32]{0:T(128)} %param.31) | copy-start | bytes 388
  2.9 31.5 %copy-start.30 = (s32[1,4]{1,0:T(1,128)S(1)}, s32[1,4]{1,0:T(1,128)}, u32[]{:S(2)}) copy-start(s32[1,4]{1,0:T(1,128)} %param.28) | copy-start | bytes 52
  6.6 29.3 %copy-start.19 = (s32[1024]{0:T(1024)}, s32[1024]{0:T(1024)S(1)}, u32[]{:S(2)}) copy-start(s32[1024]{0:T(1024)S(1)} %convert_reduce_fusion.1) | copy-start | bytes 12292
  11.3 24.5 %collective-permute-start = (bf16[64,64]{0,1:T(8,128)(2,1)S(1)}, bf16[64,64]{0,1:T(8,128)(2,1)S(1)}, u32[]{:S(2)}, u32[]{:S(2)}) collective-permute-start(bf16[64,64]{0,1:T(8,128)(2,1)S(1)} %get-tuple-element.50), channel_id=1, source_target_pairs={{0,4},{4,8},{8,12},{12,16},{16,20},{20,24},{24,28},{28,32},{32,36}... | collective-permute-start | bytes 24584 | tf_op jit(solution)/shard_map/ppermute | solution.py:31
  15.3 20.6 %collective-permute-start.1 = (bf16[64,64]{0,1:T(8,128)(2,1)S(1)}, bf16[64,64]{0,1:T(8,128)(2,1)S(1)}, u32[]{:S(2)}, u32[]{:S(2)}) collective-permute-start(bf16[64,64]{0,1:T(8,128)(2,1)S(1)} %get-tuple-element.49), channel_id=1, source_target_pairs={{4,0},{8,4},{12,8},{16,12},{20,16},{24,20},{28,24},{32,28},{36,32}... | collective-permute-start | bytes 24584 | tf_op jit(solution)/shard_map/ppermute | solution.py:34
  36.0 52.5 %collective-permute-start.2 = (bf16[128,192]{0,1:T(8,128)(2,1)}, bf16[128,192]{0,1:T(8,128)(2,1)}, u32[]{:S(2)}, u32[]{:S(2)}) collective-permute-start(bf16[128,192]{0,1:T(8,128)(2,1)} %pad_maximum_fusion.7), channel_id=1, source_target_pairs={{504,0},{508,4},{0,8},{4,12},{8,16},{12,20},{16,24},{20,28},{24,32... | collective-permute-start | bytes 147464 | tf_op jit(solution)/shard_map/ppermute | solution.py:22
  38.0 51.6 %collective-permute-start.3 = (bf16[128,192]{0,1:T(8,128)(2,1)}, bf16[128,192]{0,1:T(8,128)(2,1)}, u32[]{:S(2)}, u32[]{:S(2)}) collective-permute-start(bf16[128,192]{0,1:T(8,128)(2,1)} %pad_maximum_fusion.7), channel_id=1, source_target_pairs={{508,0},{0,4},{4,8},{8,12},{12,16},{16,20},{20,24},{24,28},{28,32}... | collective-permute-start | bytes 147464 | tf_op jit(solution)/shard_map/ppermute | solution.py:22
  39.9 50.7 %collective-permute-start.4 = (bf16[128,192]{0,1:T(8,128)(2,1)}, bf16[128,192]{0,1:T(8,128)(2,1)}, u32[]{:S(2)}, u32[]{:S(2)}) collective-permute-start(bf16[128,192]{0,1:T(8,128)(2,1)} %pad_maximum_fusion.7), channel_id=1, source_target_pairs={{4,0},{8,4},{12,8},{16,12},{20,16},{24,20},{28,24},{32,28},{36,32}... | collective-permute-start | bytes 147464 | tf_op jit(solution)/shard_map/ppermute | solution.py:22
  70.9 12.8 %collective-permute-start.6 = (bf16[64,64]{1,0:T(8,128)(2,1)S(1)}, bf16[64,64]{1,0:T(8,128)(2,1)S(1)}, u32[]{:S(2)}, u32[]{:S(2)}) collective-permute-start(bf16[64,64]{1,0:T(8,128)(2,1)S(1)} %bitcast.232), channel_id=1, source_target_pairs={{0,4},{4,8},{8,12},{12,16},{16,20},{20,24},{24,28},{28,32},{32,36}... | collective-permute-start | bytes 24584 | tf_op jit(solution)/shard_map/ppermute | solution.py:31
  72.8 13.0 %collective-permute-start.7 = (bf16[64,64]{1,0:T(8,128)(2,1)S(1)}, bf16[64,64]{1,0:T(8,128)(2,1)S(1)}, u32[]{:S(2)}, u32[]{:S(2)}) collective-permute-start(bf16[64,64]{1,0:T(8,128)(2,1)S(1)} %bitcast.234), channel_id=1, source_target_pairs={{4,0},{8,4},{12,8},{16,12},{20,16},{24,20},{28,24},{32,28},{36,32}... | collective-permute-start | bytes 24584 | tf_op jit(solution)/shard_map/ppermute | solution.py:34
  83.7 8.0 %collective-permute-start.5 = (bf16[128,192]{0,1:T(8,128)(2,1)}, bf16[128,192]{0,1:T(8,128)(2,1)S(1)}, u32[]{:S(2)}, u32[]{:S(2)}) collective-permute-start(bf16[128,192]{0,1:T(8,128)(2,1)} %pad_maximum_fusion.7), channel_id=1, source_target_pairs={{8,0},{12,4},{16,8},{20,12},{24,16},{28,20},{32,24},{36,28},{40,32... | collective-permute-start | bytes 147464 | tf_op jit(solution)/shard_map/ppermute | solution.py:22
  100.0 28.7 %copy-start.6 = (bf16[4,384,96]{1,2,0:T(8,128)(2,1)S(1)}, bf16[4,384,96]{1,2,0:T(8,128)(2,1)}, u32[]{:S(2)}) copy-start(bf16[4,384,96]{1,2,0:T(8,128)(2,1)} %param.21) | copy-start | bytes 884740
  101.8 25.9 %collective-permute-start.12 = (bf16[128,192]{1,0:T(8,128)(2,1)}, bf16[128,192]{1,0:T(8,128)(2,1)}, u32[]{:S(2)}, u32[]{:S(2)}) collective-permute-start(bf16[128,192]{1,0:T(8,128)(2,1)} %convert_element_type.246), channel_id=1, source_target_pairs={{8,0},{12,4},{16,8},{20,12},{24,16},{28,20},{32,24},{36,28},{40,32... | collective-permute-start | bytes 147464 | tf_op jit(solution)/shard_map/ppermute | solution.py:22
  107.5 20.2 %collective-permute-start.13 = (bf16[128,192]{1,0:T(8,128)(2,1)}, bf16[128,192]{1,0:T(8,128)(2,1)}, u32[]{:S(2)}, u32[]{:S(2)}) collective-permute-start(bf16[128,192]{1,0:T(8,128)(2,1)} %convert_element_type.248), channel_id=1, source_target_pairs={{4,0},{8,4},{12,8},{16,12},{20,16},{24,20},{28,24},{32,28},{36,32}... | collective-permute-start | bytes 147464 | tf_op jit(solution)/shard_map/ppermute | solution.py:22
  111.6 16.1 %collective-permute-start.14 = (bf16[128,192]{1,0:T(8,128)(2,1)}, bf16[128,192]{1,0:T(8,128)(2,1)}, u32[]{:S(2)}, u32[]{:S(2)}) collective-permute-start(bf16[128,192]{1,0:T(8,128)(2,1)} %convert_element_type.250), channel_id=1, source_target_pairs={{508,0},{0,4},{4,8},{8,12},{12,16},{16,20},{20,24},{24,28},{28,32}... | collective-permute-start | bytes 147464 | tf_op jit(solution)/shard_map/ppermute | solution.py:22
  114.8 12.9 %collective-permute-start.15 = (bf16[128,192]{1,0:T(8,128)(2,1)}, bf16[128,192]{1,0:T(8,128)(2,1)S(1)}, u32[]{:S(2)}, u32[]{:S(2)}) collective-permute-start(bf16[128,192]{1,0:T(8,128)(2,1)} %convert_element_type.252), channel_id=1, source_target_pairs={{504,0},{508,4},{0,8},{4,12},{8,16},{12,20},{16,24},{20,28},{24,32... | collective-permute-start | bytes 147464 | tf_op jit(solution)/shard_map/ppermute | solution.py:22
  121.4 8.1 %collective-permute-start.8 = (bf16[1216,128]{1,0:T(8,128)(2,1)}, bf16[1216,128]{1,0:T(8,128)(2,1)}, u32[]{:S(2)}, u32[]{:S(2)}) collective-permute-start(bf16[1216,128]{1,0:T(8,128)(2,1)} %select_convert_fusion), channel_id=1, source_target_pairs={{0,1},{1,0},{2,3},{3,2},{4,5},{5,4},{6,7},{7,6},{8,9},{9,8},{10,11... | collective-permute-start | bytes 933896 | tf_op jit(solution)/shard_map/ppermute | solution.py:57
  130.6 7.6 %collective-permute-start.9 = (bf16[608,128]{1,0:T(8,128)(2,1)S(1)}, bf16[608,128]{1,0:T(8,128)(2,1)S(1)}, u32[]{:S(2)}, u32[]{:S(2)}) collective-permute-start(bf16[608,128]{1,0:T(8,128)(2,1)S(1)} %select_convert_fusion.1), channel_id=1, source_target_pairs={{0,2},{1,3},{2,0},{3,1},{4,6},{5,7},{6,4},{7,5},{8,10},{9,11},{10,... | collective-permute-start | bytes 466952 | tf_op jit(solution)/shard_map/ppermute | solution.py:61
  133.0 8.2 %collective-permute-start.16 = (bf16[128,384]{1,0:T(8,128)(2,1)S(1)}, bf16[128,384]{1,0:T(8,128)(2,1)S(1)}, u32[]{:S(2)}, u32[]{:S(2)}) collective-permute-start(bf16[128,384]{1,0:T(8,128)(2,1)S(1)} %fusion.67), channel_id=1, source_target_pairs={{0,1},{1,0},{2,3},{3,2},{4,5},{5,4},{6,7},{7,6},{8,9},{9,8},{10,11... | collective-permute-start | bytes 294920 | tf_op jit(solution)/shard_map/ppermute | solution.py:87
  138.2 6.0 %collective-permute-start.10 = (bf16[608,128]{1,0:T(8,128)(2,1)S(1)}, bf16[608,128]{1,0:T(8,128)(2,1)S(1)}, u32[]{:S(2)}, u32[]{:S(2)}) collective-permute-start(bf16[608,128]{1,0:T(8,128)(2,1)S(1)} %add_convert_fusion), channel_id=1, source_target_pairs={{0,2},{1,3},{2,0},{3,1},{4,6},{5,7},{6,4},{7,5},{8,10},{9,11},{10,... | collective-permute-start | bytes 466952 | tf_op jit(solution)/shard_map/ppermute | solution.py:63
  141.3 9.6 %collective-permute-start.17 = (bf16[128,384]{1,0:T(8,128)(2,1)S(1)}, bf16[128,384]{1,0:T(8,128)(2,1)S(1)}, u32[]{:S(2)}, u32[]{:S(2)}) collective-permute-start(bf16[128,384]{1,0:T(8,128)(2,1)S(1)} %add_convert_fusion.2), channel_id=1, source_target_pairs={{0,2},{1,3},{2,0},{3,1},{4,6},{5,7},{6,4},{7,5},{8,10},{9,11},{10,... | collective-permute-start | bytes 294920 | tf_op jit(solution)/shard_map/ppermute | solution.py:89
  144.3 7.8 %collective-permute-start.11 = (bf16[1216,128]{1,0:T(8,128)(2,1)S(1)}, bf16[1216,128]{1,0:T(8,128)(2,1)S(1)}, u32[]{:S(2)}, u32[]{:S(2)}) collective-permute-start(bf16[1216,128]{1,0:T(8,128)(2,1)S(1)} %maximum_select_fusion.1), channel_id=1, source_target_pairs={{0,1},{1,0},{2,3},{3,2},{4,5},{5,4},{6,7},{7,6},{8,9},{9,8},{10,11... | collective-permute-start | bytes 933896 | tf_op jit(solution)/shard_map/ppermute | solution.py:67
  (26 other events, 273.0 us)

commit v13 on v11

--- a/solution.py
+++ b/solution.py
@@ -193,7 +193,7 @@
         jnp.float32
     )
     condition = jnp.dot(normed_low, w_cond, preferred_element_type=jnp.float32)
-    atom_input = (normed_atoms + jnp.dot(token_pick, condition, precision=ONE_HOT_PRECISION)).astype(
+    atom_input = (normed_atoms + jnp.take(condition, token_local, axis=0)).astype(
         jnp.bfloat16
     )
     atom_proj = [

time: 150 us -> 153 us (1.020)
  local copies, waits for them, and re-layouts: 16.1 us -> 21.7 us
  matrix products: 28.7 us -> 26 us
    gather x0 -> x1, local copies, waits for them, and re-layouts: none -> 2.81 us  [body(): jnp.take(condition, token_local, axis=0)]
  transfers between devices with their start and end apart: 16 -> 16, of which waited for: 5 -> 6; matrix products, arithmetic and copies ran while one was open for 12% -> 10% of each run, Pallas kernels for 0% -> 0%
where the time goes in v13:
time: 153 us; the launch traced here: 152 us
  starting transfers between devices  73.6 us (48%)
  matrix products  26 us (17%)
  local copies, waits for them, and re-layouts  21.7 us (14%)
  waiting for transfers between devices  15.4 us (10%)
  other arithmetic  12.3 us (8%)
  between operations  2.71 us (2%)
    ppermute x8, starting transfers between devices, shifted(): return lax.ppermute(block, axis, route)  34.8 us
    ppermute x2, starting transfers between devices, extended_2(): lax.ppermute(lax.slice_in_dim(block, 0, width, axis=dim), axis, backward)  17.2 us
    ppermute x2, starting transfers between devices, extended_2(): lax.ppermute(lax.slice_in_dim(block, block.shape[dim] - width, None, axis...  6.92 us
    ppermute x1, starting transfers between devices, head_sum(): got = lax.ppermute(give.astype(jnp.bfloat16), axis, pair_near)  5.99 us
    ppermute x1, waiting for transfers between devices, head_sum(): got = lax.ppermute(give.astype(jnp.bfloat16), axis, pair_far)  5.34 us
    ppermute x1, waiting for transfers between devices, head_sum(): got = lax.ppermute(own, axis, pair_far)  4.42 us
    ppermute x1, starting transfers between devices, head_sum(): got = lax.ppermute(half, axis, pair_near)  4.03 us
    concatenate x1, local copies, waits for them, and re-layouts, body(): jnp.concatenate([ext_groups[step:step + windows_here] for step in range(g...  3.78 us
  transfers between devices with their start and end apart: 16, of which 6 were waited for; matrix products, arithmetic and copies ran while one was open for 10% of the time, Pallas kernels for 0%

profile of v13, /device:TPU:1, one launch (start us, length us, event | category | flops | bytes accessed | tf_op | source)
XLA Modules:
  0.0 151.6 jit_solution(11718351811142444162)
XLA Ops:
  8.7 2.8 %gather_fusion = f32[1024,128]{1,0:T(8,128)S(1)} fusion(f32[128,128]{1,0:T(8,128)S(1)} %fusion.140, s32[1024]{0:T(1024)S(1)} %broadcast_clamp_fusion), kind=kCustom, calls=%fused_computation | custom fusion | bytes 1052672 | tf_op jit(solution)/shard_map/jit(_take)/gather | solution.py:196
  12.5 3.9 %collective-permute-start = (bf16[64,64]{0,1:T(8,128)(2,1)S(1)}, bf16[64,64]{0,1:T(8,128)(2,1)S(1)}, u32[]{:S(2)}, u32[]{:S(2)}) collective-permute-start(bf16[64,64]{0,1:T(8,128)(2,1)S(1)} %get-tuple-element.56), channel_id=1, source_target_pairs={{0,4},{4,8},{8,12},{12,16},{16,20},{20,24},{24,28},{28,32},{32,36}... | collective-permute-start | bytes 24584 | tf_op jit(solution)/shard_map/ppermute | solution.py:31
  16.5 14.7 %collective-permute-start.1 = (bf16[64,64]{0,1:T(8,128)(2,1)S(1)}, bf16[64,64]{0,1:T(8,128)(2,1)S(1)}, u32[]{:S(2)}, u32[]{:S(2)}) collective-permute-start(bf16[64,64]{0,1:T(8,128)(2,1)S(1)} %get-tuple-element.55), channel_id=1, source_target_pairs={{4,0},{8,4},{12,8},{16,12},{20,16},{24,20},{28,24},{32,28},{36,32}... | collective-permute-start | bytes 24584 | tf_op jit(solution)/shard_map/ppermute | solution.py:34
  39.8 3.8 %concatenate.56 = bf16[32,160,64]{1,2,0:T(8,128)(2,1)} concatenate(bf16[32,32,64]{1,2,0:T(8,128)(2,1)S(1)} %copy.91, bf16[32,32,64]{1,2,0:T(8,128)(2,1)S(1)} %copy.92, bf16[32,32,64]{1,2,0:T(8,128)(2,1)S(1)} %copy.93, bf16[32,32,64]{1,2,0:T(8,128)(2,1)S(1)} %copy.94, bf16[32,32,64]{1,2,0:T(8,128)(2,1)} %copy.95), dimensions={1} | concatenate | bytes 1310720 | tf_op jit(solution)/shard_map/concatenate | solution.py:287
  43.6 1.8 %fusion.11 = bf16[32,128,64]{1,2,0:T(8,128)(2,1)S(1)} fusion(bf16[32,160,64]{1,2,0:T(8,128)(2,1)} %concatenate.56, s32[32,128]{1,0:T(8,128)S(1)} %iota_add_fusion), kind=kOutput, calls=%fused_computation.16 | convolution fusion | flops 84803584 | bytes 1196032 | tf_op jit(solution)/shard_map/wrs,wsf->wrf/dot_general | solution.py:295
  46.8 1.8 %convolution_bitcast_fusion.1 = f32[32,32,1,32]{1,3,0,2:T(8,128)S(1)} fusion(bf16[32,128,64]{1,2,0:T(8,128)(2,1)S(1)} %fusion.11, f32[32,32]{1,0:T(8,128)S(1)} %get-tuple-element.60, f32[32,32,128]{2,1,0:T(8,128)S(1)} %fusion.17), kind=kOutput, calls=%fused_computation.24 | convolution fusion | flops 8782975 | bytes 1458176 | tf_op jit(solution)/shard_map/bhqk,bkhd->bqhd/dot_general | solution.py:114
  49.7 1.8 %convolution_bitcast_fusion = f32[32,128,32]{1,2,0:T(8,128)S(1)} fusion(bf16[32,32,32]{1,0,2:T(8,128)(2,1)S(1)} %reshape.448, f32[32,32]{1,0:T(8,128)S(1)} %get-tuple-element.60, f32[32,32,128]{2,1,0:T(8,128)S(1)} %fusion.17), kind=kOutput, calls=%fused_computation.23 | convolution fusion | flops 8782975 | bytes 1118208 | tf_op jit(solution)/shard_map/bhqk,bqhd->bkhd/dot_general | solution.py:136
  53.5 1.9 %collective-permute-start.2 = (bf16[128,192]{0,1:T(8,128)(2,1)}, bf16[128,192]{0,1:T(8,128)(2,1)S(1)}, u32[]{:S(2)}, u32[]{:S(2)}) collective-permute-start(bf16[128,192]{0,1:T(8,128)(2,1)} %pad_maximum_fusion.6), channel_id=1, source_target_pairs={{504,0},{508,4},{0,8},{4,12},{8,16},{12,20},{16,24},{20,28},{24,32... | collective-permute-start | bytes 147464 | tf_op jit(solution)/shard_map/ppermute | solution.py:22
  55.5 1.9 %collective-permute-start.3 = (bf16[128,192]{0,1:T(8,128)(2,1)}, bf16[128,192]{0,1:T(8,128)(2,1)S(1)}, u32[]{:S(2)}, u32[]{:S(2)}) collective-permute-start(bf16[128,192]{0,1:T(8,128)(2,1)} %pad_maximum_fusion.6), channel_id=1, source_target_pairs={{508,0},{0,4},{4,8},{8,12},{12,16},{16,20},{20,24},{24,28},{28,32}... | collective-permute-start | bytes 147464 | tf_op jit(solution)/shard_map/ppermute | solution.py:22
  57.4 9.1 %collective-permute-start.4 = (bf16[128,192]{0,1:T(8,128)(2,1)}, bf16[128,192]{0,1:T(8,128)(2,1)S(1)}, u32[]{:S(2)}, u32[]{:S(2)}) collective-permute-start(bf16[128,192]{0,1:T(8,128)(2,1)} %pad_maximum_fusion.6), channel_id=1, source_target_pairs={{4,0},{8,4},{12,8},{16,12},{20,16},{24,20},{28,24},{32,28},{36,32}... | collective-permute-start | bytes 147464 | tf_op jit(solution)/shard_map/ppermute | solution.py:22
  69.2 2.5 %collective-permute-start.7 = (bf16[64,64]{1,0:T(8,128)(2,1)S(1)}, bf16[64,64]{1,0:T(8,128)(2,1)S(1)}, u32[]{:S(2)}, u32[]{:S(2)}) collective-permute-start(bf16[64,64]{1,0:T(8,128)(2,1)S(1)} %bitcast.236), channel_id=1, source_target_pairs={{4,0},{8,4},{12,8},{16,12},{20,16},{24,20},{28,24},{32,28},{36,32}... | collective-permute-start | bytes 24584 | tf_op jit(solution)/shard_map/ppermute | solution.py:34
  71.7 3.0 %collective-permute-start.6 = (bf16[64,64]{1,0:T(8,128)(2,1)S(1)}, bf16[64,64]{1,0:T(8,128)(2,1)S(1)}, u32[]{:S(2)}, u32[]{:S(2)}) collective-permute-start(bf16[64,64]{1,0:T(8,128)(2,1)S(1)} %bitcast.234), channel_id=1, source_target_pairs={{0,4},{4,8},{8,12},{12,16},{16,20},{20,24},{24,28},{28,32},{32,36}... | collective-permute-start | bytes 24584 | tf_op jit(solution)/shard_map/ppermute | solution.py:31
  75.8 3.7 %collective-permute-start.5 = (bf16[128,192]{0,1:T(8,128)(2,1)}, bf16[128,192]{0,1:T(8,128)(2,1)S(1)}, u32[]{:S(2)}, u32[]{:S(2)}) collective-permute-start(bf16[128,192]{0,1:T(8,128)(2,1)} %pad_maximum_fusion.6), channel_id=1, source_target_pairs={{8,0},{12,4},{16,8},{20,12},{24,16},{28,20},{32,24},{36,28},{40,32... | collective-permute-start | bytes 147464 | tf_op jit(solution)/shard_map/ppermute | solution.py:22
  79.4 2.6 %collective-permute-done.6 = bf16[64,64]{1,0:T(8,128)(2,1)S(1)} collective-permute-done((bf16[64,64]{1,0:T(8,128)(2,1)S(1)}, bf16[64,64]{1,0:T(8,128)(2,1)S(1)}, u32[]{:S(2)}, u32[]{:S(2)}) %collective-permute-start.6) | collective-permute-done | bytes 8224 | tf_op jit(solution)/shard_map/ppermute | solution.py:31
  98.9 1.9 %collective-permute-start.11 = (bf16[128,192]{1,0:T(8,128)(2,1)S(1)}, bf16[128,192]{1,0:T(8,128)(2,1)S(1)}, u32[]{:S(2)}, u32[]{:S(2)}) collective-permute-start(bf16[128,192]{1,0:T(8,128)(2,1)S(1)} %convert_element_type.226), channel_id=1, source_target_pairs={{504,0},{508,4},{0,8},{4,12},{8,16},{12,20},{16,24},{20,28},{24,32... | collective-permute-start | bytes 147464 | tf_op jit(solution)/shard_map/ppermute | solution.py:22
  100.9 4.4 %collective-permute-start.10 = (bf16[128,192]{1,0:T(8,128)(2,1)S(1)}, bf16[128,192]{1,0:T(8,128)(2,1)S(1)}, u32[]{:S(2)}, u32[]{:S(2)}) collective-permute-start(bf16[128,192]{1,0:T(8,128)(2,1)S(1)} %convert_element_type.224), channel_id=1, source_target_pairs={{508,0},{0,4},{4,8},{8,12},{12,16},{16,20},{20,24},{24,28},{28,32}... | collective-permute-start | bytes 147464 | tf_op jit(solution)/shard_map/ppermute | solution.py:22
  105.4 8.8 %collective-permute-start.9 = (bf16[128,192]{1,0:T(8,128)(2,1)S(1)}, bf16[128,192]{1,0:T(8,128)(2,1)S(1)}, u32[]{:S(2)}, u32[]{:S(2)}) collective-permute-start(bf16[128,192]{1,0:T(8,128)(2,1)S(1)} %convert_element_type.222), channel_id=1, source_target_pairs={{4,0},{8,4},{12,8},{16,12},{20,16},{24,20},{28,24},{32,28},{36,32}... | collective-permute-start | bytes 147464 | tf_op jit(solution)/shard_map/ppermute | solution.py:22
  114.4 3.1 %collective-permute-start.8 = (bf16[128,192]{1,0:T(8,128)(2,1)S(1)}, bf16[128,192]{1,0:T(8,128)(2,1)S(1)}, u32[]{:S(2)}, u32[]{:S(2)}) collective-permute-start(bf16[128,192]{1,0:T(8,128)(2,1)S(1)} %convert_element_type.220), channel_id=1, source_target_pairs={{8,0},{12,4},{16,8},{20,12},{24,16},{28,20},{32,24},{36,28},{40,32... | collective-permute-start | bytes 147464 | tf_op jit(solution)/shard_map/ppermute | solution.py:22
  121.9 6.0 %collective-permute-start.12 = (bf16[1408,128]{1,0:T(8,128)(2,1)S(1)}, bf16[1408,128]{1,0:T(8,128)(2,1)S(1)}, u32[]{:S(2)}, u32[]{:S(2)}) collective-permute-start(bf16[1408,128]{1,0:T(8,128)(2,1)S(1)} %select_convert_fusion), channel_id=1, source_target_pairs={{0,1},{1,0},{2,3},{3,2},{4,5},{5,4},{6,7},{7,6},{8,9},{9,8},{10,11... | collective-permute-start | bytes 1081352 | tf_op jit(solution)/shard_map/ppermute | solution.py:57
  129.4 2.3 %collective-permute-start.13 = (bf16[704,128]{1,0:T(8,128)(2,1)S(1)}, bf16[704,128]{1,0:T(8,128)(2,1)S(1)}, u32[]{:S(2)}, u32[]{:S(2)}) collective-permute-start(bf16[704,128]{1,0:T(8,128)(2,1)S(1)} %select_convert_fusion.1), channel_id=1, source_target_pairs={{0,2},{1,3},{2,0},{3,1},{4,6},{5,7},{6,4},{7,5},{8,10},{9,11},{10,... | collective-permute-start | bytes 540680 | tf_op jit(solution)/shard_map/ppermute | solution.py:61
  131.7 5.3 %collective-permute-done.13 = bf16[704,128]{1,0:T(8,128)(2,1)S(1)} collective-permute-done((bf16[704,128]{1,0:T(8,128)(2,1)S(1)}, bf16[704,128]{1,0:T(8,128)(2,1)S(1)}, u32[]{:S(2)}, u32[]{:S(2)}) %collective-permute-start.13) | collective-permute-done | bytes 180256 | tf_op jit(solution)/shard_map/ppermute | solution.py:61
  137.1 2.3 %collective-permute-start.14 = (bf16[704,128]{1,0:T(8,128)(2,1)S(1)}, bf16[704,128]{1,0:T(8,128)(2,1)S(1)}, u32[]{:S(2)}, u32[]{:S(2)}) collective-permute-start(bf16[704,128]{1,0:T(8,128)(2,1)S(1)} %add_convert_fusion), channel_id=1, source_target_pairs={{0,2},{1,3},{2,0},{3,1},{4,6},{5,7},{6,4},{7,5},{8,10},{9,11},{10,... | collective-permute-start | bytes 540680 | tf_op jit(solution)/shard_map/ppermute | solution.py:63
  139.4 4.4 %collective-permute-done.14 = bf16[704,128]{1,0:T(8,128)(2,1)S(1)} collective-permute-done((bf16[704,128]{1,0:T(8,128)(2,1)S(1)}, bf16[704,128]{1,0:T(8,128)(2,1)S(1)}, u32[]{:S(2)}, u32[]{:S(2)}) %collective-permute-start.14) | collective-permute-done | bytes 180256 | tf_op jit(solution)/shard_map/ppermute | solution.py:63
  143.9 4.0 %collective-permute-start.15 = (bf16[1408,128]{1,0:T(8,128)(2,1)S(1)}, bf16[1408,128]{1,0:T(8,128)(2,1)S(1)}, u32[]{:S(2)}, u32[]{:S(2)}) collective-permute-start(bf16[1408,128]{1,0:T(8,128)(2,1)S(1)} %maximum_select_fusion.1), channel_id=1, source_target_pairs={{0,1},{1,0},{2,3},{3,2},{4,5},{5,4},{6,7},{7,6},{8,9},{9,8},{10,11... | collective-permute-start | bytes 1081352 | tf_op jit(solution)/shard_map/ppermute | solution.py:67
  (222 shorter events, 50.8 us)
Async XLA Ops:
  0.6 48.5 %copy-start = (bf16[1024,128]{1,0:T(8,128)(2,1)S(1)}, bf16[1024,128]{1,0:T(8,128)(2,1)}, u32[]{:S(2)}) copy-start(bf16[1024,128]{1,0:T(8,128)(2,1)} %param.33) | copy-start | bytes 786436
  8.6 22.6 %copy-start.5 = (bf16[4,384,96]{1,2,0:T(8,128)(2,1)S(1)}, bf16[4,384,96]{1,2,0:T(8,128)(2,1)}, u32[]{:S(2)}) copy-start(bf16[4,384,96]{1,2,0:T(8,128)(2,1)} %param.21) | copy-start | bytes 884740
  11.5 22.1 %copy-start.33 = (s32[32]{0:T(128)S(1)}, s32[32]{0:T(128)}, u32[]{:S(2)}) copy-start(s32[32]{0:T(128)} %param.31) | copy-start | bytes 388
  11.5 23.5 %copy-start.34 = (s32[1,4]{1,0:T(1,128)S(1)}, s32[1,4]{1,0:T(1,128)}, u32[]{:S(2)}) copy-start(s32[1,4]{1,0:T(1,128)} %param.28) | copy-start | bytes 52
  12.5 23.9 %collective-permute-start = (bf16[64,64]{0,1:T(8,128)(2,1)S(1)}, bf16[64,64]{0,1:T(8,128)(2,1)S(1)}, u32[]{:S(2)}, u32[]{:S(2)}) collective-permute-start(bf16[64,64]{0,1:T(8,128)(2,1)S(1)} %get-tuple-element.56), channel_id=1, source_target_pairs={{0,4},{4,8},{8,12},{12,16},{16,20},{20,24},{24,28},{28,32},{32,36}... | collective-permute-start | bytes 24584 | tf_op jit(solution)/shard_map/ppermute | solution.py:31
  16.5 19.9 %collective-permute-start.1 = (bf16[64,64]{0,1:T(8,128)(2,1)S(1)}, bf16[64,64]{0,1:T(8,128)(2,1)S(1)}, u32[]{:S(2)}, u32[]{:S(2)}) collective-permute-start(bf16[64,64]{0,1:T(8,128)(2,1)S(1)} %get-tuple-element.55), channel_id=1, source_target_pairs={{4,0},{8,4},{12,8},{16,12},{20,16},{24,20},{28,24},{32,28},{36,32}... | collective-permute-start | bytes 24584 | tf_op jit(solution)/shard_map/ppermute | solution.py:34
  53.5 31.8 %collective-permute-start.2 = (bf16[128,192]{0,1:T(8,128)(2,1)}, bf16[128,192]{0,1:T(8,128)(2,1)S(1)}, u32[]{:S(2)}, u32[]{:S(2)}) collective-permute-start(bf16[128,192]{0,1:T(8,128)(2,1)} %pad_maximum_fusion.6), channel_id=1, source_target_pairs={{504,0},{508,4},{0,8},{4,12},{8,16},{12,20},{16,24},{20,28},{24,32... | collective-permute-start | bytes 147464 | tf_op jit(solution)/shard_map/ppermute | solution.py:22
  55.5 30.1 %collective-permute-start.3 = (bf16[128,192]{0,1:T(8,128)(2,1)}, bf16[128,192]{0,1:T(8,128)(2,1)S(1)}, u32[]{:S(2)}, u32[]{:S(2)}) collective-permute-start(bf16[128,192]{0,1:T(8,128)(2,1)} %pad_maximum_fusion.6), channel_id=1, source_target_pairs={{508,0},{0,4},{4,8},{8,12},{12,16},{16,20},{20,24},{24,28},{28,32}... | collective-permute-start | bytes 147464 | tf_op jit(solution)/shard_map/ppermute | solution.py:22
  57.4 28.5 %collective-permute-start.4 = (bf16[128,192]{0,1:T(8,128)(2,1)}, bf16[128,192]{0,1:T(8,128)(2,1)S(1)}, u32[]{:S(2)}, u32[]{:S(2)}) collective-permute-start(bf16[128,192]{0,1:T(8,128)(2,1)} %pad_maximum_fusion.6), channel_id=1, source_target_pairs={{4,0},{8,4},{12,8},{16,12},{20,16},{24,20},{28,24},{32,28},{36,32}... | collective-permute-start | bytes 147464 | tf_op jit(solution)/shard_map/ppermute | solution.py:22
  69.2 6.6 %collective-permute-start.7 = (bf16[64,64]{1,0:T(8,128)(2,1)S(1)}, bf16[64,64]{1,0:T(8,128)(2,1)S(1)}, u32[]{:S(2)}, u32[]{:S(2)}) collective-permute-start(bf16[64,64]{1,0:T(8,128)(2,1)S(1)} %bitcast.236), channel_id=1, source_target_pairs={{4,0},{8,4},{12,8},{16,12},{20,16},{24,20},{28,24},{32,28},{36,32}... | collective-permute-start | bytes 24584 | tf_op jit(solution)/shard_map/ppermute | solution.py:34
  71.7 10.4 %collective-permute-start.6 = (bf16[64,64]{1,0:T(8,128)(2,1)S(1)}, bf16[64,64]{1,0:T(8,128)(2,1)S(1)}, u32[]{:S(2)}, u32[]{:S(2)}) collective-permute-start(bf16[64,64]{1,0:T(8,128)(2,1)S(1)} %bitcast.234), channel_id=1, source_target_pairs={{0,4},{4,8},{8,12},{12,16},{16,20},{20,24},{24,28},{28,32},{32,36}... | collective-permute-start | bytes 24584 | tf_op jit(solution)/shard_map/ppermute | solution.py:31
  75.8 10.4 %collective-permute-start.5 = (bf16[128,192]{0,1:T(8,128)(2,1)}, bf16[128,192]{0,1:T(8,128)(2,1)S(1)}, u32[]{:S(2)}, u32[]{:S(2)}) collective-permute-start(bf16[128,192]{0,1:T(8,128)(2,1)} %pad_maximum_fusion.6), channel_id=1, source_target_pairs={{8,0},{12,4},{16,8},{20,12},{24,16},{28,20},{32,24},{36,28},{40,32... | collective-permute-start | bytes 147464 | tf_op jit(solution)/shard_map/ppermute | solution.py:22
  96.3 25.1 %copy-start.2 = (bf16[128,384]{1,0:T(8,128)(2,1)S(1)}, bf16[128,384]{1,0:T(8,128)(2,1)}, u32[]{:S(2)}) copy-start(bf16[128,384]{1,0:T(8,128)(2,1)} %param.17) | copy-start | bytes 294916
  96.3 25.1 %copy-start.17 = (bf16[128,96]{0,1:T(8,128)(2,1)S(1)}, bf16[128,96]{0,1:T(8,128)(2,1)}, u32[]{:S(2)}) copy-start(bf16[128,96]{0,1:T(8,128)(2,1)} %get-tuple-element.49) | copy-start | bytes 73732
  96.3 25.1 %copy-start.26 = (f32[384]{0:T(512)S(1)}, f32[384]{0:T(512)}, u32[]{:S(2)}) copy-start(f32[384]{0:T(512)} %param.19) | copy-start | bytes 4612
  96.3 25.1 %copy-start.30 = (f32[128]{0:T(128)S(1)}, f32[128]{0:T(128)}, u32[]{:S(2)}) copy-start(f32[128]{0:T(128)} %copy-done.29) | copy-start | bytes 1540
  98.9 21.6 %collective-permute-start.11 = (bf16[128,192]{1,0:T(8,128)(2,1)S(1)}, bf16[128,192]{1,0:T(8,128)(2,1)S(1)}, u32[]{:S(2)}, u32[]{:S(2)}) collective-permute-start(bf16[128,192]{1,0:T(8,128)(2,1)S(1)} %convert_element_type.226), channel_id=1, source_target_pairs={{504,0},{508,4},{0,8},{4,12},{8,16},{12,20},{16,24},{20,28},{24,32... | collective-permute-start | bytes 147464 | tf_op jit(solution)/shard_map/ppermute | solution.py:22
  100.9 19.5 %collective-permute-start.10 = (bf16[128,192]{1,0:T(8,128)(2,1)S(1)}, bf16[128,192]{1,0:T(8,128)(2,1)S(1)}, u32[]{:S(2)}, u32[]{:S(2)}) collective-permute-start(bf16[128,192]{1,0:T(8,128)(2,1)S(1)} %convert_element_type.224), channel_id=1, source_target_pairs={{508,0},{0,4},{4,8},{8,12},{12,16},{16,20},{20,24},{24,28},{28,32}... | collective-permute-start | bytes 147464 | tf_op jit(solution)/shard_map/ppermute | solution.py:22
  105.4 15.0 %collective-permute-start.9 = (bf16[128,192]{1,0:T(8,128)(2,1)S(1)}, bf16[128,192]{1,0:T(8,128)(2,1)S(1)}, u32[]{:S(2)}, u32[]{:S(2)}) collective-permute-start(bf16[128,192]{1,0:T(8,128)(2,1)S(1)} %convert_element_type.222), channel_id=1, source_target_pairs={{4,0},{8,4},{12,8},{16,12},{20,16},{24,20},{28,24},{32,28},{36,32}... | collective-permute-start | bytes 147464 | tf_op jit(solution)/shard_map/ppermute | solution.py:22
  114.4 6.5 %collective-permute-start.8 = (bf16[128,192]{1,0:T(8,128)(2,1)S(1)}, bf16[128,192]{1,0:T(8,128)(2,1)S(1)}, u32[]{:S(2)}, u32[]{:S(2)}) collective-permute-start(bf16[128,192]{1,0:T(8,128)(2,1)S(1)} %convert_element_type.220), channel_id=1, source_target_pairs={{8,0},{12,4},{16,8},{20,12},{24,16},{28,20},{32,24},{36,28},{40,32... | collective-permute-start | bytes 147464 | tf_op jit(solution)/shard_map/ppermute | solution.py:22
  121.9 7.3 %collective-permute-start.12 = (bf16[1408,128]{1,0:T(8,128)(2,1)S(1)}, bf16[1408,128]{1,0:T(8,128)(2,1)S(1)}, u32[]{:S(2)}, u32[]{:S(2)}) collective-permute-start(bf16[1408,128]{1,0:T(8,128)(2,1)S(1)} %select_convert_fusion), channel_id=1, source_target_pairs={{0,1},{1,0},{2,3},{3,2},{4,5},{5,4},{6,7},{7,6},{8,9},{9,8},{10,11... | collective-permute-start | bytes 1081352 | tf_op jit(solution)/shard_map/ppermute | solution.py:57
  129.4 7.7 %collective-permute-start.13 = (bf16[704,128]{1,0:T(8,128)(2,1)S(1)}, bf16[704,128]{1,0:T(8,128)(2,1)S(1)}, u32[]{:S(2)}, u32[]{:S(2)}) collective-permute-start(bf16[704,128]{1,0:T(8,128)(2,1)S(1)} %select_convert_fusion.1), channel_id=1, source_target_pairs={{0,2},{1,3},{2,0},{3,1},{4,6},{5,7},{6,4},{7,5},{8,10},{9,11},{10,... | collective-permute-start | bytes 540680 | tf_op jit(solution)/shard_map/ppermute | solution.py:61
  137.1 6.7 %collective-permute-start.14 = (bf16[704,128]{1,0:T(8,128)(2,1)S(1)}, bf16[704,128]{1,0:T(8,128)(2,1)S(1)}, u32[]{:S(2)}, u32[]{:S(2)}) collective-permute-start(bf16[704,128]{1,0:T(8,128)(2,1)S(1)} %add_convert_fusion), channel_id=1, source_target_pairs={{0,2},{1,3},{2,0},{3,1},{4,6},{5,7},{6,4},{7,5},{8,10},{9,11},{10,... | collective-permute-start | bytes 540680 | tf_op jit(solution)/shard_map/ppermute | solution.py:63
  143.9 5.3 %collective-permute-start.15 = (bf16[1408,128]{1,0:T(8,128)(2,1)S(1)}, bf16[1408,128]{1,0:T(8,128)(2,1)S(1)}, u32[]{:S(2)}, u32[]{:S(2)}) collective-permute-start(bf16[1408,128]{1,0:T(8,128)(2,1)S(1)} %maximum_select_fusion.1), channel_id=1, source_target_pairs={{0,1},{1,0},{2,3},{3,2},{4,5},{5,4},{6,7},{7,6},{8,9},{9,8},{10,11... | collective-permute-start | bytes 1081352 | tf_op jit(solution)/shard_map/ppermute | solution.py:67
  (28 other events, 213.8 us)

commit v14 on v11

--- a/solution.py
+++ b/solution.py
@@ -44,7 +44,7 @@
     for part in parts:
         for col in range(part.shape[1] // 128):
             pieces.append(part[:, col * 128 : (col + 1) * 128])
-    buf = jnp.concatenate(pieces, axis=0)
+    buf = jnp.concatenate(pieces, axis=0).astype(jnp.bfloat16)
     rows = buf.shape[0]
     place = lax.axis_index(axis)
     low_bit = place % 2
@@ -55,7 +55,7 @@
     keep = jnp.where(low_bit == 0, halves[0], halves[1])
     give = jnp.where(low_bit == 0, halves[1], halves[0])
     got = lax.ppermute(give.astype(jnp.bfloat16), axis, pair_near)
-    summed = (keep + got.astype(jnp.float32)).reshape(2, rows // 4, 128)
+    summed = (keep.astype(jnp.float32) + got.astype(jnp.float32)).reshape(2, rows // 4, 128)
     keep = jnp.where(high_bit == 0, summed[0], summed[1])
     give = jnp.where(high_bit == 0, summed[1], summed[0])
     got = lax.ppermute(give.astype(jnp.bfloat16), axis, pair_far)

time: 150 us -> 144 us (0.960)
  matrix products: 28.7 us -> 22.6 us
  waiting for transfers between devices: 15 us -> 18.1 us
  local copies, waits for them, and re-layouts: 16.1 us -> 14.3 us
    ppermute x8, waiting for transfers between devices: 0.02 us -> 2.54 us  [shifted(): return lax.ppermute(block, axis, route)]
    dot_general x1, matrix products: 2.08 us -> 0.49 us  [body(): jnp.einsum('bsc,bsx->cx', selector_mask.astype(jnp.float32), returned_fla...]
  transfers between devices with their start and end apart: 16 -> 16, of which waited for: 5 -> 6; matrix products, arithmetic and copies ran while one was open for 12% -> 9% of each run, Pallas kernels for 0% -> 0%
where the time goes in v14:
time: 144 us; the launch traced here: 143 us
  starting transfers between devices  73.1 us (51%)
  matrix products  22.6 us (16%)
  waiting for transfers between devices  18.1 us (13%)
  local copies, waits for them, and re-layouts  14.3 us (10%)
  other arithmetic  12.5 us (9%)
  between operations  2.62 us (2%)
    ppermute x8, starting transfers between devices, shifted(): return lax.ppermute(block, axis, route)  34.4 us
    ppermute x2, starting transfers between devices, extended_2(): lax.ppermute(lax.slice_in_dim(block, 0, width, axis=dim), axis, backward)  17.4 us
    ppermute x2, starting transfers between devices, extended_2(): lax.ppermute(lax.slice_in_dim(block, block.shape[dim] - width, None, axis...  6.74 us
    ppermute x1, starting transfers between devices, head_sum(): got = lax.ppermute(give.astype(jnp.bfloat16), axis, pair_near)  5.98 us
    ppermute x1, waiting for transfers between devices, head_sum(): got = lax.ppermute(give.astype(jnp.bfloat16), axis, pair_far)  5.35 us
    ppermute x1, waiting for transfers between devices, head_sum(): got = lax.ppermute(own, axis, pair_far)  4.43 us
    ppermute x1, starting transfers between devices, head_sum(): got = lax.ppermute(half, axis, pair_near)  4.03 us
    ppermute x2, waiting for transfers between devices, extended_2(): lax.ppermute(lax.slice_in_dim(block, block.shape[dim] - width, None, axis...  3.24 us
  transfers between devices with their start and end apart: 16, of which 6 were waited for; matrix products, arithmetic and copies ran while one was open for 9% of the time, Pallas kernels for 0%

profile of v14, /device:TPU:1, one launch (start us, length us, event | category | flops | bytes accessed | tf_op | source)
XLA Modules:
  0.0 143.2 jit_solution(9680351636597600637)
XLA Ops:
  11.3 3.9 %collective-permute-start = (bf16[64,64]{0,1:T(8,128)(2,1)S(1)}, bf16[64,64]{0,1:T(8,128)(2,1)S(1)}, u32[]{:S(2)}, u32[]{:S(2)}) collective-permute-start(bf16[64,64]{0,1:T(8,128)(2,1)S(1)} %get-tuple-element.50), channel_id=1, source_target_pairs={{0,4},{4,8},{8,12},{12,16},{16,20},{20,24},{24,28},{28,32},{32,36}... | collective-permute-start | bytes 24584 | tf_op jit(solution)/shard_map/ppermute | solution.py:31
  15.3 14.7 %collective-permute-start.1 = (bf16[64,64]{0,1:T(8,128)(2,1)S(1)}, bf16[64,64]{0,1:T(8,128)(2,1)S(1)}, u32[]{:S(2)}, u32[]{:S(2)}) collective-permute-start(bf16[64,64]{0,1:T(8,128)(2,1)S(1)} %get-tuple-element.49), channel_id=1, source_target_pairs={{4,0},{8,4},{12,8},{16,12},{20,16},{24,20},{28,24},{32,28},{36,32}... | collective-permute-start | bytes 24584 | tf_op jit(solution)/shard_map/ppermute | solution.py:34
  38.4 2.3 %concatenate.57 = bf16[32,160,64]{1,2,0:T(8,128)(2,1)} concatenate(bf16[32,32,64]{1,2,0:T(8,128)(2,1)S(1)} %copy.91, bf16[32,32,64]{1,2,0:T(8,128)(2,1)S(1)} %copy.92, bf16[32,32,64]{1,2,0:T(8,128)(2,1)S(1)} %copy.93, bf16[32,32,64]{1,2,0:T(8,128)(2,1)S(1)} %copy.94, bf16[32,32,64]{1,2,0:T(8,128)(2,1)S(1)} %copy.95), dimensions={1} | concatenate | bytes 1310720 | tf_op jit(solution)/shard_map/concatenate | solution.py:287
  40.7 1.9 %fusion.11 = bf16[32,128,64]{1,2,0:T(8,128)(2,1)S(1)} fusion(bf16[32,160,64]{1,2,0:T(8,128)(2,1)} %concatenate.57, s32[32,128]{1,0:T(8,128)} %iota_add_fusion), kind=kOutput, calls=%fused_computation.15 | convolution fusion | flops 84803584 | bytes 1196032 | tf_op jit(solution)/shard_map/wrs,wsf->wrf/dot_general | solution.py:295
  44.8 1.8 %convolution_bitcast_fusion.1 = f32[32,32,1,32]{1,3,0,2:T(8,128)S(1)} fusion(bf16[32,128,64]{1,2,0:T(8,128)(2,1)S(1)} %fusion.11, f32[32,32]{1,0:T(8,128)S(1)} %get-tuple-element.60, f32[32,32,128]{2,1,0:T(8,128)S(1)} %fusion.17), kind=kOutput, calls=%fused_computation.23 | convolution fusion | flops 8782975 | bytes 1458176 | tf_op jit(solution)/shard_map/bhqk,bkhd->bqhd/dot_general | solution.py:114
  47.7 1.8 %convolution_bitcast_fusion = f32[32,128,32]{1,2,0:T(8,128)S(1)} fusion(bf16[32,32,32]{1,0,2:T(8,128)(2,1)S(1)} %reshape.430, f32[32,32]{1,0:T(8,128)S(1)} %get-tuple-element.60, f32[32,32,128]{2,1,0:T(8,128)S(1)} %fusion.17), kind=kOutput, calls=%fused_computation.22 | convolution fusion | flops 8782975 | bytes 1118208 | tf_op jit(solution)/shard_map/bhqk,bqhd->bkhd/dot_general | solution.py:136
  51.6 1.9 %collective-permute-start.2 = (bf16[128,192]{0,1:T(8,128)(2,1)S(1)}, bf16[128,192]{0,1:T(8,128)(2,1)S(1)}, u32[]{:S(2)}, u32[]{:S(2)}) collective-permute-start(bf16[128,192]{0,1:T(8,128)(2,1)S(1)} %copy-done.9), channel_id=1, source_target_pairs={{504,0},{508,4},{0,8},{4,12},{8,16},{12,20},{16,24},{20,28},{24,32... | collective-permute-start | bytes 147464 | tf_op jit(solution)/shard_map/ppermute | solution.py:22
  53.5 1.9 %collective-permute-start.3 = (bf16[128,192]{0,1:T(8,128)(2,1)S(1)}, bf16[128,192]{0,1:T(8,128)(2,1)S(1)}, u32[]{:S(2)}, u32[]{:S(2)}) collective-permute-start(bf16[128,192]{0,1:T(8,128)(2,1)S(1)} %copy-done.9), channel_id=1, source_target_pairs={{508,0},{0,4},{4,8},{8,12},{12,16},{16,20},{20,24},{24,28},{28,32}... | collective-permute-start | bytes 147464 | tf_op jit(solution)/shard_map/ppermute | solution.py:22
  55.5 9.1 %collective-permute-start.4 = (bf16[128,192]{0,1:T(8,128)(2,1)S(1)}, bf16[128,192]{0,1:T(8,128)(2,1)S(1)}, u32[]{:S(2)}, u32[]{:S(2)}) collective-permute-start(bf16[128,192]{0,1:T(8,128)(2,1)S(1)} %copy-done.9), channel_id=1, source_target_pairs={{4,0},{8,4},{12,8},{16,12},{20,16},{24,20},{28,24},{32,28},{36,32}... | collective-permute-start | bytes 147464 | tf_op jit(solution)/shard_map/ppermute | solution.py:22
  67.2 2.6 %collective-permute-start.7 = (bf16[64,64]{1,0:T(8,128)(2,1)S(1)}, bf16[64,64]{1,0:T(8,128)(2,1)S(1)}, u32[]{:S(2)}, u32[]{:S(2)}) collective-permute-start(bf16[64,64]{1,0:T(8,128)(2,1)S(1)} %bitcast.234), channel_id=1, source_target_pairs={{4,0},{8,4},{12,8},{16,12},{20,16},{24,20},{28,24},{32,28},{36,32}... | collective-permute-start | bytes 24584 | tf_op jit(solution)/shard_map/ppermute | solution.py:34
  69.9 2.8 %collective-permute-start.6 = (bf16[64,64]{1,0:T(8,128)(2,1)S(1)}, bf16[64,64]{1,0:T(8,128)(2,1)S(1)}, u32[]{:S(2)}, u32[]{:S(2)}) collective-permute-start(bf16[64,64]{1,0:T(8,128)(2,1)S(1)} %bitcast.232), channel_id=1, source_target_pairs={{0,4},{4,8},{8,12},{12,16},{16,20},{20,24},{24,28},{28,32},{32,36}... | collective-permute-start | bytes 24584 | tf_op jit(solution)/shard_map/ppermute | solution.py:31
  73.0 3.8 %collective-permute-start.5 = (bf16[128,192]{0,1:T(8,128)(2,1)S(1)}, bf16[128,192]{0,1:T(8,128)(2,1)S(1)}, u32[]{:S(2)}, u32[]{:S(2)}) collective-permute-start(bf16[128,192]{0,1:T(8,128)(2,1)S(1)} %copy-done.9), channel_id=1, source_target_pairs={{8,0},{12,4},{16,8},{20,12},{24,16},{28,20},{32,24},{36,28},{40,32... | collective-permute-start | bytes 147464 | tf_op jit(solution)/shard_map/ppermute | solution.py:22
  76.8 3.2 %collective-permute-done.6 = bf16[64,64]{1,0:T(8,128)(2,1)S(1)} collective-permute-done((bf16[64,64]{1,0:T(8,128)(2,1)S(1)}, bf16[64,64]{1,0:T(8,128)(2,1)S(1)}, u32[]{:S(2)}, u32[]{:S(2)}) %collective-permute-start.6) | collective-permute-done | bytes 8224 | tf_op jit(solution)/shard_map/ppermute | solution.py:31
  91.1 1.9 %collective-permute-start.11 = (bf16[128,192]{1,0:T(8,128)(2,1)S(1)}, bf16[128,192]{1,0:T(8,128)(2,1)S(1)}, u32[]{:S(2)}, u32[]{:S(2)}) collective-permute-start(bf16[128,192]{1,0:T(8,128)(2,1)S(1)} %convert_element_type.227), channel_id=1, source_target_pairs={{504,0},{508,4},{0,8},{4,12},{8,16},{12,20},{16,24},{20,28},{24,32... | collective-permute-start | bytes 147464 | tf_op jit(solution)/shard_map/ppermute | solution.py:22
  93.1 3.8 %collective-permute-start.10 = (bf16[128,192]{1,0:T(8,128)(2,1)S(1)}, bf16[128,192]{1,0:T(8,128)(2,1)S(1)}, u32[]{:S(2)}, u32[]{:S(2)}) collective-permute-start(bf16[128,192]{1,0:T(8,128)(2,1)S(1)} %convert_element_type.225), channel_id=1, source_target_pairs={{508,0},{0,4},{4,8},{8,12},{12,16},{16,20},{20,24},{24,28},{28,32}... | collective-permute-start | bytes 147464 | tf_op jit(solution)/shard_map/ppermute | solution.py:22
  97.0 8.8 %collective-permute-start.9 = (bf16[128,192]{1,0:T(8,128)(2,1)S(1)}, bf16[128,192]{1,0:T(8,128)(2,1)S(1)}, u32[]{:S(2)}, u32[]{:S(2)}) collective-permute-start(bf16[128,192]{1,0:T(8,128)(2,1)S(1)} %convert_element_type.223), channel_id=1, source_target_pairs={{4,0},{8,4},{12,8},{16,12},{20,16},{24,20},{28,24},{32,28},{36,32}... | collective-permute-start | bytes 147464 | tf_op jit(solution)/shard_map/ppermute | solution.py:22
  106.0 3.1 %collective-permute-start.8 = (bf16[128,192]{1,0:T(8,128)(2,1)S(1)}, bf16[128,192]{1,0:T(8,128)(2,1)S(1)}, u32[]{:S(2)}, u32[]{:S(2)}) collective-permute-start(bf16[128,192]{1,0:T(8,128)(2,1)S(1)} %convert_element_type.221), channel_id=1, source_target_pairs={{8,0},{12,4},{16,8},{20,12},{24,16},{28,20},{32,24},{36,28},{40,32... | collective-permute-start | bytes 147464 | tf_op jit(solution)/shard_map/ppermute | solution.py:22
  110.0 2.5 %collective-permute-done.8 = bf16[128,192]{1,0:T(8,128)(2,1)S(1)} collective-permute-done((bf16[128,192]{1,0:T(8,128)(2,1)S(1)}, bf16[128,192]{1,0:T(8,128)(2,1)S(1)}, u32[]{:S(2)}, u32[]{:S(2)}) %collective-permute-start.8) | collective-permute-done | bytes 49184 | tf_op jit(solution)/shard_map/ppermute | solution.py:22
  113.6 6.0 %collective-permute-start.12 = (bf16[1408,128]{1,0:T(8,128)(2,1)S(1)}, bf16[1408,128]{1,0:T(8,128)(2,1)S(1)}, u32[]{:S(2)}, u32[]{:S(2)}) collective-permute-start(bf16[1408,128]{1,0:T(8,128)(2,1)S(1)} %broadcast_select_fusion), channel_id=1, source_target_pairs={{0,1},{1,0},{2,3},{3,2},{4,5},{5,4},{6,7},{7,6},{8,9},{9,8},{10,11... | collective-permute-start | bytes 1081352 | tf_op jit(solution)/shard_map/ppermute | solution.py:57
  121.0 2.3 %collective-permute-start.13 = (bf16[704,128]{1,0:T(8,128)(2,1)S(1)}, bf16[704,128]{1,0:T(8,128)(2,1)S(1)}, u32[]{:S(2)}, u32[]{:S(2)}) collective-permute-start(bf16[704,128]{1,0:T(8,128)(2,1)S(1)} %select_convert_fusion), channel_id=1, source_target_pairs={{0,2},{1,3},{2,0},{3,1},{4,6},{5,7},{6,4},{7,5},{8,10},{9,11},{10,... | collective-permute-start | bytes 540680 | tf_op jit(solution)/shard_map/ppermute | solution.py:61
  123.3 5.3 %collective-permute-done.13 = bf16[704,128]{1,0:T(8,128)(2,1)S(1)} collective-permute-done((bf16[704,128]{1,0:T(8,128)(2,1)S(1)}, bf16[704,128]{1,0:T(8,128)(2,1)S(1)}, u32[]{:S(2)}, u32[]{:S(2)}) %collective-permute-start.13) | collective-permute-done | bytes 180256 | tf_op jit(solution)/shard_map/ppermute | solution.py:61
  128.7 2.3 %collective-permute-start.14 = (bf16[704,128]{1,0:T(8,128)(2,1)S(1)}, bf16[704,128]{1,0:T(8,128)(2,1)S(1)}, u32[]{:S(2)}, u32[]{:S(2)}) collective-permute-start(bf16[704,128]{1,0:T(8,128)(2,1)S(1)} %add_convert_fusion), channel_id=1, source_target_pairs={{0,2},{1,3},{2,0},{3,1},{4,6},{5,7},{6,4},{7,5},{8,10},{9,11},{10,... | collective-permute-start | bytes 540680 | tf_op jit(solution)/shard_map/ppermute | solution.py:63
  131.0 4.4 %collective-permute-done.14 = bf16[704,128]{1,0:T(8,128)(2,1)S(1)} collective-permute-done((bf16[704,128]{1,0:T(8,128)(2,1)S(1)}, bf16[704,128]{1,0:T(8,128)(2,1)S(1)}, u32[]{:S(2)}, u32[]{:S(2)}) %collective-permute-start.14) | collective-permute-done | bytes 180256 | tf_op jit(solution)/shard_map/ppermute | solution.py:63
  135.6 4.0 %collective-permute-start.15 = (bf16[1408,128]{1,0:T(8,128)(2,1)S(1)}, bf16[1408,128]{1,0:T(8,128)(2,1)S(1)}, u32[]{:S(2)}, u32[]{:S(2)}) collective-permute-start(bf16[1408,128]{1,0:T(8,128)(2,1)S(1)} %maximum_select_fusion.1), channel_id=1, source_target_pairs={{0,1},{1,0},{2,3},{3,2},{4,5},{5,4},{6,7},{7,6},{8,9},{9,8},{10,11... | collective-permute-start | bytes 1081352 | tf_op jit(solution)/shard_map/ppermute | solution.py:67
  (200 shorter events, 44.2 us)
Async XLA Ops:
  0.6 46.6 %copy-start = (bf16[1024,128]{1,0:T(8,128)(2,1)S(1)}, bf16[1024,128]{1,0:T(8,128)(2,1)}, u32[]{:S(2)}) copy-start(bf16[1024,128]{1,0:T(8,128)(2,1)} %param.33) | copy-start | bytes 786436
  0.7 29.4 %copy-start.5 = (bf16[4,384,96]{1,2,0:T(8,128)(2,1)S(1)}, bf16[4,384,96]{1,2,0:T(8,128)(2,1)}, u32[]{:S(2)}) copy-start(bf16[4,384,96]{1,2,0:T(8,128)(2,1)} %param.21) | copy-start | bytes 884740
  1.8 30.6 %copy-start.24 = (s32[32]{0:T(128)S(1)}, s32[32]{0:T(128)}, u32[]{:S(2)}) copy-start(s32[32]{0:T(128)} %param.31) | copy-start | bytes 388
  1.8 32.6 %copy-start.25 = (s32[1,4]{1,0:T(1,128)S(1)}, s32[1,4]{1,0:T(1,128)}, u32[]{:S(2)}) copy-start(s32[1,4]{1,0:T(1,128)} %param.28) | copy-start | bytes 52
  11.3 24.4 %collective-permute-start = (bf16[64,64]{0,1:T(8,128)(2,1)S(1)}, bf16[64,64]{0,1:T(8,128)(2,1)S(1)}, u32[]{:S(2)}, u32[]{:S(2)}) collective-permute-start(bf16[64,64]{0,1:T(8,128)(2,1)S(1)} %get-tuple-element.50), channel_id=1, source_target_pairs={{0,4},{4,8},{8,12},{12,16},{16,20},{20,24},{24,28},{28,32},{32,36}... | collective-permute-start | bytes 24584 | tf_op jit(solution)/shard_map/ppermute | solution.py:31
  15.3 20.5 %collective-permute-start.1 = (bf16[64,64]{0,1:T(8,128)(2,1)S(1)}, bf16[64,64]{0,1:T(8,128)(2,1)S(1)}, u32[]{:S(2)}, u32[]{:S(2)}) collective-permute-start(bf16[64,64]{0,1:T(8,128)(2,1)S(1)} %get-tuple-element.49), channel_id=1, source_target_pairs={{4,0},{8,4},{12,8},{16,12},{20,16},{24,20},{28,24},{32,28},{36,32}... | collective-permute-start | bytes 24584 | tf_op jit(solution)/shard_map/ppermute | solution.py:34
  51.6 31.2 %collective-permute-start.2 = (bf16[128,192]{0,1:T(8,128)(2,1)S(1)}, bf16[128,192]{0,1:T(8,128)(2,1)S(1)}, u32[]{:S(2)}, u32[]{:S(2)}) collective-permute-start(bf16[128,192]{0,1:T(8,128)(2,1)S(1)} %copy-done.9), channel_id=1, source_target_pairs={{504,0},{508,4},{0,8},{4,12},{8,16},{12,20},{16,24},{20,28},{24,32... | collective-permute-start | bytes 147464 | tf_op jit(solution)/shard_map/ppermute | solution.py:22
  53.5 29.5 %collective-permute-start.3 = (bf16[128,192]{0,1:T(8,128)(2,1)S(1)}, bf16[128,192]{0,1:T(8,128)(2,1)S(1)}, u32[]{:S(2)}, u32[]{:S(2)}) collective-permute-start(bf16[128,192]{0,1:T(8,128)(2,1)S(1)} %copy-done.9), channel_id=1, source_target_pairs={{508,0},{0,4},{4,8},{8,12},{12,16},{16,20},{20,24},{24,28},{28,32}... | collective-permute-start | bytes 147464 | tf_op jit(solution)/shard_map/ppermute | solution.py:22
  55.5 27.8 %collective-permute-start.4 = (bf16[128,192]{0,1:T(8,128)(2,1)S(1)}, bf16[128,192]{0,1:T(8,128)(2,1)S(1)}, u32[]{:S(2)}, u32[]{:S(2)}) collective-permute-start(bf16[128,192]{0,1:T(8,128)(2,1)S(1)} %copy-done.9), channel_id=1, source_target_pairs={{4,0},{8,4},{12,8},{16,12},{20,16},{24,20},{28,24},{32,28},{36,32}... | collective-permute-start | bytes 147464 | tf_op jit(solution)/shard_map/ppermute | solution.py:22
  67.2 5.7 %collective-permute-start.7 = (bf16[64,64]{1,0:T(8,128)(2,1)S(1)}, bf16[64,64]{1,0:T(8,128)(2,1)S(1)}, u32[]{:S(2)}, u32[]{:S(2)}) collective-permute-start(bf16[64,64]{1,0:T(8,128)(2,1)S(1)} %bitcast.234), channel_id=1, source_target_pairs={{4,0},{8,4},{12,8},{16,12},{20,16},{24,20},{28,24},{32,28},{36,32}... | collective-permute-start | bytes 24584 | tf_op jit(solution)/shard_map/ppermute | solution.py:34
  69.9 10.2 %collective-permute-start.6 = (bf16[64,64]{1,0:T(8,128)(2,1)S(1)}, bf16[64,64]{1,0:T(8,128)(2,1)S(1)}, u32[]{:S(2)}, u32[]{:S(2)}) collective-permute-start(bf16[64,64]{1,0:T(8,128)(2,1)S(1)} %bitcast.232), channel_id=1, source_target_pairs={{0,4},{4,8},{8,12},{12,16},{16,20},{20,24},{24,28},{28,32},{32,36}... | collective-permute-start | bytes 24584 | tf_op jit(solution)/shard_map/ppermute | solution.py:31
  73.0 10.6 %collective-permute-start.5 = (bf16[128,192]{0,1:T(8,128)(2,1)S(1)}, bf16[128,192]{0,1:T(8,128)(2,1)S(1)}, u32[]{:S(2)}, u32[]{:S(2)}) collective-permute-start(bf16[128,192]{0,1:T(8,128)(2,1)S(1)} %copy-done.9), channel_id=1, source_target_pairs={{8,0},{12,4},{16,8},{20,12},{24,16},{28,20},{32,24},{36,28},{40,32... | collective-permute-start | bytes 147464 | tf_op jit(solution)/shard_map/ppermute | solution.py:22
  88.7 20.6 %copy-start.7 = (bf16[384,128]{1,0:T(8,128)(2,1)S(1)}, bf16[384,128]{1,0:T(8,128)(2,1)}, u32[]{:S(2)}) copy-start(bf16[384,128]{1,0:T(8,128)(2,1)} %param.23) | copy-start | bytes 294916
  89.4 23.5 %copy-start.2 = (bf16[128,384]{1,0:T(8,128)(2,1)S(1)}, bf16[128,384]{1,0:T(8,128)(2,1)}, u32[]{:S(2)}) copy-start(bf16[128,384]{1,0:T(8,128)(2,1)} %param.17) | copy-start | bytes 294916
  89.4 23.5 %copy-start.17 = (f32[384]{0:T(512)S(1)}, f32[384]{0:T(512)}, u32[]{:S(2)}) copy-start(f32[384]{0:T(512)} %param.19) | copy-start | bytes 4612
  89.4 23.5 %copy-start.19 = (f32[128]{0:T(128)S(1)}, f32[128]{0:T(128)}, u32[]{:S(2)}) copy-start(f32[128]{0:T(128)} %copy-done.18) | copy-start | bytes 1540
  91.1 18.8 %collective-permute-start.11 = (bf16[128,192]{1,0:T(8,128)(2,1)S(1)}, bf16[128,192]{1,0:T(8,128)(2,1)S(1)}, u32[]{:S(2)}, u32[]{:S(2)}) collective-permute-start(bf16[128,192]{1,0:T(8,128)(2,1)S(1)} %convert_element_type.227), channel_id=1, source_target_pairs={{504,0},{508,4},{0,8},{4,12},{8,16},{12,20},{16,24},{20,28},{24,32... | collective-permute-start | bytes 147464 | tf_op jit(solution)/shard_map/ppermute | solution.py:22
  93.1 16.8 %collective-permute-start.10 = (bf16[128,192]{1,0:T(8,128)(2,1)S(1)}, bf16[128,192]{1,0:T(8,128)(2,1)S(1)}, u32[]{:S(2)}, u32[]{:S(2)}) collective-permute-start(bf16[128,192]{1,0:T(8,128)(2,1)S(1)} %convert_element_type.225), channel_id=1, source_target_pairs={{508,0},{0,4},{4,8},{8,12},{12,16},{16,20},{20,24},{24,28},{28,32}... | collective-permute-start | bytes 147464 | tf_op jit(solution)/shard_map/ppermute | solution.py:22
  97.0 12.9 %collective-permute-start.9 = (bf16[128,192]{1,0:T(8,128)(2,1)S(1)}, bf16[128,192]{1,0:T(8,128)(2,1)S(1)}, u32[]{:S(2)}, u32[]{:S(2)}) collective-permute-start(bf16[128,192]{1,0:T(8,128)(2,1)S(1)} %convert_element_type.223), channel_id=1, source_target_pairs={{4,0},{8,4},{12,8},{16,12},{20,16},{24,20},{28,24},{32,28},{36,32}... | collective-permute-start | bytes 147464 | tf_op jit(solution)/shard_map/ppermute | solution.py:22
  106.0 6.5 %collective-permute-start.8 = (bf16[128,192]{1,0:T(8,128)(2,1)S(1)}, bf16[128,192]{1,0:T(8,128)(2,1)S(1)}, u32[]{:S(2)}, u32[]{:S(2)}) collective-permute-start(bf16[128,192]{1,0:T(8,128)(2,1)S(1)} %convert_element_type.221), channel_id=1, source_target_pairs={{8,0},{12,4},{16,8},{20,12},{24,16},{28,20},{32,24},{36,28},{40,32... | collective-permute-start | bytes 147464 | tf_op jit(solution)/shard_map/ppermute | solution.py:22
  113.6 7.3 %collective-permute-start.12 = (bf16[1408,128]{1,0:T(8,128)(2,1)S(1)}, bf16[1408,128]{1,0:T(8,128)(2,1)S(1)}, u32[]{:S(2)}, u32[]{:S(2)}) collective-permute-start(bf16[1408,128]{1,0:T(8,128)(2,1)S(1)} %broadcast_select_fusion), channel_id=1, source_target_pairs={{0,1},{1,0},{2,3},{3,2},{4,5},{5,4},{6,7},{7,6},{8,9},{9,8},{10,11... | collective-permute-start | bytes 1081352 | tf_op jit(solution)/shard_map/ppermute | solution.py:57
  121.0 7.7 %collective-permute-start.13 = (bf16[704,128]{1,0:T(8,128)(2,1)S(1)}, bf16[704,128]{1,0:T(8,128)(2,1)S(1)}, u32[]{:S(2)}, u32[]{:S(2)}) collective-permute-start(bf16[704,128]{1,0:T(8,128)(2,1)S(1)} %select_convert_fusion), channel_id=1, source_target_pairs={{0,2},{1,3},{2,0},{3,1},{4,6},{5,7},{6,4},{7,5},{8,10},{9,11},{10,... | collective-permute-start | bytes 540680 | tf_op jit(solution)/shard_map/ppermute | solution.py:61
  128.7 6.7 %collective-permute-start.14 = (bf16[704,128]{1,0:T(8,128)(2,1)S(1)}, bf16[704,128]{1,0:T(8,128)(2,1)S(1)}, u32[]{:S(2)}, u32[]{:S(2)}) collective-permute-start(bf16[704,128]{1,0:T(8,128)(2,1)S(1)} %add_convert_fusion), channel_id=1, source_target_pairs={{0,2},{1,3},{2,0},{3,1},{4,6},{5,7},{6,4},{7,5},{8,10},{9,11},{10,... | collective-permute-start | bytes 540680 | tf_op jit(solution)/shard_map/ppermute | solution.py:63
  135.6 5.3 %collective-permute-start.15 = (bf16[1408,128]{1,0:T(8,128)(2,1)S(1)}, bf16[1408,128]{1,0:T(8,128)(2,1)S(1)}, u32[]{:S(2)}, u32[]{:S(2)}) collective-permute-start(bf16[1408,128]{1,0:T(8,128)(2,1)S(1)} %maximum_select_fusion.1), channel_id=1, source_target_pairs={{0,1},{1,0},{2,3},{3,2},{4,5},{5,4},{6,7},{7,6},{8,9},{9,8},{10,11... | collective-permute-start | bytes 1081352 | tf_op jit(solution)/shard_map/ppermute | solution.py:67
  (19 other events, 114.8 us)
